TPU v7x, 32 devices: a whole 2x2x4 slice. The times are simulated.
32 devices in a mesh: group: 4 (over z), member: 8 (over y, x, core).
Axes of the slice: x: 2, y: 2, z: 4, core: 2. Of those that a mesh axis runs over, the one named last changes fastest.
Arguments:
- tile_values: bfloat16 [128, 512, 512], P(('group', 'member')), may hold values from -0.0625 to 0.0625
- tile_lists: int32 [128, 3], P(('group', 'member')), may hold values from 0 to 7, as said below
- owner_map: int32 [4, 8], P('group'), may hold values from 0 to 7, as said below
- inverses: bfloat16 [32, 512, 512], P(('group', 'member')), as said below
- excitations: float32 [3, 32, 32, 512], P(None, ('group', 'member')), may hold values from -6 to 6
- history: bfloat16 [2, 32, 32, 512], P(None, ('group', 'member')), may hold values from -6 to 6
Outputs:
- currents: float32 [3, 32, 32, 512], P(None, ('group', 'member'))
Inputs may be any that keep to these rules, and one draw needn't show every extreme that they name: `owner_map`: each row is a permutation of the members. `tile_lists`: rows d * 4 to d * 4 + 3 belong to device d = g * 8 + m. Delay tag 0 marks an empty slot; a live tile has a delay tag of 1 to 2, an observer block of its own group (g * 2 to g * 2 + 1), and the live tiles of one device take their source blocks from different groups (source block // 2). Every device has 2 or more live tiles; in every group some device has 4. `inverses`: the 4 owners of one block hold the same matrix.
All inputs are finite; a program needn't handle non-finite values.
Results may differ from a plain program's by a relative error of at most 0.025.
Values may be sent and summed in bfloat16 or wider, within the bound.
No kernel may reach another device: no remote copies, remote signals or barrier semaphores. Data moves between devices by JAX's collectives and lax.ppermute only.
A program may use at most 64 MiB of HBM per device.

v0:
```python
import jax
import jax.numpy as jnp
from jax import lax
from jax.sharding import PartitionSpec as P

BLOCK = 512
EXCITE = 128
OWNERS = 4
DELAYS = 2
STEPS = 3


def select_rows(timeline, peer_lists, times_wanted, wanted, group_here, group_blocks, last_time):
    source = peer_lists[:, :, 0]
    from_here = source // group_blocks == group_here
    chosen_mask = wanted & from_here
    clipped = jnp.clip(times_wanted, 0, last_time)
    flat_index = clipped * group_blocks + source % group_blocks
    picked = jnp.sum(jnp.where(chosen_mask, flat_index, 0), axis=1)
    filled = jnp.any(chosen_mask, axis=1)
    picked_rows = jnp.take(timeline, picked, axis=0)
    return jnp.where(filled[:, None, None], picked_rows, jnp.zeros_like(picked_rows))


def body(tile_values, tile_lists, owner_map, inverses, excitations, history):
    members = lax.axis_size("member")
    group_blocks = members // OWNERS
    group_here = lax.axis_index("group")
    tiles_here = tile_lists.shape[0]
    last_time = DELAYS + STEPS - 1
    owners = owner_map[0]
    member_ids = jnp.arange(members, dtype=jnp.int32)
    matches = owners[:, None] == member_ids[None, :]
    slot_of_member = jnp.sum(jnp.where(matches, member_ids[:, None], 0), axis=0)
    peer_lists = lax.all_gather(tile_lists, "group", axis=0, tiled=True).reshape(-1, tiles_here, 3)
    peer_delays = peer_lists[:, :, 2]
    peer_active = peer_delays > 0
    gathered = lax.all_gather(history, "member", axis=1, tiled=True)
    ordered = jnp.take(gathered, owners, axis=1).reshape(DELAYS * group_blocks, EXCITE, BLOCK)
    timeline = jnp.concatenate(
        [ordered, jnp.zeros((STEPS * group_blocks, EXCITE, BLOCK), jnp.bfloat16)], axis=0
    )
    source_group = tile_lists[:, 0] // group_blocks
    observer_local = tile_lists[:, 1] % group_blocks
    delays_here = tile_lists[:, 2]
    block_ids = jnp.arange(group_blocks, dtype=jnp.int32)
    results = []
    for step in range(STEPS):
        outgoing = select_rows(
            timeline,
            peer_lists,
            DELAYS + step - peer_delays,
            peer_active,
            group_here,
            group_blocks,
            last_time,
        )
        incoming = lax.all_to_all(outgoing, "group", split_axis=0, concat_axis=0, tiled=True)
        blocks_in = jnp.take(incoming, source_group, axis=0)
        spread = (
            (observer_local[None, :] == block_ids[:, None]) & (delays_here > 0)[None, :]
        ).astype(jnp.float32)
        terms = jnp.einsum(
            "kes,kso->keo", blocks_in, tile_values, preferred_element_type=jnp.float32
        )
        slots = (
            jnp.einsum("bk,keo->beo", spread, terms, precision=lax.Precision.HIGHEST)
            .astype(jnp.bfloat16)
            .reshape(members, -1, BLOCK)
        )
        sent = jnp.take(slots, slot_of_member, axis=0).astype(jnp.float32)
        field = lax.psum_scatter(
            sent.astype(jnp.bfloat16), "member", scatter_dimension=0, tiled=True
        ).astype(jnp.float32)
        residual = (excitations[step] - field).astype(jnp.bfloat16)
        current = jnp.dot(residual[0], inverses[0], preferred_element_type=jnp.float32)
        results.append(current)
        if step + 1 < STEPS:
            piece = current.astype(jnp.bfloat16)[None]
            whole = lax.all_gather(piece, "member", axis=0, tiled=True)
            placed = jnp.take(whole, owners, axis=0).reshape(group_blocks, EXCITE, BLOCK)
            timeline = lax.dynamic_update_slice_in_dim(
                timeline, placed, (DELAYS + step) * group_blocks, 0
            )
    return jnp.stack(results)[:, None]


def solution(mesh):
    placed = (
        P(("group", "member"), None, None),
        P(("group", "member"), None),
        P("group", None),
        P(("group", "member"), None, None),
        P(None, ("group", "member"), None, None),
        P(None, ("group", "member"), None, None),
    )
    return jax.shard_map(
        body,
        mesh=mesh,
        in_specs=placed,
        out_specs=P(None, ("group", "member"), None, None),
        check_vma=False,
    )
```

profile of v0, /device:TPU:0, one launch (start us, length us, event | category | flops | bytes accessed | tf_op | source)
XLA Modules:
  0.0 260.4 jit_solution(3077911240592838105)
XLA Ops:
  6.5 13.8 %all-gather.2 = s32[4,4,3]{2,1,0:T(4,128)S(1)} all-gather(s32[1,4,3]{2,1,0:T(4,128)} %bitcast.100), channel_id=1, replica_groups=mesh['group'=4,'member'=8] {'group'}, dimensions={0}, use_global_device_ids=true | all-gather | bytes 240 | tf_op jit(solution)/shard_map/all_gather | solution.py:35
  23.6 10.1 %all_gather.13 = bf16[2,8,32,512]{3,2,1,0:T(8,128)(2,1)S(1)} all-gather(bf16[2,1,32,512]{3,2,1,0:T(8,128)(2,1)} %param.17), channel_id=1, replica_groups=mesh['group'=4,'member'=8] {'member'}, dimensions={1}, use_global_device_ids=true | all-gather | bytes 589824 | tf_op jit(solution)/shard_map/all_gather | solution.py:38
  34.6 1.4 gather_fusion.1
  36.0 2.0 select_select_fusion.2
  38.0 4.1 %all-to-all-start = ((bf16[4,128,512]{2,1,0:T(8,128)(2,1)}), bf16[4,128,512]{2,1,0:T(8,128)(2,1)}, u32[]{:S(2)}, u32[]{:S(2)}) async-start(bf16[4,128,512]{2,1,0:T(8,128)(2,1)} %select_select_fusion.2), calls=%async_computation | async-start | bytes 1048576 | tf_op jit(solution)/shard_map/all_to_all | solution.py:58
  42.6 14.8 %all-to-all-done = bf16[4,128,512]{2,1,0:T(8,128)(2,1)} async-done(((bf16[4,128,512]{2,1,0:T(8,128)(2,1)}), bf16[4,128,512]{2,1,0:T(8,128)(2,1)}, u32[]{:S(2)}, u32[]{:S(2)}) %all-to-all-start) | async-done | bytes 524320 | tf_op jit(solution)/shard_map/all_to_all | solution.py:58
  57.5 2.4 gather_fusion.2
  59.9 1.5 fusion.12
  61.4 1.7 convolution_convert_fusion.2
  63.8 2.2 gather_fusion.3
  66.1 1.7 broadcast_select_fusion.5
  67.9 31.8 %reduce-scatter.4.cloned.1.call-done = bf16[1,32,512]{2,1,0:T(8,128)(2,1)} async-done(((bf16[8,32,512]{2,1,0:T(8,128)(2,1)}), bf16[1,32,512]{2,1,0:T(8,128)(2,1)}) %reduce-scatter.4.cloned.1.call-update) | async-done | bytes 32784 | tf_op jit(solution)/shard_map/reduce_scatter | solution.py:72
  99.7 1.3 fusion.43
  101.0 10.2 %all-gather = bf16[256,512]{1,0:T(8,128)(2,1)} all-gather(bf16[32,512]{1,0:T(8,128)(2,1)S(1)} %get-tuple-element.21), channel_id=2, replica_groups=mesh['group'=4,'member'=8] {'member'}, dimensions={0}, use_global_device_ids=true | all-gather | bytes 294912 | tf_op jit(solution)/shard_map/all_gather | solution.py:80
  111.2 2.2 gather_fusion.4
  114.5 1.4 gather_fusion.5
  115.9 1.2 select_select_fusion.1
  117.1 19.5 %all_to_all.15 = bf16[4,128,512]{2,1,0:T(8,128)(2,1)} all-to-all(bf16[4,128,512]{2,1,0:T(8,128)(2,1)S(1)} %select_select_fusion.1), channel_id=1, replica_groups=mesh['group'=4,'member'=8] {'group'}, dimensions={0} | all-to-all | bytes 1048576 | tf_op jit(solution)/shard_map/all_to_all | solution.py:58
  136.6 2.4 gather_fusion.6
  139.0 1.5 fusion.10
  140.5 1.7 convolution_convert_fusion.1
  143.0 2.2 gather_fusion.7
  145.2 1.7 broadcast_select_fusion.4
  148.1 30.7 %reduce-scatter.6.cloned.1.call-done = bf16[1,32,512]{2,1,0:T(8,128)(2,1)} async-done(((bf16[8,32,512]{2,1,0:T(8,128)(2,1)}), bf16[1,32,512]{2,1,0:T(8,128)(2,1)}) %reduce-scatter.6.cloned.1.call-update) | async-done | bytes 32784 | tf_op jit(solution)/shard_map/reduce_scatter | solution.py:72
  178.8 1.3 fusion.44
  180.1 10.3 %all-gather.1 = bf16[256,512]{1,0:T(8,128)(2,1)} all-gather(bf16[32,512]{1,0:T(8,128)(2,1)S(1)} %get-tuple-element.23), channel_id=3, replica_groups=mesh['group'=4,'member'=8] {'member'}, dimensions={0}, use_global_device_ids=true | all-gather | bytes 294912 | tf_op jit(solution)/shard_map/all_gather | solution.py:80
  190.3 2.3 gather_fusion.8
  193.7 1.5 gather_fusion.9
  195.2 1.2 select_select_fusion
  196.4 19.4 %all_to_all.16 = bf16[4,128,512]{2,1,0:T(8,128)(2,1)S(1)} all-to-all(bf16[4,128,512]{2,1,0:T(8,128)(2,1)S(1)} %select_select_fusion), channel_id=1, replica_groups=mesh['group'=4,'member'=8] {'group'}, dimensions={0} | all-to-all | bytes 1048576 | tf_op jit(solution)/shard_map/all_to_all | solution.py:58
  217.0 1.7 convolution_convert_fusion
  220.2 31.9 %reduce-scatter.8.cloned.1.call-done = bf16[1,32,512]{2,1,0:T(8,128)(2,1)} async-done(((bf16[8,32,512]{2,1,0:T(8,128)(2,1)}), bf16[1,32,512]{2,1,0:T(8,128)(2,1)}) %reduce-scatter.8.cloned.1.call-update) | async-done | bytes 32784 | tf_op jit(solution)/shard_map/reduce_scatter | solution.py:72
  (69 shorter events, 13.8 us)
Async XLA Ops:
  6.5 53.4 %copy-start = (bf16[4,512,512]{2,1,0:T(8,128)(2,1)S(1)}, bf16[4,512,512]{2,1,0:T(8,128)(2,1)}, u32[]{:S(2)}) copy-start(bf16[4,512,512]{2,1,0:T(8,128)(2,1)} %param.12) | copy-start | bytes 6291460
  23.4 90.0 %copy-start.3 = (pred[8]{0:T(512)(128)(4,1)}, pred[8]{0:T(512)(128)(4,1)S(1)}, u32[]{:S(2)}) copy-start(pred[8]{0:T(512)(128)(4,1)S(1)} %get-tuple-element.29) | copy-start | bytes 28
  34.5 7.7 %copy-start.2 = (s32[4,3]{1,0:T(4,128)S(1)}, s32[4,3]{1,0:T(4,128)}, u32[]{:S(2)}) copy-start(s32[4,3]{1,0:T(4,128)} %param.13) | copy-start | bytes 148
  38.0 19.5 %all-to-all-start = ((bf16[4,128,512]{2,1,0:T(8,128)(2,1)}), bf16[4,128,512]{2,1,0:T(8,128)(2,1)}, u32[]{:S(2)}, u32[]{:S(2)}) async-start(bf16[4,128,512]{2,1,0:T(8,128)(2,1)} %select_select_fusion.2), calls=%async_computation | async-start | bytes 1048576 | tf_op jit(solution)/shard_map/all_to_all | solution.py:58
  42.1 57.6 %reduce-scatter.4.cloned.1.call-start = ((), (), s32[]{:S(2)}) async-start(), calls=%async_computation.6 | async-start | bytes 294912 | tf_op jit(solution)/shard_map/reduce_scatter | solution.py:72
  42.4 96.6 %copy-start.4 = (pred[4]{0:T(512)(128)(4,1)}, pred[4]{0:T(512)(128)(4,1)S(1)}, u32[]{:S(2)}) copy-start(pred[4]{0:T(512)(128)(4,1)S(1)} %get-tuple-element.17) | copy-start | bytes 16
  42.4 94.2 %copy-start.7 = (s32[1024]{0:T(1024)}, s32[1024]{0:T(1024)S(1)}, u32[]{:S(2)}) copy-start(s32[1024]{0:T(1024)S(1)} %pad_clamp_fusion.4) | copy-start | bytes 12292
  42.4 100.5 %copy-start.6 = (s32[1024]{0:T(1024)}, s32[1024]{0:T(1024)S(1)}, u32[]{:S(2)}) copy-start(s32[1024]{0:T(1024)S(1)} %pad_clamp_fusion.3) | copy-start | bytes 12292
  61.4 6.4 %copy-start.9 = (s32[1,8]{1,0:T(1,128)S(1)}, s32[1,8]{1,0:T(1,128)}, u32[]{:S(2)}) copy-start(s32[1,8]{1,0:T(1,128)} %param.14) | copy-start | bytes 100
  67.8 111.0 %reduce-scatter.6.cloned.1.call-start = ((), (), s32[]{:S(2)}) async-start(), calls=%async_computation.7 | async-start | bytes 294912 | tf_op jit(solution)/shard_map/reduce_scatter | solution.py:72
  67.9 49.1 %copy-start.8 = (s32[1024]{0:T(1024)}, s32[1024]{0:T(1024)S(1)}, u32[]{:S(2)}) copy-start(s32[1024]{0:T(1024)S(1)} %pad_clamp_fusion.2) | copy-start | bytes 12292
  146.9 105.2 %reduce-scatter.8.cloned.1.call-start = ((), (), s32[]{:S(2)}) async-start(), calls=%async_computation.8 | async-start | bytes 294912 | tf_op jit(solution)/shard_map/reduce_scatter | solution.py:72
  195.2 21.3 %copy-start.5 = (pred[4]{0:T(512)(128)(4,1)S(1)}, pred[4]{0:T(512)(128)(4,1)}, u32[]{:S(2)}) copy-start(pred[4]{0:T(512)(128)(4,1)} %copy-done.4) | copy-start | bytes 16
  217.0 35.1 %copy-start.1 = (bf16[1,512,512]{2,1,0:T(8,128)(2,1)S(1)}, bf16[1,512,512]{2,1,0:T(8,128)(2,1)}, u32[]{:S(2)}) copy-start(bf16[1,512,512]{2,1,0:T(8,128)(2,1)} %param.15) | copy-start | bytes 1572868
Sparse Core Ops, SparseCore 0:
  67.9 31.7 reduce-scatter.3
  147.1 31.7 reduce-scatter.5
  220.4 31.7 reduce-scatter.7
where the time goes:
time: 261 us; the launch traced here: 260 us
  waiting for transfers between devices  109 us (42%)
  blocking collectives  83.3 us (32%)
  local copies, waits for them, and re-layouts  22.1 us (8%)
  other arithmetic  15.9 us (6%)
  between operations  13.5 us (5%)
  matrix products  12.2 us (5%)
  starting transfers between devices  4.25 us (2%)
    reduce_scatter x3, waiting for transfers between devices, body(): lax.psum_scatter(sent.astype(jnp.bfloat16), 'member', scatter_dimension=0...  94.4 us
    all_to_all x2, blocking collectives, body(): lax.all_to_all(outgoing, 'group', split_axis=0, concat_axis=0, tiled=True)  38.9 us
    all_gather x2, blocking collectives, body(): whole = lax.all_gather(piece, 'member', axis=0, tiled=True)  20.5 us
    all_to_all x1, waiting for transfers between devices, body(): lax.all_to_all(outgoing, 'group', split_axis=0, concat_axis=0, tiled=True)  14.8 us
    all_gather x1, blocking collectives, body(): lax.all_gather(tile_lists, 'group', axis=0, tiled=True)  13.8 us
    all_gather x1, blocking collectives, body(): gathered = lax.all_gather(history, 'member', axis=1, tiled=True)  10.1 us
    gather x3, local copies, waits for them, and re-layouts, body(): blocks_in = jnp.take(incoming, source_group, axis=0)  5.56 us
  transfers between devices with their start and end apart: 4, of which 4 were waited for; matrix products, arithmetic and copies ran while one was open for 1% of the time, Pallas kernels for 0%

commit v1 on v0

v1 whole, which is shorter than its diff:
```python
import jax
import jax.numpy as jnp
from jax import lax
from jax.sharding import PartitionSpec as P

BLOCK = 512
EXCITE = 128
OWNERS = 4
DELAYS = 2
STEPS = 3


def shift_gather(x, axis, n):
    pieces = [x]
    for k in range(1, n):
        pieces.append(lax.ppermute(x, axis, [(i, (i + k) % n) for i in range(n)]))
    return jnp.stack(pieces)


def shift_exchange(x, axis, n, here):
    pieces = [lax.dynamic_index_in_dim(x, here, 0, keepdims=False)]
    for k in range(1, n):
        piece = lax.dynamic_index_in_dim(x, (here + k) % n, 0, keepdims=False)
        pieces.append(lax.ppermute(piece, axis, [(i, (i + k) % n) for i in range(n)]))
    return jnp.stack(pieces)


def select_rows(timeline, peer_lists, times_wanted, wanted, group_here, group_blocks, last_time):
    source = peer_lists[:, :, 0]
    from_here = source // group_blocks == group_here
    chosen_mask = wanted & from_here
    clipped = jnp.clip(times_wanted, 0, last_time)
    flat_index = clipped * group_blocks + source % group_blocks
    picked = jnp.sum(jnp.where(chosen_mask, flat_index, 0), axis=1)
    filled = jnp.any(chosen_mask, axis=1)
    picked_rows = jnp.take(timeline, picked, axis=0)
    return jnp.where(filled[:, None, None], picked_rows, jnp.zeros_like(picked_rows))


def body(tile_values, tile_lists, owner_map, inverses, excitations, history):
    members = lax.axis_size("member")
    groups = lax.axis_size("group")
    group_blocks = members // OWNERS
    share = EXCITE // OWNERS
    group_here = lax.axis_index("group")
    member_here = lax.axis_index("member")
    tiles_here = tile_lists.shape[0]
    last_time = DELAYS + STEPS - 1
    owners = owner_map[0]
    member_ids = jnp.arange(members, dtype=jnp.int32)
    matches = owners[:, None] == member_ids[None, :]
    slot_of_member = jnp.sum(jnp.where(matches, member_ids[:, None], 0), axis=0)
    by_shift = shift_gather(tile_lists, "group", groups)
    peer_lists = jnp.take(by_shift, (group_here - jnp.arange(groups)) % groups, axis=0)
    peer_delays = peer_lists[:, :, 2]
    peer_active = peer_delays > 0
    owner_shift = (member_here - owners) % members
    gathered = shift_gather(history[:, 0], "member", members)
    ordered = jnp.take(gathered, owner_shift, axis=0)
    ordered = jnp.moveaxis(ordered, 1, 0).reshape(DELAYS * group_blocks, EXCITE, BLOCK)
    timeline = jnp.concatenate(
        [ordered, jnp.zeros((STEPS * group_blocks, EXCITE, BLOCK), jnp.bfloat16)], axis=0
    )
    source_group = tile_lists[:, 0] // group_blocks
    observer_local = tile_lists[:, 1] % group_blocks
    delays_here = tile_lists[:, 2]
    source_shift = (group_here - source_group) % groups
    results = []
    for step in range(STEPS):
        outgoing = select_rows(
            timeline,
            peer_lists,
            DELAYS + step - peer_delays,
            peer_active,
            group_here,
            group_blocks,
            last_time,
        )
        incoming = shift_exchange(outgoing, "group", groups, group_here)
        blocks_in = jnp.take(incoming, source_shift, axis=0)
        terms = jnp.einsum(
            "kes,kso->keo", blocks_in, tile_values, preferred_element_type=jnp.float32
        )
        partial_sums = []
        for block in range(group_blocks):
            chosen = (observer_local == block) & (delays_here > 0)
            partial_sums.append(
                jnp.sum(jnp.where(chosen[:, None, None], terms, 0.0), axis=0)
            )
        slots = jnp.stack(partial_sums).astype(jnp.bfloat16).reshape(members, share, BLOCK)
        sent = jnp.take(slots, slot_of_member, axis=0)
        pieces = shift_exchange(sent, "member", members, member_here)
        field = jnp.sum(pieces.astype(jnp.float32), axis=0)
        residual = (excitations[step, 0] - field).astype(jnp.bfloat16)
        current = jnp.dot(residual, inverses[0], preferred_element_type=jnp.float32)
        results.append(current)
        if step + 1 < STEPS:
            whole = shift_gather(current.astype(jnp.bfloat16), "member", members)
            placed = jnp.take(whole, owner_shift, axis=0).reshape(group_blocks, EXCITE, BLOCK)
            timeline = lax.dynamic_update_slice_in_dim(
                timeline, placed, (DELAYS + step) * group_blocks, 0
            )
    return jnp.stack(results)[:, None]


def solution(mesh):
    placed = (
        P(("group", "member"), None, None),
        P(("group", "member"), None),
        P("group", None),
        P(("group", "member"), None, None),
        P(None, ("group", "member"), None, None),
        P(None, ("group", "member"), None, None),
    )
    return jax.shard_map(
        body,
        mesh=mesh,
        in_specs=placed,
        out_specs=P(None, ("group", "member"), None, None),
        check_vma=False,
    )
```

time: 261 us -> 162 us (0.62)
  blocking collectives: 83.3 us -> 0 us
  waiting for transfers between devices: 109 us -> 30.2 us
  starting transfers between devices: 4.25 us -> 68.8 us
  between operations: 13.5 us -> 0.7 us
  local copies, waits for them, and re-layouts: 22.1 us -> 31.3 us
  other arithmetic: 15.9 us -> 19.1 us
  matrix products: 12.2 us -> 9.17 us
    reduce_scatter x3 -> x0, waiting for transfers between devices: 94.4 us -> none  [body(): lax.psum_scatter(sent.astype(jnp.bfloat16), 'member', scatter_dimension=0...]
    ppermute x0 -> x54, starting transfers between devices: none -> 68.8 us  [the longest x30 36.9 us: shift_exchange(): lax.ppermute(piece, axis, [(i, (i + k) % n) for i in range(n)])]
    all_gather x4 -> x0, blocking collectives: 44.4 us -> none  [the longest x2 20.5 us: body(): whole = lax.all_gather(piece, 'member', axis=0, tiled=True)]
    all_to_all x2 -> x0, blocking collectives: 38.9 us -> none  [body(): lax.all_to_all(outgoing, 'group', split_axis=0, concat_axis=0, tiled=True)]
    ppermute x0 -> x54, waiting for transfers between devices: none -> 30.2 us  [the longest x30 28 us: shift_exchange(): lax.ppermute(piece, axis, [(i, (i + k) % n) for i in range(n)])]
    all_to_all x1 -> x0, waiting for transfers between devices: 14.8 us -> none  [body(): lax.all_to_all(outgoing, 'group', split_axis=0, concat_axis=0, tiled=True)]
    unnamed x20 -> x57, local copies, waits for them, and re-layouts: 0.05 us -> 8.36 us
    all_to_all x1 -> x0, starting transfers between devices: 4.13 us -> none  [body(): lax.all_to_all(outgoing, 'group', split_axis=0, concat_axis=0, tiled=True)]
  transfers between devices with their start and end apart: 4 -> 54, of which waited for: 4 -> 19; matrix products, arithmetic and copies ran while one was open for 1% -> 11% of each run, Pallas kernels for 0% -> 0%
where the time goes in v1:
time: 162 us; the launch traced here: 159 us
  starting transfers between devices  68.8 us (42%)
  local copies, waits for them, and re-layouts  31.3 us (19%)
  waiting for transfers between devices  30.2 us (19%)
  other arithmetic  19.1 us (12%)
  matrix products  9.17 us (6%)
    ppermute x30, starting transfers between devices, shift_exchange(): lax.ppermute(piece, axis, [(i, (i + k) % n) for i in range(n)])  36.9 us
    ppermute x24, starting transfers between devices, shift_gather(): pieces.append(lax.ppermute(x, axis, [(i, (i + k) % n) for i in range(n)]))  31.9 us
    ppermute x30, waiting for transfers between devices, shift_exchange(): lax.ppermute(piece, axis, [(i, (i + k) % n) for i in range(n)])  28 us
    unnamed x57, local copies, waits for them, and re-layouts  8.36 us
    gather x3, local copies, waits for them, and re-layouts, body(): blocks_in = jnp.take(incoming, source_shift, axis=0)  5.42 us
    gather x3, local copies, waits for them, and re-layouts, body(): sent = jnp.take(slots, slot_of_member, axis=0)  4.97 us
    dot_general x3, matrix products, body(): current = jnp.dot(residual, inverses[0], preferred_element_type=jnp.float32)  4.81 us
    gather x2, local copies, waits for them, and re-layouts, body(): jnp.take(whole, owner_shift, axis=0).reshape(group_blocks, EXCITE, BLOCK)  4.53 us
  transfers between devices with their start and end apart: 54, of which 19 were waited for; matrix products, arithmetic and copies ran while one was open for 11% of the time, Pallas kernels for 0%

profile of v1, /device:TPU:0, one launch (start us, length us, event | category | flops | bytes accessed | tf_op | source)
XLA Modules:
  0.0 159.3 jit_solution(8798639660273694734)
XLA Ops:
  0.0 3.0 %collective-permute-start = (s32[4,3]{1,0:T(4,128)}, s32[4,3]{1,0:T(4,128)S(1)}, u32[]{:S(2)}, u32[]{:S(2)}) collective-permute-start(s32[4,3]{1,0:T(4,128)} %param.13), channel_id=1, source_target_pairs={{0,8},{8,16},{16,24},{24,0},{1,9},{9,17},{17,25},{25,1},{2,10},{10... | collective-permute-start | bytes 152 | tf_op jit(solution)/shard_map/ppermute | solution.py:16
  3.0 2.6 %collective-permute-start.1 = (s32[4,3]{1,0:T(4,128)}, s32[4,3]{1,0:T(4,128)S(1)}, u32[]{:S(2)}, u32[]{:S(2)}) collective-permute-start(s32[4,3]{1,0:T(4,128)} %param.13), channel_id=1, source_target_pairs={{0,16},{8,24},{16,0},{24,8},{1,17},{9,25},{17,1},{25,9},{2,18},{10... | collective-permute-start | bytes 152 | tf_op jit(solution)/shard_map/ppermute | solution.py:16
  13.7 2.4 %collective-permute-start.5 = (bf16[2,32,512]{2,1,0:T(8,128)(2,1)}, bf16[2,32,512]{2,1,0:T(8,128)(2,1)S(1)}, u32[]{:S(2)}, u32[]{:S(2)}) collective-permute-start(bf16[2,32,512]{2,1,0:T(8,128)(2,1)} %bitcast.286), channel_id=1, source_target_pairs={{0,3},{1,4},{2,5},{3,6},{4,7},{5,0},{6,1},{7,2},{8,11},{9,12},{10,... | collective-permute-start | bytes 196616 | tf_op jit(solution)/shard_map/ppermute | solution.py:16
  20.6 2.4 %collective-permute-start.9 = (bf16[2,32,512]{2,1,0:T(8,128)(2,1)}, bf16[2,32,512]{2,1,0:T(8,128)(2,1)S(1)}, u32[]{:S(2)}, u32[]{:S(2)}) collective-permute-start(bf16[2,32,512]{2,1,0:T(8,128)(2,1)} %bitcast.290), channel_id=1, source_target_pairs={{0,7},{1,0},{2,1},{3,2},{4,3},{5,4},{6,5},{7,6},{8,15},{9,8},{10,9... | collective-permute-start | bytes 196616 | tf_op jit(solution)/shard_map/ppermute | solution.py:16
  29.8 2.8 %collective-permute-start.12 = (bf16[128,512]{1,0:T(8,128)(2,1)S(1)}, bf16[128,512]{1,0:T(8,128)(2,1)S(1)}, u32[]{:S(2)}, u32[]{:S(2)}) collective-permute-start(bf16[128,512]{1,0:T(8,128)(2,1)S(1)} %get-tuple-element.44), channel_id=1, source_target_pairs={{0,24},{8,0},{16,8},{24,16},{1,25},{9,1},{17,9},{25,17},{2,26},{10... | collective-permute-start | bytes 393224 | tf_op jit(solution)/shard_map/ppermute | solution.py:24
  33.1 4.0 %collective-permute-done.10 = bf16[128,512]{1,0:T(8,128)(2,1)S(1)} collective-permute-done((bf16[128,512]{1,0:T(8,128)(2,1)S(1)}, bf16[128,512]{1,0:T(8,128)(2,1)S(1)}, u32[]{:S(2)}, u32[]{:S(2)}) %collective-permute-start.10) | collective-permute-done | bytes 131104 | tf_op jit(solution)/shard_map/ppermute | solution.py:24
  37.0 5.2 %collective-permute-done.11 = bf16[128,512]{1,0:T(8,128)(2,1)S(1)} collective-permute-done((bf16[128,512]{1,0:T(8,128)(2,1)S(1)}, bf16[128,512]{1,0:T(8,128)(2,1)S(1)}, u32[]{:S(2)}, u32[]{:S(2)}) %collective-permute-start.11) | collective-permute-done | bytes 131104 | tf_op jit(solution)/shard_map/ppermute | solution.py:24
  43.1 2.4 %gather_fusion.3 = bf16[4,128,512]{2,1,0:T(8,128)(2,1)} fusion(bf16[4,128,512]{2,1,0:T(8,128)(2,1)} %pad_maximum_fusion, s32[1024]{0:T(1024)S(1)} %pad_clamp_fusion.4), kind=kCustom, calls=%fused_computation.1.clone | custom fusion | bytes 1048592 | tf_op jit(solution)/shard_map/jit(_take)/gather | solution.py:80
  47.9 2.2 %gather_fusion.4 = bf16[8,32,512]{2,1,0:T(8,128)(2,1)} fusion(bf16[8,32,512]{2,1,0:T(8,128)(2,1)} %bitcast.262, s32[1024]{0:T(1024)S(1)} %get-tuple-element.77), kind=kCustom, calls=%fused_computation.2.clone | custom fusion | bytes 524320 | tf_op jit(solution)/shard_map/jit(_take)/gather | solution.py:91
  53.9 1.9 %collective-permute-start.16 = (bf16[32,512]{1,0:T(8,128)(2,1)S(1)}, bf16[32,512]{1,0:T(8,128)(2,1)S(1)}, u32[]{:S(2)}, u32[]{:S(2)}) collective-permute-start(bf16[32,512]{1,0:T(8,128)(2,1)S(1)} %get-tuple-element.66), channel_id=1, source_target_pairs={{0,4},{1,5},{2,6},{3,7},{4,0},{5,1},{6,2},{7,3},{8,12},{9,13},{10,... | collective-permute-start | bytes 98312 | tf_op jit(solution)/shard_map/ppermute | solution.py:24
  55.8 1.9 %collective-permute-start.18 = (bf16[32,512]{1,0:T(8,128)(2,1)S(1)}, bf16[32,512]{1,0:T(8,128)(2,1)S(1)}, u32[]{:S(2)}, u32[]{:S(2)}) collective-permute-start(bf16[32,512]{1,0:T(8,128)(2,1)S(1)} %get-tuple-element.64), channel_id=1, source_target_pairs={{0,6},{1,7},{2,0},{3,1},{4,2},{5,3},{6,4},{7,5},{8,14},{9,15},{10,... | collective-permute-start | bytes 98312 | tf_op jit(solution)/shard_map/ppermute | solution.py:24
  60.7 1.9 %constant_dynamic-update-slice_fusion.23 = (bf16[8,32,512]{2,1,0:T(8,128)(2,1)}, bf16[32,512]{1,0:T(8,128)(2,1)S(1)}, f32[32,512]{1,0:T(8,128)S(1)}) fusion(bf16[1,512,512]{2,1,0:T(8,128)(2,1)} %param.15, f32[32,512]{1,0:T(8,128)S(1)} %convert_reduce_fusion.2, f32[3,1,32,512]{3,2,1,0:T(8,128)} %param.16), kind=kOutput, calls=%fused_computation.96 | convolution fusion | flops 16826368 | bytes 786432 | tf_op jit(solution)/shard_map/dot_general | solution.py:95
  63.1 2.6 %collective-permute-start.21 = (bf16[32,512]{1,0:T(8,128)(2,1)S(1)}, bf16[32,512]{1,0:T(8,128)(2,1)S(1)}, u32[]{:S(2)}, u32[]{:S(2)}) collective-permute-start(bf16[32,512]{1,0:T(8,128)(2,1)S(1)} %get-tuple-element.26), channel_id=1, source_target_pairs={{0,2},{1,3},{2,4},{3,5},{4,6},{5,7},{6,0},{7,1},{8,10},{9,11},{10,... | collective-permute-start | bytes 98312 | tf_op jit(solution)/shard_map/ppermute | solution.py:16
  69.5 2.1 %collective-permute-start.26 = (bf16[32,512]{1,0:T(8,128)(2,1)S(1)}, bf16[32,512]{1,0:T(8,128)(2,1)S(1)}, u32[]{:S(2)}, u32[]{:S(2)}) collective-permute-start(bf16[32,512]{1,0:T(8,128)(2,1)S(1)} %get-tuple-element.26), channel_id=1, source_target_pairs={{0,7},{1,0},{2,1},{3,2},{4,3},{5,4},{6,5},{7,6},{8,15},{9,8},{10,9... | collective-permute-start | bytes 98312 | tf_op jit(solution)/shard_map/ppermute | solution.py:16
  75.3 2.2 %gather_fusion.5 = bf16[8,32,512]{2,1,0:T(8,128)(2,1)} fusion(bf16[8,32,512]{2,1,0:T(8,128)(2,1)} %constant_dynamic-update-slice_fusion.16, s32[1024]{0:T(1024)S(1)} %pad_clamp_fusion.2), kind=kCustom, calls=%fused_computation.7.clone | custom fusion | bytes 524320 | tf_op jit(solution)/shard_map/jit(_take)/gather | solution.py:99
  81.2 2.9 %collective-permute-start.27 = (bf16[128,512]{1,0:T(8,128)(2,1)S(1)}, bf16[128,512]{1,0:T(8,128)(2,1)S(1)}, u32[]{:S(2)}, u32[]{:S(2)}) collective-permute-start(bf16[128,512]{1,0:T(8,128)(2,1)S(1)} %get-tuple-element.42), channel_id=1, source_target_pairs={{0,8},{8,16},{16,24},{24,0},{1,9},{9,17},{17,25},{25,1},{2,10},{10... | collective-permute-start | bytes 393224 | tf_op jit(solution)/shard_map/ppermute | solution.py:24
  84.3 2.1 %collective-permute-start.29 = (bf16[128,512]{1,0:T(8,128)(2,1)S(1)}, bf16[128,512]{1,0:T(8,128)(2,1)S(1)}, u32[]{:S(2)}, u32[]{:S(2)}) collective-permute-start(bf16[128,512]{1,0:T(8,128)(2,1)S(1)} %get-tuple-element.40), channel_id=1, source_target_pairs={{0,24},{8,0},{16,8},{24,16},{1,25},{9,1},{17,9},{25,17},{2,26},{10... | collective-permute-start | bytes 393224 | tf_op jit(solution)/shard_map/ppermute | solution.py:24
  86.5 3.0 %collective-permute-done.27 = bf16[128,512]{1,0:T(8,128)(2,1)S(1)} collective-permute-done((bf16[128,512]{1,0:T(8,128)(2,1)S(1)}, bf16[128,512]{1,0:T(8,128)(2,1)S(1)}, u32[]{:S(2)}, u32[]{:S(2)}) %collective-permute-start.27) | collective-permute-done | bytes 131104 | tf_op jit(solution)/shard_map/ppermute | solution.py:24
  89.4 3.8 %collective-permute-done.28 = bf16[128,512]{1,0:T(8,128)(2,1)S(1)} collective-permute-done((bf16[128,512]{1,0:T(8,128)(2,1)S(1)}, bf16[128,512]{1,0:T(8,128)(2,1)S(1)}, u32[]{:S(2)}, u32[]{:S(2)}) %collective-permute-start.28) | collective-permute-done | bytes 131104 | tf_op jit(solution)/shard_map/ppermute | solution.py:24
  94.1 2.4 %gather_fusion.7 = bf16[4,128,512]{2,1,0:T(8,128)(2,1)} fusion(bf16[4,128,512]{2,1,0:T(8,128)(2,1)} %pad_maximum_fusion.1, s32[1024]{0:T(1024)S(1)} %pad_clamp_fusion.4), kind=kCustom, calls=%fused_computation.5.clone | custom fusion | bytes 1048592 | tf_op jit(solution)/shard_map/jit(_take)/gather | solution.py:80
  98.8 2.2 %gather_fusion.8 = bf16[8,32,512]{2,1,0:T(8,128)(2,1)} fusion(bf16[8,32,512]{2,1,0:T(8,128)(2,1)} %bitcast.266, s32[1024]{0:T(1024)S(1)} %get-tuple-element.77), kind=kCustom, calls=%fused_computation.8.clone | custom fusion | bytes 524320 | tf_op jit(solution)/shard_map/jit(_take)/gather | solution.py:91
  103.7 2.0 %collective-permute-start.32 = (bf16[32,512]{1,0:T(8,128)(2,1)S(1)}, bf16[32,512]{1,0:T(8,128)(2,1)S(1)}, u32[]{:S(2)}, u32[]{:S(2)}) collective-permute-start(bf16[32,512]{1,0:T(8,128)(2,1)S(1)} %get-tuple-element.59), channel_id=1, source_target_pairs={{0,3},{1,4},{2,5},{3,6},{4,7},{5,0},{6,1},{7,2},{8,11},{9,12},{10,... | collective-permute-start | bytes 98312 | tf_op jit(solution)/shard_map/ppermute | solution.py:24
  111.2 1.9 %constant_dynamic-update-slice_fusion.39 = (bf16[8,32,512]{2,1,0:T(8,128)(2,1)}, bf16[32,512]{1,0:T(8,128)(2,1)S(1)}, f32[32,512]{1,0:T(8,128)S(1)}) fusion(bf16[1,512,512]{2,1,0:T(8,128)(2,1)} %param.15, f32[32,512]{1,0:T(8,128)S(1)} %convert_reduce_fusion.1, f32[3,1,32,512]{3,2,1,0:T(8,128)} %param.16), kind=kOutput, calls=%fused_computation.112 | convolution fusion | flops 16826368 | bytes 786432 | tf_op jit(solution)/shard_map/dot_general | solution.py:95
  115.5 1.8 %collective-permute-start.38 = (bf16[32,512]{1,0:T(8,128)(2,1)S(1)}, bf16[32,512]{1,0:T(8,128)(2,1)S(1)}, u32[]{:S(2)}, u32[]{:S(2)}) collective-permute-start(bf16[32,512]{1,0:T(8,128)(2,1)S(1)} %get-tuple-element.24), channel_id=1, source_target_pairs={{0,2},{1,3},{2,4},{3,5},{4,6},{5,7},{6,0},{7,1},{8,10},{9,11},{10,... | collective-permute-start | bytes 98312 | tf_op jit(solution)/shard_map/ppermute | solution.py:16
  121.4 1.6 %collective-permute-start.43 = (bf16[32,512]{1,0:T(8,128)(2,1)S(1)}, bf16[32,512]{1,0:T(8,128)(2,1)S(1)}, u32[]{:S(2)}, u32[]{:S(2)}) collective-permute-start(bf16[32,512]{1,0:T(8,128)(2,1)S(1)} %get-tuple-element.24), channel_id=1, source_target_pairs={{0,7},{1,0},{2,1},{3,2},{4,3},{5,4},{6,5},{7,6},{8,15},{9,8},{10,9... | collective-permute-start | bytes 98312 | tf_op jit(solution)/shard_map/ppermute | solution.py:16
  126.7 2.3 %gather_fusion.9 = bf16[8,32,512]{2,1,0:T(8,128)(2,1)} fusion(bf16[8,32,512]{2,1,0:T(8,128)(2,1)} %constant_dynamic-update-slice_fusion.32, s32[1024]{0:T(1024)} %copy-done.2), kind=kCustom, calls=%fused_computation.9.clone | custom fusion | bytes 524320 | tf_op jit(solution)/shard_map/jit(_take)/gather | solution.py:99
  132.9 2.9 %collective-permute-start.44 = (bf16[128,512]{1,0:T(8,128)(2,1)S(1)}, bf16[128,512]{1,0:T(8,128)(2,1)S(1)}, u32[]{:S(2)}, u32[]{:S(2)}) collective-permute-start(bf16[128,512]{1,0:T(8,128)(2,1)S(1)} %get-tuple-element.38), channel_id=1, source_target_pairs={{0,8},{8,16},{16,24},{24,0},{1,9},{9,17},{17,25},{25,1},{2,10},{10... | collective-permute-start | bytes 393224 | tf_op jit(solution)/shard_map/ppermute | solution.py:24
  135.8 1.6 %collective-permute-start.45 = (bf16[128,512]{1,0:T(8,128)(2,1)S(1)}, bf16[128,512]{1,0:T(8,128)(2,1)S(1)}, u32[]{:S(2)}, u32[]{:S(2)}) collective-permute-start(bf16[128,512]{1,0:T(8,128)(2,1)S(1)} %get-tuple-element.37), channel_id=1, source_target_pairs={{0,16},{8,24},{16,0},{24,8},{1,17},{9,25},{17,1},{25,9},{2,18},{10... | collective-permute-start | bytes 393224 | tf_op jit(solution)/shard_map/ppermute | solution.py:24
  138.3 3.1 %collective-permute-done.44 = bf16[128,512]{1,0:T(8,128)(2,1)S(1)} collective-permute-done((bf16[128,512]{1,0:T(8,128)(2,1)S(1)}, bf16[128,512]{1,0:T(8,128)(2,1)S(1)}, u32[]{:S(2)}, u32[]{:S(2)}) %collective-permute-start.44) | collective-permute-done | bytes 131104 | tf_op jit(solution)/shard_map/ppermute | solution.py:24
  141.3 4.2 %collective-permute-done.45 = bf16[128,512]{1,0:T(8,128)(2,1)S(1)} collective-permute-done((bf16[128,512]{1,0:T(8,128)(2,1)S(1)}, bf16[128,512]{1,0:T(8,128)(2,1)S(1)}, u32[]{:S(2)}, u32[]{:S(2)}) %collective-permute-start.45) | collective-permute-done | bytes 131104 | tf_op jit(solution)/shard_map/ppermute | solution.py:24
  148.3 1.6 %collective-permute-start.48 = (bf16[32,512]{1,0:T(8,128)(2,1)S(1)}, bf16[32,512]{1,0:T(8,128)(2,1)S(1)}, u32[]{:S(2)}, u32[]{:S(2)}) collective-permute-start(bf16[32,512]{1,0:T(8,128)(2,1)S(1)} %get-tuple-element.52), channel_id=1, source_target_pairs={{0,2},{1,3},{2,4},{3,5},{4,6},{5,7},{6,0},{7,1},{8,10},{9,11},{10,... | collective-permute-start | bytes 98312 | tf_op jit(solution)/shard_map/ppermute | solution.py:24
  154.2 1.7 %collective-permute-start.53 = (bf16[32,512]{1,0:T(8,128)(2,1)S(1)}, bf16[32,512]{1,0:T(8,128)(2,1)S(1)}, u32[]{:S(2)}, u32[]{:S(2)}) collective-permute-start(bf16[32,512]{1,0:T(8,128)(2,1)S(1)} %get-tuple-element.47), channel_id=1, source_target_pairs={{0,7},{1,0},{2,1},{3,2},{4,3},{5,4},{6,5},{7,6},{8,15},{9,8},{10,9... | collective-permute-start | bytes 98312 | tf_op jit(solution)/shard_map/ppermute | solution.py:24
  (216 shorter events, 77.8 us)
Async XLA Ops:
  0.0 13.7 %collective-permute-start = (s32[4,3]{1,0:T(4,128)}, s32[4,3]{1,0:T(4,128)S(1)}, u32[]{:S(2)}, u32[]{:S(2)}) collective-permute-start(s32[4,3]{1,0:T(4,128)} %param.13), channel_id=1, source_target_pairs={{0,8},{8,16},{16,24},{24,0},{1,9},{9,17},{17,25},{25,1},{2,10},{10... | collective-permute-start | bytes 152 | tf_op jit(solution)/shard_map/ppermute | solution.py:16
  3.0 13.1 %collective-permute-start.1 = (s32[4,3]{1,0:T(4,128)}, s32[4,3]{1,0:T(4,128)S(1)}, u32[]{:S(2)}, u32[]{:S(2)}) collective-permute-start(s32[4,3]{1,0:T(4,128)} %param.13), channel_id=1, source_target_pairs={{0,16},{8,24},{16,0},{24,8},{1,17},{9,25},{17,1},{25,9},{2,18},{10... | collective-permute-start | bytes 152 | tf_op jit(solution)/shard_map/ppermute | solution.py:16
  5.6 11.1 %collective-permute-start.2 = (s32[4,3]{1,0:T(4,128)}, s32[4,3]{1,0:T(4,128)S(1)}, u32[]{:S(2)}, u32[]{:S(2)}) collective-permute-start(s32[4,3]{1,0:T(4,128)} %param.13), channel_id=1, source_target_pairs={{0,24},{8,0},{16,8},{24,16},{1,25},{9,1},{17,9},{25,17},{2,26},{10... | collective-permute-start | bytes 152 | tf_op jit(solution)/shard_map/ppermute | solution.py:16
  7.0 12.1 %collective-permute-start.3 = (bf16[2,32,512]{2,1,0:T(8,128)(2,1)}, bf16[2,32,512]{2,1,0:T(8,128)(2,1)S(1)}, u32[]{:S(2)}, u32[]{:S(2)}) collective-permute-start(bf16[2,32,512]{2,1,0:T(8,128)(2,1)} %bitcast.284), channel_id=1, source_target_pairs={{0,1},{1,2},{2,3},{3,4},{4,5},{5,6},{6,7},{7,0},{8,9},{9,10},{10,1... | collective-permute-start | bytes 196616 | tf_op jit(solution)/shard_map/ppermute | solution.py:16
  7.0 13.6 %collective-permute-start.4 = (bf16[2,32,512]{2,1,0:T(8,128)(2,1)}, bf16[2,32,512]{2,1,0:T(8,128)(2,1)S(1)}, u32[]{:S(2)}, u32[]{:S(2)}) collective-permute-start(bf16[2,32,512]{2,1,0:T(8,128)(2,1)} %bitcast.285), channel_id=1, source_target_pairs={{0,2},{1,3},{2,4},{3,5},{4,6},{5,7},{6,0},{7,1},{8,10},{9,11},{10,... | collective-permute-start | bytes 196616 | tf_op jit(solution)/shard_map/ppermute | solution.py:16
  13.7 9.3 %collective-permute-start.5 = (bf16[2,32,512]{2,1,0:T(8,128)(2,1)}, bf16[2,32,512]{2,1,0:T(8,128)(2,1)S(1)}, u32[]{:S(2)}, u32[]{:S(2)}) collective-permute-start(bf16[2,32,512]{2,1,0:T(8,128)(2,1)} %bitcast.286), channel_id=1, source_target_pairs={{0,3},{1,4},{2,5},{3,6},{4,7},{5,0},{6,1},{7,2},{8,11},{9,12},{10,... | collective-permute-start | bytes 196616 | tf_op jit(solution)/shard_map/ppermute | solution.py:16
  16.2 6.8 %collective-permute-start.6 = (bf16[2,32,512]{2,1,0:T(8,128)(2,1)}, bf16[2,32,512]{2,1,0:T(8,128)(2,1)S(1)}, u32[]{:S(2)}, u32[]{:S(2)}) collective-permute-start(bf16[2,32,512]{2,1,0:T(8,128)(2,1)} %bitcast.287), channel_id=1, source_target_pairs={{0,4},{1,5},{2,6},{3,7},{4,0},{5,1},{6,2},{7,3},{8,12},{9,13},{10,... | collective-permute-start | bytes 196616 | tf_op jit(solution)/shard_map/ppermute | solution.py:16
  16.7 6.4 %collective-permute-start.7 = (bf16[2,32,512]{2,1,0:T(8,128)(2,1)}, bf16[2,32,512]{2,1,0:T(8,128)(2,1)S(1)}, u32[]{:S(2)}, u32[]{:S(2)}) collective-permute-start(bf16[2,32,512]{2,1,0:T(8,128)(2,1)} %bitcast.288), channel_id=1, source_target_pairs={{0,5},{1,6},{2,7},{3,0},{4,1},{5,2},{6,3},{7,4},{8,13},{9,14},{10,... | collective-permute-start | bytes 196616 | tf_op jit(solution)/shard_map/ppermute | solution.py:16
  28.7 8.4 %collective-permute-start.10 = (bf16[128,512]{1,0:T(8,128)(2,1)S(1)}, bf16[128,512]{1,0:T(8,128)(2,1)S(1)}, u32[]{:S(2)}, u32[]{:S(2)}) collective-permute-start(bf16[128,512]{1,0:T(8,128)(2,1)S(1)} %get-tuple-element.46), channel_id=1, source_target_pairs={{0,8},{8,16},{16,24},{24,0},{1,9},{9,17},{17,25},{25,1},{2,10},{10... | collective-permute-start | bytes 393224 | tf_op jit(solution)/shard_map/ppermute | solution.py:24
  29.4 12.9 %collective-permute-start.11 = (bf16[128,512]{1,0:T(8,128)(2,1)S(1)}, bf16[128,512]{1,0:T(8,128)(2,1)S(1)}, u32[]{:S(2)}, u32[]{:S(2)}) collective-permute-start(bf16[128,512]{1,0:T(8,128)(2,1)S(1)} %get-tuple-element.45), channel_id=1, source_target_pairs={{0,16},{8,24},{16,0},{24,8},{1,17},{9,25},{17,1},{25,9},{2,18},{10... | collective-permute-start | bytes 393224 | tf_op jit(solution)/shard_map/ppermute | solution.py:24
  29.8 12.5 %collective-permute-start.12 = (bf16[128,512]{1,0:T(8,128)(2,1)S(1)}, bf16[128,512]{1,0:T(8,128)(2,1)S(1)}, u32[]{:S(2)}, u32[]{:S(2)}) collective-permute-start(bf16[128,512]{1,0:T(8,128)(2,1)S(1)} %get-tuple-element.44), channel_id=1, source_target_pairs={{0,24},{8,0},{16,8},{24,16},{1,25},{9,1},{17,9},{25,17},{2,26},{10... | collective-permute-start | bytes 393224 | tf_op jit(solution)/shard_map/ppermute | solution.py:24
  52.9 6.2 %collective-permute-start.15 = (bf16[32,512]{1,0:T(8,128)(2,1)S(1)}, bf16[32,512]{1,0:T(8,128)(2,1)S(1)}, u32[]{:S(2)}, u32[]{:S(2)}) collective-permute-start(bf16[32,512]{1,0:T(8,128)(2,1)S(1)} %get-tuple-element.67), channel_id=1, source_target_pairs={{0,3},{1,4},{2,5},{3,6},{4,7},{5,0},{6,1},{7,2},{8,11},{9,12},{10,... | collective-permute-start | bytes 98312 | tf_op jit(solution)/shard_map/ppermute | solution.py:24
  63.1 6.3 %collective-permute-start.21 = (bf16[32,512]{1,0:T(8,128)(2,1)S(1)}, bf16[32,512]{1,0:T(8,128)(2,1)S(1)}, u32[]{:S(2)}, u32[]{:S(2)}) collective-permute-start(bf16[32,512]{1,0:T(8,128)(2,1)S(1)} %get-tuple-element.26), channel_id=1, source_target_pairs={{0,2},{1,3},{2,4},{3,5},{4,6},{5,7},{6,0},{7,1},{8,10},{9,11},{10,... | collective-permute-start | bytes 98312 | tf_op jit(solution)/shard_map/ppermute | solution.py:16
  65.7 6.5 %collective-permute-start.22 = (bf16[32,512]{1,0:T(8,128)(2,1)S(1)}, bf16[32,512]{1,0:T(8,128)(2,1)S(1)}, u32[]{:S(2)}, u32[]{:S(2)}) collective-permute-start(bf16[32,512]{1,0:T(8,128)(2,1)S(1)} %get-tuple-element.26), channel_id=1, source_target_pairs={{0,3},{1,4},{2,5},{3,6},{4,7},{5,0},{6,1},{7,2},{8,11},{9,12},{10,... | collective-permute-start | bytes 98312 | tf_op jit(solution)/shard_map/ppermute | solution.py:16
  66.0 6.8 %collective-permute-start.23 = (bf16[32,512]{1,0:T(8,128)(2,1)S(1)}, bf16[32,512]{1,0:T(8,128)(2,1)S(1)}, u32[]{:S(2)}, u32[]{:S(2)}) collective-permute-start(bf16[32,512]{1,0:T(8,128)(2,1)S(1)} %get-tuple-element.26), channel_id=1, source_target_pairs={{0,4},{1,5},{2,6},{3,7},{4,0},{5,1},{6,2},{7,3},{8,12},{9,13},{10,... | collective-permute-start | bytes 98312 | tf_op jit(solution)/shard_map/ppermute | solution.py:16
  66.6 6.8 %collective-permute-start.24 = (bf16[32,512]{1,0:T(8,128)(2,1)S(1)}, bf16[32,512]{1,0:T(8,128)(2,1)S(1)}, u32[]{:S(2)}, u32[]{:S(2)}) collective-permute-start(bf16[32,512]{1,0:T(8,128)(2,1)S(1)} %get-tuple-element.26), channel_id=1, source_target_pairs={{0,5},{1,6},{2,7},{3,0},{4,1},{5,2},{6,3},{7,4},{8,13},{9,14},{10,... | collective-permute-start | bytes 98312 | tf_op jit(solution)/shard_map/ppermute | solution.py:16
  67.7 6.4 %collective-permute-start.25 = (bf16[32,512]{1,0:T(8,128)(2,1)S(1)}, bf16[32,512]{1,0:T(8,128)(2,1)S(1)}, u32[]{:S(2)}, u32[]{:S(2)}) collective-permute-start(bf16[32,512]{1,0:T(8,128)(2,1)S(1)} %get-tuple-element.26), channel_id=1, source_target_pairs={{0,6},{1,7},{2,0},{3,1},{4,2},{5,3},{6,4},{7,5},{8,14},{9,15},{10,... | collective-permute-start | bytes 98312 | tf_op jit(solution)/shard_map/ppermute | solution.py:16
  81.2 8.3 %collective-permute-start.27 = (bf16[128,512]{1,0:T(8,128)(2,1)S(1)}, bf16[128,512]{1,0:T(8,128)(2,1)S(1)}, u32[]{:S(2)}, u32[]{:S(2)}) collective-permute-start(bf16[128,512]{1,0:T(8,128)(2,1)S(1)} %get-tuple-element.42), channel_id=1, source_target_pairs={{0,8},{8,16},{16,24},{24,0},{1,9},{9,17},{17,25},{25,1},{2,10},{10... | collective-permute-start | bytes 393224 | tf_op jit(solution)/shard_map/ppermute | solution.py:24
  84.0 9.2 %collective-permute-start.28 = (bf16[128,512]{1,0:T(8,128)(2,1)S(1)}, bf16[128,512]{1,0:T(8,128)(2,1)S(1)}, u32[]{:S(2)}, u32[]{:S(2)}) collective-permute-start(bf16[128,512]{1,0:T(8,128)(2,1)S(1)} %get-tuple-element.41), channel_id=1, source_target_pairs={{0,16},{8,24},{16,0},{24,8},{1,17},{9,25},{17,1},{25,9},{2,18},{10... | collective-permute-start | bytes 393224 | tf_op jit(solution)/shard_map/ppermute | solution.py:24
  84.3 8.9 %collective-permute-start.29 = (bf16[128,512]{1,0:T(8,128)(2,1)S(1)}, bf16[128,512]{1,0:T(8,128)(2,1)S(1)}, u32[]{:S(2)}, u32[]{:S(2)}) collective-permute-start(bf16[128,512]{1,0:T(8,128)(2,1)S(1)} %get-tuple-element.40), channel_id=1, source_target_pairs={{0,24},{8,0},{16,8},{24,16},{1,25},{9,1},{17,9},{25,17},{2,26},{10... | collective-permute-start | bytes 393224 | tf_op jit(solution)/shard_map/ppermute | solution.py:24
  102.2 5.9 %collective-permute-start.31 = (bf16[32,512]{1,0:T(8,128)(2,1)S(1)}, bf16[32,512]{1,0:T(8,128)(2,1)S(1)}, u32[]{:S(2)}, u32[]{:S(2)}) collective-permute-start(bf16[32,512]{1,0:T(8,128)(2,1)S(1)} %get-tuple-element.60), channel_id=1, source_target_pairs={{0,2},{1,3},{2,4},{3,5},{4,6},{5,7},{6,0},{7,1},{8,10},{9,11},{10,... | collective-permute-start | bytes 98312 | tf_op jit(solution)/shard_map/ppermute | solution.py:24
  113.0 6.3 %collective-permute-start.37 = (bf16[32,512]{1,0:T(8,128)(2,1)S(1)}, bf16[32,512]{1,0:T(8,128)(2,1)S(1)}, u32[]{:S(2)}, u32[]{:S(2)}) collective-permute-start(bf16[32,512]{1,0:T(8,128)(2,1)S(1)} %get-tuple-element.24), channel_id=1, source_target_pairs={{0,1},{1,2},{2,3},{3,4},{4,5},{5,6},{6,7},{7,0},{8,9},{9,10},{10,1... | collective-permute-start | bytes 98312 | tf_op jit(solution)/shard_map/ppermute | solution.py:16
  115.5 5.9 %collective-permute-start.38 = (bf16[32,512]{1,0:T(8,128)(2,1)S(1)}, bf16[32,512]{1,0:T(8,128)(2,1)S(1)}, u32[]{:S(2)}, u32[]{:S(2)}) collective-permute-start(bf16[32,512]{1,0:T(8,128)(2,1)S(1)} %get-tuple-element.24), channel_id=1, source_target_pairs={{0,2},{1,3},{2,4},{3,5},{4,6},{5,7},{6,0},{7,1},{8,10},{9,11},{10,... | collective-permute-start | bytes 98312 | tf_op jit(solution)/shard_map/ppermute | solution.py:16
  117.2 6.4 %collective-permute-start.39 = (bf16[32,512]{1,0:T(8,128)(2,1)S(1)}, bf16[32,512]{1,0:T(8,128)(2,1)S(1)}, u32[]{:S(2)}, u32[]{:S(2)}) collective-permute-start(bf16[32,512]{1,0:T(8,128)(2,1)S(1)} %get-tuple-element.24), channel_id=1, source_target_pairs={{0,3},{1,4},{2,5},{3,6},{4,7},{5,0},{6,1},{7,2},{8,11},{9,12},{10,... | collective-permute-start | bytes 98312 | tf_op jit(solution)/shard_map/ppermute | solution.py:16
  117.5 6.7 %collective-permute-start.40 = (bf16[32,512]{1,0:T(8,128)(2,1)S(1)}, bf16[32,512]{1,0:T(8,128)(2,1)S(1)}, u32[]{:S(2)}, u32[]{:S(2)}) collective-permute-start(bf16[32,512]{1,0:T(8,128)(2,1)S(1)} %get-tuple-element.24), channel_id=1, source_target_pairs={{0,4},{1,5},{2,6},{3,7},{4,0},{5,1},{6,2},{7,3},{8,12},{9,13},{10,... | collective-permute-start | bytes 98312 | tf_op jit(solution)/shard_map/ppermute | solution.py:16
  118.3 6.6 %collective-permute-start.41 = (bf16[32,512]{1,0:T(8,128)(2,1)S(1)}, bf16[32,512]{1,0:T(8,128)(2,1)S(1)}, u32[]{:S(2)}, u32[]{:S(2)}) collective-permute-start(bf16[32,512]{1,0:T(8,128)(2,1)S(1)} %get-tuple-element.24), channel_id=1, source_target_pairs={{0,5},{1,6},{2,7},{3,0},{4,1},{5,2},{6,3},{7,4},{8,13},{9,14},{10,... | collective-permute-start | bytes 98312 | tf_op jit(solution)/shard_map/ppermute | solution.py:16
  119.3 6.2 %collective-permute-start.42 = (bf16[32,512]{1,0:T(8,128)(2,1)S(1)}, bf16[32,512]{1,0:T(8,128)(2,1)S(1)}, u32[]{:S(2)}, u32[]{:S(2)}) collective-permute-start(bf16[32,512]{1,0:T(8,128)(2,1)S(1)} %get-tuple-element.24), channel_id=1, source_target_pairs={{0,6},{1,7},{2,0},{3,1},{4,2},{5,3},{6,4},{7,5},{8,14},{9,15},{10,... | collective-permute-start | bytes 98312 | tf_op jit(solution)/shard_map/ppermute | solution.py:16
  132.9 8.5 %collective-permute-start.44 = (bf16[128,512]{1,0:T(8,128)(2,1)S(1)}, bf16[128,512]{1,0:T(8,128)(2,1)S(1)}, u32[]{:S(2)}, u32[]{:S(2)}) collective-permute-start(bf16[128,512]{1,0:T(8,128)(2,1)S(1)} %get-tuple-element.38), channel_id=1, source_target_pairs={{0,8},{8,16},{16,24},{24,0},{1,9},{9,17},{17,25},{25,1},{2,10},{10... | collective-permute-start | bytes 393224 | tf_op jit(solution)/shard_map/ppermute | solution.py:24
  135.8 9.7 %collective-permute-start.45 = (bf16[128,512]{1,0:T(8,128)(2,1)S(1)}, bf16[128,512]{1,0:T(8,128)(2,1)S(1)}, u32[]{:S(2)}, u32[]{:S(2)}) collective-permute-start(bf16[128,512]{1,0:T(8,128)(2,1)S(1)} %get-tuple-element.37), channel_id=1, source_target_pairs={{0,16},{8,24},{16,0},{24,8},{1,17},{9,25},{17,1},{25,9},{2,18},{10... | collective-permute-start | bytes 393224 | tf_op jit(solution)/shard_map/ppermute | solution.py:24
  137.4 8.2 %collective-permute-start.46 = (bf16[128,512]{1,0:T(8,128)(2,1)S(1)}, bf16[128,512]{1,0:T(8,128)(2,1)S(1)}, u32[]{:S(2)}, u32[]{:S(2)}) collective-permute-start(bf16[128,512]{1,0:T(8,128)(2,1)S(1)} %get-tuple-element.36), channel_id=1, source_target_pairs={{0,24},{8,0},{16,8},{24,16},{1,25},{9,1},{17,9},{25,17},{2,26},{10... | collective-permute-start | bytes 393224 | tf_op jit(solution)/shard_map/ppermute | solution.py:24
  148.3 5.9 %collective-permute-start.48 = (bf16[32,512]{1,0:T(8,128)(2,1)S(1)}, bf16[32,512]{1,0:T(8,128)(2,1)S(1)}, u32[]{:S(2)}, u32[]{:S(2)}) collective-permute-start(bf16[32,512]{1,0:T(8,128)(2,1)S(1)} %get-tuple-element.52), channel_id=1, source_target_pairs={{0,2},{1,3},{2,4},{3,5},{4,6},{5,7},{6,0},{7,1},{8,10},{9,11},{10,... | collective-permute-start | bytes 98312 | tf_op jit(solution)/shard_map/ppermute | solution.py:24
  150.0 5.9 %collective-permute-start.49 = (bf16[32,512]{1,0:T(8,128)(2,1)S(1)}, bf16[32,512]{1,0:T(8,128)(2,1)S(1)}, u32[]{:S(2)}, u32[]{:S(2)}) collective-permute-start(bf16[32,512]{1,0:T(8,128)(2,1)S(1)} %get-tuple-element.51), channel_id=1, source_target_pairs={{0,3},{1,4},{2,5},{3,6},{4,7},{5,0},{6,1},{7,2},{8,11},{9,12},{10,... | collective-permute-start | bytes 98312 | tf_op jit(solution)/shard_map/ppermute | solution.py:24
  (32 other events, 530.1 us)

commit v2 on v1

v2 whole, which is shorter than its diff:
```python
import jax
import jax.numpy as jnp
from jax import lax
from jax.sharding import PartitionSpec as P

BLOCK = 512
EXCITE = 128
OWNERS = 4
DELAYS = 2
STEPS = 3


def shifted(x, axis, n, k):
    return lax.ppermute(x, axis, [(i, (i + k) % n) for i in range(n)])


def shift_gather(x, axis, n):
    return [x] + [shifted(x, axis, n, k) for k in range(1, n)]


def pick(pieces, index):
    if len(pieces) <= 8:
        return jnp.stack([lax.select_n(index[i], *pieces) for i in range(index.shape[0])])
    return jnp.take(jnp.stack(pieces), index, axis=0)


def body(tile_values, tile_lists, owner_map, inverses, excitations, history):
    members = lax.axis_size("member")
    groups = lax.axis_size("group")
    group_blocks = members // OWNERS
    share = EXCITE // OWNERS
    group_here = lax.axis_index("group")
    member_here = lax.axis_index("member")
    owners = owner_map[0]
    member_ids = jnp.arange(members, dtype=jnp.int32)
    matches = owners[:, None] == member_ids[None, :]
    slot_of_member = jnp.sum(jnp.where(matches, member_ids[:, None], 0), axis=0)
    owner_shift = (member_here - owners) % members
    send_slot = jnp.take(slot_of_member, (member_here + member_ids) % members)

    lists_by_shift = jnp.stack(shift_gather(tile_lists, "group", groups))
    group_ids = jnp.arange(groups, dtype=jnp.int32)
    ahead = jnp.take(lists_by_shift, (groups - group_ids) % groups, axis=0)
    wanted = (ahead[:, :, 0] // group_blocks == group_here) & (ahead[:, :, 2] > 0)
    want_block = jnp.sum(jnp.where(wanted, ahead[:, :, 0] % group_blocks, 0), axis=1)
    want_delay = jnp.sum(jnp.where(wanted, ahead[:, :, 2], 0), axis=1)

    source_group = tile_lists[:, 0] // group_blocks
    observer_local = tile_lists[:, 1] % group_blocks
    delays_here = tile_lists[:, 2]
    source_shift = (group_here - source_group) % groups

    hist_pieces = shift_gather(history[:, 0], "member", members)
    hist_placed = pick(hist_pieces, owner_shift)
    blocks = [
        hist_placed[:, t].reshape(group_blocks, EXCITE, BLOCK) for t in range(DELAYS)
    ]
    results = []
    for step in range(STEPS):
        near = blocks[DELAYS + step - 1]
        far = blocks[DELAYS + step - 2]
        received = []
        for k in range(groups):
            a = lax.dynamic_index_in_dim(near, want_block[k], 0, keepdims=False)
            b = lax.dynamic_index_in_dim(far, want_block[k], 0, keepdims=False)
            piece = jnp.where(
                want_delay[k] == 1, a, jnp.where(want_delay[k] == 2, b, jnp.zeros_like(a))
            )
            received.append(piece if k == 0 else shifted(piece, "group", groups, k))
        blocks_in = pick(received, source_shift)
        terms = jnp.einsum(
            "kes,kso->keo", blocks_in, tile_values, preferred_element_type=jnp.float32
        )
        partial_sums = []
        for block in range(group_blocks):
            chosen = (observer_local == block) & (delays_here > 0)
            partial_sums.append(
                jnp.sum(jnp.where(chosen[:, None, None], terms, 0.0), axis=0)
            )
        slots = jnp.stack(partial_sums).astype(jnp.bfloat16).reshape(members, share, BLOCK)
        field = slots[0].astype(jnp.float32) * 0.0
        for k in range(members):
            piece = lax.dynamic_index_in_dim(slots, send_slot[k], 0, keepdims=False)
            if k:
                piece = shifted(piece, "member", members, k)
            field = field + piece.astype(jnp.float32)
        residual = (excitations[step, 0] - field).astype(jnp.bfloat16)
        current = jnp.dot(residual, inverses[0], preferred_element_type=jnp.float32)
        results.append(current)
        if step + 1 < STEPS:
            pieces = shift_gather(current.astype(jnp.bfloat16), "member", members)
            blocks.append(pick(pieces, owner_shift).reshape(group_blocks, EXCITE, BLOCK))
    return jnp.stack(results)[:, None]


def solution(mesh):
    placed = (
        P(("group", "member"), None, None),
        P(("group", "member"), None),
        P("group", None),
        P(("group", "member"), None, None),
        P(None, ("group", "member"), None, None),
        P(None, ("group", "member"), None, None),
    )
    return jax.shard_map(
        body,
        mesh=mesh,
        in_specs=placed,
        out_specs=P(None, ("group", "member"), None, None),
        check_vma=False,
    )
```

time: 162 us -> 193 us (1.19)
  between operations: 0.7 us -> 71.3 us
  local copies, waits for them, and re-layouts: 31.3 us -> 5.54 us
  other arithmetic: 19.1 us -> 8.5 us
  matrix products: 9.17 us -> 2.86 us
  starting transfers between devices: 68.8 us -> 71.3 us
    gather x13 -> x2, local copies, waits for them, and re-layouts: 20.3 us -> 1.21 us  [the longest x1 0.64 us: body(): send_slot = jnp.take(slot_of_member, (member_here + member_ids) % members)]
    unnamed x57 -> x8, local copies, waits for them, and re-layouts: 8.36 us -> 0.02 us
    select_n x15 -> x7, other arithmetic: 9.23 us -> 0.95 us  [the longest x2 0.69 us: body(): send_slot = jnp.take(slot_of_member, (member_here + member_ids) % members)]
    dot_general x3, matrix products: 4.81 us -> 1.41 us  [body(): current = jnp.dot(residual, inverses[0], preferred_element_type=jnp.float32)]
    dot_general x3, matrix products: 4.36 us -> 1.45 us  [body(): jnp.einsum('kes,kso->keo', blocks_in, tile_values, preferred_element_type...]
    unnamed x0 -> x21, other arithmetic: none -> 2.83 us
    slice x1 -> x7, local copies, waits for them, and re-layouts: 0.97 us -> 3.6 us  [the longest x2 1.33 us: pick(): index[i]]
    ppermute x54, starting transfers between devices: 68.8 us -> 71.3 us  [shifted(): return lax.ppermute(x, axis, [(i, (i + k) % n) for i in range(n)])]
  transfers between devices with their start and end apart: 54 -> 54, of which waited for: 19 -> 19; matrix products, arithmetic and copies ran while one was open for 11% -> 5% of each run, Pallas kernels for 0% -> 0%
where the time goes in v2:
time: 193 us; the launch traced here: 190 us
  starting transfers between devices  71.3 us (37%)
  between operations  71.3 us (37%)
  waiting for transfers between devices  30.7 us (16%)
  other arithmetic  8.5 us (4%)
  local copies, waits for them, and re-layouts  5.54 us (3%)
  matrix products  2.86 us (1%)
    ppermute x54, starting transfers between devices, shifted(): return lax.ppermute(x, axis, [(i, (i + k) % n) for i in range(n)])  71.3 us
    ppermute x54, waiting for transfers between devices, shifted(): return lax.ppermute(x, axis, [(i, (i + k) % n) for i in range(n)])  30.7 us
  transfers between devices with their start and end apart: 54, of which 19 were waited for; matrix products, arithmetic and copies ran while one was open for 5% of the time, Pallas kernels for 0%

profile of v2, /device:TPU:0, one launch (start us, length us, event | category | flops | bytes accessed | tf_op | source)
XLA Modules:
  0.0 190.2 jit_solution(17759941344961377242)
XLA Ops:
  0.5 2.5 %collective-permute-start.4 = (bf16[2,32,512]{2,1,0:T(8,128)(2,1)}, bf16[2,32,512]{2,1,0:T(8,128)(2,1)S(1)}, u32[]{:S(2)}, u32[]{:S(2)}) collective-permute-start(bf16[2,32,512]{2,1,0:T(8,128)(2,1)} %bitcast.430), channel_id=1, source_target_pairs={{0,2},{1,3},{2,4},{3,5},{4,6},{5,7},{6,0},{7,1},{8,10},{9,11},{10,... | collective-permute-start | bytes 196616 | tf_op jit(solution)/shard_map/ppermute | solution.py:14
  3.0 2.4 %collective-permute-start.5 = (bf16[2,32,512]{2,1,0:T(8,128)(2,1)}, bf16[2,32,512]{2,1,0:T(8,128)(2,1)S(1)}, u32[]{:S(2)}, u32[]{:S(2)}) collective-permute-start(bf16[2,32,512]{2,1,0:T(8,128)(2,1)} %bitcast.431), channel_id=1, source_target_pairs={{0,3},{1,4},{2,5},{3,6},{4,7},{5,0},{6,1},{7,2},{8,11},{9,12},{10,... | collective-permute-start | bytes 196616 | tf_op jit(solution)/shard_map/ppermute | solution.py:14
  5.9 1.6 collective-permute-start
  69.9 2.7 %collective-permute-start.1 = (s32[4,3]{1,0:T(4,128)}, s32[4,3]{1,0:T(4,128)S(1)}, u32[]{:S(2)}, u32[]{:S(2)}) collective-permute-start(s32[4,3]{1,0:T(4,128)} %param.7), channel_id=1, source_target_pairs={{0,16},{8,24},{16,0},{24,8},{1,17},{9,25},{17,1},{25,9},{2,18},{10... | collective-permute-start | bytes 152 | tf_op jit(solution)/shard_map/ppermute | solution.py:14
  72.6 2.1 %collective-permute-done.1 = s32[4,3]{1,0:T(4,128)S(1)} collective-permute-done((s32[4,3]{1,0:T(4,128)}, s32[4,3]{1,0:T(4,128)S(1)}, u32[]{:S(2)}, u32[]{:S(2)}) %collective-permute-start.1) | collective-permute-done | bytes 80 | tf_op jit(solution)/shard_map/ppermute | solution.py:14
  74.7 2.2 %collective-permute-start.2 = (s32[4,3]{1,0:T(4,128)}, s32[4,3]{1,0:T(4,128)S(1)}, u32[]{:S(2)}, u32[]{:S(2)}) collective-permute-start(s32[4,3]{1,0:T(4,128)} %param.7), channel_id=1, source_target_pairs={{0,24},{8,0},{16,8},{24,16},{1,25},{9,1},{17,9},{25,17},{2,26},{10... | collective-permute-start | bytes 152 | tf_op jit(solution)/shard_map/ppermute | solution.py:14
  77.0 1.5 collective-permute-done.2
  84.6 1.5 collective-permute-start.8
  86.1 2.4 %collective-permute-start.9 = (bf16[2,32,512]{2,1,0:T(8,128)(2,1)}, bf16[2,32,512]{2,1,0:T(8,128)(2,1)S(1)}, u32[]{:S(2)}, u32[]{:S(2)}) collective-permute-start(bf16[2,32,512]{2,1,0:T(8,128)(2,1)} %bitcast.435), channel_id=1, source_target_pairs={{0,7},{1,0},{2,1},{3,2},{4,3},{5,4},{6,5},{7,6},{8,15},{9,8},{10,9... | collective-permute-start | bytes 196616 | tf_op jit(solution)/shard_map/ppermute | solution.py:14
  97.2 1.6 collective-permute-start.10
  98.8 3.0 %collective-permute-start.11 = (bf16[128,512]{1,0:T(8,128)(2,1)S(1)}, bf16[128,512]{1,0:T(8,128)(2,1)S(1)}, u32[]{:S(2)}, u32[]{:S(2)}) collective-permute-start(bf16[128,512]{1,0:T(8,128)(2,1)S(1)} %get-tuple-element.41), channel_id=1, source_target_pairs={{0,16},{8,24},{16,0},{24,8},{1,17},{9,25},{17,1},{25,9},{2,18},{10... | collective-permute-start | bytes 393224 | tf_op jit(solution)/shard_map/ppermute | solution.py:14
  106.0 3.6 %collective-permute-done.11 = bf16[128,512]{1,0:T(8,128)(2,1)S(1)} collective-permute-done((bf16[128,512]{1,0:T(8,128)(2,1)S(1)}, bf16[128,512]{1,0:T(8,128)(2,1)S(1)}, u32[]{:S(2)}, u32[]{:S(2)}) %collective-permute-start.11) | collective-permute-done | bytes 131104 | tf_op jit(solution)/shard_map/ppermute | solution.py:14
  111.4 2.4 %collective-permute-start.15 = (bf16[32,512]{1,0:T(8,128)(2,1)}, bf16[32,512]{1,0:T(8,128)(2,1)S(1)}, u32[]{:S(2)}, u32[]{:S(2)}) collective-permute-start(bf16[32,512]{1,0:T(8,128)(2,1)} %get-tuple-element.63), channel_id=1, source_target_pairs={{0,3},{1,4},{2,5},{3,6},{4,7},{5,0},{6,1},{7,2},{8,11},{9,12},{10,... | collective-permute-start | bytes 98312 | tf_op jit(solution)/shard_map/ppermute | solution.py:14
  115.3 1.6 collective-permute-start.18
  121.6 2.5 %collective-permute-start.21 = (bf16[32,512]{1,0:T(8,128)(2,1)S(1)}, bf16[32,512]{1,0:T(8,128)(2,1)S(1)}, u32[]{:S(2)}, u32[]{:S(2)}) collective-permute-start(bf16[32,512]{1,0:T(8,128)(2,1)S(1)} %get-tuple-element.94), channel_id=1, source_target_pairs={{0,2},{1,3},{2,4},{3,5},{4,6},{5,7},{6,0},{7,1},{8,10},{9,11},{10,... | collective-permute-start | bytes 98312 | tf_op jit(solution)/shard_map/ppermute | solution.py:14
  127.3 2.3 %collective-permute-start.26 = (bf16[32,512]{1,0:T(8,128)(2,1)S(1)}, bf16[32,512]{1,0:T(8,128)(2,1)S(1)}, u32[]{:S(2)}, u32[]{:S(2)}) collective-permute-start(bf16[32,512]{1,0:T(8,128)(2,1)S(1)} %get-tuple-element.94), channel_id=1, source_target_pairs={{0,7},{1,0},{2,1},{3,2},{4,3},{5,4},{6,5},{7,6},{8,15},{9,8},{10,9... | collective-permute-start | bytes 98312 | tf_op jit(solution)/shard_map/ppermute | solution.py:14
  131.6 3.2 %collective-permute-start.27 = (bf16[128,512]{1,0:T(8,128)(2,1)S(1)}, bf16[128,512]{1,0:T(8,128)(2,1)S(1)}, u32[]{:S(2)}, u32[]{:S(2)}) collective-permute-start(bf16[128,512]{1,0:T(8,128)(2,1)S(1)} %get-tuple-element.36), channel_id=1, source_target_pairs={{0,8},{8,16},{16,24},{24,0},{1,9},{9,17},{17,25},{25,1},{2,10},{10... | collective-permute-start | bytes 393224 | tf_op jit(solution)/shard_map/ppermute | solution.py:14
  137.3 2.7 %collective-permute-done.27 = bf16[128,512]{1,0:T(8,128)(2,1)S(1)} collective-permute-done((bf16[128,512]{1,0:T(8,128)(2,1)S(1)}, bf16[128,512]{1,0:T(8,128)(2,1)S(1)}, u32[]{:S(2)}, u32[]{:S(2)}) %collective-permute-start.27) | collective-permute-done | bytes 131104 | tf_op jit(solution)/shard_map/ppermute | solution.py:14
  140.0 5.1 %collective-permute-done.28 = bf16[128,512]{1,0:T(8,128)(2,1)S(1)} collective-permute-done((bf16[128,512]{1,0:T(8,128)(2,1)S(1)}, bf16[128,512]{1,0:T(8,128)(2,1)S(1)}, u32[]{:S(2)}, u32[]{:S(2)}) %collective-permute-start.28) | collective-permute-done | bytes 131104 | tf_op jit(solution)/shard_map/ppermute | solution.py:14
  145.8 1.5 collective-permute-start.31
  147.4 1.9 %collective-permute-start.32 = (bf16[32,512]{1,0:T(8,128)(2,1)S(1)}, bf16[32,512]{1,0:T(8,128)(2,1)S(1)}, u32[]{:S(2)}, u32[]{:S(2)}) collective-permute-start(bf16[32,512]{1,0:T(8,128)(2,1)S(1)} %get-tuple-element.56), channel_id=1, source_target_pairs={{0,3},{1,4},{2,5},{3,6},{4,7},{5,0},{6,1},{7,2},{8,11},{9,12},{10,... | collective-permute-start | bytes 98312 | tf_op jit(solution)/shard_map/ppermute | solution.py:14
  150.2 1.5 collective-permute-start.35
  151.7 1.8 collective-permute-start.36
  156.2 1.8 collective-permute-start.38
  161.5 1.7 collective-permute-start.43
  165.3 3.3 %collective-permute-start.44 = (bf16[128,512]{1,0:T(8,128)(2,1)S(1)}, bf16[128,512]{1,0:T(8,128)(2,1)S(1)}, u32[]{:S(2)}, u32[]{:S(2)}) collective-permute-start(bf16[128,512]{1,0:T(8,128)(2,1)S(1)} %get-tuple-element.30), channel_id=1, source_target_pairs={{0,8},{8,16},{16,24},{24,0},{1,9},{9,17},{17,25},{25,1},{2,10},{10... | collective-permute-start | bytes 393224 | tf_op jit(solution)/shard_map/ppermute | solution.py:14
  168.6 1.6 collective-permute-start.45
  171.1 3.0 %collective-permute-done.44 = bf16[128,512]{1,0:T(8,128)(2,1)S(1)} collective-permute-done((bf16[128,512]{1,0:T(8,128)(2,1)S(1)}, bf16[128,512]{1,0:T(8,128)(2,1)S(1)}, u32[]{:S(2)}, u32[]{:S(2)}) %collective-permute-start.44) | collective-permute-done | bytes 131104 | tf_op jit(solution)/shard_map/ppermute | solution.py:14
  174.1 5.1 %collective-permute-done.45 = bf16[128,512]{1,0:T(8,128)(2,1)S(1)} collective-permute-done((bf16[128,512]{1,0:T(8,128)(2,1)S(1)}, bf16[128,512]{1,0:T(8,128)(2,1)S(1)}, u32[]{:S(2)}, u32[]{:S(2)}) %collective-permute-start.45) | collective-permute-done | bytes 131104 | tf_op jit(solution)/shard_map/ppermute | solution.py:14
  179.9 1.7 collective-permute-start.48
  181.7 1.8 collective-permute-start.49
  185.8 1.8 collective-permute-start.53
  (153 shorter events, 43.1 us)
Async XLA Ops:
  0.0 84.6 %collective-permute-start.3 = (bf16[2,32,512]{2,1,0:T(8,128)(2,1)}, bf16[2,32,512]{2,1,0:T(8,128)(2,1)S(1)}, u32[]{:S(2)}, u32[]{:S(2)}) collective-permute-start(bf16[2,32,512]{2,1,0:T(8,128)(2,1)} %bitcast.429), channel_id=1, source_target_pairs={{0,1},{1,2},{2,3},{3,4},{4,5},{5,6},{6,7},{7,0},{8,9},{9,10},{10,1... | collective-permute-start | bytes 196616 | tf_op jit(solution)/shard_map/ppermute | solution.py:14
  0.5 85.6 %collective-permute-start.4 = (bf16[2,32,512]{2,1,0:T(8,128)(2,1)}, bf16[2,32,512]{2,1,0:T(8,128)(2,1)S(1)}, u32[]{:S(2)}, u32[]{:S(2)}) collective-permute-start(bf16[2,32,512]{2,1,0:T(8,128)(2,1)} %bitcast.430), channel_id=1, source_target_pairs={{0,2},{1,3},{2,4},{3,5},{4,6},{5,7},{6,0},{7,1},{8,10},{9,11},{10,... | collective-permute-start | bytes 196616 | tf_op jit(solution)/shard_map/ppermute | solution.py:14
  3.0 91.7 %collective-permute-start.5 = (bf16[2,32,512]{2,1,0:T(8,128)(2,1)}, bf16[2,32,512]{2,1,0:T(8,128)(2,1)S(1)}, u32[]{:S(2)}, u32[]{:S(2)}) collective-permute-start(bf16[2,32,512]{2,1,0:T(8,128)(2,1)} %bitcast.431), channel_id=1, source_target_pairs={{0,3},{1,4},{2,5},{3,6},{4,7},{5,0},{6,1},{7,2},{8,11},{9,12},{10,... | collective-permute-start | bytes 196616 | tf_op jit(solution)/shard_map/ppermute | solution.py:14
  5.4 89.3 %collective-permute-start.6 = (bf16[2,32,512]{2,1,0:T(8,128)(2,1)}, bf16[2,32,512]{2,1,0:T(8,128)(2,1)S(1)}, u32[]{:S(2)}, u32[]{:S(2)}) collective-permute-start(bf16[2,32,512]{2,1,0:T(8,128)(2,1)} %bitcast.432), channel_id=1, source_target_pairs={{0,4},{1,5},{2,6},{3,7},{4,0},{5,1},{6,2},{7,3},{8,12},{9,13},{10,... | collective-permute-start | bytes 196616 | tf_op jit(solution)/shard_map/ppermute | solution.py:14
  5.9 64.1 %collective-permute-start = (s32[4,3]{1,0:T(4,128)}, s32[4,3]{1,0:T(4,128)S(1)}, u32[]{:S(2)}, u32[]{:S(2)}) collective-permute-start(s32[4,3]{1,0:T(4,128)} %param.7), channel_id=1, source_target_pairs={{0,8},{8,16},{16,24},{24,0},{1,9},{9,17},{17,25},{25,1},{2,10},{10... | collective-permute-start | bytes 152 | tf_op jit(solution)/shard_map/ppermute | solution.py:14
  78.5 16.2 %collective-permute-start.7 = (bf16[2,32,512]{2,1,0:T(8,128)(2,1)}, bf16[2,32,512]{2,1,0:T(8,128)(2,1)S(1)}, u32[]{:S(2)}, u32[]{:S(2)}) collective-permute-start(bf16[2,32,512]{2,1,0:T(8,128)(2,1)} %bitcast.433), channel_id=1, source_target_pairs={{0,5},{1,6},{2,7},{3,0},{4,1},{5,2},{6,3},{7,4},{8,13},{9,14},{10,... | collective-permute-start | bytes 196616 | tf_op jit(solution)/shard_map/ppermute | solution.py:14
  84.6 10.1 %collective-permute-start.8 = (bf16[2,32,512]{2,1,0:T(8,128)(2,1)}, bf16[2,32,512]{2,1,0:T(8,128)(2,1)S(1)}, u32[]{:S(2)}, u32[]{:S(2)}) collective-permute-start(bf16[2,32,512]{2,1,0:T(8,128)(2,1)} %bitcast.434), channel_id=1, source_target_pairs={{0,6},{1,7},{2,0},{3,1},{4,2},{5,3},{6,4},{7,5},{8,14},{9,15},{10,... | collective-permute-start | bytes 196616 | tf_op jit(solution)/shard_map/ppermute | solution.py:14
  86.1 8.6 %collective-permute-start.9 = (bf16[2,32,512]{2,1,0:T(8,128)(2,1)}, bf16[2,32,512]{2,1,0:T(8,128)(2,1)S(1)}, u32[]{:S(2)}, u32[]{:S(2)}) collective-permute-start(bf16[2,32,512]{2,1,0:T(8,128)(2,1)} %bitcast.435), channel_id=1, source_target_pairs={{0,7},{1,0},{2,1},{3,2},{4,3},{5,4},{6,5},{7,6},{8,15},{9,8},{10,9... | collective-permute-start | bytes 196616 | tf_op jit(solution)/shard_map/ppermute | solution.py:14
  97.2 8.8 %collective-permute-start.10 = (bf16[128,512]{1,0:T(8,128)(2,1)S(1)}, bf16[128,512]{1,0:T(8,128)(2,1)S(1)}, u32[]{:S(2)}, u32[]{:S(2)}) collective-permute-start(bf16[128,512]{1,0:T(8,128)(2,1)S(1)} %get-tuple-element.42), channel_id=1, source_target_pairs={{0,8},{8,16},{16,24},{24,0},{1,9},{9,17},{17,25},{25,1},{2,10},{10... | collective-permute-start | bytes 393224 | tf_op jit(solution)/shard_map/ppermute | solution.py:14
  98.8 10.8 %collective-permute-start.11 = (bf16[128,512]{1,0:T(8,128)(2,1)S(1)}, bf16[128,512]{1,0:T(8,128)(2,1)S(1)}, u32[]{:S(2)}, u32[]{:S(2)}) collective-permute-start(bf16[128,512]{1,0:T(8,128)(2,1)S(1)} %get-tuple-element.41), channel_id=1, source_target_pairs={{0,16},{8,24},{16,0},{24,8},{1,17},{9,25},{17,1},{25,9},{2,18},{10... | collective-permute-start | bytes 393224 | tf_op jit(solution)/shard_map/ppermute | solution.py:14
  101.9 7.9 %collective-permute-start.12 = (bf16[128,512]{1,0:T(8,128)(2,1)S(1)}, bf16[128,512]{1,0:T(8,128)(2,1)S(1)}, u32[]{:S(2)}, u32[]{:S(2)}) collective-permute-start(bf16[128,512]{1,0:T(8,128)(2,1)S(1)} %get-tuple-element.40), channel_id=1, source_target_pairs={{0,24},{8,0},{16,8},{24,16},{1,25},{9,1},{17,9},{25,17},{2,26},{10... | collective-permute-start | bytes 393224 | tf_op jit(solution)/shard_map/ppermute | solution.py:14
  111.1 5.9 %collective-permute-start.14 = (bf16[32,512]{1,0:T(8,128)(2,1)S(1)}, bf16[32,512]{1,0:T(8,128)(2,1)S(1)}, u32[]{:S(2)}, u32[]{:S(2)}) collective-permute-start(bf16[32,512]{1,0:T(8,128)(2,1)S(1)} %get-tuple-element.64), channel_id=1, source_target_pairs={{0,2},{1,3},{2,4},{3,5},{4,6},{5,7},{6,0},{7,1},{8,10},{9,11},{10,... | collective-permute-start | bytes 98312 | tf_op jit(solution)/shard_map/ppermute | solution.py:14
  111.4 8.8 %collective-permute-start.15 = (bf16[32,512]{1,0:T(8,128)(2,1)}, bf16[32,512]{1,0:T(8,128)(2,1)S(1)}, u32[]{:S(2)}, u32[]{:S(2)}) collective-permute-start(bf16[32,512]{1,0:T(8,128)(2,1)} %get-tuple-element.63), channel_id=1, source_target_pairs={{0,3},{1,4},{2,5},{3,6},{4,7},{5,0},{6,1},{7,2},{8,11},{9,12},{10,... | collective-permute-start | bytes 98312 | tf_op jit(solution)/shard_map/ppermute | solution.py:14
  113.8 6.4 %collective-permute-start.16 = (bf16[32,512]{1,0:T(8,128)(2,1)}, bf16[32,512]{1,0:T(8,128)(2,1)S(1)}, u32[]{:S(2)}, u32[]{:S(2)}) collective-permute-start(bf16[32,512]{1,0:T(8,128)(2,1)} %get-tuple-element.62), channel_id=1, source_target_pairs={{0,4},{1,5},{2,6},{3,7},{4,0},{5,1},{6,2},{7,3},{8,12},{9,13},{10,... | collective-permute-start | bytes 98312 | tf_op jit(solution)/shard_map/ppermute | solution.py:14
  114.4 5.9 %collective-permute-start.17 = (bf16[32,512]{1,0:T(8,128)(2,1)}, bf16[32,512]{1,0:T(8,128)(2,1)}, u32[]{:S(2)}, u32[]{:S(2)}) collective-permute-start(bf16[32,512]{1,0:T(8,128)(2,1)} %get-tuple-element.61), channel_id=1, source_target_pairs={{0,5},{1,6},{2,7},{3,0},{4,1},{5,2},{6,3},{7,4},{8,13},{9,14},{10,... | collective-permute-start | bytes 98312 | tf_op jit(solution)/shard_map/ppermute | solution.py:14
  115.3 5.0 %collective-permute-start.18 = (bf16[32,512]{1,0:T(8,128)(2,1)S(1)}, bf16[32,512]{1,0:T(8,128)(2,1)}, u32[]{:S(2)}, u32[]{:S(2)}) collective-permute-start(bf16[32,512]{1,0:T(8,128)(2,1)S(1)} %get-tuple-element.60), channel_id=1, source_target_pairs={{0,6},{1,7},{2,0},{3,1},{4,2},{5,3},{6,4},{7,5},{8,14},{9,15},{10,... | collective-permute-start | bytes 98312 | tf_op jit(solution)/shard_map/ppermute | solution.py:14
  121.6 5.6 %collective-permute-start.21 = (bf16[32,512]{1,0:T(8,128)(2,1)S(1)}, bf16[32,512]{1,0:T(8,128)(2,1)S(1)}, u32[]{:S(2)}, u32[]{:S(2)}) collective-permute-start(bf16[32,512]{1,0:T(8,128)(2,1)S(1)} %get-tuple-element.94), channel_id=1, source_target_pairs={{0,2},{1,3},{2,4},{3,5},{4,6},{5,7},{6,0},{7,1},{8,10},{9,11},{10,... | collective-permute-start | bytes 98312 | tf_op jit(solution)/shard_map/ppermute | solution.py:14
  124.2 5.4 %collective-permute-start.22 = (bf16[32,512]{1,0:T(8,128)(2,1)S(1)}, bf16[32,512]{1,0:T(8,128)(2,1)S(1)}, u32[]{:S(2)}, u32[]{:S(2)}) collective-permute-start(bf16[32,512]{1,0:T(8,128)(2,1)S(1)} %get-tuple-element.94), channel_id=1, source_target_pairs={{0,3},{1,4},{2,5},{3,6},{4,7},{5,0},{6,1},{7,2},{8,11},{9,12},{10,... | collective-permute-start | bytes 98312 | tf_op jit(solution)/shard_map/ppermute | solution.py:14
  124.6 4.9 %collective-permute-start.23 = (bf16[32,512]{1,0:T(8,128)(2,1)S(1)}, bf16[32,512]{1,0:T(8,128)(2,1)S(1)}, u32[]{:S(2)}, u32[]{:S(2)}) collective-permute-start(bf16[32,512]{1,0:T(8,128)(2,1)S(1)} %get-tuple-element.94), channel_id=1, source_target_pairs={{0,4},{1,5},{2,6},{3,7},{4,0},{5,1},{6,2},{7,3},{8,12},{9,13},{10,... | collective-permute-start | bytes 98312 | tf_op jit(solution)/shard_map/ppermute | solution.py:14
  131.6 8.3 %collective-permute-start.27 = (bf16[128,512]{1,0:T(8,128)(2,1)S(1)}, bf16[128,512]{1,0:T(8,128)(2,1)S(1)}, u32[]{:S(2)}, u32[]{:S(2)}) collective-permute-start(bf16[128,512]{1,0:T(8,128)(2,1)S(1)} %get-tuple-element.36), channel_id=1, source_target_pairs={{0,8},{8,16},{16,24},{24,0},{1,9},{9,17},{17,25},{25,1},{2,10},{10... | collective-permute-start | bytes 393224 | tf_op jit(solution)/shard_map/ppermute | solution.py:14
  134.8 10.3 %collective-permute-start.28 = (bf16[128,512]{1,0:T(8,128)(2,1)S(1)}, bf16[128,512]{1,0:T(8,128)(2,1)S(1)}, u32[]{:S(2)}, u32[]{:S(2)}) collective-permute-start(bf16[128,512]{1,0:T(8,128)(2,1)S(1)} %get-tuple-element.35), channel_id=1, source_target_pairs={{0,16},{8,24},{16,0},{24,8},{1,17},{9,25},{17,1},{25,9},{2,18},{10... | collective-permute-start | bytes 393224 | tf_op jit(solution)/shard_map/ppermute | solution.py:14
  136.1 8.9 %collective-permute-start.29 = (bf16[128,512]{1,0:T(8,128)(2,1)S(1)}, bf16[128,512]{1,0:T(8,128)(2,1)S(1)}, u32[]{:S(2)}, u32[]{:S(2)}) collective-permute-start(bf16[128,512]{1,0:T(8,128)(2,1)S(1)} %get-tuple-element.34), channel_id=1, source_target_pairs={{0,24},{8,0},{16,8},{24,16},{1,25},{9,1},{17,9},{25,17},{2,26},{10... | collective-permute-start | bytes 393224 | tf_op jit(solution)/shard_map/ppermute | solution.py:14
  145.8 5.9 %collective-permute-start.31 = (bf16[32,512]{1,0:T(8,128)(2,1)S(1)}, bf16[32,512]{1,0:T(8,128)(2,1)S(1)}, u32[]{:S(2)}, u32[]{:S(2)}) collective-permute-start(bf16[32,512]{1,0:T(8,128)(2,1)S(1)} %get-tuple-element.57), channel_id=1, source_target_pairs={{0,2},{1,3},{2,4},{3,5},{4,6},{5,7},{6,0},{7,1},{8,10},{9,11},{10,... | collective-permute-start | bytes 98312 | tf_op jit(solution)/shard_map/ppermute | solution.py:14
  147.4 6.1 %collective-permute-start.32 = (bf16[32,512]{1,0:T(8,128)(2,1)S(1)}, bf16[32,512]{1,0:T(8,128)(2,1)S(1)}, u32[]{:S(2)}, u32[]{:S(2)}) collective-permute-start(bf16[32,512]{1,0:T(8,128)(2,1)S(1)} %get-tuple-element.56), channel_id=1, source_target_pairs={{0,3},{1,4},{2,5},{3,6},{4,7},{5,0},{6,1},{7,2},{8,11},{9,12},{10,... | collective-permute-start | bytes 98312 | tf_op jit(solution)/shard_map/ppermute | solution.py:14
  155.3 5.1 %collective-permute-start.37 = (bf16[32,512]{1,0:T(8,128)(2,1)S(1)}, bf16[32,512]{1,0:T(8,128)(2,1)S(1)}, u32[]{:S(2)}, u32[]{:S(2)}) collective-permute-start(bf16[32,512]{1,0:T(8,128)(2,1)S(1)} %get-tuple-element.96), channel_id=1, source_target_pairs={{0,1},{1,2},{2,3},{3,4},{4,5},{5,6},{6,7},{7,0},{8,9},{9,10},{10,1... | collective-permute-start | bytes 98312 | tf_op jit(solution)/shard_map/ppermute | solution.py:14
  156.2 5.3 %collective-permute-start.38 = (bf16[32,512]{1,0:T(8,128)(2,1)S(1)}, bf16[32,512]{1,0:T(8,128)(2,1)S(1)}, u32[]{:S(2)}, u32[]{:S(2)}) collective-permute-start(bf16[32,512]{1,0:T(8,128)(2,1)S(1)} %get-tuple-element.96), channel_id=1, source_target_pairs={{0,2},{1,3},{2,4},{3,5},{4,6},{5,7},{6,0},{7,1},{8,10},{9,11},{10,... | collective-permute-start | bytes 98312 | tf_op jit(solution)/shard_map/ppermute | solution.py:14
  158.0 5.2 %collective-permute-start.39 = (bf16[32,512]{1,0:T(8,128)(2,1)S(1)}, bf16[32,512]{1,0:T(8,128)(2,1)S(1)}, u32[]{:S(2)}, u32[]{:S(2)}) collective-permute-start(bf16[32,512]{1,0:T(8,128)(2,1)S(1)} %get-tuple-element.96), channel_id=1, source_target_pairs={{0,3},{1,4},{2,5},{3,6},{4,7},{5,0},{6,1},{7,2},{8,11},{9,12},{10,... | collective-permute-start | bytes 98312 | tf_op jit(solution)/shard_map/ppermute | solution.py:14
  165.3 8.8 %collective-permute-start.44 = (bf16[128,512]{1,0:T(8,128)(2,1)S(1)}, bf16[128,512]{1,0:T(8,128)(2,1)S(1)}, u32[]{:S(2)}, u32[]{:S(2)}) collective-permute-start(bf16[128,512]{1,0:T(8,128)(2,1)S(1)} %get-tuple-element.30), channel_id=1, source_target_pairs={{0,8},{8,16},{16,24},{24,0},{1,9},{9,17},{17,25},{25,1},{2,10},{10... | collective-permute-start | bytes 393224 | tf_op jit(solution)/shard_map/ppermute | solution.py:14
  168.6 10.6 %collective-permute-start.45 = (bf16[128,512]{1,0:T(8,128)(2,1)S(1)}, bf16[128,512]{1,0:T(8,128)(2,1)S(1)}, u32[]{:S(2)}, u32[]{:S(2)}) collective-permute-start(bf16[128,512]{1,0:T(8,128)(2,1)S(1)} %get-tuple-element.29), channel_id=1, source_target_pairs={{0,16},{8,24},{16,0},{24,8},{1,17},{9,25},{17,1},{25,9},{2,18},{10... | collective-permute-start | bytes 393224 | tf_op jit(solution)/shard_map/ppermute | solution.py:14
  170.2 8.9 %collective-permute-start.46 = (bf16[128,512]{1,0:T(8,128)(2,1)S(1)}, bf16[128,512]{1,0:T(8,128)(2,1)S(1)}, u32[]{:S(2)}, u32[]{:S(2)}) collective-permute-start(bf16[128,512]{1,0:T(8,128)(2,1)S(1)} %get-tuple-element.28), channel_id=1, source_target_pairs={{0,24},{8,0},{16,8},{24,16},{1,25},{9,1},{17,9},{25,17},{2,26},{10... | collective-permute-start | bytes 393224 | tf_op jit(solution)/shard_map/ppermute | solution.py:14
  179.9 5.9 %collective-permute-start.48 = (bf16[32,512]{1,0:T(8,128)(2,1)S(1)}, bf16[32,512]{1,0:T(8,128)(2,1)S(1)}, u32[]{:S(2)}, u32[]{:S(2)}) collective-permute-start(bf16[32,512]{1,0:T(8,128)(2,1)S(1)} %get-tuple-element.50), channel_id=1, source_target_pairs={{0,2},{1,3},{2,4},{3,5},{4,6},{5,7},{6,0},{7,1},{8,10},{9,11},{10,... | collective-permute-start | bytes 98312 | tf_op jit(solution)/shard_map/ppermute | solution.py:14
  181.7 6.0 %collective-permute-start.49 = (bf16[32,512]{1,0:T(8,128)(2,1)S(1)}, bf16[32,512]{1,0:T(8,128)(2,1)S(1)}, u32[]{:S(2)}, u32[]{:S(2)}) collective-permute-start(bf16[32,512]{1,0:T(8,128)(2,1)S(1)} %get-tuple-element.49), channel_id=1, source_target_pairs={{0,3},{1,4},{2,5},{3,6},{4,7},{5,0},{6,1},{7,2},{8,11},{9,12},{10,... | collective-permute-start | bytes 98312 | tf_op jit(solution)/shard_map/ppermute | solution.py:14
  (26 other events, 316.0 us)

commit v3 on v2

--- a/solution.py
+++ b/solution.py
@@ -19,9 +19,15 @@
 
 
 def pick(pieces, index):
-    if len(pieces) <= 8:
-        return jnp.stack([lax.select_n(index[i], *pieces) for i in range(index.shape[0])])
-    return jnp.take(jnp.stack(pieces), index, axis=0)
+    if len(pieces) > 8:
+        return jnp.take(jnp.stack(pieces), index, axis=0)
+    chosen = index[:, None] == jnp.arange(len(pieces), dtype=index.dtype)[None, :]
+    spread = (slice(None),) + (None,) * pieces[0].ndim
+    total = None
+    for k, piece in enumerate(pieces):
+        term = jnp.where(chosen[:, k][spread], piece[None], jnp.zeros_like(piece)[None])
+        total = term if total is None else total + term
+    return total
 
 
 def body(tile_values, tile_lists, owner_map, inverses, excitations, history):
@@ -44,6 +50,10 @@
     wanted = (ahead[:, :, 0] // group_blocks == group_here) & (ahead[:, :, 2] > 0)
     want_block = jnp.sum(jnp.where(wanted, ahead[:, :, 0] % group_blocks, 0), axis=1)
     want_delay = jnp.sum(jnp.where(wanted, ahead[:, :, 2], 0), axis=1)
+    block_ids = jnp.arange(group_blocks, dtype=jnp.int32)
+    which_block = want_block[:, None] == block_ids[None, :]
+    from_near = which_block & (want_delay[:, None] == 1)
+    from_far = which_block & (want_delay[:, None] == 2)
 
     source_group = tile_lists[:, 0] // group_blocks
     observer_local = tile_lists[:, 1] % group_blocks
@@ -59,14 +69,15 @@
     for step in range(STEPS):
         near = blocks[DELAYS + step - 1]
         far = blocks[DELAYS + step - 2]
-        received = []
-        for k in range(groups):
-            a = lax.dynamic_index_in_dim(near, want_block[k], 0, keepdims=False)
-            b = lax.dynamic_index_in_dim(far, want_block[k], 0, keepdims=False)
-            piece = jnp.where(
-                want_delay[k] == 1, a, jnp.where(want_delay[k] == 2, b, jnp.zeros_like(a))
+        outgoing = None
+        for block in range(group_blocks):
+            term = jnp.where(from_near[:, block, None, None], near[block][None], 0) + jnp.where(
+                from_far[:, block, None, None], far[block][None], 0
             )
-            received.append(piece if k == 0 else shifted(piece, "group", groups, k))
+            outgoing = term if outgoing is None else outgoing + term
+        received = [outgoing[0]] + [
+            shifted(outgoing[k], "group", groups, k) for k in range(1, groups)
+        ]
         blocks_in = pick(received, source_shift)
         terms = jnp.einsum(
             "kes,kso->keo", blocks_in, tile_values, preferred_element_type=jnp.float32

time: 193 us -> 137 us (0.71); the launches traced: 190 us -> 137 us
  between operations: 71.3 us -> 15.9 us
  waiting for transfers between devices: 30.7 us -> 42.9 us
  starting transfers between devices: 71.3 us -> 62.4 us
  local copies, waits for them, and re-layouts: 5.54 us -> 3.2 us
    ppermute x54, waiting for transfers between devices: 30.7 us -> 42.9 us  [shifted(): return lax.ppermute(x, axis, [(i, (i + k) % n) for i in range(n)])]
    ppermute x54, starting transfers between devices: 71.3 us -> 62.4 us  [shifted(): return lax.ppermute(x, axis, [(i, (i + k) % n) for i in range(n)])]
    add x0 -> x6, other arithmetic: none -> 3.18 us  [the longest x3 2.52 us: pick(): total = term if total is None else total + term]
    unnamed x21 -> x0, other arithmetic: 2.83 us -> none
    slice x5 -> x3, local copies, waits for them, and re-layouts: 2.68 us -> 0.08 us  [body(): near[block][None]]
  transfers between devices with their start and end apart: 54 -> 54, of which waited for: 19 -> 20; matrix products, arithmetic and copies ran while one was open for 5% -> 5% of each run, Pallas kernels for 0% -> 0%
where the time goes in v3:
time: 137 us
  starting transfers between devices  62.4 us (46%)
  waiting for transfers between devices  42.9 us (31%)
  between operations  15.9 us (12%)
  other arithmetic  8.23 us (6%)
  matrix products  3.93 us (3%)
  local copies, waits for them, and re-layouts  3.2 us (2%)
    ppermute x54, starting transfers between devices, shifted(): return lax.ppermute(x, axis, [(i, (i + k) % n) for i in range(n)])  62.4 us
    ppermute x54, waiting for transfers between devices, shifted(): return lax.ppermute(x, axis, [(i, (i + k) % n) for i in range(n)])  42.9 us
  transfers between devices with their start and end apart: 54, of which 20 were waited for; matrix products, arithmetic and copies ran while one was open for 5% of the time, Pallas kernels for 0%

profile of v3, /device:TPU:0, one launch (start us, length us, event | category | flops | bytes accessed | tf_op | source)
XLA Modules:
  0.0 136.6 jit_solution(3188943818128262769)
XLA Ops:
  0.0 3.0 %collective-permute-start = (s32[4,3]{1,0:T(4,128)}, s32[4,3]{1,0:T(4,128)S(1)}, u32[]{:S(2)}, u32[]{:S(2)}) collective-permute-start(s32[4,3]{1,0:T(4,128)} %param.7), channel_id=1, source_target_pairs={{0,8},{8,16},{16,24},{24,0},{1,9},{9,17},{17,25},{25,1},{2,10},{10... | collective-permute-start | bytes 152 | tf_op jit(solution)/shard_map/ppermute | solution.py:14
  3.0 2.1 %collective-permute-start.2 = (s32[4,3]{1,0:T(4,128)}, s32[4,3]{1,0:T(4,128)S(1)}, u32[]{:S(2)}, u32[]{:S(2)}) collective-permute-start(s32[4,3]{1,0:T(4,128)} %param.7), channel_id=1, source_target_pairs={{0,24},{8,0},{16,8},{24,16},{1,25},{9,1},{17,9},{25,17},{2,26},{10... | collective-permute-start | bytes 152 | tf_op jit(solution)/shard_map/ppermute | solution.py:14
  27.0 1.5 %collective-permute-start.6 = (bf16[2,32,512]{2,1,0:T(8,128)(2,1)}, bf16[2,32,512]{2,1,0:T(8,128)(2,1)S(1)}, u32[]{:S(2)}, u32[]{:S(2)}) collective-permute-start(bf16[2,32,512]{2,1,0:T(8,128)(2,1)} %bitcast.269), channel_id=1, source_target_pairs={{0,4},{1,5},{2,6},{3,7},{4,0},{5,1},{6,2},{7,3},{8,12},{9,13},{10,... | collective-permute-start | bytes 196616 | tf_op jit(solution)/shard_map/ppermute | solution.py:14
  30.4 1.6 %collective-permute-start.4 = (bf16[2,32,512]{2,1,0:T(8,128)(2,1)}, bf16[2,32,512]{2,1,0:T(8,128)(2,1)S(1)}, u32[]{:S(2)}, u32[]{:S(2)}) collective-permute-start(bf16[2,32,512]{2,1,0:T(8,128)(2,1)} %bitcast.271), channel_id=1, source_target_pairs={{0,2},{1,3},{2,4},{3,5},{4,6},{5,7},{6,0},{7,1},{8,10},{9,11},{10,... | collective-permute-start | bytes 196616 | tf_op jit(solution)/shard_map/ppermute | solution.py:14
  32.9 3.1 %collective-permute-done.4 = bf16[2,32,512]{2,1,0:T(8,128)(2,1)S(1)} collective-permute-done((bf16[2,32,512]{2,1,0:T(8,128)(2,1)}, bf16[2,32,512]{2,1,0:T(8,128)(2,1)S(1)}, u32[]{:S(2)}, u32[]{:S(2)}) %collective-permute-start.4) | collective-permute-done | bytes 65568 | tf_op jit(solution)/shard_map/ppermute | solution.py:14
  39.9 1.7 %collective-permute-start.11 = (bf16[128,512]{1,0:T(8,128)(2,1)S(1)}, bf16[128,512]{1,0:T(8,128)(2,1)S(1)}, u32[]{:S(2)}, u32[]{:S(2)}) collective-permute-start(bf16[128,512]{1,0:T(8,128)(2,1)S(1)} %get-tuple-element.29), channel_id=1, source_target_pairs={{0,16},{8,24},{16,0},{24,8},{1,17},{9,25},{17,1},{25,9},{2,18},{10... | collective-permute-start | bytes 393224 | tf_op jit(solution)/shard_map/ppermute | solution.py:14
  44.2 8.2 %collective-permute-done.11 = bf16[128,512]{1,0:T(8,128)(2,1)S(1)} collective-permute-done((bf16[128,512]{1,0:T(8,128)(2,1)S(1)}, bf16[128,512]{1,0:T(8,128)(2,1)S(1)}, u32[]{:S(2)}, u32[]{:S(2)}) %collective-permute-start.11) | collective-permute-done | bytes 131104 | tf_op jit(solution)/shard_map/ppermute | solution.py:14
  54.7 3.0 %collective-permute-start.17 = (bf16[32,512]{1,0:T(8,128)(2,1)}, bf16[32,512]{1,0:T(8,128)(2,1)S(1)}, u32[]{:S(2)}, u32[]{:S(2)}) collective-permute-start(bf16[32,512]{1,0:T(8,128)(2,1)} %get-tuple-element.55), channel_id=1, source_target_pairs={{0,5},{1,6},{2,7},{3,0},{4,1},{5,2},{6,3},{7,4},{8,13},{9,14},{10,... | collective-permute-start | bytes 98312 | tf_op jit(solution)/shard_map/ppermute | solution.py:14
  58.2 1.5 %collective-permute-start.14 = (bf16[32,512]{1,0:T(8,128)(2,1)S(1)}, bf16[32,512]{1,0:T(8,128)(2,1)}, u32[]{:S(2)}, u32[]{:S(2)}) collective-permute-start(bf16[32,512]{1,0:T(8,128)(2,1)S(1)} %get-tuple-element.58), channel_id=1, source_target_pairs={{0,2},{1,3},{2,4},{3,5},{4,6},{5,7},{6,0},{7,1},{8,10},{9,11},{10,... | collective-permute-start | bytes 98312 | tf_op jit(solution)/shard_map/ppermute | solution.py:14
  59.8 2.4 %collective-permute-start.19 = (bf16[32,512]{1,0:T(8,128)(2,1)S(1)}, bf16[32,512]{1,0:T(8,128)(2,1)}, u32[]{:S(2)}, u32[]{:S(2)}) collective-permute-start(bf16[32,512]{1,0:T(8,128)(2,1)S(1)} %get-tuple-element.59), channel_id=1, source_target_pairs={{0,7},{1,0},{2,1},{3,2},{4,3},{5,4},{6,5},{7,6},{8,15},{9,8},{10,9... | collective-permute-start | bytes 98312 | tf_op jit(solution)/shard_map/ppermute | solution.py:14
  65.1 2.4 %collective-permute-start.26 = (bf16[32,512]{1,0:T(8,128)(2,1)S(1)}, bf16[32,512]{1,0:T(8,128)(2,1)S(1)}, u32[]{:S(2)}, u32[]{:S(2)}) collective-permute-start(bf16[32,512]{1,0:T(8,128)(2,1)S(1)} %get-tuple-element.88), channel_id=1, source_target_pairs={{0,7},{1,0},{2,1},{3,2},{4,3},{5,4},{6,5},{7,6},{8,15},{9,8},{10,9... | collective-permute-start | bytes 98312 | tf_op jit(solution)/shard_map/ppermute | solution.py:14
  67.8 1.5 %collective-permute-start.23 = (bf16[32,512]{1,0:T(8,128)(2,1)S(1)}, bf16[32,512]{1,0:T(8,128)(2,1)S(1)}, u32[]{:S(2)}, u32[]{:S(2)}) collective-permute-start(bf16[32,512]{1,0:T(8,128)(2,1)S(1)} %get-tuple-element.88), channel_id=1, source_target_pairs={{0,4},{1,5},{2,6},{3,7},{4,0},{5,1},{6,2},{7,3},{8,12},{9,13},{10,... | collective-permute-start | bytes 98312 | tf_op jit(solution)/shard_map/ppermute | solution.py:14
  69.5 2.9 %collective-permute-start.21 = (bf16[32,512]{1,0:T(8,128)(2,1)S(1)}, bf16[32,512]{1,0:T(8,128)(2,1)S(1)}, u32[]{:S(2)}, u32[]{:S(2)}) collective-permute-start(bf16[32,512]{1,0:T(8,128)(2,1)S(1)} %get-tuple-element.88), channel_id=1, source_target_pairs={{0,2},{1,3},{2,4},{3,5},{4,6},{5,7},{6,0},{7,1},{8,10},{9,11},{10,... | collective-permute-start | bytes 98312 | tf_op jit(solution)/shard_map/ppermute | solution.py:14
  72.9 2.7 %collective-permute-done.21 = bf16[32,512]{1,0:T(8,128)(2,1)S(1)} collective-permute-done((bf16[32,512]{1,0:T(8,128)(2,1)S(1)}, bf16[32,512]{1,0:T(8,128)(2,1)S(1)}, u32[]{:S(2)}, u32[]{:S(2)}) %collective-permute-start.21) | collective-permute-done | bytes 32800 | tf_op jit(solution)/shard_map/ppermute | solution.py:14
  79.2 1.9 %collective-permute-start.27 = (bf16[128,512]{1,0:T(8,128)(2,1)S(1)}, bf16[128,512]{1,0:T(8,128)(2,1)S(1)}, u32[]{:S(2)}, u32[]{:S(2)}) collective-permute-start(bf16[128,512]{1,0:T(8,128)(2,1)S(1)} %get-tuple-element.26), channel_id=1, source_target_pairs={{0,8},{8,16},{16,24},{24,0},{1,9},{9,17},{17,25},{25,1},{2,10},{10... | collective-permute-start | bytes 393224 | tf_op jit(solution)/shard_map/ppermute | solution.py:14
  81.2 2.5 %collective-permute-done.29 = bf16[128,512]{1,0:T(8,128)(2,1)S(1)} collective-permute-done((bf16[128,512]{1,0:T(8,128)(2,1)S(1)}, bf16[128,512]{1,0:T(8,128)(2,1)S(1)}, u32[]{:S(2)}, u32[]{:S(2)}) %collective-permute-start.29) | collective-permute-done | bytes 131104 | tf_op jit(solution)/shard_map/ppermute | solution.py:14
  83.7 6.0 %collective-permute-done.28 = bf16[128,512]{1,0:T(8,128)(2,1)S(1)} collective-permute-done((bf16[128,512]{1,0:T(8,128)(2,1)S(1)}, bf16[128,512]{1,0:T(8,128)(2,1)S(1)}, u32[]{:S(2)}, u32[]{:S(2)}) %collective-permute-start.28) | collective-permute-done | bytes 131104 | tf_op jit(solution)/shard_map/ppermute | solution.py:14
  91.3 1.5 %collective-permute-start.35 = (bf16[32,512]{1,0:T(8,128)(2,1)S(1)}, bf16[32,512]{1,0:T(8,128)(2,1)S(1)}, u32[]{:S(2)}, u32[]{:S(2)}) collective-permute-start(bf16[32,512]{1,0:T(8,128)(2,1)S(1)} %get-tuple-element.45), channel_id=1, source_target_pairs={{0,6},{1,7},{2,0},{3,1},{4,2},{5,3},{6,4},{7,5},{8,14},{9,15},{10,... | collective-permute-start | bytes 98312 | tf_op jit(solution)/shard_map/ppermute | solution.py:14
  92.8 1.5 %collective-permute-start.34 = (bf16[32,512]{1,0:T(8,128)(2,1)S(1)}, bf16[32,512]{1,0:T(8,128)(2,1)S(1)}, u32[]{:S(2)}, u32[]{:S(2)}) collective-permute-start(bf16[32,512]{1,0:T(8,128)(2,1)S(1)} %get-tuple-element.46), channel_id=1, source_target_pairs={{0,5},{1,6},{2,7},{3,0},{4,1},{5,2},{6,3},{7,4},{8,13},{9,14},{10,... | collective-permute-start | bytes 98312 | tf_op jit(solution)/shard_map/ppermute | solution.py:14
  94.3 1.4 %collective-permute-start.33 = (bf16[32,512]{1,0:T(8,128)(2,1)S(1)}, bf16[32,512]{1,0:T(8,128)(2,1)S(1)}, u32[]{:S(2)}, u32[]{:S(2)}) collective-permute-start(bf16[32,512]{1,0:T(8,128)(2,1)S(1)} %get-tuple-element.47), channel_id=1, source_target_pairs={{0,4},{1,5},{2,6},{3,7},{4,0},{5,1},{6,2},{7,3},{8,12},{9,13},{10,... | collective-permute-start | bytes 98312 | tf_op jit(solution)/shard_map/ppermute | solution.py:14
  96.9 1.7 %collective-permute-start.36 = (bf16[32,512]{1,0:T(8,128)(2,1)S(1)}, bf16[32,512]{1,0:T(8,128)(2,1)S(1)}, u32[]{:S(2)}, u32[]{:S(2)}) collective-permute-start(bf16[32,512]{1,0:T(8,128)(2,1)S(1)} %get-tuple-element.50), channel_id=1, source_target_pairs={{0,7},{1,0},{2,1},{3,2},{4,3},{5,4},{6,5},{7,6},{8,15},{9,8},{10,9... | collective-permute-start | bytes 98312 | tf_op jit(solution)/shard_map/ppermute | solution.py:14
  100.8 2.3 %collective-permute-start.43 = (bf16[32,512]{1,0:T(8,128)(2,1)S(1)}, bf16[32,512]{1,0:T(8,128)(2,1)S(1)}, u32[]{:S(2)}, u32[]{:S(2)}) collective-permute-start(bf16[32,512]{1,0:T(8,128)(2,1)S(1)} %get-tuple-element.90), channel_id=1, source_target_pairs={{0,7},{1,0},{2,1},{3,2},{4,3},{5,4},{6,5},{7,6},{8,15},{9,8},{10,9... | collective-permute-start | bytes 98312 | tf_op jit(solution)/shard_map/ppermute | solution.py:14
  106.1 2.9 %collective-permute-start.38 = (bf16[32,512]{1,0:T(8,128)(2,1)S(1)}, bf16[32,512]{1,0:T(8,128)(2,1)S(1)}, u32[]{:S(2)}, u32[]{:S(2)}) collective-permute-start(bf16[32,512]{1,0:T(8,128)(2,1)S(1)} %get-tuple-element.90), channel_id=1, source_target_pairs={{0,2},{1,3},{2,4},{3,5},{4,6},{5,7},{6,0},{7,1},{8,10},{9,11},{10,... | collective-permute-start | bytes 98312 | tf_op jit(solution)/shard_map/ppermute | solution.py:14
  109.4 1.8 %collective-permute-done.38 = bf16[32,512]{1,0:T(8,128)(2,1)S(1)} collective-permute-done((bf16[32,512]{1,0:T(8,128)(2,1)S(1)}, bf16[32,512]{1,0:T(8,128)(2,1)S(1)}, u32[]{:S(2)}, u32[]{:S(2)}) %collective-permute-start.38) | collective-permute-done | bytes 32800 | tf_op jit(solution)/shard_map/ppermute | solution.py:14
  111.2 2.0 %collective-permute-done.37 = bf16[32,512]{1,0:T(8,128)(2,1)S(1)} collective-permute-done((bf16[32,512]{1,0:T(8,128)(2,1)S(1)}, bf16[32,512]{1,0:T(8,128)(2,1)S(1)}, u32[]{:S(2)}, u32[]{:S(2)}) %collective-permute-start.37) | collective-permute-done | bytes 32800 | tf_op jit(solution)/shard_map/ppermute | solution.py:14
  114.1 1.5 %collective-permute-start.45 = (bf16[128,512]{1,0:T(8,128)(2,1)S(1)}, bf16[128,512]{1,0:T(8,128)(2,1)S(1)}, u32[]{:S(2)}, u32[]{:S(2)}) collective-permute-start(bf16[128,512]{1,0:T(8,128)(2,1)S(1)} %get-tuple-element.21), channel_id=1, source_target_pairs={{0,16},{8,24},{16,0},{24,8},{1,17},{9,25},{17,1},{25,9},{2,18},{10... | collective-permute-start | bytes 393224 | tf_op jit(solution)/shard_map/ppermute | solution.py:14
  115.6 1.9 %collective-permute-start.44 = (bf16[128,512]{1,0:T(8,128)(2,1)S(1)}, bf16[128,512]{1,0:T(8,128)(2,1)S(1)}, u32[]{:S(2)}, u32[]{:S(2)}) collective-permute-start(bf16[128,512]{1,0:T(8,128)(2,1)S(1)} %get-tuple-element.22), channel_id=1, source_target_pairs={{0,8},{8,16},{16,24},{24,0},{1,9},{9,17},{17,25},{25,1},{2,10},{10... | collective-permute-start | bytes 393224 | tf_op jit(solution)/shard_map/ppermute | solution.py:14
  117.6 3.3 %collective-permute-done.46 = bf16[128,512]{1,0:T(8,128)(2,1)S(1)} collective-permute-done((bf16[128,512]{1,0:T(8,128)(2,1)S(1)}, bf16[128,512]{1,0:T(8,128)(2,1)S(1)}, u32[]{:S(2)}, u32[]{:S(2)}) %collective-permute-start.46) | collective-permute-done | bytes 131104 | tf_op jit(solution)/shard_map/ppermute | solution.py:14
  120.8 4.7 %collective-permute-done.45 = bf16[128,512]{1,0:T(8,128)(2,1)S(1)} collective-permute-done((bf16[128,512]{1,0:T(8,128)(2,1)S(1)}, bf16[128,512]{1,0:T(8,128)(2,1)S(1)}, u32[]{:S(2)}, u32[]{:S(2)}) %collective-permute-start.45) | collective-permute-done | bytes 131104 | tf_op jit(solution)/shard_map/ppermute | solution.py:14
  126.3 2.0 %collective-permute-start.52 = (bf16[32,512]{1,0:T(8,128)(2,1)S(1)}, bf16[32,512]{1,0:T(8,128)(2,1)S(1)}, u32[]{:S(2)}, u32[]{:S(2)}) collective-permute-start(bf16[32,512]{1,0:T(8,128)(2,1)S(1)} %get-tuple-element.36), channel_id=1, source_target_pairs={{0,6},{1,7},{2,0},{3,1},{4,2},{5,3},{6,4},{7,5},{8,14},{9,15},{10,... | collective-permute-start | bytes 98312 | tf_op jit(solution)/shard_map/ppermute | solution.py:14
  128.3 1.4 %collective-permute-start.51 = (bf16[32,512]{1,0:T(8,128)(2,1)S(1)}, bf16[32,512]{1,0:T(8,128)(2,1)S(1)}, u32[]{:S(2)}, u32[]{:S(2)}) collective-permute-start(bf16[32,512]{1,0:T(8,128)(2,1)S(1)} %get-tuple-element.37), channel_id=1, source_target_pairs={{0,5},{1,6},{2,7},{3,0},{4,1},{5,2},{6,3},{7,4},{8,13},{9,14},{10,... | collective-permute-start | bytes 98312 | tf_op jit(solution)/shard_map/ppermute | solution.py:14
  131.9 2.2 %collective-permute-start.53 = (bf16[32,512]{1,0:T(8,128)(2,1)S(1)}, bf16[32,512]{1,0:T(8,128)(2,1)S(1)}, u32[]{:S(2)}, u32[]{:S(2)}) collective-permute-start(bf16[32,512]{1,0:T(8,128)(2,1)S(1)} %get-tuple-element.41), channel_id=1, source_target_pairs={{0,7},{1,0},{2,1},{3,2},{4,3},{5,4},{6,5},{7,6},{8,15},{9,8},{10,9... | collective-permute-start | bytes 98312 | tf_op jit(solution)/shard_map/ppermute | solution.py:14
  (188 shorter events, 40.4 us)
Async XLA Ops:
  0.0 26.6 %collective-permute-start = (s32[4,3]{1,0:T(4,128)}, s32[4,3]{1,0:T(4,128)S(1)}, u32[]{:S(2)}, u32[]{:S(2)}) collective-permute-start(s32[4,3]{1,0:T(4,128)} %param.7), channel_id=1, source_target_pairs={{0,8},{8,16},{16,24},{24,0},{1,9},{9,17},{17,25},{25,1},{2,10},{10... | collective-permute-start | bytes 152 | tf_op jit(solution)/shard_map/ppermute | solution.py:14
  3.0 23.9 %collective-permute-start.2 = (s32[4,3]{1,0:T(4,128)}, s32[4,3]{1,0:T(4,128)S(1)}, u32[]{:S(2)}, u32[]{:S(2)}) collective-permute-start(s32[4,3]{1,0:T(4,128)} %param.7), channel_id=1, source_target_pairs={{0,24},{8,0},{16,8},{24,16},{1,25},{9,1},{17,9},{25,17},{2,26},{10... | collective-permute-start | bytes 152 | tf_op jit(solution)/shard_map/ppermute | solution.py:14
  5.1 23.4 %collective-permute-start.1 = (s32[4,3]{1,0:T(4,128)}, s32[4,3]{1,0:T(4,128)S(1)}, u32[]{:S(2)}, u32[]{:S(2)}) collective-permute-start(s32[4,3]{1,0:T(4,128)} %param.7), channel_id=1, source_target_pairs={{0,16},{8,24},{16,0},{24,8},{1,17},{9,25},{17,1},{25,9},{2,18},{10... | collective-permute-start | bytes 152 | tf_op jit(solution)/shard_map/ppermute | solution.py:14
  6.1 24.3 %collective-permute-start.9 = (bf16[2,32,512]{2,1,0:T(8,128)(2,1)}, bf16[2,32,512]{2,1,0:T(8,128)(2,1)S(1)}, u32[]{:S(2)}, u32[]{:S(2)}) collective-permute-start(bf16[2,32,512]{2,1,0:T(8,128)(2,1)} %bitcast.266), channel_id=1, source_target_pairs={{0,7},{1,0},{2,1},{3,2},{4,3},{5,4},{6,5},{7,6},{8,15},{9,8},{10,9... | collective-permute-start | bytes 196616 | tf_op jit(solution)/shard_map/ppermute | solution.py:14
  7.1 24.9 %collective-permute-start.8 = (bf16[2,32,512]{2,1,0:T(8,128)(2,1)}, bf16[2,32,512]{2,1,0:T(8,128)(2,1)S(1)}, u32[]{:S(2)}, u32[]{:S(2)}) collective-permute-start(bf16[2,32,512]{2,1,0:T(8,128)(2,1)} %bitcast.267), channel_id=1, source_target_pairs={{0,6},{1,7},{2,0},{3,1},{4,2},{5,3},{6,4},{7,5},{8,14},{9,15},{10,... | collective-permute-start | bytes 196616 | tf_op jit(solution)/shard_map/ppermute | solution.py:14
  26.6 5.4 %collective-permute-start.7 = (bf16[2,32,512]{2,1,0:T(8,128)(2,1)}, bf16[2,32,512]{2,1,0:T(8,128)(2,1)S(1)}, u32[]{:S(2)}, u32[]{:S(2)}) collective-permute-start(bf16[2,32,512]{2,1,0:T(8,128)(2,1)} %bitcast.268), channel_id=1, source_target_pairs={{0,5},{1,6},{2,7},{3,0},{4,1},{5,2},{6,3},{7,4},{8,13},{9,14},{10,... | collective-permute-start | bytes 196616 | tf_op jit(solution)/shard_map/ppermute | solution.py:14
  27.0 5.7 %collective-permute-start.6 = (bf16[2,32,512]{2,1,0:T(8,128)(2,1)}, bf16[2,32,512]{2,1,0:T(8,128)(2,1)S(1)}, u32[]{:S(2)}, u32[]{:S(2)}) collective-permute-start(bf16[2,32,512]{2,1,0:T(8,128)(2,1)} %bitcast.269), channel_id=1, source_target_pairs={{0,4},{1,5},{2,6},{3,7},{4,0},{5,1},{6,2},{7,3},{8,12},{9,13},{10,... | collective-permute-start | bytes 196616 | tf_op jit(solution)/shard_map/ppermute | solution.py:14
  30.4 5.7 %collective-permute-start.4 = (bf16[2,32,512]{2,1,0:T(8,128)(2,1)}, bf16[2,32,512]{2,1,0:T(8,128)(2,1)S(1)}, u32[]{:S(2)}, u32[]{:S(2)}) collective-permute-start(bf16[2,32,512]{2,1,0:T(8,128)(2,1)} %bitcast.271), channel_id=1, source_target_pairs={{0,2},{1,3},{2,4},{3,5},{4,6},{5,7},{6,0},{7,1},{8,10},{9,11},{10,... | collective-permute-start | bytes 196616 | tf_op jit(solution)/shard_map/ppermute | solution.py:14
  38.5 5.7 %collective-permute-start.12 = (bf16[128,512]{1,0:T(8,128)(2,1)S(1)}, bf16[128,512]{1,0:T(8,128)(2,1)S(1)}, u32[]{:S(2)}, u32[]{:S(2)}) collective-permute-start(bf16[128,512]{1,0:T(8,128)(2,1)S(1)} %get-tuple-element.28), channel_id=1, source_target_pairs={{0,24},{8,0},{16,8},{24,16},{1,25},{9,1},{17,9},{25,17},{2,26},{10... | collective-permute-start | bytes 393224 | tf_op jit(solution)/shard_map/ppermute | solution.py:14
  39.9 12.5 %collective-permute-start.11 = (bf16[128,512]{1,0:T(8,128)(2,1)S(1)}, bf16[128,512]{1,0:T(8,128)(2,1)S(1)}, u32[]{:S(2)}, u32[]{:S(2)}) collective-permute-start(bf16[128,512]{1,0:T(8,128)(2,1)S(1)} %get-tuple-element.29), channel_id=1, source_target_pairs={{0,16},{8,24},{16,0},{24,8},{1,17},{9,25},{17,1},{25,9},{2,18},{10... | collective-permute-start | bytes 393224 | tf_op jit(solution)/shard_map/ppermute | solution.py:14
  41.6 10.8 %collective-permute-start.10 = (bf16[128,512]{1,0:T(8,128)(2,1)S(1)}, bf16[128,512]{1,0:T(8,128)(2,1)S(1)}, u32[]{:S(2)}, u32[]{:S(2)}) collective-permute-start(bf16[128,512]{1,0:T(8,128)(2,1)S(1)} %get-tuple-element.30), channel_id=1, source_target_pairs={{0,8},{8,16},{16,24},{24,0},{1,9},{9,17},{17,25},{25,1},{2,10},{10... | collective-permute-start | bytes 393224 | tf_op jit(solution)/shard_map/ppermute | solution.py:14
  53.8 5.9 %collective-permute-start.18 = (bf16[32,512]{1,0:T(8,128)(2,1)S(1)}, bf16[32,512]{1,0:T(8,128)(2,1)S(1)}, u32[]{:S(2)}, u32[]{:S(2)}) collective-permute-start(bf16[32,512]{1,0:T(8,128)(2,1)S(1)} %get-tuple-element.54), channel_id=1, source_target_pairs={{0,6},{1,7},{2,0},{3,1},{4,2},{5,3},{6,4},{7,5},{8,14},{9,15},{10,... | collective-permute-start | bytes 98312 | tf_op jit(solution)/shard_map/ppermute | solution.py:14
  54.7 9.3 %collective-permute-start.17 = (bf16[32,512]{1,0:T(8,128)(2,1)}, bf16[32,512]{1,0:T(8,128)(2,1)S(1)}, u32[]{:S(2)}, u32[]{:S(2)}) collective-permute-start(bf16[32,512]{1,0:T(8,128)(2,1)} %get-tuple-element.55), channel_id=1, source_target_pairs={{0,5},{1,6},{2,7},{3,0},{4,1},{5,2},{6,3},{7,4},{8,13},{9,14},{10,... | collective-permute-start | bytes 98312 | tf_op jit(solution)/shard_map/ppermute | solution.py:14
  57.7 6.3 %collective-permute-start.16 = (bf16[32,512]{1,0:T(8,128)(2,1)}, bf16[32,512]{1,0:T(8,128)(2,1)S(1)}, u32[]{:S(2)}, u32[]{:S(2)}) collective-permute-start(bf16[32,512]{1,0:T(8,128)(2,1)} %get-tuple-element.56), channel_id=1, source_target_pairs={{0,4},{1,5},{2,6},{3,7},{4,0},{5,1},{6,2},{7,3},{8,12},{9,13},{10,... | collective-permute-start | bytes 98312 | tf_op jit(solution)/shard_map/ppermute | solution.py:14
  58.2 5.8 %collective-permute-start.15 = (bf16[32,512]{1,0:T(8,128)(2,1)}, bf16[32,512]{1,0:T(8,128)(2,1)}, u32[]{:S(2)}, u32[]{:S(2)}) collective-permute-start(bf16[32,512]{1,0:T(8,128)(2,1)} %get-tuple-element.57), channel_id=1, source_target_pairs={{0,3},{1,4},{2,5},{3,6},{4,7},{5,0},{6,1},{7,2},{8,11},{9,12},{10,... | collective-permute-start | bytes 98312 | tf_op jit(solution)/shard_map/ppermute | solution.py:14
  58.2 5.8 %collective-permute-start.14 = (bf16[32,512]{1,0:T(8,128)(2,1)S(1)}, bf16[32,512]{1,0:T(8,128)(2,1)}, u32[]{:S(2)}, u32[]{:S(2)}) collective-permute-start(bf16[32,512]{1,0:T(8,128)(2,1)S(1)} %get-tuple-element.58), channel_id=1, source_target_pairs={{0,2},{1,3},{2,4},{3,5},{4,6},{5,7},{6,0},{7,1},{8,10},{9,11},{10,... | collective-permute-start | bytes 98312 | tf_op jit(solution)/shard_map/ppermute | solution.py:14
  69.5 6.1 %collective-permute-start.21 = (bf16[32,512]{1,0:T(8,128)(2,1)S(1)}, bf16[32,512]{1,0:T(8,128)(2,1)S(1)}, u32[]{:S(2)}, u32[]{:S(2)}) collective-permute-start(bf16[32,512]{1,0:T(8,128)(2,1)S(1)} %get-tuple-element.88), channel_id=1, source_target_pairs={{0,2},{1,3},{2,4},{3,5},{4,6},{5,7},{6,0},{7,1},{8,10},{9,11},{10,... | collective-permute-start | bytes 98312 | tf_op jit(solution)/shard_map/ppermute | solution.py:14
  77.9 5.8 %collective-permute-start.29 = (bf16[128,512]{1,0:T(8,128)(2,1)S(1)}, bf16[128,512]{1,0:T(8,128)(2,1)S(1)}, u32[]{:S(2)}, u32[]{:S(2)}) collective-permute-start(bf16[128,512]{1,0:T(8,128)(2,1)S(1)} %get-tuple-element.24), channel_id=1, source_target_pairs={{0,24},{8,0},{16,8},{24,16},{1,25},{9,1},{17,9},{25,17},{2,26},{10... | collective-permute-start | bytes 393224 | tf_op jit(solution)/shard_map/ppermute | solution.py:14
  77.9 11.8 %collective-permute-start.28 = (bf16[128,512]{1,0:T(8,128)(2,1)S(1)}, bf16[128,512]{1,0:T(8,128)(2,1)S(1)}, u32[]{:S(2)}, u32[]{:S(2)}) collective-permute-start(bf16[128,512]{1,0:T(8,128)(2,1)S(1)} %get-tuple-element.25), channel_id=1, source_target_pairs={{0,16},{8,24},{16,0},{24,8},{1,17},{9,25},{17,1},{25,9},{2,18},{10... | collective-permute-start | bytes 393224 | tf_op jit(solution)/shard_map/ppermute | solution.py:14
  79.2 10.5 %collective-permute-start.27 = (bf16[128,512]{1,0:T(8,128)(2,1)S(1)}, bf16[128,512]{1,0:T(8,128)(2,1)S(1)}, u32[]{:S(2)}, u32[]{:S(2)}) collective-permute-start(bf16[128,512]{1,0:T(8,128)(2,1)S(1)} %get-tuple-element.26), channel_id=1, source_target_pairs={{0,8},{8,16},{16,24},{24,0},{1,9},{9,17},{17,25},{25,1},{2,10},{10... | collective-permute-start | bytes 393224 | tf_op jit(solution)/shard_map/ppermute | solution.py:14
  91.3 5.6 %collective-permute-start.35 = (bf16[32,512]{1,0:T(8,128)(2,1)S(1)}, bf16[32,512]{1,0:T(8,128)(2,1)S(1)}, u32[]{:S(2)}, u32[]{:S(2)}) collective-permute-start(bf16[32,512]{1,0:T(8,128)(2,1)S(1)} %get-tuple-element.45), channel_id=1, source_target_pairs={{0,6},{1,7},{2,0},{3,1},{4,2},{5,3},{6,4},{7,5},{8,14},{9,15},{10,... | collective-permute-start | bytes 98312 | tf_op jit(solution)/shard_map/ppermute | solution.py:14
  92.8 5.9 %collective-permute-start.34 = (bf16[32,512]{1,0:T(8,128)(2,1)S(1)}, bf16[32,512]{1,0:T(8,128)(2,1)S(1)}, u32[]{:S(2)}, u32[]{:S(2)}) collective-permute-start(bf16[32,512]{1,0:T(8,128)(2,1)S(1)} %get-tuple-element.46), channel_id=1, source_target_pairs={{0,5},{1,6},{2,7},{3,0},{4,1},{5,2},{6,3},{7,4},{8,13},{9,14},{10,... | collective-permute-start | bytes 98312 | tf_op jit(solution)/shard_map/ppermute | solution.py:14
  100.8 5.3 %collective-permute-start.43 = (bf16[32,512]{1,0:T(8,128)(2,1)S(1)}, bf16[32,512]{1,0:T(8,128)(2,1)S(1)}, u32[]{:S(2)}, u32[]{:S(2)}) collective-permute-start(bf16[32,512]{1,0:T(8,128)(2,1)S(1)} %get-tuple-element.90), channel_id=1, source_target_pairs={{0,7},{1,0},{2,1},{3,2},{4,3},{5,4},{6,5},{7,6},{8,15},{9,8},{10,9... | collective-permute-start | bytes 98312 | tf_op jit(solution)/shard_map/ppermute | solution.py:14
  103.1 5.8 %collective-permute-start.42 = (bf16[32,512]{1,0:T(8,128)(2,1)S(1)}, bf16[32,512]{1,0:T(8,128)(2,1)S(1)}, u32[]{:S(2)}, u32[]{:S(2)}) collective-permute-start(bf16[32,512]{1,0:T(8,128)(2,1)S(1)} %get-tuple-element.90), channel_id=1, source_target_pairs={{0,6},{1,7},{2,0},{3,1},{4,2},{5,3},{6,4},{7,5},{8,14},{9,15},{10,... | collective-permute-start | bytes 98312 | tf_op jit(solution)/shard_map/ppermute | solution.py:14
  103.1 5.8 %collective-permute-start.41 = (bf16[32,512]{1,0:T(8,128)(2,1)S(1)}, bf16[32,512]{1,0:T(8,128)(2,1)S(1)}, u32[]{:S(2)}, u32[]{:S(2)}) collective-permute-start(bf16[32,512]{1,0:T(8,128)(2,1)S(1)} %get-tuple-element.90), channel_id=1, source_target_pairs={{0,5},{1,6},{2,7},{3,0},{4,1},{5,2},{6,3},{7,4},{8,13},{9,14},{10,... | collective-permute-start | bytes 98312 | tf_op jit(solution)/shard_map/ppermute | solution.py:14
  106.1 5.1 %collective-permute-start.38 = (bf16[32,512]{1,0:T(8,128)(2,1)S(1)}, bf16[32,512]{1,0:T(8,128)(2,1)S(1)}, u32[]{:S(2)}, u32[]{:S(2)}) collective-permute-start(bf16[32,512]{1,0:T(8,128)(2,1)S(1)} %get-tuple-element.90), channel_id=1, source_target_pairs={{0,2},{1,3},{2,4},{3,5},{4,6},{5,7},{6,0},{7,1},{8,10},{9,11},{10,... | collective-permute-start | bytes 98312 | tf_op jit(solution)/shard_map/ppermute | solution.py:14
  113.8 7.0 %collective-permute-start.46 = (bf16[128,512]{1,0:T(8,128)(2,1)S(1)}, bf16[128,512]{1,0:T(8,128)(2,1)S(1)}, u32[]{:S(2)}, u32[]{:S(2)}) collective-permute-start(bf16[128,512]{1,0:T(8,128)(2,1)S(1)} %get-tuple-element.20), channel_id=1, source_target_pairs={{0,24},{8,0},{16,8},{24,16},{1,25},{9,1},{17,9},{25,17},{2,26},{10... | collective-permute-start | bytes 393224 | tf_op jit(solution)/shard_map/ppermute | solution.py:14
  114.1 11.4 %collective-permute-start.45 = (bf16[128,512]{1,0:T(8,128)(2,1)S(1)}, bf16[128,512]{1,0:T(8,128)(2,1)S(1)}, u32[]{:S(2)}, u32[]{:S(2)}) collective-permute-start(bf16[128,512]{1,0:T(8,128)(2,1)S(1)} %get-tuple-element.21), channel_id=1, source_target_pairs={{0,16},{8,24},{16,0},{24,8},{1,17},{9,25},{17,1},{25,9},{2,18},{10... | collective-permute-start | bytes 393224 | tf_op jit(solution)/shard_map/ppermute | solution.py:14
  115.6 9.9 %collective-permute-start.44 = (bf16[128,512]{1,0:T(8,128)(2,1)S(1)}, bf16[128,512]{1,0:T(8,128)(2,1)S(1)}, u32[]{:S(2)}, u32[]{:S(2)}) collective-permute-start(bf16[128,512]{1,0:T(8,128)(2,1)S(1)} %get-tuple-element.22), channel_id=1, source_target_pairs={{0,8},{8,16},{16,24},{24,0},{1,9},{9,17},{17,25},{25,1},{2,10},{10... | collective-permute-start | bytes 393224 | tf_op jit(solution)/shard_map/ppermute | solution.py:14
  126.3 5.6 %collective-permute-start.52 = (bf16[32,512]{1,0:T(8,128)(2,1)S(1)}, bf16[32,512]{1,0:T(8,128)(2,1)S(1)}, u32[]{:S(2)}, u32[]{:S(2)}) collective-permute-start(bf16[32,512]{1,0:T(8,128)(2,1)S(1)} %get-tuple-element.36), channel_id=1, source_target_pairs={{0,6},{1,7},{2,0},{3,1},{4,2},{5,3},{6,4},{7,5},{8,14},{9,15},{10,... | collective-permute-start | bytes 98312 | tf_op jit(solution)/shard_map/ppermute | solution.py:14
  128.3 5.8 %collective-permute-start.51 = (bf16[32,512]{1,0:T(8,128)(2,1)S(1)}, bf16[32,512]{1,0:T(8,128)(2,1)S(1)}, u32[]{:S(2)}, u32[]{:S(2)}) collective-permute-start(bf16[32,512]{1,0:T(8,128)(2,1)S(1)} %get-tuple-element.37), channel_id=1, source_target_pairs={{0,5},{1,6},{2,7},{3,0},{4,1},{5,2},{6,3},{7,4},{8,13},{9,14},{10,... | collective-permute-start | bytes 98312 | tf_op jit(solution)/shard_map/ppermute | solution.py:14
  130.7 5.0 %collective-permute-start.48 = (bf16[32,512]{1,0:T(8,128)(2,1)S(1)}, bf16[32,512]{1,0:T(8,128)(2,1)S(1)}, u32[]{:S(2)}, u32[]{:S(2)}) collective-permute-start(bf16[32,512]{1,0:T(8,128)(2,1)S(1)} %get-tuple-element.40), channel_id=1, source_target_pairs={{0,2},{1,3},{2,4},{3,5},{4,6},{5,7},{6,0},{7,1},{8,10},{9,11},{10,... | collective-permute-start | bytes 98312 | tf_op jit(solution)/shard_map/ppermute | solution.py:14
  (53 other events, 846.7 us)

commit v4 on v3

--- a/solution.py
+++ b/solution.py
@@ -89,12 +89,10 @@
                 jnp.sum(jnp.where(chosen[:, None, None], terms, 0.0), axis=0)
             )
         slots = jnp.stack(partial_sums).astype(jnp.bfloat16).reshape(members, share, BLOCK)
-        field = slots[0].astype(jnp.float32) * 0.0
-        for k in range(members):
-            piece = lax.dynamic_index_in_dim(slots, send_slot[k], 0, keepdims=False)
-            if k:
-                piece = shifted(piece, "member", members, k)
-            field = field + piece.astype(jnp.float32)
+        sent = pick([slots[s] for s in range(members)], send_slot)
+        field = sent[0].astype(jnp.float32)
+        for k in range(1, members):
+            field = field + shifted(sent[k], "member", members, k).astype(jnp.float32)
         residual = (excitations[step, 0] - field).astype(jnp.bfloat16)
         current = jnp.dot(residual, inverses[0], preferred_element_type=jnp.float32)
         results.append(current)

time: 137 us -> 121 us (0.88)
  between operations: 15.9 us -> 0.45 us
  waiting for transfers between devices: 42.9 us -> 47.9 us
  starting transfers between devices: 62.4 us -> 59.4 us
  matrix products: 3.93 us -> 2.48 us
  local copies, waits for them, and re-layouts: 3.2 us -> 1.82 us
    ppermute x54, waiting for transfers between devices: 42.9 us -> 47.9 us  [shifted(): return lax.ppermute(x, axis, [(i, (i + k) % n) for i in range(n)])]
    ppermute x54, starting transfers between devices: 62.4 us -> 59.4 us  [shifted(): return lax.ppermute(x, axis, [(i, (i + k) % n) for i in range(n)])]
  transfers between devices with their start and end apart: 54 -> 54, of which waited for: 20 -> 23; matrix products, arithmetic and copies ran while one was open for 5% -> 5% of each run, Pallas kernels for 0% -> 0%
where the time goes in v4:
time: 121 us; the launch traced here: 120 us
  starting transfers between devices  59.4 us (49%)
  waiting for transfers between devices  47.9 us (40%)
  other arithmetic  8.38 us (7%)
  matrix products  2.48 us (2%)
  local copies, waits for them, and re-layouts  1.82 us (2%)
    ppermute x54, starting transfers between devices, shifted(): return lax.ppermute(x, axis, [(i, (i + k) % n) for i in range(n)])  59.4 us
    ppermute x54, waiting for transfers between devices, shifted(): return lax.ppermute(x, axis, [(i, (i + k) % n) for i in range(n)])  47.9 us
    add x6, other arithmetic, pick(): total = term if total is None else total + term  2.54 us
  transfers between devices with their start and end apart: 54, of which 23 were waited for; matrix products, arithmetic and copies ran while one was open for 5% of the time, Pallas kernels for 0%

profile of v4, /device:TPU:0, one launch (start us, length us, event | category | flops | bytes accessed | tf_op | source)
XLA Modules:
  0.0 120.3 jit_solution(11036863549072156966)
XLA Ops:
  0.0 3.0 %collective-permute-start = (s32[4,3]{1,0:T(4,128)}, s32[4,3]{1,0:T(4,128)S(1)}, u32[]{:S(2)}, u32[]{:S(2)}) collective-permute-start(s32[4,3]{1,0:T(4,128)} %param.7), channel_id=1, source_target_pairs={{0,8},{8,16},{16,24},{24,0},{1,9},{9,17},{17,25},{25,1},{2,10},{10... | collective-permute-start | bytes 152 | tf_op jit(solution)/shard_map/ppermute | solution.py:14
  3.0 2.1 %collective-permute-start.2 = (s32[4,3]{1,0:T(4,128)}, s32[4,3]{1,0:T(4,128)S(1)}, u32[]{:S(2)}, u32[]{:S(2)}) collective-permute-start(s32[4,3]{1,0:T(4,128)} %param.7), channel_id=1, source_target_pairs={{0,24},{8,0},{16,8},{24,16},{1,25},{9,1},{17,9},{25,17},{2,26},{10... | collective-permute-start | bytes 152 | tf_op jit(solution)/shard_map/ppermute | solution.py:14
  7.1 1.4 %collective-permute-start.8 = (bf16[2,32,512]{2,1,0:T(8,128)(2,1)}, bf16[2,32,512]{2,1,0:T(8,128)(2,1)S(1)}, u32[]{:S(2)}, u32[]{:S(2)}) collective-permute-start(bf16[2,32,512]{2,1,0:T(8,128)(2,1)} %bitcast.281), channel_id=1, source_target_pairs={{0,6},{1,7},{2,0},{3,1},{4,2},{5,3},{6,4},{7,5},{8,14},{9,15},{10,... | collective-permute-start | bytes 196616 | tf_op jit(solution)/shard_map/ppermute | solution.py:14
  13.1 1.5 %collective-permute-start.6 = (bf16[2,32,512]{2,1,0:T(8,128)(2,1)}, bf16[2,32,512]{2,1,0:T(8,128)(2,1)S(1)}, u32[]{:S(2)}, u32[]{:S(2)}) collective-permute-start(bf16[2,32,512]{2,1,0:T(8,128)(2,1)} %bitcast.283), channel_id=1, source_target_pairs={{0,4},{1,5},{2,6},{3,7},{4,0},{5,1},{6,2},{7,3},{8,12},{9,13},{10,... | collective-permute-start | bytes 196616 | tf_op jit(solution)/shard_map/ppermute | solution.py:14
  16.5 1.6 %collective-permute-start.4 = (bf16[2,32,512]{2,1,0:T(8,128)(2,1)}, bf16[2,32,512]{2,1,0:T(8,128)(2,1)S(1)}, u32[]{:S(2)}, u32[]{:S(2)}) collective-permute-start(bf16[2,32,512]{2,1,0:T(8,128)(2,1)} %bitcast.285), channel_id=1, source_target_pairs={{0,2},{1,3},{2,4},{3,5},{4,6},{5,7},{6,0},{7,1},{8,10},{9,11},{10,... | collective-permute-start | bytes 196616 | tf_op jit(solution)/shard_map/ppermute | solution.py:14
  19.1 3.1 %collective-permute-done.4 = bf16[2,32,512]{2,1,0:T(8,128)(2,1)S(1)} collective-permute-done((bf16[2,32,512]{2,1,0:T(8,128)(2,1)}, bf16[2,32,512]{2,1,0:T(8,128)(2,1)S(1)}, u32[]{:S(2)}, u32[]{:S(2)}) %collective-permute-start.4) | collective-permute-done | bytes 65568 | tf_op jit(solution)/shard_map/ppermute | solution.py:14
  24.6 1.4 %collective-permute-start.12 = (bf16[128,512]{1,0:T(8,128)(2,1)S(1)}, bf16[128,512]{1,0:T(8,128)(2,1)S(1)}, u32[]{:S(2)}, u32[]{:S(2)}) collective-permute-start(bf16[128,512]{1,0:T(8,128)(2,1)S(1)} %get-tuple-element.28), channel_id=1, source_target_pairs={{0,24},{8,0},{16,8},{24,16},{1,25},{9,1},{17,9},{25,17},{2,26},{10... | collective-permute-start | bytes 393224 | tf_op jit(solution)/shard_map/ppermute | solution.py:14
  26.0 1.7 %collective-permute-start.11 = (bf16[128,512]{1,0:T(8,128)(2,1)S(1)}, bf16[128,512]{1,0:T(8,128)(2,1)S(1)}, u32[]{:S(2)}, u32[]{:S(2)}) collective-permute-start(bf16[128,512]{1,0:T(8,128)(2,1)S(1)} %get-tuple-element.29), channel_id=1, source_target_pairs={{0,16},{8,24},{16,0},{24,8},{1,17},{9,25},{17,1},{25,9},{2,18},{10... | collective-permute-start | bytes 393224 | tf_op jit(solution)/shard_map/ppermute | solution.py:14
  30.3 8.2 %collective-permute-done.11 = bf16[128,512]{1,0:T(8,128)(2,1)S(1)} collective-permute-done((bf16[128,512]{1,0:T(8,128)(2,1)S(1)}, bf16[128,512]{1,0:T(8,128)(2,1)S(1)}, u32[]{:S(2)}, u32[]{:S(2)}) %collective-permute-start.11) | collective-permute-done | bytes 131104 | tf_op jit(solution)/shard_map/ppermute | solution.py:14
  39.6 2.6 %collective-permute-start.19 = (bf16[32,512]{1,0:T(8,128)(2,1)S(1)}, bf16[32,512]{1,0:T(8,128)(2,1)S(1)}, u32[]{:S(2)}, u32[]{:S(2)}) collective-permute-start(bf16[32,512]{1,0:T(8,128)(2,1)S(1)} %get-tuple-element.70), channel_id=1, source_target_pairs={{0,7},{1,0},{2,1},{3,2},{4,3},{5,4},{6,5},{7,6},{8,15},{9,8},{10,9... | collective-permute-start | bytes 98312 | tf_op jit(solution)/shard_map/ppermute | solution.py:14
  45.3 2.9 %collective-permute-start.14 = (bf16[32,512]{1,0:T(8,128)(2,1)S(1)}, bf16[32,512]{1,0:T(8,128)(2,1)S(1)}, u32[]{:S(2)}, u32[]{:S(2)}) collective-permute-start(bf16[32,512]{1,0:T(8,128)(2,1)S(1)} %get-tuple-element.75), channel_id=1, source_target_pairs={{0,2},{1,3},{2,4},{3,5},{4,6},{5,7},{6,0},{7,1},{8,10},{9,11},{10,... | collective-permute-start | bytes 98312 | tf_op jit(solution)/shard_map/ppermute | solution.py:14
  48.6 1.7 %collective-permute-done.14 = bf16[32,512]{1,0:T(8,128)(2,1)S(1)} collective-permute-done((bf16[32,512]{1,0:T(8,128)(2,1)S(1)}, bf16[32,512]{1,0:T(8,128)(2,1)S(1)}, u32[]{:S(2)}, u32[]{:S(2)}) %collective-permute-start.14) | collective-permute-done | bytes 32800 | tf_op jit(solution)/shard_map/ppermute | solution.py:14
  50.6 2.1 %collective-permute-start.25 = (bf16[32,512]{1,0:T(8,128)(2,1)S(1)}, bf16[32,512]{1,0:T(8,128)(2,1)S(1)}, u32[]{:S(2)}, u32[]{:S(2)}) collective-permute-start(bf16[32,512]{1,0:T(8,128)(2,1)S(1)} %get-tuple-element.112), channel_id=1, source_target_pairs={{0,6},{1,7},{2,0},{3,1},{4,2},{5,3},{6,4},{7,5},{8,14},{9,15},{10,... | collective-permute-start | bytes 98312 | tf_op jit(solution)/shard_map/ppermute | solution.py:14
  57.8 2.3 %collective-permute-done.21 = bf16[32,512]{1,0:T(8,128)(2,1)S(1)} collective-permute-done((bf16[32,512]{1,0:T(8,128)(2,1)S(1)}, bf16[32,512]{1,0:T(8,128)(2,1)S(1)}, u32[]{:S(2)}, u32[]{:S(2)}) %collective-permute-start.21) | collective-permute-done | bytes 32800 | tf_op jit(solution)/shard_map/ppermute | solution.py:14
  62.7 1.9 %collective-permute-start.27 = (bf16[128,512]{1,0:T(8,128)(2,1)S(1)}, bf16[128,512]{1,0:T(8,128)(2,1)S(1)}, u32[]{:S(2)}, u32[]{:S(2)}) collective-permute-start(bf16[128,512]{1,0:T(8,128)(2,1)S(1)} %get-tuple-element.26), channel_id=1, source_target_pairs={{0,8},{8,16},{16,24},{24,0},{1,9},{9,17},{17,25},{25,1},{2,10},{10... | collective-permute-start | bytes 393224 | tf_op jit(solution)/shard_map/ppermute | solution.py:14
  64.6 1.9 %collective-permute-done.29 = bf16[128,512]{1,0:T(8,128)(2,1)S(1)} collective-permute-done((bf16[128,512]{1,0:T(8,128)(2,1)S(1)}, bf16[128,512]{1,0:T(8,128)(2,1)S(1)}, u32[]{:S(2)}, u32[]{:S(2)}) %collective-permute-start.29) | collective-permute-done | bytes 131104 | tf_op jit(solution)/shard_map/ppermute | solution.py:14
  66.5 6.9 %collective-permute-done.28 = bf16[128,512]{1,0:T(8,128)(2,1)S(1)} collective-permute-done((bf16[128,512]{1,0:T(8,128)(2,1)S(1)}, bf16[128,512]{1,0:T(8,128)(2,1)S(1)}, u32[]{:S(2)}, u32[]{:S(2)}) %collective-permute-start.28) | collective-permute-done | bytes 131104 | tf_op jit(solution)/shard_map/ppermute | solution.py:14
  74.5 2.6 %collective-permute-start.36 = (bf16[32,512]{1,0:T(8,128)(2,1)S(1)}, bf16[32,512]{1,0:T(8,128)(2,1)S(1)}, u32[]{:S(2)}, u32[]{:S(2)}) collective-permute-start(bf16[32,512]{1,0:T(8,128)(2,1)S(1)} %get-tuple-element.53), channel_id=1, source_target_pairs={{0,7},{1,0},{2,1},{3,2},{4,3},{5,4},{6,5},{7,6},{8,15},{9,8},{10,9... | collective-permute-start | bytes 98312 | tf_op jit(solution)/shard_map/ppermute | solution.py:14
  77.5 1.4 %collective-permute-start.33 = (bf16[32,512]{1,0:T(8,128)(2,1)S(1)}, bf16[32,512]{1,0:T(8,128)(2,1)S(1)}, u32[]{:S(2)}, u32[]{:S(2)}) collective-permute-start(bf16[32,512]{1,0:T(8,128)(2,1)S(1)} %get-tuple-element.56), channel_id=1, source_target_pairs={{0,4},{1,5},{2,6},{3,7},{4,0},{5,1},{6,2},{7,3},{8,12},{9,13},{10,... | collective-permute-start | bytes 98312 | tf_op jit(solution)/shard_map/ppermute | solution.py:14
  79.4 2.8 %collective-permute-start.31 = (bf16[32,512]{1,0:T(8,128)(2,1)S(1)}, bf16[32,512]{1,0:T(8,128)(2,1)S(1)}, u32[]{:S(2)}, u32[]{:S(2)}) collective-permute-start(bf16[32,512]{1,0:T(8,128)(2,1)S(1)} %get-tuple-element.58), channel_id=1, source_target_pairs={{0,2},{1,3},{2,4},{3,5},{4,6},{5,7},{6,0},{7,1},{8,10},{9,11},{10,... | collective-permute-start | bytes 98312 | tf_op jit(solution)/shard_map/ppermute | solution.py:14
  82.6 2.6 %collective-permute-done.31 = bf16[32,512]{1,0:T(8,128)(2,1)S(1)} collective-permute-done((bf16[32,512]{1,0:T(8,128)(2,1)S(1)}, bf16[32,512]{1,0:T(8,128)(2,1)S(1)}, u32[]{:S(2)}, u32[]{:S(2)}) %collective-permute-start.31) | collective-permute-done | bytes 32800 | tf_op jit(solution)/shard_map/ppermute | solution.py:14
  85.4 1.7 %collective-permute-start.42 = (bf16[32,512]{1,0:T(8,128)(2,1)S(1)}, bf16[32,512]{1,0:T(8,128)(2,1)S(1)}, u32[]{:S(2)}, u32[]{:S(2)}) collective-permute-start(bf16[32,512]{1,0:T(8,128)(2,1)S(1)} %get-tuple-element.114), channel_id=1, source_target_pairs={{0,6},{1,7},{2,0},{3,1},{4,2},{5,3},{6,4},{7,5},{8,14},{9,15},{10,... | collective-permute-start | bytes 98312 | tf_op jit(solution)/shard_map/ppermute | solution.py:14
  87.6 1.4 %collective-permute-start.40 = (bf16[32,512]{1,0:T(8,128)(2,1)S(1)}, bf16[32,512]{1,0:T(8,128)(2,1)S(1)}, u32[]{:S(2)}, u32[]{:S(2)}) collective-permute-start(bf16[32,512]{1,0:T(8,128)(2,1)S(1)} %get-tuple-element.114), channel_id=1, source_target_pairs={{0,4},{1,5},{2,6},{3,7},{4,0},{5,1},{6,2},{7,3},{8,12},{9,13},{10,... | collective-permute-start | bytes 98312 | tf_op jit(solution)/shard_map/ppermute | solution.py:14
  92.3 2.0 %collective-permute-done.38 = bf16[32,512]{1,0:T(8,128)(2,1)S(1)} collective-permute-done((bf16[32,512]{1,0:T(8,128)(2,1)S(1)}, bf16[32,512]{1,0:T(8,128)(2,1)S(1)}, u32[]{:S(2)}, u32[]{:S(2)}) %collective-permute-start.38) | collective-permute-done | bytes 32800 | tf_op jit(solution)/shard_map/ppermute | solution.py:14
  95.3 1.7 %collective-permute-start.45 = (bf16[128,512]{1,0:T(8,128)(2,1)S(1)}, bf16[128,512]{1,0:T(8,128)(2,1)S(1)}, u32[]{:S(2)}, u32[]{:S(2)}) collective-permute-start(bf16[128,512]{1,0:T(8,128)(2,1)S(1)} %get-tuple-element.21), channel_id=1, source_target_pairs={{0,16},{8,24},{16,0},{24,8},{1,17},{9,25},{17,1},{25,9},{2,18},{10... | collective-permute-start | bytes 393224 | tf_op jit(solution)/shard_map/ppermute | solution.py:14
  97.1 1.9 %collective-permute-start.44 = (bf16[128,512]{1,0:T(8,128)(2,1)S(1)}, bf16[128,512]{1,0:T(8,128)(2,1)S(1)}, u32[]{:S(2)}, u32[]{:S(2)}) collective-permute-start(bf16[128,512]{1,0:T(8,128)(2,1)S(1)} %get-tuple-element.22), channel_id=1, source_target_pairs={{0,8},{8,16},{16,24},{24,0},{1,9},{9,17},{17,25},{25,1},{2,10},{10... | collective-permute-start | bytes 393224 | tf_op jit(solution)/shard_map/ppermute | solution.py:14
  99.0 1.5 %collective-permute-done.46 = bf16[128,512]{1,0:T(8,128)(2,1)S(1)} collective-permute-done((bf16[128,512]{1,0:T(8,128)(2,1)S(1)}, bf16[128,512]{1,0:T(8,128)(2,1)S(1)}, u32[]{:S(2)}, u32[]{:S(2)}) %collective-permute-start.46) | collective-permute-done | bytes 131104 | tf_op jit(solution)/shard_map/ppermute | solution.py:14
  100.5 7.2 %collective-permute-done.45 = bf16[128,512]{1,0:T(8,128)(2,1)S(1)} collective-permute-done((bf16[128,512]{1,0:T(8,128)(2,1)S(1)}, bf16[128,512]{1,0:T(8,128)(2,1)S(1)}, u32[]{:S(2)}, u32[]{:S(2)}) %collective-permute-start.45) | collective-permute-done | bytes 131104 | tf_op jit(solution)/shard_map/ppermute | solution.py:14
  108.7 2.6 %collective-permute-start.53 = (bf16[32,512]{1,0:T(8,128)(2,1)S(1)}, bf16[32,512]{1,0:T(8,128)(2,1)S(1)}, u32[]{:S(2)}, u32[]{:S(2)}) collective-permute-start(bf16[32,512]{1,0:T(8,128)(2,1)S(1)} %get-tuple-element.36), channel_id=1, source_target_pairs={{0,7},{1,0},{2,1},{3,2},{4,3},{5,4},{6,5},{7,6},{8,15},{9,8},{10,9... | collective-permute-start | bytes 98312 | tf_op jit(solution)/shard_map/ppermute | solution.py:14
  113.1 1.4 %collective-permute-start.49 = (bf16[32,512]{1,0:T(8,128)(2,1)S(1)}, bf16[32,512]{1,0:T(8,128)(2,1)S(1)}, u32[]{:S(2)}, u32[]{:S(2)}) collective-permute-start(bf16[32,512]{1,0:T(8,128)(2,1)S(1)} %get-tuple-element.40), channel_id=1, source_target_pairs={{0,3},{1,4},{2,5},{3,6},{4,7},{5,0},{6,1},{7,2},{8,11},{9,12},{10,... | collective-permute-start | bytes 98312 | tf_op jit(solution)/shard_map/ppermute | solution.py:14
  114.5 2.6 %collective-permute-start.48 = (bf16[32,512]{1,0:T(8,128)(2,1)S(1)}, bf16[32,512]{1,0:T(8,128)(2,1)S(1)}, u32[]{:S(2)}, u32[]{:S(2)}) collective-permute-start(bf16[32,512]{1,0:T(8,128)(2,1)S(1)} %get-tuple-element.41), channel_id=1, source_target_pairs={{0,2},{1,3},{2,4},{3,5},{4,6},{5,7},{6,0},{7,1},{8,10},{9,11},{10,... | collective-permute-start | bytes 98312 | tf_op jit(solution)/shard_map/ppermute | solution.py:14
  117.6 1.8 %collective-permute-done.48 = bf16[32,512]{1,0:T(8,128)(2,1)S(1)} collective-permute-done((bf16[32,512]{1,0:T(8,128)(2,1)S(1)}, bf16[32,512]{1,0:T(8,128)(2,1)S(1)}, u32[]{:S(2)}, u32[]{:S(2)}) %collective-permute-start.48) | collective-permute-done | bytes 32800 | tf_op jit(solution)/shard_map/ppermute | solution.py:14
  (139 shorter events, 38.2 us)
Async XLA Ops:
  0.0 12.7 %collective-permute-start = (s32[4,3]{1,0:T(4,128)}, s32[4,3]{1,0:T(4,128)S(1)}, u32[]{:S(2)}, u32[]{:S(2)}) collective-permute-start(s32[4,3]{1,0:T(4,128)} %param.7), channel_id=1, source_target_pairs={{0,8},{8,16},{16,24},{24,0},{1,9},{9,17},{17,25},{25,1},{2,10},{10... | collective-permute-start | bytes 152 | tf_op jit(solution)/shard_map/ppermute | solution.py:14
  3.0 10.1 %collective-permute-start.2 = (s32[4,3]{1,0:T(4,128)}, s32[4,3]{1,0:T(4,128)S(1)}, u32[]{:S(2)}, u32[]{:S(2)}) collective-permute-start(s32[4,3]{1,0:T(4,128)} %param.7), channel_id=1, source_target_pairs={{0,24},{8,0},{16,8},{24,16},{1,25},{9,1},{17,9},{25,17},{2,26},{10... | collective-permute-start | bytes 152 | tf_op jit(solution)/shard_map/ppermute | solution.py:14
  5.1 9.5 %collective-permute-start.1 = (s32[4,3]{1,0:T(4,128)}, s32[4,3]{1,0:T(4,128)S(1)}, u32[]{:S(2)}, u32[]{:S(2)}) collective-permute-start(s32[4,3]{1,0:T(4,128)} %param.7), channel_id=1, source_target_pairs={{0,16},{8,24},{16,0},{24,8},{1,17},{9,25},{17,1},{25,9},{2,18},{10... | collective-permute-start | bytes 152 | tf_op jit(solution)/shard_map/ppermute | solution.py:14
  6.1 10.5 %collective-permute-start.9 = (bf16[2,32,512]{2,1,0:T(8,128)(2,1)}, bf16[2,32,512]{2,1,0:T(8,128)(2,1)S(1)}, u32[]{:S(2)}, u32[]{:S(2)}) collective-permute-start(bf16[2,32,512]{2,1,0:T(8,128)(2,1)} %bitcast.280), channel_id=1, source_target_pairs={{0,7},{1,0},{2,1},{3,2},{4,3},{5,4},{6,5},{7,6},{8,15},{9,8},{10,9... | collective-permute-start | bytes 196616 | tf_op jit(solution)/shard_map/ppermute | solution.py:14
  7.1 11.0 %collective-permute-start.8 = (bf16[2,32,512]{2,1,0:T(8,128)(2,1)}, bf16[2,32,512]{2,1,0:T(8,128)(2,1)S(1)}, u32[]{:S(2)}, u32[]{:S(2)}) collective-permute-start(bf16[2,32,512]{2,1,0:T(8,128)(2,1)} %bitcast.281), channel_id=1, source_target_pairs={{0,6},{1,7},{2,0},{3,1},{4,2},{5,3},{6,4},{7,5},{8,14},{9,15},{10,... | collective-permute-start | bytes 196616 | tf_op jit(solution)/shard_map/ppermute | solution.py:14
  12.7 5.4 %collective-permute-start.7 = (bf16[2,32,512]{2,1,0:T(8,128)(2,1)}, bf16[2,32,512]{2,1,0:T(8,128)(2,1)S(1)}, u32[]{:S(2)}, u32[]{:S(2)}) collective-permute-start(bf16[2,32,512]{2,1,0:T(8,128)(2,1)} %bitcast.282), channel_id=1, source_target_pairs={{0,5},{1,6},{2,7},{3,0},{4,1},{5,2},{6,3},{7,4},{8,13},{9,14},{10,... | collective-permute-start | bytes 196616 | tf_op jit(solution)/shard_map/ppermute | solution.py:14
  13.1 5.7 %collective-permute-start.6 = (bf16[2,32,512]{2,1,0:T(8,128)(2,1)}, bf16[2,32,512]{2,1,0:T(8,128)(2,1)S(1)}, u32[]{:S(2)}, u32[]{:S(2)}) collective-permute-start(bf16[2,32,512]{2,1,0:T(8,128)(2,1)} %bitcast.283), channel_id=1, source_target_pairs={{0,4},{1,5},{2,6},{3,7},{4,0},{5,1},{6,2},{7,3},{8,12},{9,13},{10,... | collective-permute-start | bytes 196616 | tf_op jit(solution)/shard_map/ppermute | solution.py:14
  16.5 5.7 %collective-permute-start.4 = (bf16[2,32,512]{2,1,0:T(8,128)(2,1)}, bf16[2,32,512]{2,1,0:T(8,128)(2,1)S(1)}, u32[]{:S(2)}, u32[]{:S(2)}) collective-permute-start(bf16[2,32,512]{2,1,0:T(8,128)(2,1)} %bitcast.285), channel_id=1, source_target_pairs={{0,2},{1,3},{2,4},{3,5},{4,6},{5,7},{6,0},{7,1},{8,10},{9,11},{10,... | collective-permute-start | bytes 196616 | tf_op jit(solution)/shard_map/ppermute | solution.py:14
  24.6 5.7 %collective-permute-start.12 = (bf16[128,512]{1,0:T(8,128)(2,1)S(1)}, bf16[128,512]{1,0:T(8,128)(2,1)S(1)}, u32[]{:S(2)}, u32[]{:S(2)}) collective-permute-start(bf16[128,512]{1,0:T(8,128)(2,1)S(1)} %get-tuple-element.28), channel_id=1, source_target_pairs={{0,24},{8,0},{16,8},{24,16},{1,25},{9,1},{17,9},{25,17},{2,26},{10... | collective-permute-start | bytes 393224 | tf_op jit(solution)/shard_map/ppermute | solution.py:14
  26.0 12.5 %collective-permute-start.11 = (bf16[128,512]{1,0:T(8,128)(2,1)S(1)}, bf16[128,512]{1,0:T(8,128)(2,1)S(1)}, u32[]{:S(2)}, u32[]{:S(2)}) collective-permute-start(bf16[128,512]{1,0:T(8,128)(2,1)S(1)} %get-tuple-element.29), channel_id=1, source_target_pairs={{0,16},{8,24},{16,0},{24,8},{1,17},{9,25},{17,1},{25,9},{2,18},{10... | collective-permute-start | bytes 393224 | tf_op jit(solution)/shard_map/ppermute | solution.py:14
  27.7 10.8 %collective-permute-start.10 = (bf16[128,512]{1,0:T(8,128)(2,1)S(1)}, bf16[128,512]{1,0:T(8,128)(2,1)S(1)}, u32[]{:S(2)}, u32[]{:S(2)}) collective-permute-start(bf16[128,512]{1,0:T(8,128)(2,1)S(1)} %get-tuple-element.30), channel_id=1, source_target_pairs={{0,8},{8,16},{16,24},{24,0},{1,9},{9,17},{17,25},{25,1},{2,10},{10... | collective-permute-start | bytes 393224 | tf_op jit(solution)/shard_map/ppermute | solution.py:14
  39.6 5.7 %collective-permute-start.19 = (bf16[32,512]{1,0:T(8,128)(2,1)S(1)}, bf16[32,512]{1,0:T(8,128)(2,1)S(1)}, u32[]{:S(2)}, u32[]{:S(2)}) collective-permute-start(bf16[32,512]{1,0:T(8,128)(2,1)S(1)} %get-tuple-element.70), channel_id=1, source_target_pairs={{0,7},{1,0},{2,1},{3,2},{4,3},{5,4},{6,5},{7,6},{8,15},{9,8},{10,9... | collective-permute-start | bytes 98312 | tf_op jit(solution)/shard_map/ppermute | solution.py:14
  42.2 5.9 %collective-permute-start.18 = (bf16[32,512]{1,0:T(8,128)(2,1)S(1)}, bf16[32,512]{1,0:T(8,128)(2,1)S(1)}, u32[]{:S(2)}, u32[]{:S(2)}) collective-permute-start(bf16[32,512]{1,0:T(8,128)(2,1)S(1)} %get-tuple-element.71), channel_id=1, source_target_pairs={{0,6},{1,7},{2,0},{3,1},{4,2},{5,3},{6,4},{7,5},{8,14},{9,15},{10,... | collective-permute-start | bytes 98312 | tf_op jit(solution)/shard_map/ppermute | solution.py:14
  42.3 5.9 %collective-permute-start.17 = (bf16[32,512]{1,0:T(8,128)(2,1)S(1)}, bf16[32,512]{1,0:T(8,128)(2,1)S(1)}, u32[]{:S(2)}, u32[]{:S(2)}) collective-permute-start(bf16[32,512]{1,0:T(8,128)(2,1)S(1)} %get-tuple-element.72), channel_id=1, source_target_pairs={{0,5},{1,6},{2,7},{3,0},{4,1},{5,2},{6,3},{7,4},{8,13},{9,14},{10,... | collective-permute-start | bytes 98312 | tf_op jit(solution)/shard_map/ppermute | solution.py:14
  45.3 5.1 %collective-permute-start.14 = (bf16[32,512]{1,0:T(8,128)(2,1)S(1)}, bf16[32,512]{1,0:T(8,128)(2,1)S(1)}, u32[]{:S(2)}, u32[]{:S(2)}) collective-permute-start(bf16[32,512]{1,0:T(8,128)(2,1)S(1)} %get-tuple-element.75), channel_id=1, source_target_pairs={{0,2},{1,3},{2,4},{3,5},{4,6},{5,7},{6,0},{7,1},{8,10},{9,11},{10,... | collective-permute-start | bytes 98312 | tf_op jit(solution)/shard_map/ppermute | solution.py:14
  50.6 6.0 %collective-permute-start.25 = (bf16[32,512]{1,0:T(8,128)(2,1)S(1)}, bf16[32,512]{1,0:T(8,128)(2,1)S(1)}, u32[]{:S(2)}, u32[]{:S(2)}) collective-permute-start(bf16[32,512]{1,0:T(8,128)(2,1)S(1)} %get-tuple-element.112), channel_id=1, source_target_pairs={{0,6},{1,7},{2,0},{3,1},{4,2},{5,3},{6,4},{7,5},{8,14},{9,15},{10,... | collective-permute-start | bytes 98312 | tf_op jit(solution)/shard_map/ppermute | solution.py:14
  55.3 4.8 %collective-permute-start.21 = (bf16[32,512]{1,0:T(8,128)(2,1)S(1)}, bf16[32,512]{1,0:T(8,128)(2,1)S(1)}, u32[]{:S(2)}, u32[]{:S(2)}) collective-permute-start(bf16[32,512]{1,0:T(8,128)(2,1)S(1)} %get-tuple-element.112), channel_id=1, source_target_pairs={{0,2},{1,3},{2,4},{3,5},{4,6},{5,7},{6,0},{7,1},{8,10},{9,11},{10,... | collective-permute-start | bytes 98312 | tf_op jit(solution)/shard_map/ppermute | solution.py:14
  61.3 5.2 %collective-permute-start.29 = (bf16[128,512]{1,0:T(8,128)(2,1)S(1)}, bf16[128,512]{1,0:T(8,128)(2,1)S(1)}, u32[]{:S(2)}, u32[]{:S(2)}) collective-permute-start(bf16[128,512]{1,0:T(8,128)(2,1)S(1)} %get-tuple-element.24), channel_id=1, source_target_pairs={{0,24},{8,0},{16,8},{24,16},{1,25},{9,1},{17,9},{25,17},{2,26},{10... | collective-permute-start | bytes 393224 | tf_op jit(solution)/shard_map/ppermute | solution.py:14
  61.4 12.0 %collective-permute-start.28 = (bf16[128,512]{1,0:T(8,128)(2,1)S(1)}, bf16[128,512]{1,0:T(8,128)(2,1)S(1)}, u32[]{:S(2)}, u32[]{:S(2)}) collective-permute-start(bf16[128,512]{1,0:T(8,128)(2,1)S(1)} %get-tuple-element.25), channel_id=1, source_target_pairs={{0,16},{8,24},{16,0},{24,8},{1,17},{9,25},{17,1},{25,9},{2,18},{10... | collective-permute-start | bytes 393224 | tf_op jit(solution)/shard_map/ppermute | solution.py:14
  62.7 10.7 %collective-permute-start.27 = (bf16[128,512]{1,0:T(8,128)(2,1)S(1)}, bf16[128,512]{1,0:T(8,128)(2,1)S(1)}, u32[]{:S(2)}, u32[]{:S(2)}) collective-permute-start(bf16[128,512]{1,0:T(8,128)(2,1)S(1)} %get-tuple-element.26), channel_id=1, source_target_pairs={{0,8},{8,16},{16,24},{24,0},{1,9},{9,17},{17,25},{25,1},{2,10},{10... | collective-permute-start | bytes 393224 | tf_op jit(solution)/shard_map/ppermute | solution.py:14
  74.5 4.9 %collective-permute-start.36 = (bf16[32,512]{1,0:T(8,128)(2,1)S(1)}, bf16[32,512]{1,0:T(8,128)(2,1)S(1)}, u32[]{:S(2)}, u32[]{:S(2)}) collective-permute-start(bf16[32,512]{1,0:T(8,128)(2,1)S(1)} %get-tuple-element.53), channel_id=1, source_target_pairs={{0,7},{1,0},{2,1},{3,2},{4,3},{5,4},{6,5},{7,6},{8,15},{9,8},{10,9... | collective-permute-start | bytes 98312 | tf_op jit(solution)/shard_map/ppermute | solution.py:14
  77.1 5.0 %collective-permute-start.35 = (bf16[32,512]{1,0:T(8,128)(2,1)S(1)}, bf16[32,512]{1,0:T(8,128)(2,1)S(1)}, u32[]{:S(2)}, u32[]{:S(2)}) collective-permute-start(bf16[32,512]{1,0:T(8,128)(2,1)S(1)} %get-tuple-element.54), channel_id=1, source_target_pairs={{0,6},{1,7},{2,0},{3,1},{4,2},{5,3},{6,4},{7,5},{8,14},{9,15},{10,... | collective-permute-start | bytes 98312 | tf_op jit(solution)/shard_map/ppermute | solution.py:14
  79.4 5.8 %collective-permute-start.31 = (bf16[32,512]{1,0:T(8,128)(2,1)S(1)}, bf16[32,512]{1,0:T(8,128)(2,1)S(1)}, u32[]{:S(2)}, u32[]{:S(2)}) collective-permute-start(bf16[32,512]{1,0:T(8,128)(2,1)S(1)} %get-tuple-element.58), channel_id=1, source_target_pairs={{0,2},{1,3},{2,4},{3,5},{4,6},{5,7},{6,0},{7,1},{8,10},{9,11},{10,... | collective-permute-start | bytes 98312 | tf_op jit(solution)/shard_map/ppermute | solution.py:14
  85.4 5.1 %collective-permute-start.42 = (bf16[32,512]{1,0:T(8,128)(2,1)S(1)}, bf16[32,512]{1,0:T(8,128)(2,1)S(1)}, u32[]{:S(2)}, u32[]{:S(2)}) collective-permute-start(bf16[32,512]{1,0:T(8,128)(2,1)S(1)} %get-tuple-element.114), channel_id=1, source_target_pairs={{0,6},{1,7},{2,0},{3,1},{4,2},{5,3},{6,4},{7,5},{8,14},{9,15},{10,... | collective-permute-start | bytes 98312 | tf_op jit(solution)/shard_map/ppermute | solution.py:14
  89.4 4.8 %collective-permute-start.38 = (bf16[32,512]{1,0:T(8,128)(2,1)S(1)}, bf16[32,512]{1,0:T(8,128)(2,1)S(1)}, u32[]{:S(2)}, u32[]{:S(2)}) collective-permute-start(bf16[32,512]{1,0:T(8,128)(2,1)S(1)} %get-tuple-element.114), channel_id=1, source_target_pairs={{0,2},{1,3},{2,4},{3,5},{4,6},{5,7},{6,0},{7,1},{8,10},{9,11},{10,... | collective-permute-start | bytes 98312 | tf_op jit(solution)/shard_map/ppermute | solution.py:14
  95.3 5.2 %collective-permute-start.46 = (bf16[128,512]{1,0:T(8,128)(2,1)S(1)}, bf16[128,512]{1,0:T(8,128)(2,1)S(1)}, u32[]{:S(2)}, u32[]{:S(2)}) collective-permute-start(bf16[128,512]{1,0:T(8,128)(2,1)S(1)} %get-tuple-element.20), channel_id=1, source_target_pairs={{0,24},{8,0},{16,8},{24,16},{1,25},{9,1},{17,9},{25,17},{2,26},{10... | collective-permute-start | bytes 393224 | tf_op jit(solution)/shard_map/ppermute | solution.py:14
  95.3 12.4 %collective-permute-start.45 = (bf16[128,512]{1,0:T(8,128)(2,1)S(1)}, bf16[128,512]{1,0:T(8,128)(2,1)S(1)}, u32[]{:S(2)}, u32[]{:S(2)}) collective-permute-start(bf16[128,512]{1,0:T(8,128)(2,1)S(1)} %get-tuple-element.21), channel_id=1, source_target_pairs={{0,16},{8,24},{16,0},{24,8},{1,17},{9,25},{17,1},{25,9},{2,18},{10... | collective-permute-start | bytes 393224 | tf_op jit(solution)/shard_map/ppermute | solution.py:14
  97.1 10.7 %collective-permute-start.44 = (bf16[128,512]{1,0:T(8,128)(2,1)S(1)}, bf16[128,512]{1,0:T(8,128)(2,1)S(1)}, u32[]{:S(2)}, u32[]{:S(2)}) collective-permute-start(bf16[128,512]{1,0:T(8,128)(2,1)S(1)} %get-tuple-element.22), channel_id=1, source_target_pairs={{0,8},{8,16},{16,24},{24,0},{1,9},{9,17},{17,25},{25,1},{2,10},{10... | collective-permute-start | bytes 393224 | tf_op jit(solution)/shard_map/ppermute | solution.py:14
  108.7 5.8 %collective-permute-start.53 = (bf16[32,512]{1,0:T(8,128)(2,1)S(1)}, bf16[32,512]{1,0:T(8,128)(2,1)S(1)}, u32[]{:S(2)}, u32[]{:S(2)}) collective-permute-start(bf16[32,512]{1,0:T(8,128)(2,1)S(1)} %get-tuple-element.36), channel_id=1, source_target_pairs={{0,7},{1,0},{2,1},{3,2},{4,3},{5,4},{6,5},{7,6},{8,15},{9,8},{10,9... | collective-permute-start | bytes 98312 | tf_op jit(solution)/shard_map/ppermute | solution.py:14
  111.4 5.8 %collective-permute-start.52 = (bf16[32,512]{1,0:T(8,128)(2,1)S(1)}, bf16[32,512]{1,0:T(8,128)(2,1)S(1)}, u32[]{:S(2)}, u32[]{:S(2)}) collective-permute-start(bf16[32,512]{1,0:T(8,128)(2,1)S(1)} %get-tuple-element.37), channel_id=1, source_target_pairs={{0,6},{1,7},{2,0},{3,1},{4,2},{5,3},{6,4},{7,5},{8,14},{9,15},{10,... | collective-permute-start | bytes 98312 | tf_op jit(solution)/shard_map/ppermute | solution.py:14
  111.6 5.5 %collective-permute-start.51 = (bf16[32,512]{1,0:T(8,128)(2,1)S(1)}, bf16[32,512]{1,0:T(8,128)(2,1)S(1)}, u32[]{:S(2)}, u32[]{:S(2)}) collective-permute-start(bf16[32,512]{1,0:T(8,128)(2,1)S(1)} %get-tuple-element.38), channel_id=1, source_target_pairs={{0,5},{1,6},{2,7},{3,0},{4,1},{5,2},{6,3},{7,4},{8,13},{9,14},{10,... | collective-permute-start | bytes 98312 | tf_op jit(solution)/shard_map/ppermute | solution.py:14
  114.5 4.9 %collective-permute-start.48 = (bf16[32,512]{1,0:T(8,128)(2,1)S(1)}, bf16[32,512]{1,0:T(8,128)(2,1)S(1)}, u32[]{:S(2)}, u32[]{:S(2)}) collective-permute-start(bf16[32,512]{1,0:T(8,128)(2,1)S(1)} %get-tuple-element.41), channel_id=1, source_target_pairs={{0,2},{1,3},{2,4},{3,5},{4,6},{5,7},{6,0},{7,1},{8,10},{9,11},{10,... | collective-permute-start | bytes 98312 | tf_op jit(solution)/shard_map/ppermute | solution.py:14
  (25 other events, 154.8 us)

commit v5 on v4

--- a/solution.py
+++ b/solution.py
@@ -89,16 +89,17 @@
                 jnp.sum(jnp.where(chosen[:, None, None], terms, 0.0), axis=0)
             )
         slots = jnp.stack(partial_sums).astype(jnp.bfloat16).reshape(members, share, BLOCK)
-        sent = pick([slots[s] for s in range(members)], send_slot)
-        field = sent[0].astype(jnp.float32)
-        for k in range(1, members):
-            field = field + shifted(sent[k], "member", members, k).astype(jnp.float32)
+        sent = pick([slots[s] for s in range(members)], slot_of_member)
+        got = lax.all_to_all(sent, "member", 0, 0, tiled=True)
+        field = jnp.sum(got.astype(jnp.float32), axis=0)
         residual = (excitations[step, 0] - field).astype(jnp.bfloat16)
         current = jnp.dot(residual, inverses[0], preferred_element_type=jnp.float32)
         results.append(current)
         if step + 1 < STEPS:
-            pieces = shift_gather(current.astype(jnp.bfloat16), "member", members)
-            blocks.append(pick(pieces, owner_shift).reshape(group_blocks, EXCITE, BLOCK))
+            spread = jnp.broadcast_to(current.astype(jnp.bfloat16)[None], (members, share, BLOCK))
+            got = lax.all_to_all(spread, "member", 0, 0, tiled=True)
+            placed = pick([got[m] for m in range(members)], owners)
+            blocks.append(placed.reshape(group_blocks, EXCITE, BLOCK))
     return jnp.stack(results)[:, None]
 
 

time: 121 us -> 118 us (0.975)
  blocking collectives: 0 us -> 37.6 us
  starting transfers between devices: 59.4 us -> 26.8 us
  waiting for transfers between devices: 47.9 us -> 39.8 us
    all_to_all x0 -> x4, blocking collectives: none -> 37.6 us  [the longest x3 28.2 us: body(): got = lax.all_to_all(sent, 'member', 0, 0, tiled=True)]
    ppermute x54 -> x19, starting transfers between devices: 59.4 us -> 23.4 us  [shifted(): return lax.ppermute(x, axis, [(i, (i + k) % n) for i in range(n)])]
    ppermute x54 -> x19, waiting for transfers between devices: 47.9 us -> 32.9 us  [shifted(): return lax.ppermute(x, axis, [(i, (i + k) % n) for i in range(n)])]
    all_to_all x0 -> x1, waiting for transfers between devices: none -> 6.82 us  [body(): got = lax.all_to_all(spread, 'member', 0, 0, tiled=True)]
    all_to_all x0 -> x1, starting transfers between devices: none -> 3.41 us  [body(): got = lax.all_to_all(spread, 'member', 0, 0, tiled=True)]
  transfers between devices with their start and end apart: 54 -> 20, of which waited for: 23 -> 11; matrix products, arithmetic and copies ran while one was open for 5% -> 5% of each run, Pallas kernels for 0% -> 0%
where the time goes in v5:
time: 118 us; the launch traced here: 117 us
  waiting for transfers between devices  39.8 us (34%)
  blocking collectives  37.6 us (32%)
  starting transfers between devices  26.8 us (23%)
  other arithmetic  8.49 us (7%)
  matrix products  2.35 us (2%)
  local copies, waits for them, and re-layouts  1.94 us (2%)
    ppermute x19, waiting for transfers between devices, shifted(): return lax.ppermute(x, axis, [(i, (i + k) % n) for i in range(n)])  32.9 us
    all_to_all x3, blocking collectives, body(): got = lax.all_to_all(sent, 'member', 0, 0, tiled=True)  28.2 us
    ppermute x19, starting transfers between devices, shifted(): return lax.ppermute(x, axis, [(i, (i + k) % n) for i in range(n)])  23.4 us
    all_to_all x1, blocking collectives, body(): got = lax.all_to_all(spread, 'member', 0, 0, tiled=True)  9.35 us
    all_to_all x1, waiting for transfers between devices, body(): got = lax.all_to_all(spread, 'member', 0, 0, tiled=True)  6.82 us
    all_to_all x1, starting transfers between devices, body(): got = lax.all_to_all(spread, 'member', 0, 0, tiled=True)  3.41 us
    add x6, other arithmetic, pick(): total = term if total is None else total + term  2.53 us
  transfers between devices with their start and end apart: 20, of which 11 were waited for; matrix products, arithmetic and copies ran while one was open for 5% of the time, Pallas kernels for 0%

profile of v5, /device:TPU:0, one launch (start us, length us, event | category | flops | bytes accessed | tf_op | source)
XLA Modules:
  0.0 117.3 jit_solution(14070532370679965529)
XLA Ops:
  0.0 3.0 %collective-permute-start = (s32[4,3]{1,0:T(4,128)}, s32[4,3]{1,0:T(4,128)S(1)}, u32[]{:S(2)}, u32[]{:S(2)}) collective-permute-start(s32[4,3]{1,0:T(4,128)} %param.7), channel_id=1, source_target_pairs={{0,8},{8,16},{16,24},{24,0},{1,9},{9,17},{17,25},{25,1},{2,10},{10... | collective-permute-start | bytes 152 | tf_op jit(solution)/shard_map/ppermute | solution.py:14
  3.0 2.1 %collective-permute-start.2 = (s32[4,3]{1,0:T(4,128)}, s32[4,3]{1,0:T(4,128)S(1)}, u32[]{:S(2)}, u32[]{:S(2)}) collective-permute-start(s32[4,3]{1,0:T(4,128)} %param.7), channel_id=1, source_target_pairs={{0,24},{8,0},{16,8},{24,16},{1,25},{9,1},{17,9},{25,17},{2,26},{10... | collective-permute-start | bytes 152 | tf_op jit(solution)/shard_map/ppermute | solution.py:14
  5.1 1.0 collective-permute-start.1
  6.1 1.0 collective-permute-start.9
  7.1 1.4 %collective-permute-start.8 = (bf16[2,32,512]{2,1,0:T(8,128)(2,1)}, bf16[2,32,512]{2,1,0:T(8,128)(2,1)S(1)}, u32[]{:S(2)}, u32[]{:S(2)}) collective-permute-start(bf16[2,32,512]{2,1,0:T(8,128)(2,1)} %bitcast.288), channel_id=1, source_target_pairs={{0,6},{1,7},{2,0},{3,1},{4,2},{5,3},{6,4},{7,5},{8,14},{9,15},{10,... | collective-permute-start | bytes 196616 | tf_op jit(solution)/shard_map/ppermute | solution.py:14
  8.5 0.9 fusion.74
  10.2 0.8 select_reduce_fusion.6
  11.0 1.0 slice_reduce_fusion.2
  12.5 1.5 %collective-permute-start.6 = (bf16[2,32,512]{2,1,0:T(8,128)(2,1)}, bf16[2,32,512]{2,1,0:T(8,128)(2,1)S(1)}, u32[]{:S(2)}, u32[]{:S(2)}) collective-permute-start(bf16[2,32,512]{2,1,0:T(8,128)(2,1)} %bitcast.290), channel_id=1, source_target_pairs={{0,4},{1,5},{2,6},{3,7},{4,0},{5,1},{6,2},{7,3},{8,12},{9,13},{10,... | collective-permute-start | bytes 196616 | tf_op jit(solution)/shard_map/ppermute | solution.py:14
  15.9 1.6 %collective-permute-start.4 = (bf16[2,32,512]{2,1,0:T(8,128)(2,1)}, bf16[2,32,512]{2,1,0:T(8,128)(2,1)S(1)}, u32[]{:S(2)}, u32[]{:S(2)}) collective-permute-start(bf16[2,32,512]{2,1,0:T(8,128)(2,1)} %bitcast.292), channel_id=1, source_target_pairs={{0,2},{1,3},{2,4},{3,5},{4,6},{5,7},{6,0},{7,1},{8,10},{9,11},{10,... | collective-permute-start | bytes 196616 | tf_op jit(solution)/shard_map/ppermute | solution.py:14
  18.4 3.1 %collective-permute-done.4 = bf16[2,32,512]{2,1,0:T(8,128)(2,1)S(1)} collective-permute-done((bf16[2,32,512]{2,1,0:T(8,128)(2,1)}, bf16[2,32,512]{2,1,0:T(8,128)(2,1)S(1)}, u32[]{:S(2)}, u32[]{:S(2)}) %collective-permute-start.4) | collective-permute-done | bytes 65568 | tf_op jit(solution)/shard_map/ppermute | solution.py:14
  22.3 1.3 %select_add_fusion = bf16[8,2,32,512]{3,2,0,1:T(8,128)(2,1)S(1)} fusion(pred[8]{0:T(512)(128)(4,1)S(1)} %get-tuple-element.80, pred[8]{0:T(512)(128)(4,1)S(1)} %get-tuple-element.81, pred[8]{0:T(512)(128)(4,1)S(1)} %get-tuple-element.82, pred[8]{0:T(512)(128)(4,1)S(1)} %get-tuple-element.83, pred[8]{0:T(512)(128)(4,1)S(1)} %get-tuple-element.84, ...), kind=kLoop, calls=%fused_computation.43 | loop fusion | flops 3932160 | bytes 1048640 | tf_op jit(solution)/shard_map/add | solution.py:29
  23.9 1.4 %collective-permute-start.12 = (bf16[128,512]{1,0:T(8,128)(2,1)S(1)}, bf16[128,512]{1,0:T(8,128)(2,1)S(1)}, u32[]{:S(2)}, u32[]{:S(2)}) collective-permute-start(bf16[128,512]{1,0:T(8,128)(2,1)S(1)} %get-tuple-element.28), channel_id=1, source_target_pairs={{0,24},{8,0},{16,8},{24,16},{1,25},{9,1},{17,9},{25,17},{2,26},{10... | collective-permute-start | bytes 393224 | tf_op jit(solution)/shard_map/ppermute | solution.py:14
  25.3 1.7 %collective-permute-start.11 = (bf16[128,512]{1,0:T(8,128)(2,1)S(1)}, bf16[128,512]{1,0:T(8,128)(2,1)S(1)}, u32[]{:S(2)}, u32[]{:S(2)}) collective-permute-start(bf16[128,512]{1,0:T(8,128)(2,1)S(1)} %get-tuple-element.29), channel_id=1, source_target_pairs={{0,16},{8,24},{16,0},{24,8},{1,17},{9,25},{17,1},{25,9},{2,18},{10... | collective-permute-start | bytes 393224 | tf_op jit(solution)/shard_map/ppermute | solution.py:14
  27.0 1.3 %collective-permute-start.10 = (bf16[128,512]{1,0:T(8,128)(2,1)S(1)}, bf16[128,512]{1,0:T(8,128)(2,1)S(1)}, u32[]{:S(2)}, u32[]{:S(2)}) collective-permute-start(bf16[128,512]{1,0:T(8,128)(2,1)S(1)} %get-tuple-element.30), channel_id=1, source_target_pairs={{0,8},{8,16},{16,24},{24,0},{1,9},{9,17},{17,25},{25,1},{2,10},{10... | collective-permute-start | bytes 393224 | tf_op jit(solution)/shard_map/ppermute | solution.py:14
  28.3 1.3 %collective-permute-done.12 = bf16[128,512]{1,0:T(8,128)(2,1)S(1)} collective-permute-done((bf16[128,512]{1,0:T(8,128)(2,1)S(1)}, bf16[128,512]{1,0:T(8,128)(2,1)S(1)}, u32[]{:S(2)}, u32[]{:S(2)}) %collective-permute-start.12) | collective-permute-done | bytes 131104 | tf_op jit(solution)/shard_map/ppermute | solution.py:14
  29.6 8.2 %collective-permute-done.11 = bf16[128,512]{1,0:T(8,128)(2,1)S(1)} collective-permute-done((bf16[128,512]{1,0:T(8,128)(2,1)S(1)}, bf16[128,512]{1,0:T(8,128)(2,1)S(1)}, u32[]{:S(2)}, u32[]{:S(2)}) %collective-permute-start.11) | collective-permute-done | bytes 131104 | tf_op jit(solution)/shard_map/ppermute | solution.py:14
  38.8 9.5 %all_to_all.25 = bf16[8,32,512]{2,1,0:T(8,128)(2,1)S(1)} all-to-all(bf16[8,32,512]{2,1,0:T(8,128)(2,1)S(1)} %select_add_fusion.5), channel_id=1, replica_groups=mesh['group'=4,'member'=8] {'member'}, dimensions={0} | all-to-all | bytes 524288 | tf_op jit(solution)/shard_map/all_to_all | solution.py:93
  48.5 0.7 broadcast_in_dim.1248
  49.3 3.4 %all-to-all-start.1 = ((bf16[8,32,512]{2,1,0:T(8,128)(2,1)}), bf16[8,32,512]{2,1,0:T(8,128)(2,1)S(1)}, u32[]{:S(2)}, u32[]{:S(2)}) async-start(bf16[8,32,512]{2,1,0:T(8,128)(2,1)} %broadcast_in_dim.1248), calls=%async_computation.1 | async-start | bytes 524288 | tf_op jit(solution)/shard_map/all_to_all | solution.py:100
  52.7 6.8 %all-to-all-done.1 = bf16[8,32,512]{2,1,0:T(8,128)(2,1)S(1)} async-done(((bf16[8,32,512]{2,1,0:T(8,128)(2,1)}), bf16[8,32,512]{2,1,0:T(8,128)(2,1)S(1)}, u32[]{:S(2)}, u32[]{:S(2)}) %all-to-all-start.1) | async-done | bytes 262176 | tf_op jit(solution)/shard_map/all_to_all | solution.py:100
  60.2 1.3 %collective-permute-start.14 = (bf16[128,512]{1,0:T(8,128)(2,1)S(1)}, bf16[128,512]{1,0:T(8,128)(2,1)S(1)}, u32[]{:S(2)}, u32[]{:S(2)}) collective-permute-start(bf16[128,512]{1,0:T(8,128)(2,1)S(1)} %get-tuple-element.25), channel_id=1, source_target_pairs={{0,16},{8,24},{16,0},{24,8},{1,17},{9,25},{17,1},{25,9},{2,18},{10... | collective-permute-start | bytes 393224 | tf_op jit(solution)/shard_map/ppermute | solution.py:14
  61.5 1.9 %collective-permute-start.13 = (bf16[128,512]{1,0:T(8,128)(2,1)S(1)}, bf16[128,512]{1,0:T(8,128)(2,1)S(1)}, u32[]{:S(2)}, u32[]{:S(2)}) collective-permute-start(bf16[128,512]{1,0:T(8,128)(2,1)S(1)} %get-tuple-element.26), channel_id=1, source_target_pairs={{0,8},{8,16},{16,24},{24,0},{1,9},{9,17},{17,25},{25,1},{2,10},{10... | collective-permute-start | bytes 393224 | tf_op jit(solution)/shard_map/ppermute | solution.py:14
  63.4 2.2 %collective-permute-done.15 = bf16[128,512]{1,0:T(8,128)(2,1)S(1)} collective-permute-done((bf16[128,512]{1,0:T(8,128)(2,1)S(1)}, bf16[128,512]{1,0:T(8,128)(2,1)S(1)}, u32[]{:S(2)}, u32[]{:S(2)}) %collective-permute-start.15) | collective-permute-done | bytes 131104 | tf_op jit(solution)/shard_map/ppermute | solution.py:14
  65.7 7.1 %collective-permute-done.14 = bf16[128,512]{1,0:T(8,128)(2,1)S(1)} collective-permute-done((bf16[128,512]{1,0:T(8,128)(2,1)S(1)}, bf16[128,512]{1,0:T(8,128)(2,1)S(1)}, u32[]{:S(2)}, u32[]{:S(2)}) %collective-permute-start.14) | collective-permute-done | bytes 131104 | tf_op jit(solution)/shard_map/ppermute | solution.py:14
  73.7 9.3 %all_to_all.26 = bf16[8,32,512]{2,1,0:T(8,128)(2,1)S(1)} all-to-all(bf16[8,32,512]{2,1,0:T(8,128)(2,1)S(1)} %select_add_fusion.3), channel_id=1, replica_groups=mesh['group'=4,'member'=8] {'member'}, dimensions={0} | all-to-all | bytes 524288 | tf_op jit(solution)/shard_map/all_to_all | solution.py:93
  83.3 9.3 %all_to_all.27 = bf16[8,32,512]{2,1,0:T(8,128)(2,1)S(1)} all-to-all(bf16[8,32,512]{2,1,0:T(8,128)(2,1)S(1)} %broadcast_in_dim.1304), channel_id=1, replica_groups=mesh['group'=4,'member'=8] {'member'}, dimensions={0} | all-to-all | bytes 524288 | tf_op jit(solution)/shard_map/all_to_all | solution.py:100
  93.3 1.7 %collective-permute-start.17 = (bf16[128,512]{1,0:T(8,128)(2,1)S(1)}, bf16[128,512]{1,0:T(8,128)(2,1)S(1)}, u32[]{:S(2)}, u32[]{:S(2)}) collective-permute-start(bf16[128,512]{1,0:T(8,128)(2,1)S(1)} %get-tuple-element.21), channel_id=1, source_target_pairs={{0,16},{8,24},{16,0},{24,8},{1,17},{9,25},{17,1},{25,9},{2,18},{10... | collective-permute-start | bytes 393224 | tf_op jit(solution)/shard_map/ppermute | solution.py:14
  95.0 1.9 %collective-permute-start.16 = (bf16[128,512]{1,0:T(8,128)(2,1)S(1)}, bf16[128,512]{1,0:T(8,128)(2,1)S(1)}, u32[]{:S(2)}, u32[]{:S(2)}) collective-permute-start(bf16[128,512]{1,0:T(8,128)(2,1)S(1)} %get-tuple-element.22), channel_id=1, source_target_pairs={{0,8},{8,16},{16,24},{24,0},{1,9},{9,17},{17,25},{25,1},{2,10},{10... | collective-permute-start | bytes 393224 | tf_op jit(solution)/shard_map/ppermute | solution.py:14
  96.9 1.9 %collective-permute-done.18 = bf16[128,512]{1,0:T(8,128)(2,1)S(1)} collective-permute-done((bf16[128,512]{1,0:T(8,128)(2,1)S(1)}, bf16[128,512]{1,0:T(8,128)(2,1)S(1)}, u32[]{:S(2)}, u32[]{:S(2)}) %collective-permute-start.18) | collective-permute-done | bytes 131104 | tf_op jit(solution)/shard_map/ppermute | solution.py:14
  98.8 7.4 %collective-permute-done.17 = bf16[128,512]{1,0:T(8,128)(2,1)S(1)} collective-permute-done((bf16[128,512]{1,0:T(8,128)(2,1)S(1)}, bf16[128,512]{1,0:T(8,128)(2,1)S(1)}, u32[]{:S(2)}, u32[]{:S(2)}) %collective-permute-start.17) | collective-permute-done | bytes 131104 | tf_op jit(solution)/shard_map/ppermute | solution.py:14
  107.1 9.3 %all_to_all.28 = bf16[8,32,512]{2,1,0:T(8,128)(2,1)S(1)} all-to-all(bf16[8,32,512]{2,1,0:T(8,128)(2,1)S(1)} %select_add_fusion.1), channel_id=1, replica_groups=mesh['group'=4,'member'=8] {'member'}, dimensions={0} | all-to-all | bytes 524288 | tf_op jit(solution)/shard_map/all_to_all | solution.py:93
  (80 shorter events, 10.4 us)
Async XLA Ops:
  0.0 37.8 %copy-start = (bf16[4,512,512]{2,1,0:T(8,128)(2,1)S(1)}, bf16[4,512,512]{2,1,0:T(8,128)(2,1)}, u32[]{:S(2)}) copy-start(bf16[4,512,512]{2,1,0:T(8,128)(2,1)} %param.6) | copy-start | bytes 6291460
  0.0 12.1 %collective-permute-start = (s32[4,3]{1,0:T(4,128)}, s32[4,3]{1,0:T(4,128)S(1)}, u32[]{:S(2)}, u32[]{:S(2)}) collective-permute-start(s32[4,3]{1,0:T(4,128)} %param.7), channel_id=1, source_target_pairs={{0,8},{8,16},{16,24},{24,0},{1,9},{9,17},{17,25},{25,1},{2,10},{10... | collective-permute-start | bytes 152 | tf_op jit(solution)/shard_map/ppermute | solution.py:14
  3.0 9.4 %collective-permute-start.2 = (s32[4,3]{1,0:T(4,128)}, s32[4,3]{1,0:T(4,128)S(1)}, u32[]{:S(2)}, u32[]{:S(2)}) collective-permute-start(s32[4,3]{1,0:T(4,128)} %param.7), channel_id=1, source_target_pairs={{0,24},{8,0},{16,8},{24,16},{1,25},{9,1},{17,9},{25,17},{2,26},{10... | collective-permute-start | bytes 152 | tf_op jit(solution)/shard_map/ppermute | solution.py:14
  5.1 8.9 %collective-permute-start.1 = (s32[4,3]{1,0:T(4,128)}, s32[4,3]{1,0:T(4,128)S(1)}, u32[]{:S(2)}, u32[]{:S(2)}) collective-permute-start(s32[4,3]{1,0:T(4,128)} %param.7), channel_id=1, source_target_pairs={{0,16},{8,24},{16,0},{24,8},{1,17},{9,25},{17,1},{25,9},{2,18},{10... | collective-permute-start | bytes 152 | tf_op jit(solution)/shard_map/ppermute | solution.py:14
  6.1 9.8 %collective-permute-start.9 = (bf16[2,32,512]{2,1,0:T(8,128)(2,1)}, bf16[2,32,512]{2,1,0:T(8,128)(2,1)S(1)}, u32[]{:S(2)}, u32[]{:S(2)}) collective-permute-start(bf16[2,32,512]{2,1,0:T(8,128)(2,1)} %bitcast.287), channel_id=1, source_target_pairs={{0,7},{1,0},{2,1},{3,2},{4,3},{5,4},{6,5},{7,6},{8,15},{9,8},{10,9... | collective-permute-start | bytes 196616 | tf_op jit(solution)/shard_map/ppermute | solution.py:14
  7.1 10.3 %collective-permute-start.8 = (bf16[2,32,512]{2,1,0:T(8,128)(2,1)}, bf16[2,32,512]{2,1,0:T(8,128)(2,1)S(1)}, u32[]{:S(2)}, u32[]{:S(2)}) collective-permute-start(bf16[2,32,512]{2,1,0:T(8,128)(2,1)} %bitcast.288), channel_id=1, source_target_pairs={{0,6},{1,7},{2,0},{3,1},{4,2},{5,3},{6,4},{7,5},{8,14},{9,15},{10,... | collective-permute-start | bytes 196616 | tf_op jit(solution)/shard_map/ppermute | solution.py:14
  12.1 5.4 %collective-permute-start.7 = (bf16[2,32,512]{2,1,0:T(8,128)(2,1)}, bf16[2,32,512]{2,1,0:T(8,128)(2,1)S(1)}, u32[]{:S(2)}, u32[]{:S(2)}) collective-permute-start(bf16[2,32,512]{2,1,0:T(8,128)(2,1)} %bitcast.289), channel_id=1, source_target_pairs={{0,5},{1,6},{2,7},{3,0},{4,1},{5,2},{6,3},{7,4},{8,13},{9,14},{10,... | collective-permute-start | bytes 196616 | tf_op jit(solution)/shard_map/ppermute | solution.py:14
  12.5 5.7 %collective-permute-start.6 = (bf16[2,32,512]{2,1,0:T(8,128)(2,1)}, bf16[2,32,512]{2,1,0:T(8,128)(2,1)S(1)}, u32[]{:S(2)}, u32[]{:S(2)}) collective-permute-start(bf16[2,32,512]{2,1,0:T(8,128)(2,1)} %bitcast.290), channel_id=1, source_target_pairs={{0,4},{1,5},{2,6},{3,7},{4,0},{5,1},{6,2},{7,3},{8,12},{9,13},{10,... | collective-permute-start | bytes 196616 | tf_op jit(solution)/shard_map/ppermute | solution.py:14
  14.0 4.4 %collective-permute-start.5 = (bf16[2,32,512]{2,1,0:T(8,128)(2,1)}, bf16[2,32,512]{2,1,0:T(8,128)(2,1)S(1)}, u32[]{:S(2)}, u32[]{:S(2)}) collective-permute-start(bf16[2,32,512]{2,1,0:T(8,128)(2,1)} %bitcast.291), channel_id=1, source_target_pairs={{0,3},{1,4},{2,5},{3,6},{4,7},{5,0},{6,1},{7,2},{8,11},{9,12},{10,... | collective-permute-start | bytes 196616 | tf_op jit(solution)/shard_map/ppermute | solution.py:14
  15.9 5.7 %collective-permute-start.4 = (bf16[2,32,512]{2,1,0:T(8,128)(2,1)}, bf16[2,32,512]{2,1,0:T(8,128)(2,1)S(1)}, u32[]{:S(2)}, u32[]{:S(2)}) collective-permute-start(bf16[2,32,512]{2,1,0:T(8,128)(2,1)} %bitcast.292), channel_id=1, source_target_pairs={{0,2},{1,3},{2,4},{3,5},{4,6},{5,7},{6,0},{7,1},{8,10},{9,11},{10,... | collective-permute-start | bytes 196616 | tf_op jit(solution)/shard_map/ppermute | solution.py:14
  17.5 4.8 %collective-permute-start.3 = (bf16[2,32,512]{2,1,0:T(8,128)(2,1)}, bf16[2,32,512]{2,1,0:T(8,128)(2,1)S(1)}, u32[]{:S(2)}, u32[]{:S(2)}) collective-permute-start(bf16[2,32,512]{2,1,0:T(8,128)(2,1)} %bitcast.293), channel_id=1, source_target_pairs={{0,1},{1,2},{2,3},{3,4},{4,5},{5,6},{6,7},{7,0},{8,9},{9,10},{10,1... | collective-permute-start | bytes 196616 | tf_op jit(solution)/shard_map/ppermute | solution.py:14
  23.9 5.7 %collective-permute-start.12 = (bf16[128,512]{1,0:T(8,128)(2,1)S(1)}, bf16[128,512]{1,0:T(8,128)(2,1)S(1)}, u32[]{:S(2)}, u32[]{:S(2)}) collective-permute-start(bf16[128,512]{1,0:T(8,128)(2,1)S(1)} %get-tuple-element.28), channel_id=1, source_target_pairs={{0,24},{8,0},{16,8},{24,16},{1,25},{9,1},{17,9},{25,17},{2,26},{10... | collective-permute-start | bytes 393224 | tf_op jit(solution)/shard_map/ppermute | solution.py:14
  25.3 12.5 %collective-permute-start.11 = (bf16[128,512]{1,0:T(8,128)(2,1)S(1)}, bf16[128,512]{1,0:T(8,128)(2,1)S(1)}, u32[]{:S(2)}, u32[]{:S(2)}) collective-permute-start(bf16[128,512]{1,0:T(8,128)(2,1)S(1)} %get-tuple-element.29), channel_id=1, source_target_pairs={{0,16},{8,24},{16,0},{24,8},{1,17},{9,25},{17,1},{25,9},{2,18},{10... | collective-permute-start | bytes 393224 | tf_op jit(solution)/shard_map/ppermute | solution.py:14
  27.0 10.8 %collective-permute-start.10 = (bf16[128,512]{1,0:T(8,128)(2,1)S(1)}, bf16[128,512]{1,0:T(8,128)(2,1)S(1)}, u32[]{:S(2)}, u32[]{:S(2)}) collective-permute-start(bf16[128,512]{1,0:T(8,128)(2,1)S(1)} %get-tuple-element.30), channel_id=1, source_target_pairs={{0,8},{8,16},{16,24},{24,0},{1,9},{9,17},{17,25},{25,1},{2,10},{10... | collective-permute-start | bytes 393224 | tf_op jit(solution)/shard_map/ppermute | solution.py:14
  38.4 9.9 %copy-start.1 = (bf16[1,512,512]{2,1,0:T(8,128)(2,1)S(1)}, bf16[1,512,512]{2,1,0:T(8,128)(2,1)}, u32[]{:S(2)}) copy-start(bf16[1,512,512]{2,1,0:T(8,128)(2,1)} %param.9) | copy-start | bytes 1572868
  38.4 9.9 %copy-start.2 = (f32[3,1,32,512]{3,2,1,0:T(8,128)S(1)}, f32[3,1,32,512]{3,2,1,0:T(8,128)}, u32[]{:S(2)}) copy-start(f32[3,1,32,512]{3,2,1,0:T(8,128)} %param.10) | copy-start | bytes 589828
  38.4 14.2 %copy-start.3 = (s32[1,8]{1,0:T(1,128)S(1)}, s32[1,8]{1,0:T(1,128)}, u32[]{:S(2)}) copy-start(s32[1,8]{1,0:T(1,128)} %param.8) | copy-start | bytes 100
  49.3 10.3 %all-to-all-start.1 = ((bf16[8,32,512]{2,1,0:T(8,128)(2,1)}), bf16[8,32,512]{2,1,0:T(8,128)(2,1)S(1)}, u32[]{:S(2)}, u32[]{:S(2)}) async-start(bf16[8,32,512]{2,1,0:T(8,128)(2,1)} %broadcast_in_dim.1248), calls=%async_computation.1 | async-start | bytes 524288 | tf_op jit(solution)/shard_map/all_to_all | solution.py:100
  60.1 5.5 %collective-permute-start.15 = (bf16[128,512]{1,0:T(8,128)(2,1)S(1)}, bf16[128,512]{1,0:T(8,128)(2,1)S(1)}, u32[]{:S(2)}, u32[]{:S(2)}) collective-permute-start(bf16[128,512]{1,0:T(8,128)(2,1)S(1)} %get-tuple-element.24), channel_id=1, source_target_pairs={{0,24},{8,0},{16,8},{24,16},{1,25},{9,1},{17,9},{25,17},{2,26},{10... | collective-permute-start | bytes 393224 | tf_op jit(solution)/shard_map/ppermute | solution.py:14
  60.2 12.6 %collective-permute-start.14 = (bf16[128,512]{1,0:T(8,128)(2,1)S(1)}, bf16[128,512]{1,0:T(8,128)(2,1)S(1)}, u32[]{:S(2)}, u32[]{:S(2)}) collective-permute-start(bf16[128,512]{1,0:T(8,128)(2,1)S(1)} %get-tuple-element.25), channel_id=1, source_target_pairs={{0,16},{8,24},{16,0},{24,8},{1,17},{9,25},{17,1},{25,9},{2,18},{10... | collective-permute-start | bytes 393224 | tf_op jit(solution)/shard_map/ppermute | solution.py:14
  61.5 11.3 %collective-permute-start.13 = (bf16[128,512]{1,0:T(8,128)(2,1)S(1)}, bf16[128,512]{1,0:T(8,128)(2,1)S(1)}, u32[]{:S(2)}, u32[]{:S(2)}) collective-permute-start(bf16[128,512]{1,0:T(8,128)(2,1)S(1)} %get-tuple-element.26), channel_id=1, source_target_pairs={{0,8},{8,16},{16,24},{24,0},{1,9},{9,17},{17,25},{25,1},{2,10},{10... | collective-permute-start | bytes 393224 | tf_op jit(solution)/shard_map/ppermute | solution.py:14
  93.2 5.6 %collective-permute-start.18 = (bf16[128,512]{1,0:T(8,128)(2,1)S(1)}, bf16[128,512]{1,0:T(8,128)(2,1)S(1)}, u32[]{:S(2)}, u32[]{:S(2)}) collective-permute-start(bf16[128,512]{1,0:T(8,128)(2,1)S(1)} %get-tuple-element.20), channel_id=1, source_target_pairs={{0,24},{8,0},{16,8},{24,16},{1,25},{9,1},{17,9},{25,17},{2,26},{10... | collective-permute-start | bytes 393224 | tf_op jit(solution)/shard_map/ppermute | solution.py:14
  93.3 12.9 %collective-permute-start.17 = (bf16[128,512]{1,0:T(8,128)(2,1)S(1)}, bf16[128,512]{1,0:T(8,128)(2,1)S(1)}, u32[]{:S(2)}, u32[]{:S(2)}) collective-permute-start(bf16[128,512]{1,0:T(8,128)(2,1)S(1)} %get-tuple-element.21), channel_id=1, source_target_pairs={{0,16},{8,24},{16,0},{24,8},{1,17},{9,25},{17,1},{25,9},{2,18},{10... | collective-permute-start | bytes 393224 | tf_op jit(solution)/shard_map/ppermute | solution.py:14
  95.0 11.2 %collective-permute-start.16 = (bf16[128,512]{1,0:T(8,128)(2,1)S(1)}, bf16[128,512]{1,0:T(8,128)(2,1)S(1)}, u32[]{:S(2)}, u32[]{:S(2)}) collective-permute-start(bf16[128,512]{1,0:T(8,128)(2,1)S(1)} %get-tuple-element.22), channel_id=1, source_target_pairs={{0,8},{8,16},{16,24},{24,0},{1,9},{9,17},{17,25},{25,1},{2,10},{10... | collective-permute-start | bytes 393224 | tf_op jit(solution)/shard_map/ppermute | solution.py:14

commit v6 on v5

v6 whole, which is shorter than its diff:
```python
import jax
import jax.numpy as jnp
from jax import lax
from jax.sharding import PartitionSpec as P

BLOCK = 512
EXCITE = 128
OWNERS = 4
DELAYS = 2
STEPS = 3
WHOLE_TIME_DEVICES = 64


def shifted(x, axis, n, k):
    return lax.ppermute(x, axis, [(i, (i + k) % n) for i in range(n)])


def shift_gather(x, axis, n):
    return [x] + [shifted(x, axis, n, k) for k in range(1, n)]


def pick(pieces, index):
    if len(pieces) > 8:
        return jnp.take(jnp.stack(pieces), index, axis=0)
    chosen = index[:, None] == jnp.arange(len(pieces), dtype=index.dtype)[None, :]
    spread = (slice(None),) + (None,) * pieces[0].ndim
    total = None
    for k, piece in enumerate(pieces):
        term = jnp.where(chosen[:, k][spread], piece[None], jnp.zeros_like(piece)[None])
        total = term if total is None else total + term
    return total


def member_gather(x, members):
    spread = jnp.broadcast_to(x[None], (members,) + x.shape)
    return lax.all_to_all(spread, "member", 0, 0, tiled=True)


def body(tile_values, tile_lists, owner_map, inverses, excitations, history):
    members = lax.axis_size("member")
    groups = lax.axis_size("group")
    group_blocks = members // OWNERS
    share = EXCITE // OWNERS
    group_here = lax.axis_index("group")
    member_here = lax.axis_index("member")
    owners = owner_map[0]
    member_ids = jnp.arange(members, dtype=jnp.int32)
    group_ids = jnp.arange(groups, dtype=jnp.int32)
    block_ids = jnp.arange(group_blocks, dtype=jnp.int32)
    matches = owners[:, None] == member_ids[None, :]
    slot_of_member = jnp.sum(jnp.where(matches, member_ids[:, None], 0), axis=0)
    tiles_here = tile_lists.shape[0]

    source_group = tile_lists[:, 0] // group_blocks
    source_local = tile_lists[:, 0] % group_blocks
    observer_local = tile_lists[:, 1] % group_blocks
    delays_here = tile_lists[:, 2]
    source_shift = (group_here - source_group) % groups
    whole_time = members * groups <= WHOLE_TIME_DEVICES

    if whole_time:
        maps_by_shift = jnp.stack(shift_gather(owners, "group", groups))
        slots_wanted = OWNERS * source_local[:, None] + jnp.arange(OWNERS, dtype=jnp.int32)[None, :]
        owner_wanted = jnp.take_along_axis(maps_by_shift[source_shift], slots_wanted, axis=1)
        flat_wanted = owner_wanted * groups + source_shift[:, None]
        selector = (
            flat_wanted[:, :, None] == jnp.arange(members * groups, dtype=jnp.int32)[None, None, :]
        ).astype(jnp.bfloat16)

        def rows_for_tiles(gathered):
            flat = gathered.reshape(members * groups, share * BLOCK)
            rows = jnp.einsum("iqf,fx->iqx", selector, flat, preferred_element_type=jnp.float32)
            return rows.astype(jnp.bfloat16).reshape(tiles_here, EXCITE, BLOCK)

        def spread_currents(piece):
            across = jnp.stack(shift_gather(piece, "group", groups))
            return member_gather(across, members)

        hist = spread_currents(history[:, 0])
        rows_at = [rows_for_tiles(hist[:, :, t]) for t in range(DELAYS)]
    else:
        owner_shift = (member_here - owners) % members
        lists_by_shift = jnp.stack(shift_gather(tile_lists, "group", groups))
        ahead = jnp.take(lists_by_shift, (groups - group_ids) % groups, axis=0)
        wanted = (ahead[:, :, 0] // group_blocks == group_here) & (ahead[:, :, 2] > 0)
        want_block = jnp.sum(jnp.where(wanted, ahead[:, :, 0] % group_blocks, 0), axis=1)
        want_delay = jnp.sum(jnp.where(wanted, ahead[:, :, 2], 0), axis=1)
        which_block = want_block[:, None] == block_ids[None, :]
        from_near = which_block & (want_delay[:, None] == 1)
        from_far = which_block & (want_delay[:, None] == 2)
        hist = member_gather(history[:, 0], members)
        hist_placed = pick([hist[m] for m in range(members)], owners)
        blocks = [
            hist_placed[:, t].reshape(group_blocks, EXCITE, BLOCK) for t in range(DELAYS)
        ]

    results = []
    for step in range(STEPS):
        if whole_time:
            blocks_in = jnp.where(
                (delays_here == 1)[:, None, None], rows_at[DELAYS + step - 1], rows_at[DELAYS + step - 2]
            )
        else:
            near = blocks[DELAYS + step - 1]
            far = blocks[DELAYS + step - 2]
            outgoing = None
            for block in range(group_blocks):
                term = jnp.where(from_near[:, block, None, None], near[block][None], 0) + jnp.where(
                    from_far[:, block, None, None], far[block][None], 0
                )
                outgoing = term if outgoing is None else outgoing + term
            received = [outgoing[0]] + [
                shifted(outgoing[k], "group", groups, k) for k in range(1, groups)
            ]
            blocks_in = pick(received, source_shift)
        terms = jnp.einsum(
            "kes,kso->keo", blocks_in, tile_values, preferred_element_type=jnp.float32
        )
        partial_sums = []
        for block in range(group_blocks):
            chosen = (observer_local == block) & (delays_here > 0)
            partial_sums.append(
                jnp.sum(jnp.where(chosen[:, None, None], terms, 0.0), axis=0)
            )
        slots = jnp.stack(partial_sums).astype(jnp.bfloat16).reshape(members, share, BLOCK)
        sent = pick([slots[s] for s in range(members)], slot_of_member)
        got = lax.all_to_all(sent, "member", 0, 0, tiled=True)
        field = jnp.sum(got.astype(jnp.float32), axis=0)
        residual = (excitations[step, 0] - field).astype(jnp.bfloat16)
        current = jnp.dot(residual, inverses[0], preferred_element_type=jnp.float32)
        results.append(current)
        if step + 1 < STEPS:
            piece = current.astype(jnp.bfloat16)
            if whole_time:
                rows_at.append(rows_for_tiles(spread_currents(piece)))
            else:
                got = member_gather(piece, members)
                placed = pick([got[m] for m in range(members)], owners)
                blocks.append(placed.reshape(group_blocks, EXCITE, BLOCK))
    return jnp.stack(results)[:, None]


def solution(mesh):
    placed = (
        P(("group", "member"), None, None),
        P(("group", "member"), None),
        P("group", None),
        P(("group", "member"), None, None),
        P(None, ("group", "member"), None, None),
        P(None, ("group", "member"), None, None),
    )
    return jax.shard_map(
        body,
        mesh=mesh,
        in_specs=placed,
        out_specs=P(None, ("group", "member"), None, None),
        check_vma=False,
    )
```

time: 118 us -> 158 us (1.34)
  blocking collectives: 37.6 us -> 65 us
  local copies, waits for them, and re-layouts: 1.94 us -> 19.9 us
  matrix products: 2.35 us -> 12.1 us
  waiting for transfers between devices: 39.8 us -> 33.6 us
  starting transfers between devices: 26.8 us -> 22.1 us
  other arithmetic: 8.49 us -> 4.14 us
    all_to_all x1 -> x2, blocking collectives: 9.35 us -> 36.9 us  [member_gather(): return lax.all_to_all(spread, 'member', 0, 0, tiled=True)]
    ppermute x19 -> x12, waiting for transfers between devices: 32.9 us -> 9.12 us  [shifted(): return lax.ppermute(x, axis, [(i, (i + k) % n) for i in range(n)])]
    all_to_all x1, waiting for transfers between devices: 6.82 us -> 24.5 us  [member_gather(): return lax.all_to_all(spread, 'member', 0, 0, tiled=True)]
    reshape x0 -> x6, local copies, waits for them, and re-layouts: none -> 8.59 us  [the longest x2 4.69 us: rows_for_tiles(): flat = gathered.reshape(members * groups, share * BLOCK)]
    dot_general x0 -> x4, matrix products: none -> 6.35 us  [rows_for_tiles(): jnp.einsum('iqf,fx->iqx', selector, flat, preferred_element_type=jnp.floa...]
    ppermute x19 -> x12, starting transfers between devices: 23.4 us -> 17.6 us  [shifted(): return lax.ppermute(x, axis, [(i, (i + k) % n) for i in range(n)])]
    another operation x0 -> x3, local copies, waits for them, and re-layouts: none -> 4.9 us  [the longest x2 4.89 us: rows_for_tiles(): flat = gathered.reshape(members * groups, share * BLOCK)]
    dot_general x3, matrix products: 1.79 us -> 5.14 us  [body(): jnp.einsum('kes,kso->keo', blocks_in, tile_values, preferred_element_type...]
  transfers between devices with their start and end apart: 20 -> 13, of which waited for: 11 -> 9; matrix products, arithmetic and copies ran while one was open for 5% -> 3% of each run, Pallas kernels for 0% -> 0%
where the time goes in v6:
time: 158 us; the launch traced here: 157 us
  blocking collectives  65 us (41%)
  waiting for transfers between devices  33.6 us (21%)
  starting transfers between devices  22.1 us (14%)
  local copies, waits for them, and re-layouts  19.9 us (13%)
  matrix products  12.1 us (8%)
  other arithmetic  4.14 us (3%)
    all_to_all x2, blocking collectives, member_gather(): return lax.all_to_all(spread, 'member', 0, 0, tiled=True)  36.9 us
    all_to_all x3, blocking collectives, body(): got = lax.all_to_all(sent, 'member', 0, 0, tiled=True)  28 us
    all_to_all x1, waiting for transfers between devices, member_gather(): return lax.all_to_all(spread, 'member', 0, 0, tiled=True)  24.5 us
    ppermute x12, starting transfers between devices, shifted(): return lax.ppermute(x, axis, [(i, (i + k) % n) for i in range(n)])  17.6 us
    ppermute x12, waiting for transfers between devices, shifted(): return lax.ppermute(x, axis, [(i, (i + k) % n) for i in range(n)])  9.12 us
    dot_general x4, matrix products, rows_for_tiles(): jnp.einsum('iqf,fx->iqx', selector, flat, preferred_element_type=jnp.floa...  6.35 us
    dot_general x3, matrix products, body(): jnp.einsum('kes,kso->keo', blocks_in, tile_values, preferred_element_type...  5.14 us
    another operation x2, local copies, waits for them, and re-layouts, rows_for_tiles(): flat = gathered.reshape(members * groups, share * BLOCK)  4.89 us
  transfers between devices with their start and end apart: 13, of which 9 were waited for; matrix products, arithmetic and copies ran while one was open for 3% of the time, Pallas kernels for 0%

profile of v6, /device:TPU:0, one launch (start us, length us, event | category | flops | bytes accessed | tf_op | source)
XLA Modules:
  0.0 157.0 jit_solution(4640394876434643139)
XLA Ops:
  0.0 3.0 %collective-permute-start = (s32[8]{0:T(128)}, s32[8]{0:T(128)S(1)}, u32[]{:S(2)}, u32[]{:S(2)}) collective-permute-start(s32[8]{0:T(128)} %bitcast.206), channel_id=1, source_target_pairs={{0,8},{8,16},{16,24},{24,0},{1,9},{9,17},{17,25},{25,1},{2,10},{10... | collective-permute-start | bytes 104 | tf_op jit(solution)/shard_map/ppermute | solution.py:15
  3.0 2.6 %collective-permute-start.1 = (s32[8]{0:T(128)}, s32[8]{0:T(128)S(1)}, u32[]{:S(2)}, u32[]{:S(2)}) collective-permute-start(s32[8]{0:T(128)} %bitcast.207), channel_id=1, source_target_pairs={{0,16},{8,24},{16,0},{24,8},{1,17},{9,25},{17,1},{25,9},{2,18},{10... | collective-permute-start | bytes 104 | tf_op jit(solution)/shard_map/ppermute | solution.py:15
  5.7 1.8 %collective-permute-start.4 = (bf16[2,32,512]{2,1,0:T(8,128)(2,1)}, bf16[2,32,512]{2,1,0:T(8,128)(2,1)S(1)}, u32[]{:S(2)}, u32[]{:S(2)}) collective-permute-start(bf16[2,32,512]{2,1,0:T(8,128)(2,1)} %bitcast.194), channel_id=1, source_target_pairs={{0,16},{8,24},{16,0},{24,8},{1,17},{9,25},{17,1},{25,9},{2,18},{10... | collective-permute-start | bytes 196616 | tf_op jit(solution)/shard_map/ppermute | solution.py:15
  7.5 1.9 %collective-permute-start.5 = (bf16[2,32,512]{2,1,0:T(8,128)(2,1)}, bf16[2,32,512]{2,1,0:T(8,128)(2,1)S(1)}, u32[]{:S(2)}, u32[]{:S(2)}) collective-permute-start(bf16[2,32,512]{2,1,0:T(8,128)(2,1)} %bitcast.195), channel_id=1, source_target_pairs={{0,24},{8,0},{16,8},{24,16},{1,25},{9,1},{17,9},{25,17},{2,26},{10... | collective-permute-start | bytes 196616 | tf_op jit(solution)/shard_map/ppermute | solution.py:15
  10.4 1.9 %collective-permute-done.3 = bf16[2,32,512]{2,1,0:T(8,128)(2,1)S(1)} collective-permute-done((bf16[2,32,512]{2,1,0:T(8,128)(2,1)}, bf16[2,32,512]{2,1,0:T(8,128)(2,1)S(1)}, u32[]{:S(2)}, u32[]{:S(2)}) %collective-permute-start.3) | collective-permute-done | bytes 65568 | tf_op jit(solution)/shard_map/ppermute | solution.py:15
  12.3 1.3 collective-permute-done.4
  14.5 1.5 broadcast_in_dim.465
  16.1 4.5 %all-to-all-start = ((bf16[8,4,2,32,512]{4,3,1,2,0:T(8,128)(2,1)}), bf16[8,4,2,32,512]{4,3,1,2,0:T(8,128)(2,1)}, u32[]{:S(2)}, u32[]{:S(2)}) async-start(bf16[8,4,2,32,512]{4,3,1,2,0:T(8,128)(2,1)} %broadcast_in_dim.465), calls=%async_computation | async-start | bytes 4194304 | tf_op jit(solution)/shard_map/all_to_all | solution.py:36
  22.7 24.5 %all-to-all-done = bf16[8,4,2,32,512]{4,3,1,2,0:T(8,128)(2,1)} async-done(((bf16[8,4,2,32,512]{4,3,1,2,0:T(8,128)(2,1)}), bf16[8,4,2,32,512]{4,3,1,2,0:T(8,128)(2,1)}, u32[]{:S(2)}, u32[]{:S(2)}) %all-to-all-start) | async-done | bytes 2097184 | tf_op jit(solution)/shard_map/all_to_all | solution.py:36
  47.2 3.1 %fusion.41 = (bf16[8,4,1,32,512]{4,3,1,2,0:T(8,128)(2,1)}, bf16[8,4,1,32,512]{4,3,1,2,0:T(8,128)(2,1)}) fusion(bf16[8,4,2,32,512]{4,3,1,2,0:T(8,128)(2,1)} %all-to-all-done), kind=kLoop, calls=%fused_computation.134 | loop fusion | bytes 4194304 | tf_op jit(solution)/shard_map/slice | solution.py:80
  50.3 2.3 %reshape.216 = bf16[32,16384,1]{1,0,2:T(8,128)(2,1)} reshape(bf16[8,4,1,32,512]{4,3,1,2,0:T(8,128)(2,1)} %get-tuple-element.21) | data formatting | bytes 2097152 | tf_op jit(solution)/shard_map/reshape;squeeze | solution.py:71
  52.7 1.6 %convolution_convert_fusion.3 = bf16[4,4,16384]{2,1,0:T(4,128)(2,1)S(1)} fusion(bf16[32,16384,1]{1,0,2:T(8,128)(2,1)} %reshape.216, s32[4,4]{1,0:T(4,128)S(1)} %multiply_add_fusion), kind=kOutput, calls=%fused_computation.5 | convolution fusion | flops 17039872 | bytes 1572928 | tf_op jit(solution)/shard_map/iqf,fx->iqx/dot_general | solution.py:72
  54.7 2.5 %reshape.217 = bf16[32,16384,1]{1,0,2:T(8,128)(2,1)} reshape(bf16[8,4,1,32,512]{4,3,1,2,0:T(8,128)(2,1)} %get-tuple-element.20) | data formatting | bytes 2097152 | tf_op jit(solution)/shard_map/reshape;squeeze | solution.py:71
  57.2 1.6 %convolution_convert_fusion.2 = bf16[4,4,16384]{2,1,0:T(4,128)(2,1)S(1)} fusion(bf16[32,16384,1]{1,0,2:T(8,128)(2,1)} %reshape.217, s32[4,4]{1,0:T(4,128)S(1)} %multiply_add_fusion), kind=kOutput, calls=%fused_computation.4 | convolution fusion | flops 17039872 | bytes 1572928 | tf_op jit(solution)/shard_map/iqf,fx->iqx/dot_general | solution.py:72
  60.0 1.6 %select_reduce_fusion.5 = (bf16[128,512]{1,0:T(8,128)(2,1)S(1)}, bf16[128,512]{1,0:T(8,128)(2,1)S(1)}) fusion(pred[4]{0:T(512)(128)(4,1)S(1)} %compare_and_fusion.1, pred[4]{0:T(512)(128)(4,1)S(1)} %get-tuple-element.17, bf16[4,512,512]{2,1,0:T(8,128)(2,1)S(1)} %copy-done, bf16[4,128,512]{2,1,0:T(8,128)(2,1)S(1)} %reshape.196, ...), kind=kOutput, calls=%fused_computation.12 | convolution fusion | flops 269615104 | bytes 3407884 | tf_op jit(solution)/shard_map/kes,kso->keo/dot_general | solution.py:116
  61.9 9.3 %all_to_all.30 = bf16[8,32,512]{2,1,0:T(8,128)(2,1)S(1)} all-to-all(bf16[8,32,512]{2,1,0:T(8,128)(2,1)S(1)} %select_add_fusion.2), channel_id=1, replica_groups=mesh['group'=4,'member'=8] {'member'}, dimensions={0} | all-to-all | bytes 524288 | tf_op jit(solution)/shard_map/all_to_all | solution.py:127
  71.5 1.3 collective-permute-start.6
  72.9 1.4 collective-permute-start.7
  75.4 1.9 %collective-permute-done.6 = bf16[32,512]{1,0:T(8,128)(2,1)S(1)} collective-permute-done((bf16[32,512]{1,0:T(8,128)(2,1)S(1)}, bf16[32,512]{1,0:T(8,128)(2,1)S(1)}, u32[]{:S(2)}, u32[]{:S(2)}) %collective-permute-start.6) | collective-permute-done | bytes 32800 | tf_op jit(solution)/shard_map/ppermute | solution.py:15
  78.5 18.5 %all_to_all.31 = bf16[8,4,32,512]{3,2,1,0:T(8,128)(2,1)} all-to-all(bf16[8,4,32,512]{3,2,1,0:T(8,128)(2,1)S(1)} %broadcast_in_dim.499), channel_id=1, replica_groups=mesh['group'=4,'member'=8] {'member'}, dimensions={0} | all-to-all | bytes 2097152 | tf_op jit(solution)/shard_map/all_to_all | solution.py:36
  96.9 2.3 %reshape.218 = bf16[32,16384,1]{1,0,2:T(8,128)(2,1)} reshape(bf16[8,4,32,512]{3,2,1,0:T(8,128)(2,1)} %all_to_all.31) | data formatting | bytes 2097152 | tf_op jit(solution)/shard_map/reshape | solution.py:71
  99.3 1.6 %convolution_convert_fusion.1 = bf16[4,4,16384]{2,1,0:T(4,128)(2,1)S(1)} fusion(bf16[32,16384,1]{1,0,2:T(8,128)(2,1)} %reshape.218, s32[4,4]{1,0:T(4,128)S(1)} %multiply_add_fusion), kind=kOutput, calls=%fused_computation.3 | convolution fusion | flops 17039872 | bytes 1572928 | tf_op jit(solution)/shard_map/iqf,fx->iqx/dot_general | solution.py:72
  102.1 1.8 %select_reduce_fusion.3 = (bf16[128,512]{1,0:T(8,128)(2,1)S(1)}, bf16[128,512]{1,0:T(8,128)(2,1)S(1)}) fusion(pred[4]{0:T(512)(128)(4,1)S(1)} %compare_and_fusion.1, pred[4]{0:T(512)(128)(4,1)S(1)} %get-tuple-element.17, bf16[4,512,512]{2,1,0:T(8,128)(2,1)S(1)} %copy-done, bf16[4,128,512]{2,1,0:T(8,128)(2,1)} %reshape.199, ...), kind=kOutput, calls=%fused_computation.10 | convolution fusion | flops 269615104 | bytes 3407884 | tf_op jit(solution)/shard_map/kes,kso->keo/dot_general | solution.py:116
  104.1 9.3 %all_to_all.32 = bf16[8,32,512]{2,1,0:T(8,128)(2,1)S(1)} all-to-all(bf16[8,32,512]{2,1,0:T(8,128)(2,1)S(1)} %select_add_fusion.1), channel_id=1, replica_groups=mesh['group'=4,'member'=8] {'member'}, dimensions={0} | all-to-all | bytes 524288 | tf_op jit(solution)/shard_map/all_to_all | solution.py:127
  113.7 1.5 collective-permute-start.9
  115.2 1.8 %collective-permute-start.10 = (bf16[32,512]{1,0:T(8,128)(2,1)S(1)}, bf16[32,512]{1,0:T(8,128)(2,1)S(1)}, u32[]{:S(2)}, u32[]{:S(2)}) collective-permute-start(bf16[32,512]{1,0:T(8,128)(2,1)S(1)} %get-tuple-element.56), channel_id=1, source_target_pairs={{0,16},{8,24},{16,0},{24,8},{1,17},{9,25},{17,1},{25,9},{2,18},{10... | collective-permute-start | bytes 98312 | tf_op jit(solution)/shard_map/ppermute | solution.py:15
  118.0 1.5 collective-permute-done.9
  121.1 18.5 %all_to_all.33 = bf16[8,4,32,512]{3,2,1,0:T(8,128)(2,1)} all-to-all(bf16[8,4,32,512]{3,2,1,0:T(8,128)(2,1)S(1)} %broadcast_in_dim.516), channel_id=1, replica_groups=mesh['group'=4,'member'=8] {'member'}, dimensions={0} | all-to-all | bytes 2097152 | tf_op jit(solution)/shard_map/all_to_all | solution.py:36
  139.6 2.3 %reshape.219 = bf16[32,16384,1]{1,0,2:T(8,128)(2,1)} reshape(bf16[8,4,32,512]{3,2,1,0:T(8,128)(2,1)} %all_to_all.33) | data formatting | bytes 2097152 | tf_op jit(solution)/shard_map/reshape | solution.py:71
  141.9 1.6 %convolution_convert_fusion = bf16[4,4,16384]{2,1,0:T(4,128)(2,1)S(1)} fusion(bf16[32,16384,1]{1,0,2:T(8,128)(2,1)} %reshape.219, s32[4,4]{1,0:T(4,128)S(1)} %multiply_add_fusion), kind=kOutput, calls=%fused_computation.2 | convolution fusion | flops 17039872 | bytes 1572928 | tf_op jit(solution)/shard_map/iqf,fx->iqx/dot_general | solution.py:72
  144.7 1.8 %select_reduce_fusion.1 = (bf16[128,512]{1,0:T(8,128)(2,1)S(1)}, bf16[128,512]{1,0:T(8,128)(2,1)S(1)}) fusion(pred[4]{0:T(512)(128)(4,1)S(1)} %compare_and_fusion.1, pred[4]{0:T(512)(128)(4,1)S(1)} %get-tuple-element.17, bf16[4,512,512]{2,1,0:T(8,128)(2,1)S(1)} %copy-done, bf16[4,128,512]{2,1,0:T(8,128)(2,1)} %reshape.201, ...), kind=kOutput, calls=%fused_computation.8 | convolution fusion | flops 269615104 | bytes 3407884 | tf_op jit(solution)/shard_map/kes,kso->keo/dot_general | solution.py:116
  146.8 9.3 %all_to_all.34 = bf16[8,32,512]{2,1,0:T(8,128)(2,1)S(1)} all-to-all(bf16[8,32,512]{2,1,0:T(8,128)(2,1)S(1)} %select_add_fusion), channel_id=1, replica_groups=mesh['group'=4,'member'=8] {'member'}, dimensions={0} | all-to-all | bytes 524288 | tf_op jit(solution)/shard_map/all_to_all | solution.py:127
  (66 shorter events, 15.0 us)
Async XLA Ops:
  0.0 60.0 %copy-start = (bf16[4,512,512]{2,1,0:T(8,128)(2,1)S(1)}, bf16[4,512,512]{2,1,0:T(8,128)(2,1)}, u32[]{:S(2)}) copy-start(bf16[4,512,512]{2,1,0:T(8,128)(2,1)} %param.6) | copy-start | bytes 6291460
  0.0 21.3 %collective-permute-start = (s32[8]{0:T(128)}, s32[8]{0:T(128)S(1)}, u32[]{:S(2)}, u32[]{:S(2)}) collective-permute-start(s32[8]{0:T(128)} %bitcast.206), channel_id=1, source_target_pairs={{0,8},{8,16},{16,24},{24,0},{1,9},{9,17},{17,25},{25,1},{2,10},{10... | collective-permute-start | bytes 104 | tf_op jit(solution)/shard_map/ppermute | solution.py:15
  3.0 18.2 %collective-permute-start.1 = (s32[8]{0:T(128)}, s32[8]{0:T(128)S(1)}, u32[]{:S(2)}, u32[]{:S(2)}) collective-permute-start(s32[8]{0:T(128)} %bitcast.207), channel_id=1, source_target_pairs={{0,16},{8,24},{16,0},{24,8},{1,17},{9,25},{17,1},{25,9},{2,18},{10... | collective-permute-start | bytes 104 | tf_op jit(solution)/shard_map/ppermute | solution.py:15
  5.6 6.7 %collective-permute-start.3 = (bf16[2,32,512]{2,1,0:T(8,128)(2,1)}, bf16[2,32,512]{2,1,0:T(8,128)(2,1)S(1)}, u32[]{:S(2)}, u32[]{:S(2)}) collective-permute-start(bf16[2,32,512]{2,1,0:T(8,128)(2,1)} %bitcast.193), channel_id=1, source_target_pairs={{0,8},{8,16},{16,24},{24,0},{1,9},{9,17},{17,25},{25,1},{2,10},{10... | collective-permute-start | bytes 196616 | tf_op jit(solution)/shard_map/ppermute | solution.py:15
  5.7 8.0 %collective-permute-start.4 = (bf16[2,32,512]{2,1,0:T(8,128)(2,1)}, bf16[2,32,512]{2,1,0:T(8,128)(2,1)S(1)}, u32[]{:S(2)}, u32[]{:S(2)}) collective-permute-start(bf16[2,32,512]{2,1,0:T(8,128)(2,1)} %bitcast.194), channel_id=1, source_target_pairs={{0,16},{8,24},{16,0},{24,8},{1,17},{9,25},{17,1},{25,9},{2,18},{10... | collective-permute-start | bytes 196616 | tf_op jit(solution)/shard_map/ppermute | solution.py:15
  7.5 6.1 %collective-permute-start.5 = (bf16[2,32,512]{2,1,0:T(8,128)(2,1)}, bf16[2,32,512]{2,1,0:T(8,128)(2,1)S(1)}, u32[]{:S(2)}, u32[]{:S(2)}) collective-permute-start(bf16[2,32,512]{2,1,0:T(8,128)(2,1)} %bitcast.195), channel_id=1, source_target_pairs={{0,24},{8,0},{16,8},{24,16},{1,25},{9,1},{17,9},{25,17},{2,26},{10... | collective-permute-start | bytes 196616 | tf_op jit(solution)/shard_map/ppermute | solution.py:15
  12.3 8.9 %collective-permute-start.2 = (s32[8]{0:T(128)}, s32[8]{0:T(128)S(1)}, u32[]{:S(2)}, u32[]{:S(2)}) collective-permute-start(s32[8]{0:T(128)} %bitcast.208), channel_id=1, source_target_pairs={{0,24},{8,0},{16,8},{24,16},{1,25},{9,1},{17,9},{25,17},{2,26},{10... | collective-permute-start | bytes 104 | tf_op jit(solution)/shard_map/ppermute | solution.py:15
  16.1 4.6 %copy-start.4 = (s32[4,3]{1,0:T(4,128)S(1)}, s32[4,3]{1,0:T(4,128)}, u32[]{:S(2)}) copy-start(s32[4,3]{1,0:T(4,128)} %param.7) | copy-start | bytes 148
  16.1 5.0 %copy-start.5 = (s32[1,8]{1,0:T(1,128)S(1)}, s32[1,8]{1,0:T(1,128)}, u32[]{:S(2)}) copy-start(s32[1,8]{1,0:T(1,128)} %param.8) | copy-start | bytes 100
  16.1 31.1 %all-to-all-start = ((bf16[8,4,2,32,512]{4,3,1,2,0:T(8,128)(2,1)}), bf16[8,4,2,32,512]{4,3,1,2,0:T(8,128)(2,1)}, u32[]{:S(2)}, u32[]{:S(2)}) async-start(bf16[8,4,2,32,512]{4,3,1,2,0:T(8,128)(2,1)} %broadcast_in_dim.465), calls=%async_computation | async-start | bytes 4194304 | tf_op jit(solution)/shard_map/all_to_all | solution.py:36
  54.6 5.3 %copy-start.2 = (bf16[4,128,512]{2,1,0:T(8,128)(2,1)}, bf16[4,128,512]{2,1,0:T(8,128)(2,1)S(1)}, u32[]{:S(2)}) copy-start(bf16[4,128,512]{2,1,0:T(8,128)(2,1)S(1)} %reshape.196) | copy-start | bytes 1572868
  61.6 9.7 %copy-start.1 = (bf16[1,512,512]{2,1,0:T(8,128)(2,1)S(1)}, bf16[1,512,512]{2,1,0:T(8,128)(2,1)}, u32[]{:S(2)}) copy-start(bf16[1,512,512]{2,1,0:T(8,128)(2,1)} %param.9) | copy-start | bytes 1572868
  61.6 9.7 %copy-start.3 = (f32[3,1,32,512]{3,2,1,0:T(8,128)S(1)}, f32[3,1,32,512]{3,2,1,0:T(8,128)}, u32[]{:S(2)}) copy-start(f32[3,1,32,512]{3,2,1,0:T(8,128)} %param.10) | copy-start | bytes 589828
  71.5 5.8 %collective-permute-start.6 = (bf16[32,512]{1,0:T(8,128)(2,1)S(1)}, bf16[32,512]{1,0:T(8,128)(2,1)S(1)}, u32[]{:S(2)}, u32[]{:S(2)}) collective-permute-start(bf16[32,512]{1,0:T(8,128)(2,1)S(1)} %get-tuple-element.54), channel_id=1, source_target_pairs={{0,8},{8,16},{16,24},{24,0},{1,9},{9,17},{17,25},{25,1},{2,10},{10... | collective-permute-start | bytes 98312 | tf_op jit(solution)/shard_map/ppermute | solution.py:15
  72.9 5.1 %collective-permute-start.7 = (bf16[32,512]{1,0:T(8,128)(2,1)S(1)}, bf16[32,512]{1,0:T(8,128)(2,1)S(1)}, u32[]{:S(2)}, u32[]{:S(2)}) collective-permute-start(bf16[32,512]{1,0:T(8,128)(2,1)S(1)} %get-tuple-element.54), channel_id=1, source_target_pairs={{0,16},{8,24},{16,0},{24,8},{1,17},{9,25},{17,1},{25,9},{2,18},{10... | collective-permute-start | bytes 98312 | tf_op jit(solution)/shard_map/ppermute | solution.py:15
  74.3 4.0 %collective-permute-start.8 = (bf16[32,512]{1,0:T(8,128)(2,1)S(1)}, bf16[32,512]{1,0:T(8,128)(2,1)S(1)}, u32[]{:S(2)}, u32[]{:S(2)}) collective-permute-start(bf16[32,512]{1,0:T(8,128)(2,1)S(1)} %get-tuple-element.54), channel_id=1, source_target_pairs={{0,24},{8,0},{16,8},{24,16},{1,25},{9,1},{17,9},{25,17},{2,26},{10... | collective-permute-start | bytes 98312 | tf_op jit(solution)/shard_map/ppermute | solution.py:15
  113.7 5.8 %collective-permute-start.9 = (bf16[32,512]{1,0:T(8,128)(2,1)S(1)}, bf16[32,512]{1,0:T(8,128)(2,1)S(1)}, u32[]{:S(2)}, u32[]{:S(2)}) collective-permute-start(bf16[32,512]{1,0:T(8,128)(2,1)S(1)} %get-tuple-element.56), channel_id=1, source_target_pairs={{0,8},{8,16},{16,24},{24,0},{1,9},{9,17},{17,25},{25,1},{2,10},{10... | collective-permute-start | bytes 98312 | tf_op jit(solution)/shard_map/ppermute | solution.py:15
  115.2 5.0 %collective-permute-start.10 = (bf16[32,512]{1,0:T(8,128)(2,1)S(1)}, bf16[32,512]{1,0:T(8,128)(2,1)S(1)}, u32[]{:S(2)}, u32[]{:S(2)}) collective-permute-start(bf16[32,512]{1,0:T(8,128)(2,1)S(1)} %get-tuple-element.56), channel_id=1, source_target_pairs={{0,16},{8,24},{16,0},{24,8},{1,17},{9,25},{17,1},{25,9},{2,18},{10... | collective-permute-start | bytes 98312 | tf_op jit(solution)/shard_map/ppermute | solution.py:15
  117.0 3.9 %collective-permute-start.11 = (bf16[32,512]{1,0:T(8,128)(2,1)S(1)}, bf16[32,512]{1,0:T(8,128)(2,1)S(1)}, u32[]{:S(2)}, u32[]{:S(2)}) collective-permute-start(bf16[32,512]{1,0:T(8,128)(2,1)S(1)} %get-tuple-element.56), channel_id=1, source_target_pairs={{0,24},{8,0},{16,8},{24,16},{1,25},{9,1},{17,9},{25,17},{2,26},{10... | collective-permute-start | bytes 98312 | tf_op jit(solution)/shard_map/ppermute | solution.py:15

commit v7 on v5

--- a/solution.py
+++ b/solution.py
@@ -41,7 +41,6 @@
     member_ids = jnp.arange(members, dtype=jnp.int32)
     matches = owners[:, None] == member_ids[None, :]
     slot_of_member = jnp.sum(jnp.where(matches, member_ids[:, None], 0), axis=0)
-    owner_shift = (member_here - owners) % members
     send_slot = jnp.take(slot_of_member, (member_here + member_ids) % members)
 
     lists_by_shift = jnp.stack(shift_gather(tile_lists, "group", groups))
@@ -60,8 +59,9 @@
     delays_here = tile_lists[:, 2]
     source_shift = (group_here - source_group) % groups
 
-    hist_pieces = shift_gather(history[:, 0], "member", members)
-    hist_placed = pick(hist_pieces, owner_shift)
+    spread_hist = jnp.broadcast_to(history[:, 0][None], (members,) + history[:, 0].shape)
+    hist_got = lax.all_to_all(spread_hist, "member", 0, 0, tiled=True)
+    hist_placed = pick([hist_got[m] for m in range(members)], owners)
     blocks = [
         hist_placed[:, t].reshape(group_blocks, EXCITE, BLOCK) for t in range(DELAYS)
     ]

time: 118 us -> 114 us (0.966)
  blocking collectives: 37.6 us -> 48.5 us
  waiting for transfers between devices: 39.8 us -> 31.2 us
  starting transfers between devices: 26.8 us -> 21 us
    all_to_all x1 -> x2, blocking collectives: 9.35 us -> 18.7 us  [body(): got = lax.all_to_all(spread, 'member', 0, 0, tiled=True)]
    ppermute x19 -> x12, starting transfers between devices: 23.4 us -> 17.3 us  [shifted(): return lax.ppermute(x, axis, [(i, (i + k) % n) for i in range(n)])]
    ppermute x19 -> x12, waiting for transfers between devices: 32.9 us -> 26.8 us  [shifted(): return lax.ppermute(x, axis, [(i, (i + k) % n) for i in range(n)])]
    all_to_all x1, waiting for transfers between devices: 6.82 us -> 4.4 us  [body(): hist_got = lax.all_to_all(spread_hist, 'member', 0, 0, tiled=True)]
    broadcast_in_dim x0 -> x1, local copies, waits for them, and re-layouts: none -> 1.68 us  [body(): jnp.broadcast_to(history[:, 0][None], (members,) + history[:, 0].shape)]
    all_to_all x3, blocking collectives: 28.2 us -> 29.8 us  [body(): got = lax.all_to_all(sent, 'member', 0, 0, tiled=True)]
  transfers between devices with their start and end apart: 20 -> 13, of which waited for: 11 -> 7; matrix products, arithmetic and copies ran while one was open for 5% -> 6% of each run, Pallas kernels for 0% -> 0%
where the time goes in v7:
time: 114 us
  blocking collectives  48.5 us (43%)
  waiting for transfers between devices  31.2 us (27%)
  starting transfers between devices  21 us (18%)
  other arithmetic  7.67 us (7%)
  local copies, waits for them, and re-layouts  2.94 us (3%)
  matrix products  2.31 us (2%)
    all_to_all x3, blocking collectives, body(): got = lax.all_to_all(sent, 'member', 0, 0, tiled=True)  29.8 us
    ppermute x12, waiting for transfers between devices, shifted(): return lax.ppermute(x, axis, [(i, (i + k) % n) for i in range(n)])  26.8 us
    all_to_all x2, blocking collectives, body(): got = lax.all_to_all(spread, 'member', 0, 0, tiled=True)  18.7 us
    ppermute x12, starting transfers between devices, shifted(): return lax.ppermute(x, axis, [(i, (i + k) % n) for i in range(n)])  17.3 us
    all_to_all x1, waiting for transfers between devices, body(): hist_got = lax.all_to_all(spread_hist, 'member', 0, 0, tiled=True)  4.4 us
    all_to_all x1, starting transfers between devices, body(): hist_got = lax.all_to_all(spread_hist, 'member', 0, 0, tiled=True)  3.72 us
  transfers between devices with their start and end apart: 13, of which 7 were waited for; matrix products, arithmetic and copies ran while one was open for 6% of the time, Pallas kernels for 0%

profile of v7, /device:TPU:0, one launch (start us, length us, event | category | flops | bytes accessed | tf_op | source)
XLA Modules:
  0.0 113.9 jit_solution(12149825869395835918)
XLA Ops:
  0.0 3.0 %collective-permute-start = (s32[4,3]{1,0:T(4,128)}, s32[4,3]{1,0:T(4,128)S(1)}, u32[]{:S(2)}, u32[]{:S(2)}) collective-permute-start(s32[4,3]{1,0:T(4,128)} %param.7), channel_id=1, source_target_pairs={{0,8},{8,16},{16,24},{24,0},{1,9},{9,17},{17,25},{25,1},{2,10},{10... | collective-permute-start | bytes 152 | tf_op jit(solution)/shard_map/ppermute | solution.py:14
  3.0 2.1 %collective-permute-start.2 = (s32[4,3]{1,0:T(4,128)}, s32[4,3]{1,0:T(4,128)S(1)}, u32[]{:S(2)}, u32[]{:S(2)}) collective-permute-start(s32[4,3]{1,0:T(4,128)} %param.7), channel_id=1, source_target_pairs={{0,24},{8,0},{16,8},{24,16},{1,25},{9,1},{17,9},{25,17},{2,26},{10... | collective-permute-start | bytes 152 | tf_op jit(solution)/shard_map/ppermute | solution.py:14
  5.1 1.0 collective-permute-start.1
  6.1 1.7 %broadcast_in_dim.1161 = bf16[8,2,32,512]{3,2,1,0:T(8,128)(2,1)} broadcast(bf16[2,32,512]{2,1,0:T(8,128)(2,1)} %bitcast.286), dimensions={1,2,3} | broadcast | bytes 589824 | tf_op jit(solution)/shard_map/broadcast_in_dim | solution.py:62
  7.7 3.7 %all-to-all-start = ((bf16[8,2,32,512]{3,2,1,0:T(8,128)(2,1)}), bf16[8,2,32,512]{3,2,1,0:T(8,128)(2,1)S(1)}, u32[]{:S(2)}, u32[]{:S(2)}) async-start(bf16[8,2,32,512]{3,2,1,0:T(8,128)(2,1)} %broadcast_in_dim.1161), calls=%async_computation | async-start | bytes 1048576 | tf_op jit(solution)/shard_map/all_to_all | solution.py:63
  11.5 0.9 fusion.74
  12.5 0.8 select_reduce_fusion.6
  13.3 0.7 iota_compare_fusion.1
  13.9 1.0 slice_reduce_fusion.2
  15.0 0.7 pad_add_fusion
  16.8 4.4 %all-to-all-done = bf16[8,2,32,512]{3,2,1,0:T(8,128)(2,1)S(1)} async-done(((bf16[8,2,32,512]{3,2,1,0:T(8,128)(2,1)}), bf16[8,2,32,512]{3,2,1,0:T(8,128)(2,1)S(1)}, u32[]{:S(2)}, u32[]{:S(2)}) %all-to-all-start) | async-done | bytes 524320 | tf_op jit(solution)/shard_map/all_to_all | solution.py:63
  22.1 1.4 %collective-permute-start.5 = (bf16[128,512]{1,0:T(8,128)(2,1)S(1)}, bf16[128,512]{1,0:T(8,128)(2,1)S(1)}, u32[]{:S(2)}, u32[]{:S(2)}) collective-permute-start(bf16[128,512]{1,0:T(8,128)(2,1)S(1)} %get-tuple-element.28), channel_id=1, source_target_pairs={{0,24},{8,0},{16,8},{24,16},{1,25},{9,1},{17,9},{25,17},{2,26},{10... | collective-permute-start | bytes 393224 | tf_op jit(solution)/shard_map/ppermute | solution.py:14
  23.5 1.7 %collective-permute-start.4 = (bf16[128,512]{1,0:T(8,128)(2,1)S(1)}, bf16[128,512]{1,0:T(8,128)(2,1)S(1)}, u32[]{:S(2)}, u32[]{:S(2)}) collective-permute-start(bf16[128,512]{1,0:T(8,128)(2,1)S(1)} %get-tuple-element.29), channel_id=1, source_target_pairs={{0,16},{8,24},{16,0},{24,8},{1,17},{9,25},{17,1},{25,9},{2,18},{10... | collective-permute-start | bytes 393224 | tf_op jit(solution)/shard_map/ppermute | solution.py:14
  25.2 1.1 collective-permute-start.3
  26.3 2.7 %collective-permute-done.5 = bf16[128,512]{1,0:T(8,128)(2,1)S(1)} collective-permute-done((bf16[128,512]{1,0:T(8,128)(2,1)S(1)}, bf16[128,512]{1,0:T(8,128)(2,1)S(1)}, u32[]{:S(2)}, u32[]{:S(2)}) %collective-permute-start.5) | collective-permute-done | bytes 131104 | tf_op jit(solution)/shard_map/ppermute | solution.py:14
  29.0 5.5 %collective-permute-done.4 = bf16[128,512]{1,0:T(8,128)(2,1)S(1)} collective-permute-done((bf16[128,512]{1,0:T(8,128)(2,1)S(1)}, bf16[128,512]{1,0:T(8,128)(2,1)S(1)}, u32[]{:S(2)}, u32[]{:S(2)}) %collective-permute-start.4) | collective-permute-done | bytes 131104 | tf_op jit(solution)/shard_map/ppermute | solution.py:14
  34.5 0.6 select_reduce_fusion.5
  35.4 11.1 %all_to_all.30 = bf16[8,32,512]{2,1,0:T(8,128)(2,1)S(1)} all-to-all(bf16[8,32,512]{2,1,0:T(8,128)(2,1)S(1)} %select_add_fusion.5), channel_id=1, replica_groups=mesh['group'=4,'member'=8] {'member'}, dimensions={0} | all-to-all | bytes 524288 | tf_op jit(solution)/shard_map/all_to_all | solution.py:93
  46.9 9.3 %all_to_all.31 = bf16[8,32,512]{2,1,0:T(8,128)(2,1)S(1)} all-to-all(bf16[8,32,512]{2,1,0:T(8,128)(2,1)S(1)} %broadcast_in_dim.1253), channel_id=1, replica_groups=mesh['group'=4,'member'=8] {'member'}, dimensions={0} | all-to-all | bytes 524288 | tf_op jit(solution)/shard_map/all_to_all | solution.py:100
  56.8 1.3 %collective-permute-start.7 = (bf16[128,512]{1,0:T(8,128)(2,1)S(1)}, bf16[128,512]{1,0:T(8,128)(2,1)S(1)}, u32[]{:S(2)}, u32[]{:S(2)}) collective-permute-start(bf16[128,512]{1,0:T(8,128)(2,1)S(1)} %get-tuple-element.25), channel_id=1, source_target_pairs={{0,16},{8,24},{16,0},{24,8},{1,17},{9,25},{17,1},{25,9},{2,18},{10... | collective-permute-start | bytes 393224 | tf_op jit(solution)/shard_map/ppermute | solution.py:14
  58.1 1.9 %collective-permute-start.6 = (bf16[128,512]{1,0:T(8,128)(2,1)S(1)}, bf16[128,512]{1,0:T(8,128)(2,1)S(1)}, u32[]{:S(2)}, u32[]{:S(2)}) collective-permute-start(bf16[128,512]{1,0:T(8,128)(2,1)S(1)} %get-tuple-element.26), channel_id=1, source_target_pairs={{0,8},{8,16},{16,24},{24,0},{1,9},{9,17},{17,25},{25,1},{2,10},{10... | collective-permute-start | bytes 393224 | tf_op jit(solution)/shard_map/ppermute | solution.py:14
  60.1 2.2 %collective-permute-done.8 = bf16[128,512]{1,0:T(8,128)(2,1)S(1)} collective-permute-done((bf16[128,512]{1,0:T(8,128)(2,1)S(1)}, bf16[128,512]{1,0:T(8,128)(2,1)S(1)}, u32[]{:S(2)}, u32[]{:S(2)}) %collective-permute-start.8) | collective-permute-done | bytes 131104 | tf_op jit(solution)/shard_map/ppermute | solution.py:14
  62.3 7.1 %collective-permute-done.7 = bf16[128,512]{1,0:T(8,128)(2,1)S(1)} collective-permute-done((bf16[128,512]{1,0:T(8,128)(2,1)S(1)}, bf16[128,512]{1,0:T(8,128)(2,1)S(1)}, u32[]{:S(2)}, u32[]{:S(2)}) %collective-permute-start.7) | collective-permute-done | bytes 131104 | tf_op jit(solution)/shard_map/ppermute | solution.py:14
  70.3 9.3 %all_to_all.32 = bf16[8,32,512]{2,1,0:T(8,128)(2,1)S(1)} all-to-all(bf16[8,32,512]{2,1,0:T(8,128)(2,1)S(1)} %select_add_fusion.3), channel_id=1, replica_groups=mesh['group'=4,'member'=8] {'member'}, dimensions={0} | all-to-all | bytes 524288 | tf_op jit(solution)/shard_map/all_to_all | solution.py:93
  79.9 9.3 %all_to_all.33 = bf16[8,32,512]{2,1,0:T(8,128)(2,1)S(1)} all-to-all(bf16[8,32,512]{2,1,0:T(8,128)(2,1)S(1)} %broadcast_in_dim.1302), channel_id=1, replica_groups=mesh['group'=4,'member'=8] {'member'}, dimensions={0} | all-to-all | bytes 524288 | tf_op jit(solution)/shard_map/all_to_all | solution.py:100
  89.9 1.7 %collective-permute-start.10 = (bf16[128,512]{1,0:T(8,128)(2,1)S(1)}, bf16[128,512]{1,0:T(8,128)(2,1)S(1)}, u32[]{:S(2)}, u32[]{:S(2)}) collective-permute-start(bf16[128,512]{1,0:T(8,128)(2,1)S(1)} %get-tuple-element.21), channel_id=1, source_target_pairs={{0,16},{8,24},{16,0},{24,8},{1,17},{9,25},{17,1},{25,9},{2,18},{10... | collective-permute-start | bytes 393224 | tf_op jit(solution)/shard_map/ppermute | solution.py:14
  91.6 1.9 %collective-permute-start.9 = (bf16[128,512]{1,0:T(8,128)(2,1)S(1)}, bf16[128,512]{1,0:T(8,128)(2,1)S(1)}, u32[]{:S(2)}, u32[]{:S(2)}) collective-permute-start(bf16[128,512]{1,0:T(8,128)(2,1)S(1)} %get-tuple-element.22), channel_id=1, source_target_pairs={{0,8},{8,16},{16,24},{24,0},{1,9},{9,17},{17,25},{25,1},{2,10},{10... | collective-permute-start | bytes 393224 | tf_op jit(solution)/shard_map/ppermute | solution.py:14
  93.5 1.9 %collective-permute-done.11 = bf16[128,512]{1,0:T(8,128)(2,1)S(1)} collective-permute-done((bf16[128,512]{1,0:T(8,128)(2,1)S(1)}, bf16[128,512]{1,0:T(8,128)(2,1)S(1)}, u32[]{:S(2)}, u32[]{:S(2)}) %collective-permute-start.11) | collective-permute-done | bytes 131104 | tf_op jit(solution)/shard_map/ppermute | solution.py:14
  95.4 7.4 %collective-permute-done.10 = bf16[128,512]{1,0:T(8,128)(2,1)S(1)} collective-permute-done((bf16[128,512]{1,0:T(8,128)(2,1)S(1)}, bf16[128,512]{1,0:T(8,128)(2,1)S(1)}, u32[]{:S(2)}, u32[]{:S(2)}) %collective-permute-start.10) | collective-permute-done | bytes 131104 | tf_op jit(solution)/shard_map/ppermute | solution.py:14
  102.8 0.6 select_reduce_fusion.1
  103.7 9.3 %all_to_all.34 = bf16[8,32,512]{2,1,0:T(8,128)(2,1)S(1)} all-to-all(bf16[8,32,512]{2,1,0:T(8,128)(2,1)S(1)} %select_add_fusion.1), channel_id=1, replica_groups=mesh['group'=4,'member'=8] {'member'}, dimensions={0} | all-to-all | bytes 524288 | tf_op jit(solution)/shard_map/all_to_all | solution.py:93
  113.2 0.7 maximum_bitcast_fusion
  (64 shorter events, 5.5 us)
Async XLA Ops:
  0.0 34.5 %copy-start = (bf16[4,512,512]{2,1,0:T(8,128)(2,1)S(1)}, bf16[4,512,512]{2,1,0:T(8,128)(2,1)}, u32[]{:S(2)}) copy-start(bf16[4,512,512]{2,1,0:T(8,128)(2,1)} %param.6) | copy-start | bytes 6291460
  0.0 15.0 %collective-permute-start = (s32[4,3]{1,0:T(4,128)}, s32[4,3]{1,0:T(4,128)S(1)}, u32[]{:S(2)}, u32[]{:S(2)}) collective-permute-start(s32[4,3]{1,0:T(4,128)} %param.7), channel_id=1, source_target_pairs={{0,8},{8,16},{16,24},{24,0},{1,9},{9,17},{17,25},{25,1},{2,10},{10... | collective-permute-start | bytes 152 | tf_op jit(solution)/shard_map/ppermute | solution.py:14
  3.0 12.0 %collective-permute-start.2 = (s32[4,3]{1,0:T(4,128)}, s32[4,3]{1,0:T(4,128)S(1)}, u32[]{:S(2)}, u32[]{:S(2)}) collective-permute-start(s32[4,3]{1,0:T(4,128)} %param.7), channel_id=1, source_target_pairs={{0,24},{8,0},{16,8},{24,16},{1,25},{9,1},{17,9},{25,17},{2,26},{10... | collective-permute-start | bytes 152 | tf_op jit(solution)/shard_map/ppermute | solution.py:14
  5.1 9.9 %collective-permute-start.1 = (s32[4,3]{1,0:T(4,128)}, s32[4,3]{1,0:T(4,128)S(1)}, u32[]{:S(2)}, u32[]{:S(2)}) collective-permute-start(s32[4,3]{1,0:T(4,128)} %param.7), channel_id=1, source_target_pairs={{0,16},{8,24},{16,0},{24,8},{1,17},{9,25},{17,1},{25,9},{2,18},{10... | collective-permute-start | bytes 152 | tf_op jit(solution)/shard_map/ppermute | solution.py:14
  7.7 13.5 %all-to-all-start = ((bf16[8,2,32,512]{3,2,1,0:T(8,128)(2,1)}), bf16[8,2,32,512]{3,2,1,0:T(8,128)(2,1)S(1)}, u32[]{:S(2)}, u32[]{:S(2)}) async-start(bf16[8,2,32,512]{3,2,1,0:T(8,128)(2,1)} %broadcast_in_dim.1161), calls=%async_computation | async-start | bytes 1048576 | tf_op jit(solution)/shard_map/all_to_all | solution.py:63
  22.1 6.9 %collective-permute-start.5 = (bf16[128,512]{1,0:T(8,128)(2,1)S(1)}, bf16[128,512]{1,0:T(8,128)(2,1)S(1)}, u32[]{:S(2)}, u32[]{:S(2)}) collective-permute-start(bf16[128,512]{1,0:T(8,128)(2,1)S(1)} %get-tuple-element.28), channel_id=1, source_target_pairs={{0,24},{8,0},{16,8},{24,16},{1,25},{9,1},{17,9},{25,17},{2,26},{10... | collective-permute-start | bytes 393224 | tf_op jit(solution)/shard_map/ppermute | solution.py:14
  23.5 11.0 %collective-permute-start.4 = (bf16[128,512]{1,0:T(8,128)(2,1)S(1)}, bf16[128,512]{1,0:T(8,128)(2,1)S(1)}, u32[]{:S(2)}, u32[]{:S(2)}) collective-permute-start(bf16[128,512]{1,0:T(8,128)(2,1)S(1)} %get-tuple-element.29), channel_id=1, source_target_pairs={{0,16},{8,24},{16,0},{24,8},{1,17},{9,25},{17,1},{25,9},{2,18},{10... | collective-permute-start | bytes 393224 | tf_op jit(solution)/shard_map/ppermute | solution.py:14
  25.2 9.3 %collective-permute-start.3 = (bf16[128,512]{1,0:T(8,128)(2,1)S(1)}, bf16[128,512]{1,0:T(8,128)(2,1)S(1)}, u32[]{:S(2)}, u32[]{:S(2)}) collective-permute-start(bf16[128,512]{1,0:T(8,128)(2,1)S(1)} %get-tuple-element.30), channel_id=1, source_target_pairs={{0,8},{8,16},{16,24},{24,0},{1,9},{9,17},{17,25},{25,1},{2,10},{10... | collective-permute-start | bytes 393224 | tf_op jit(solution)/shard_map/ppermute | solution.py:14
  35.1 11.5 %copy-start.1 = (bf16[1,512,512]{2,1,0:T(8,128)(2,1)S(1)}, bf16[1,512,512]{2,1,0:T(8,128)(2,1)}, u32[]{:S(2)}) copy-start(bf16[1,512,512]{2,1,0:T(8,128)(2,1)} %param.9) | copy-start | bytes 1572868
  35.1 11.5 %copy-start.2 = (f32[3,1,32,512]{3,2,1,0:T(8,128)S(1)}, f32[3,1,32,512]{3,2,1,0:T(8,128)}, u32[]{:S(2)}) copy-start(f32[3,1,32,512]{3,2,1,0:T(8,128)} %param.10) | copy-start | bytes 589828
  56.8 5.5 %collective-permute-start.8 = (bf16[128,512]{1,0:T(8,128)(2,1)S(1)}, bf16[128,512]{1,0:T(8,128)(2,1)S(1)}, u32[]{:S(2)}, u32[]{:S(2)}) collective-permute-start(bf16[128,512]{1,0:T(8,128)(2,1)S(1)} %get-tuple-element.24), channel_id=1, source_target_pairs={{0,24},{8,0},{16,8},{24,16},{1,25},{9,1},{17,9},{25,17},{2,26},{10... | collective-permute-start | bytes 393224 | tf_op jit(solution)/shard_map/ppermute | solution.py:14
  56.8 12.6 %collective-permute-start.7 = (bf16[128,512]{1,0:T(8,128)(2,1)S(1)}, bf16[128,512]{1,0:T(8,128)(2,1)S(1)}, u32[]{:S(2)}, u32[]{:S(2)}) collective-permute-start(bf16[128,512]{1,0:T(8,128)(2,1)S(1)} %get-tuple-element.25), channel_id=1, source_target_pairs={{0,16},{8,24},{16,0},{24,8},{1,17},{9,25},{17,1},{25,9},{2,18},{10... | collective-permute-start | bytes 393224 | tf_op jit(solution)/shard_map/ppermute | solution.py:14
  58.1 11.3 %collective-permute-start.6 = (bf16[128,512]{1,0:T(8,128)(2,1)S(1)}, bf16[128,512]{1,0:T(8,128)(2,1)S(1)}, u32[]{:S(2)}, u32[]{:S(2)}) collective-permute-start(bf16[128,512]{1,0:T(8,128)(2,1)S(1)} %get-tuple-element.26), channel_id=1, source_target_pairs={{0,8},{8,16},{16,24},{24,0},{1,9},{9,17},{17,25},{25,1},{2,10},{10... | collective-permute-start | bytes 393224 | tf_op jit(solution)/shard_map/ppermute | solution.py:14
  89.8 5.6 %collective-permute-start.11 = (bf16[128,512]{1,0:T(8,128)(2,1)S(1)}, bf16[128,512]{1,0:T(8,128)(2,1)S(1)}, u32[]{:S(2)}, u32[]{:S(2)}) collective-permute-start(bf16[128,512]{1,0:T(8,128)(2,1)S(1)} %get-tuple-element.20), channel_id=1, source_target_pairs={{0,24},{8,0},{16,8},{24,16},{1,25},{9,1},{17,9},{25,17},{2,26},{10... | collective-permute-start | bytes 393224 | tf_op jit(solution)/shard_map/ppermute | solution.py:14
  89.9 12.9 %collective-permute-start.10 = (bf16[128,512]{1,0:T(8,128)(2,1)S(1)}, bf16[128,512]{1,0:T(8,128)(2,1)S(1)}, u32[]{:S(2)}, u32[]{:S(2)}) collective-permute-start(bf16[128,512]{1,0:T(8,128)(2,1)S(1)} %get-tuple-element.21), channel_id=1, source_target_pairs={{0,16},{8,24},{16,0},{24,8},{1,17},{9,25},{17,1},{25,9},{2,18},{10... | collective-permute-start | bytes 393224 | tf_op jit(solution)/shard_map/ppermute | solution.py:14
  91.6 11.2 %collective-permute-start.9 = (bf16[128,512]{1,0:T(8,128)(2,1)S(1)}, bf16[128,512]{1,0:T(8,128)(2,1)S(1)}, u32[]{:S(2)}, u32[]{:S(2)}) collective-permute-start(bf16[128,512]{1,0:T(8,128)(2,1)S(1)} %get-tuple-element.22), channel_id=1, source_target_pairs={{0,8},{8,16},{16,24},{24,0},{1,9},{9,17},{17,25},{25,1},{2,10},{10... | collective-permute-start | bytes 393224 | tf_op jit(solution)/shard_map/ppermute | solution.py:14

commit v8 on v7

--- a/solution.py
+++ b/solution.py
@@ -75,8 +75,16 @@
                 from_far[:, block, None, None], far[block][None], 0
             )
             outgoing = term if outgoing is None else outgoing + term
+        half = EXCITE // 2
         received = [outgoing[0]] + [
-            shifted(outgoing[k], "group", groups, k) for k in range(1, groups)
+            jnp.concatenate(
+                [
+                    shifted(outgoing[k, :half], "group", groups, k),
+                    shifted(outgoing[k, half:], "group", groups, k),
+                ],
+                axis=0,
+            )
+            for k in range(1, groups)
         ]
         blocks_in = pick(received, source_shift)
         terms = jnp.einsum(

time: 114 us -> 118 us (1.035)
  starting transfers between devices: 21 us -> 32.1 us
  waiting for transfers between devices: 31.2 us -> 24.4 us
  blocking collectives: 48.5 us -> 47.3 us
    ppermute x12 -> x21, starting transfers between devices: 17.3 us -> 28.4 us  [shifted(): return lax.ppermute(x, axis, [(i, (i + k) % n) for i in range(n)])]
    ppermute x12 -> x21, waiting for transfers between devices: 26.8 us -> 20 us  [shifted(): return lax.ppermute(x, axis, [(i, (i + k) % n) for i in range(n)])]
    all_to_all x3, blocking collectives: 29.8 us -> 28.6 us  [body(): got = lax.all_to_all(sent, 'member', 0, 0, tiled=True)]
  transfers between devices with their start and end apart: 13 -> 22, of which waited for: 7 -> 7; matrix products, arithmetic and copies ran while one was open for 6% -> 6% of each run, Pallas kernels for 0% -> 0%
where the time goes in v8:
time: 118 us; the launch traced here: 117 us
  blocking collectives  47.3 us (40%)
  starting transfers between devices  32.1 us (27%)
  waiting for transfers between devices  24.4 us (21%)
  other arithmetic  7.76 us (7%)
  local copies, waits for them, and re-layouts  2.94 us (2%)
  matrix products  2.4 us (2%)
    all_to_all x3, blocking collectives, body(): got = lax.all_to_all(sent, 'member', 0, 0, tiled=True)  28.6 us
    ppermute x21, starting transfers between devices, shifted(): return lax.ppermute(x, axis, [(i, (i + k) % n) for i in range(n)])  28.4 us
    ppermute x21, waiting for transfers between devices, shifted(): return lax.ppermute(x, axis, [(i, (i + k) % n) for i in range(n)])  20 us
    all_to_all x2, blocking collectives, body(): got = lax.all_to_all(spread, 'member', 0, 0, tiled=True)  18.7 us
    all_to_all x1, waiting for transfers between devices, body(): hist_got = lax.all_to_all(spread_hist, 'member', 0, 0, tiled=True)  4.38 us
    all_to_all x1, starting transfers between devices, body(): hist_got = lax.all_to_all(spread_hist, 'member', 0, 0, tiled=True)  3.72 us
  transfers between devices with their start and end apart: 22, of which 7 were waited for; matrix products, arithmetic and copies ran while one was open for 6% of the time, Pallas kernels for 0%

profile of v8, /device:TPU:0, one launch (start us, length us, event | category | flops | bytes accessed | tf_op | source)
XLA Modules:
  0.0 117.3 jit_solution(6154510770883275629)
XLA Ops:
  0.0 3.0 %collective-permute-start = (s32[4,3]{1,0:T(4,128)}, s32[4,3]{1,0:T(4,128)S(1)}, u32[]{:S(2)}, u32[]{:S(2)}) collective-permute-start(s32[4,3]{1,0:T(4,128)} %param.7), channel_id=1, source_target_pairs={{0,8},{8,16},{16,24},{24,0},{1,9},{9,17},{17,25},{25,1},{2,10},{10... | collective-permute-start | bytes 152 | tf_op jit(solution)/shard_map/ppermute | solution.py:14
  3.0 2.1 %collective-permute-start.2 = (s32[4,3]{1,0:T(4,128)}, s32[4,3]{1,0:T(4,128)S(1)}, u32[]{:S(2)}, u32[]{:S(2)}) collective-permute-start(s32[4,3]{1,0:T(4,128)} %param.7), channel_id=1, source_target_pairs={{0,24},{8,0},{16,8},{24,16},{1,25},{9,1},{17,9},{25,17},{2,26},{10... | collective-permute-start | bytes 152 | tf_op jit(solution)/shard_map/ppermute | solution.py:14
  5.1 1.0 collective-permute-start.1
  6.1 1.7 %broadcast_in_dim.1161 = bf16[8,2,32,512]{3,2,1,0:T(8,128)(2,1)} broadcast(bf16[2,32,512]{2,1,0:T(8,128)(2,1)} %bitcast.304), dimensions={1,2,3} | broadcast | bytes 589824 | tf_op jit(solution)/shard_map/broadcast_in_dim | solution.py:62
  7.7 3.7 %all-to-all-start = ((bf16[8,2,32,512]{3,2,1,0:T(8,128)(2,1)}), bf16[8,2,32,512]{3,2,1,0:T(8,128)(2,1)S(1)}, u32[]{:S(2)}, u32[]{:S(2)}) async-start(bf16[8,2,32,512]{3,2,1,0:T(8,128)(2,1)} %broadcast_in_dim.1161), calls=%async_computation | async-start | bytes 1048576 | tf_op jit(solution)/shard_map/all_to_all | solution.py:63
  11.5 0.9 fusion.74
  12.5 0.8 select_reduce_fusion.6
  13.9 1.0 slice_reduce_fusion.2
  16.8 4.4 %all-to-all-done = bf16[8,2,32,512]{3,2,1,0:T(8,128)(2,1)S(1)} async-done(((bf16[8,2,32,512]{3,2,1,0:T(8,128)(2,1)}), bf16[8,2,32,512]{3,2,1,0:T(8,128)(2,1)S(1)}, u32[]{:S(2)}, u32[]{:S(2)}) %all-to-all-start) | async-done | bytes 524320 | tf_op jit(solution)/shard_map/all_to_all | solution.py:63
  22.1 1.4 %collective-permute-start.8 = (bf16[64,512]{1,0:T(8,128)(2,1)S(1)}, bf16[64,512]{1,0:T(8,128)(2,1)S(1)}, u32[]{:S(2)}, u32[]{:S(2)}) collective-permute-start(bf16[64,512]{1,0:T(8,128)(2,1)S(1)} %get-tuple-element.32), channel_id=1, source_target_pairs={{0,24},{8,0},{16,8},{24,16},{1,25},{9,1},{17,9},{25,17},{2,26},{10... | collective-permute-start | bytes 196616 | tf_op jit(solution)/shard_map/ppermute | solution.py:14
  23.5 2.2 %collective-permute-start.7 = (bf16[64,512]{1,0:T(8,128)(2,1)S(1)}, bf16[64,512]{1,0:T(8,128)(2,1)S(1)}, u32[]{:S(2)}, u32[]{:S(2)}) collective-permute-start(bf16[64,512]{1,0:T(8,128)(2,1)S(1)} %get-tuple-element.33), channel_id=1, source_target_pairs={{0,24},{8,0},{16,8},{24,16},{1,25},{9,1},{17,9},{25,17},{2,26},{10... | collective-permute-start | bytes 196616 | tf_op jit(solution)/shard_map/ppermute | solution.py:14
  25.8 1.5 %collective-permute-start.6 = (bf16[64,512]{1,0:T(8,128)(2,1)S(1)}, bf16[64,512]{1,0:T(8,128)(2,1)S(1)}, u32[]{:S(2)}, u32[]{:S(2)}) collective-permute-start(bf16[64,512]{1,0:T(8,128)(2,1)S(1)} %get-tuple-element.34), channel_id=1, source_target_pairs={{0,16},{8,24},{16,0},{24,8},{1,17},{9,25},{17,1},{25,9},{2,18},{10... | collective-permute-start | bytes 196616 | tf_op jit(solution)/shard_map/ppermute | solution.py:14
  27.3 1.5 %collective-permute-start.5 = (bf16[64,512]{1,0:T(8,128)(2,1)S(1)}, bf16[64,512]{1,0:T(8,128)(2,1)S(1)}, u32[]{:S(2)}, u32[]{:S(2)}) collective-permute-start(bf16[64,512]{1,0:T(8,128)(2,1)S(1)} %get-tuple-element.35), channel_id=1, source_target_pairs={{0,16},{8,24},{16,0},{24,8},{1,17},{9,25},{17,1},{25,9},{2,18},{10... | collective-permute-start | bytes 196616 | tf_op jit(solution)/shard_map/ppermute | solution.py:14
  28.8 1.4 %collective-permute-start.4 = (bf16[64,512]{1,0:T(8,128)(2,1)S(1)}, bf16[64,512]{1,0:T(8,128)(2,1)S(1)}, u32[]{:S(2)}, u32[]{:S(2)}) collective-permute-start(bf16[64,512]{1,0:T(8,128)(2,1)S(1)} %get-tuple-element.36), channel_id=1, source_target_pairs={{0,8},{8,16},{16,24},{24,0},{1,9},{9,17},{17,25},{25,1},{2,10},{10... | collective-permute-start | bytes 196616 | tf_op jit(solution)/shard_map/ppermute | solution.py:14
  30.2 3.8 %collective-permute-done.6 = bf16[64,512]{1,0:T(8,128)(2,1)S(1)} collective-permute-done((bf16[64,512]{1,0:T(8,128)(2,1)S(1)}, bf16[64,512]{1,0:T(8,128)(2,1)S(1)}, u32[]{:S(2)}, u32[]{:S(2)}) %collective-permute-start.6) | collective-permute-done | bytes 65568 | tf_op jit(solution)/shard_map/ppermute | solution.py:14
  34.0 2.1 %collective-permute-done.5 = bf16[64,512]{1,0:T(8,128)(2,1)S(1)} collective-permute-done((bf16[64,512]{1,0:T(8,128)(2,1)S(1)}, bf16[64,512]{1,0:T(8,128)(2,1)S(1)}, u32[]{:S(2)}, u32[]{:S(2)}) %collective-permute-start.5) | collective-permute-done | bytes 65568 | tf_op jit(solution)/shard_map/ppermute | solution.py:14
  37.2 9.9 %all_to_all.30 = bf16[8,32,512]{2,1,0:T(8,128)(2,1)S(1)} all-to-all(bf16[8,32,512]{2,1,0:T(8,128)(2,1)S(1)} %select_add_fusion.5), channel_id=1, replica_groups=mesh['group'=4,'member'=8] {'member'}, dimensions={0} | all-to-all | bytes 524288 | tf_op jit(solution)/shard_map/all_to_all | solution.py:101
  47.3 9.3 %all_to_all.31 = bf16[8,32,512]{2,1,0:T(8,128)(2,1)S(1)} all-to-all(bf16[8,32,512]{2,1,0:T(8,128)(2,1)S(1)} %broadcast_in_dim.1253), channel_id=1, replica_groups=mesh['group'=4,'member'=8] {'member'}, dimensions={0} | all-to-all | bytes 524288 | tf_op jit(solution)/shard_map/all_to_all | solution.py:108
  57.2 1.1 collective-permute-start.14
  58.3 1.3 %collective-permute-start.13 = (bf16[64,512]{1,0:T(8,128)(2,1)S(1)}, bf16[64,512]{1,0:T(8,128)(2,1)S(1)}, u32[]{:S(2)}, u32[]{:S(2)}) collective-permute-start(bf16[64,512]{1,0:T(8,128)(2,1)S(1)} %get-tuple-element.27), channel_id=1, source_target_pairs={{0,24},{8,0},{16,8},{24,16},{1,25},{9,1},{17,9},{25,17},{2,26},{10... | collective-permute-start | bytes 196616 | tf_op jit(solution)/shard_map/ppermute | solution.py:14
  59.6 0.8 collective-permute-start.9
  60.9 2.4 %collective-permute-start.11 = (bf16[64,512]{1,0:T(8,128)(2,1)S(1)}, bf16[64,512]{1,0:T(8,128)(2,1)S(1)}, u32[]{:S(2)}, u32[]{:S(2)}) collective-permute-start(bf16[64,512]{1,0:T(8,128)(2,1)S(1)} %get-tuple-element.29), channel_id=1, source_target_pairs={{0,16},{8,24},{16,0},{24,8},{1,17},{9,25},{17,1},{25,9},{2,18},{10... | collective-permute-start | bytes 196616 | tf_op jit(solution)/shard_map/ppermute | solution.py:14
  63.3 1.0 collective-permute-start.10
  64.3 6.3 %collective-permute-done.12 = bf16[64,512]{1,0:T(8,128)(2,1)S(1)} collective-permute-done((bf16[64,512]{1,0:T(8,128)(2,1)S(1)}, bf16[64,512]{1,0:T(8,128)(2,1)S(1)}, u32[]{:S(2)}, u32[]{:S(2)}) %collective-permute-start.12) | collective-permute-done | bytes 65568 | tf_op jit(solution)/shard_map/ppermute | solution.py:14
  72.3 9.3 %all_to_all.32 = bf16[8,32,512]{2,1,0:T(8,128)(2,1)S(1)} all-to-all(bf16[8,32,512]{2,1,0:T(8,128)(2,1)S(1)} %select_add_fusion.3), channel_id=1, replica_groups=mesh['group'=4,'member'=8] {'member'}, dimensions={0} | all-to-all | bytes 524288 | tf_op jit(solution)/shard_map/all_to_all | solution.py:101
  81.9 9.3 %all_to_all.33 = bf16[8,32,512]{2,1,0:T(8,128)(2,1)S(1)} all-to-all(bf16[8,32,512]{2,1,0:T(8,128)(2,1)S(1)} %broadcast_in_dim.1302), channel_id=1, replica_groups=mesh['group'=4,'member'=8] {'member'}, dimensions={0} | all-to-all | bytes 524288 | tf_op jit(solution)/shard_map/all_to_all | solution.py:108
  91.9 1.4 %collective-permute-start.20 = (bf16[64,512]{1,0:T(8,128)(2,1)S(1)}, bf16[64,512]{1,0:T(8,128)(2,1)S(1)}, u32[]{:S(2)}, u32[]{:S(2)}) collective-permute-start(bf16[64,512]{1,0:T(8,128)(2,1)S(1)} %get-tuple-element.20), channel_id=1, source_target_pairs={{0,24},{8,0},{16,8},{24,16},{1,25},{9,1},{17,9},{25,17},{2,26},{10... | collective-permute-start | bytes 196616 | tf_op jit(solution)/shard_map/ppermute | solution.py:14
  93.3 1.2 %collective-permute-start.19 = (bf16[64,512]{1,0:T(8,128)(2,1)S(1)}, bf16[64,512]{1,0:T(8,128)(2,1)S(1)}, u32[]{:S(2)}, u32[]{:S(2)}) collective-permute-start(bf16[64,512]{1,0:T(8,128)(2,1)S(1)} %get-tuple-element.21), channel_id=1, source_target_pairs={{0,24},{8,0},{16,8},{24,16},{1,25},{9,1},{17,9},{25,17},{2,26},{10... | collective-permute-start | bytes 196616 | tf_op jit(solution)/shard_map/ppermute | solution.py:14
  94.5 0.8 collective-permute-start.15
  95.5 2.8 %collective-permute-start.17 = (bf16[64,512]{1,0:T(8,128)(2,1)S(1)}, bf16[64,512]{1,0:T(8,128)(2,1)S(1)}, u32[]{:S(2)}, u32[]{:S(2)}) collective-permute-start(bf16[64,512]{1,0:T(8,128)(2,1)S(1)} %get-tuple-element.23), channel_id=1, source_target_pairs={{0,16},{8,24},{16,0},{24,8},{1,17},{9,25},{17,1},{25,9},{2,18},{10... | collective-permute-start | bytes 196616 | tf_op jit(solution)/shard_map/ppermute | solution.py:14
  99.0 6.3 %collective-permute-done.18 = bf16[64,512]{1,0:T(8,128)(2,1)S(1)} collective-permute-done((bf16[64,512]{1,0:T(8,128)(2,1)S(1)}, bf16[64,512]{1,0:T(8,128)(2,1)S(1)}, u32[]{:S(2)}, u32[]{:S(2)}) %collective-permute-start.18) | collective-permute-done | bytes 65568 | tf_op jit(solution)/shard_map/ppermute | solution.py:14
  107.0 9.3 %all_to_all.34 = bf16[8,32,512]{2,1,0:T(8,128)(2,1)S(1)} all-to-all(bf16[8,32,512]{2,1,0:T(8,128)(2,1)S(1)} %select_add_fusion.1), channel_id=1, replica_groups=mesh['group'=4,'member'=8] {'member'}, dimensions={0} | all-to-all | bytes 524288 | tf_op jit(solution)/shard_map/all_to_all | solution.py:101
  (94 shorter events, 11.7 us)
Async XLA Ops:
  0.0 36.2 %copy-start = (bf16[4,512,512]{2,1,0:T(8,128)(2,1)S(1)}, bf16[4,512,512]{2,1,0:T(8,128)(2,1)}, u32[]{:S(2)}) copy-start(bf16[4,512,512]{2,1,0:T(8,128)(2,1)} %param.6) | copy-start | bytes 6291460
  0.0 15.0 %collective-permute-start = (s32[4,3]{1,0:T(4,128)}, s32[4,3]{1,0:T(4,128)S(1)}, u32[]{:S(2)}, u32[]{:S(2)}) collective-permute-start(s32[4,3]{1,0:T(4,128)} %param.7), channel_id=1, source_target_pairs={{0,8},{8,16},{16,24},{24,0},{1,9},{9,17},{17,25},{25,1},{2,10},{10... | collective-permute-start | bytes 152 | tf_op jit(solution)/shard_map/ppermute | solution.py:14
  3.0 12.0 %collective-permute-start.2 = (s32[4,3]{1,0:T(4,128)}, s32[4,3]{1,0:T(4,128)S(1)}, u32[]{:S(2)}, u32[]{:S(2)}) collective-permute-start(s32[4,3]{1,0:T(4,128)} %param.7), channel_id=1, source_target_pairs={{0,24},{8,0},{16,8},{24,16},{1,25},{9,1},{17,9},{25,17},{2,26},{10... | collective-permute-start | bytes 152 | tf_op jit(solution)/shard_map/ppermute | solution.py:14
  5.1 9.9 %collective-permute-start.1 = (s32[4,3]{1,0:T(4,128)}, s32[4,3]{1,0:T(4,128)S(1)}, u32[]{:S(2)}, u32[]{:S(2)}) collective-permute-start(s32[4,3]{1,0:T(4,128)} %param.7), channel_id=1, source_target_pairs={{0,16},{8,24},{16,0},{24,8},{1,17},{9,25},{17,1},{25,9},{2,18},{10... | collective-permute-start | bytes 152 | tf_op jit(solution)/shard_map/ppermute | solution.py:14
  7.7 13.5 %all-to-all-start = ((bf16[8,2,32,512]{3,2,1,0:T(8,128)(2,1)}), bf16[8,2,32,512]{3,2,1,0:T(8,128)(2,1)S(1)}, u32[]{:S(2)}, u32[]{:S(2)}) async-start(bf16[8,2,32,512]{3,2,1,0:T(8,128)(2,1)} %broadcast_in_dim.1161), calls=%async_computation | async-start | bytes 1048576 | tf_op jit(solution)/shard_map/all_to_all | solution.py:63
  22.1 6.7 %collective-permute-start.8 = (bf16[64,512]{1,0:T(8,128)(2,1)S(1)}, bf16[64,512]{1,0:T(8,128)(2,1)S(1)}, u32[]{:S(2)}, u32[]{:S(2)}) collective-permute-start(bf16[64,512]{1,0:T(8,128)(2,1)S(1)} %get-tuple-element.32), channel_id=1, source_target_pairs={{0,24},{8,0},{16,8},{24,16},{1,25},{9,1},{17,9},{25,17},{2,26},{10... | collective-permute-start | bytes 196616 | tf_op jit(solution)/shard_map/ppermute | solution.py:14
  23.5 6.7 %collective-permute-start.7 = (bf16[64,512]{1,0:T(8,128)(2,1)S(1)}, bf16[64,512]{1,0:T(8,128)(2,1)S(1)}, u32[]{:S(2)}, u32[]{:S(2)}) collective-permute-start(bf16[64,512]{1,0:T(8,128)(2,1)S(1)} %get-tuple-element.33), channel_id=1, source_target_pairs={{0,24},{8,0},{16,8},{24,16},{1,25},{9,1},{17,9},{25,17},{2,26},{10... | collective-permute-start | bytes 196616 | tf_op jit(solution)/shard_map/ppermute | solution.py:14
  25.8 10.4 %collective-permute-start.3 = (bf16[64,512]{1,0:T(8,128)(2,1)S(1)}, bf16[64,512]{1,0:T(8,128)(2,1)S(1)}, u32[]{:S(2)}, u32[]{:S(2)}) collective-permute-start(bf16[64,512]{1,0:T(8,128)(2,1)S(1)} %get-tuple-element.31), channel_id=1, source_target_pairs={{0,8},{8,16},{16,24},{24,0},{1,9},{9,17},{17,25},{25,1},{2,10},{10... | collective-permute-start | bytes 196616 | tf_op jit(solution)/shard_map/ppermute | solution.py:14
  25.8 8.2 %collective-permute-start.6 = (bf16[64,512]{1,0:T(8,128)(2,1)S(1)}, bf16[64,512]{1,0:T(8,128)(2,1)S(1)}, u32[]{:S(2)}, u32[]{:S(2)}) collective-permute-start(bf16[64,512]{1,0:T(8,128)(2,1)S(1)} %get-tuple-element.34), channel_id=1, source_target_pairs={{0,16},{8,24},{16,0},{24,8},{1,17},{9,25},{17,1},{25,9},{2,18},{10... | collective-permute-start | bytes 196616 | tf_op jit(solution)/shard_map/ppermute | solution.py:14
  27.3 8.9 %collective-permute-start.5 = (bf16[64,512]{1,0:T(8,128)(2,1)S(1)}, bf16[64,512]{1,0:T(8,128)(2,1)S(1)}, u32[]{:S(2)}, u32[]{:S(2)}) collective-permute-start(bf16[64,512]{1,0:T(8,128)(2,1)S(1)} %get-tuple-element.35), channel_id=1, source_target_pairs={{0,16},{8,24},{16,0},{24,8},{1,17},{9,25},{17,1},{25,9},{2,18},{10... | collective-permute-start | bytes 196616 | tf_op jit(solution)/shard_map/ppermute | solution.py:14
  28.8 7.3 %collective-permute-start.4 = (bf16[64,512]{1,0:T(8,128)(2,1)S(1)}, bf16[64,512]{1,0:T(8,128)(2,1)S(1)}, u32[]{:S(2)}, u32[]{:S(2)}) collective-permute-start(bf16[64,512]{1,0:T(8,128)(2,1)S(1)} %get-tuple-element.36), channel_id=1, source_target_pairs={{0,8},{8,16},{16,24},{24,0},{1,9},{9,17},{17,25},{25,1},{2,10},{10... | collective-permute-start | bytes 196616 | tf_op jit(solution)/shard_map/ppermute | solution.py:14
  36.8 10.2 %copy-start.1 = (bf16[1,512,512]{2,1,0:T(8,128)(2,1)S(1)}, bf16[1,512,512]{2,1,0:T(8,128)(2,1)}, u32[]{:S(2)}) copy-start(bf16[1,512,512]{2,1,0:T(8,128)(2,1)} %param.9) | copy-start | bytes 1572868
  36.8 10.2 %copy-start.2 = (f32[3,1,32,512]{3,2,1,0:T(8,128)S(1)}, f32[3,1,32,512]{3,2,1,0:T(8,128)}, u32[]{:S(2)}) copy-start(f32[3,1,32,512]{3,2,1,0:T(8,128)} %param.10) | copy-start | bytes 589828
  57.2 6.1 %collective-permute-start.14 = (bf16[64,512]{1,0:T(8,128)(2,1)S(1)}, bf16[64,512]{1,0:T(8,128)(2,1)S(1)}, u32[]{:S(2)}, u32[]{:S(2)}) collective-permute-start(bf16[64,512]{1,0:T(8,128)(2,1)S(1)} %get-tuple-element.26), channel_id=1, source_target_pairs={{0,24},{8,0},{16,8},{24,16},{1,25},{9,1},{17,9},{25,17},{2,26},{10... | collective-permute-start | bytes 196616 | tf_op jit(solution)/shard_map/ppermute | solution.py:14
  58.3 6.0 %collective-permute-start.13 = (bf16[64,512]{1,0:T(8,128)(2,1)S(1)}, bf16[64,512]{1,0:T(8,128)(2,1)S(1)}, u32[]{:S(2)}, u32[]{:S(2)}) collective-permute-start(bf16[64,512]{1,0:T(8,128)(2,1)S(1)} %get-tuple-element.27), channel_id=1, source_target_pairs={{0,24},{8,0},{16,8},{24,16},{1,25},{9,1},{17,9},{25,17},{2,26},{10... | collective-permute-start | bytes 196616 | tf_op jit(solution)/shard_map/ppermute | solution.py:14
  59.6 11.8 %collective-permute-start.9 = (bf16[64,512]{1,0:T(8,128)(2,1)S(1)}, bf16[64,512]{1,0:T(8,128)(2,1)S(1)}, u32[]{:S(2)}, u32[]{:S(2)}) collective-permute-start(bf16[64,512]{1,0:T(8,128)(2,1)S(1)} %get-tuple-element.25), channel_id=1, source_target_pairs={{0,8},{8,16},{16,24},{24,0},{1,9},{9,17},{17,25},{25,1},{2,10},{10... | collective-permute-start | bytes 196616 | tf_op jit(solution)/shard_map/ppermute | solution.py:14
  60.4 10.3 %collective-permute-start.12 = (bf16[64,512]{1,0:T(8,128)(2,1)S(1)}, bf16[64,512]{1,0:T(8,128)(2,1)S(1)}, u32[]{:S(2)}, u32[]{:S(2)}) collective-permute-start(bf16[64,512]{1,0:T(8,128)(2,1)S(1)} %get-tuple-element.28), channel_id=1, source_target_pairs={{0,16},{8,24},{16,0},{24,8},{1,17},{9,25},{17,1},{25,9},{2,18},{10... | collective-permute-start | bytes 196616 | tf_op jit(solution)/shard_map/ppermute | solution.py:14
  60.9 10.4 %collective-permute-start.11 = (bf16[64,512]{1,0:T(8,128)(2,1)S(1)}, bf16[64,512]{1,0:T(8,128)(2,1)S(1)}, u32[]{:S(2)}, u32[]{:S(2)}) collective-permute-start(bf16[64,512]{1,0:T(8,128)(2,1)S(1)} %get-tuple-element.29), channel_id=1, source_target_pairs={{0,16},{8,24},{16,0},{24,8},{1,17},{9,25},{17,1},{25,9},{2,18},{10... | collective-permute-start | bytes 196616 | tf_op jit(solution)/shard_map/ppermute | solution.py:14
  63.3 8.1 %collective-permute-start.10 = (bf16[64,512]{1,0:T(8,128)(2,1)S(1)}, bf16[64,512]{1,0:T(8,128)(2,1)S(1)}, u32[]{:S(2)}, u32[]{:S(2)}) collective-permute-start(bf16[64,512]{1,0:T(8,128)(2,1)S(1)} %get-tuple-element.30), channel_id=1, source_target_pairs={{0,8},{8,16},{16,24},{24,0},{1,9},{9,17},{17,25},{25,1},{2,10},{10... | collective-permute-start | bytes 196616 | tf_op jit(solution)/shard_map/ppermute | solution.py:14
  91.9 6.4 %collective-permute-start.20 = (bf16[64,512]{1,0:T(8,128)(2,1)S(1)}, bf16[64,512]{1,0:T(8,128)(2,1)S(1)}, u32[]{:S(2)}, u32[]{:S(2)}) collective-permute-start(bf16[64,512]{1,0:T(8,128)(2,1)S(1)} %get-tuple-element.20), channel_id=1, source_target_pairs={{0,24},{8,0},{16,8},{24,16},{1,25},{9,1},{17,9},{25,17},{2,26},{10... | collective-permute-start | bytes 196616 | tf_op jit(solution)/shard_map/ppermute | solution.py:14
  93.3 5.7 %collective-permute-start.19 = (bf16[64,512]{1,0:T(8,128)(2,1)S(1)}, bf16[64,512]{1,0:T(8,128)(2,1)S(1)}, u32[]{:S(2)}, u32[]{:S(2)}) collective-permute-start(bf16[64,512]{1,0:T(8,128)(2,1)S(1)} %get-tuple-element.21), channel_id=1, source_target_pairs={{0,24},{8,0},{16,8},{24,16},{1,25},{9,1},{17,9},{25,17},{2,26},{10... | collective-permute-start | bytes 196616 | tf_op jit(solution)/shard_map/ppermute | solution.py:14
  94.5 11.5 %collective-permute-start.15 = (bf16[64,512]{1,0:T(8,128)(2,1)S(1)}, bf16[64,512]{1,0:T(8,128)(2,1)S(1)}, u32[]{:S(2)}, u32[]{:S(2)}) collective-permute-start(bf16[64,512]{1,0:T(8,128)(2,1)S(1)} %get-tuple-element.19), channel_id=1, source_target_pairs={{0,8},{8,16},{16,24},{24,0},{1,9},{9,17},{17,25},{25,1},{2,10},{10... | collective-permute-start | bytes 196616 | tf_op jit(solution)/shard_map/ppermute | solution.py:14
  95.4 10.0 %collective-permute-start.18 = (bf16[64,512]{1,0:T(8,128)(2,1)S(1)}, bf16[64,512]{1,0:T(8,128)(2,1)S(1)}, u32[]{:S(2)}, u32[]{:S(2)}) collective-permute-start(bf16[64,512]{1,0:T(8,128)(2,1)S(1)} %get-tuple-element.22), channel_id=1, source_target_pairs={{0,16},{8,24},{16,0},{24,8},{1,17},{9,25},{17,1},{25,9},{2,18},{10... | collective-permute-start | bytes 196616 | tf_op jit(solution)/shard_map/ppermute | solution.py:14
  95.5 10.5 %collective-permute-start.17 = (bf16[64,512]{1,0:T(8,128)(2,1)S(1)}, bf16[64,512]{1,0:T(8,128)(2,1)S(1)}, u32[]{:S(2)}, u32[]{:S(2)}) collective-permute-start(bf16[64,512]{1,0:T(8,128)(2,1)S(1)} %get-tuple-element.23), channel_id=1, source_target_pairs={{0,16},{8,24},{16,0},{24,8},{1,17},{9,25},{17,1},{25,9},{2,18},{10... | collective-permute-start | bytes 196616 | tf_op jit(solution)/shard_map/ppermute | solution.py:14
  98.3 7.8 %collective-permute-start.16 = (bf16[64,512]{1,0:T(8,128)(2,1)S(1)}, bf16[64,512]{1,0:T(8,128)(2,1)S(1)}, u32[]{:S(2)}, u32[]{:S(2)}) collective-permute-start(bf16[64,512]{1,0:T(8,128)(2,1)S(1)} %get-tuple-element.24), channel_id=1, source_target_pairs={{0,8},{8,16},{16,24},{24,0},{1,9},{9,17},{17,25},{25,1},{2,10},{10... | collective-permute-start | bytes 196616 | tf_op jit(solution)/shard_map/ppermute | solution.py:14

commit v9 on v7

--- a/solution.py
+++ b/solution.py
@@ -59,8 +59,7 @@
     delays_here = tile_lists[:, 2]
     source_shift = (group_here - source_group) % groups
 
-    spread_hist = jnp.broadcast_to(history[:, 0][None], (members,) + history[:, 0].shape)
-    hist_got = lax.all_to_all(spread_hist, "member", 0, 0, tiled=True)
+    hist_got = lax.all_gather(history[:, 0], "member", axis=0, tiled=False)
     hist_placed = pick([hist_got[m] for m in range(members)], owners)
     blocks = [
         hist_placed[:, t].reshape(group_blocks, EXCITE, BLOCK) for t in range(DELAYS)
@@ -96,8 +95,7 @@
         current = jnp.dot(residual, inverses[0], preferred_element_type=jnp.float32)
         results.append(current)
         if step + 1 < STEPS:
-            spread = jnp.broadcast_to(current.astype(jnp.bfloat16)[None], (members, share, BLOCK))
-            got = lax.all_to_all(spread, "member", 0, 0, tiled=True)
+            got = lax.all_gather(current.astype(jnp.bfloat16), "member", axis=0, tiled=False)
             placed = pick([got[m] for m in range(members)], owners)
             blocks.append(placed.reshape(group_blocks, EXCITE, BLOCK))
     return jnp.stack(results)[:, None]

time: 114 us -> 116 us (1.018)
  blocking collectives: 48.5 us -> 55.3 us
  starting transfers between devices: 21 us -> 17.3 us
  local copies, waits for them, and re-layouts: 2.94 us -> 1.2 us
    all_gather x0 -> x3, blocking collectives: none -> 26.9 us  [the longest x2 16.7 us: body(): lax.all_gather(current.astype(jnp.bfloat16), 'member', axis=0, tiled=False)]
    all_to_all x2 -> x0, blocking collectives: 18.7 us -> none  [body(): got = lax.all_to_all(spread, 'member', 0, 0, tiled=True)]
    ppermute x12, waiting for transfers between devices: 26.8 us -> 31.9 us  [shifted(): return lax.ppermute(x, axis, [(i, (i + k) % n) for i in range(n)])]
    all_to_all x1 -> x0, waiting for transfers between devices: 4.4 us -> none  [body(): hist_got = lax.all_to_all(spread_hist, 'member', 0, 0, tiled=True)]
    all_to_all x1 -> x0, starting transfers between devices: 3.72 us -> none  [body(): hist_got = lax.all_to_all(spread_hist, 'member', 0, 0, tiled=True)]
    broadcast_in_dim x3 -> x0, local copies, waits for them, and re-layouts: 1.74 us -> none  [the longest x1 1.68 us: body(): jnp.broadcast_to(history[:, 0][None], (members,) + history[:, 0].shape)]
    all_to_all x3, blocking collectives: 29.8 us -> 28.4 us  [body(): got = lax.all_to_all(sent, 'member', 0, 0, tiled=True)]
  transfers between devices with their start and end apart: 13 -> 12, of which waited for: 7 -> 6; matrix products, arithmetic and copies ran while one was open for 6% -> 4% of each run, Pallas kernels for 0% -> 0%
where the time goes in v9:
time: 116 us; the launch traced here: 115 us
  blocking collectives  55.3 us (48%)
  waiting for transfers between devices  31.9 us (28%)
  starting transfers between devices  17.3 us (15%)
  other arithmetic  7.02 us (6%)
  matrix products  2.3 us (2%)
  local copies, waits for them, and re-layouts  1.2 us (1%)
    ppermute x12, waiting for transfers between devices, shifted(): return lax.ppermute(x, axis, [(i, (i + k) % n) for i in range(n)])  31.9 us
    all_to_all x3, blocking collectives, body(): got = lax.all_to_all(sent, 'member', 0, 0, tiled=True)  28.4 us
    ppermute x12, starting transfers between devices, shifted(): return lax.ppermute(x, axis, [(i, (i + k) % n) for i in range(n)])  17.3 us
    all_gather x2, blocking collectives, body(): lax.all_gather(current.astype(jnp.bfloat16), 'member', axis=0, tiled=False)  16.7 us
    all_gather x1, blocking collectives, body(): hist_got = lax.all_gather(history[:, 0], 'member', axis=0, tiled=False)  10.2 us
  transfers between devices with their start and end apart: 12, of which 6 were waited for; matrix products, arithmetic and copies ran while one was open for 4% of the time, Pallas kernels for 0%

profile of v9, /device:TPU:0, one launch (start us, length us, event | category | flops | bytes accessed | tf_op | source)
XLA Modules:
  0.0 115.4 jit_solution(3526462575469569766)
XLA Ops:
  0.0 3.0 %collective-permute-start = (s32[4,3]{1,0:T(4,128)}, s32[4,3]{1,0:T(4,128)S(1)}, u32[]{:S(2)}, u32[]{:S(2)}) collective-permute-start(s32[4,3]{1,0:T(4,128)} %param.7), channel_id=1, source_target_pairs={{0,8},{8,16},{16,24},{24,0},{1,9},{9,17},{17,25},{25,1},{2,10},{10... | collective-permute-start | bytes 152 | tf_op jit(solution)/shard_map/ppermute | solution.py:14
  3.0 2.1 %collective-permute-start.2 = (s32[4,3]{1,0:T(4,128)}, s32[4,3]{1,0:T(4,128)S(1)}, u32[]{:S(2)}, u32[]{:S(2)}) collective-permute-start(s32[4,3]{1,0:T(4,128)} %param.7), channel_id=1, source_target_pairs={{0,24},{8,0},{16,8},{24,16},{1,25},{9,1},{17,9},{25,17},{2,26},{10... | collective-permute-start | bytes 152 | tf_op jit(solution)/shard_map/ppermute | solution.py:14
  5.1 0.9 collective-permute-start.1
  6.1 0.9 fusion.74
  7.1 0.8 select_reduce_fusion.6
  7.9 0.7 iota_compare_fusion.1
  8.6 1.0 slice_reduce_fusion.2
  9.6 10.2 %all-gather = bf16[16,1,32,512]{3,2,1,0:T(8,128)(2,1)S(1)} all-gather(bf16[2,1,32,512]{3,2,1,0:T(8,128)(2,1)} %param.11), channel_id=2, replica_groups=mesh['group'=4,'member'=8] {'member'}, dimensions={0}, use_global_device_ids=true | all-gather | bytes 589824 | tf_op jit(solution)/shard_map/all_gather | solution.py:62
  19.8 0.5 select_add_fusion
  20.4 0.6 gather_fusion
  21.8 1.4 %collective-permute-start.5 = (bf16[128,512]{1,0:T(8,128)(2,1)S(1)}, bf16[128,512]{1,0:T(8,128)(2,1)S(1)}, u32[]{:S(2)}, u32[]{:S(2)}) collective-permute-start(bf16[128,512]{1,0:T(8,128)(2,1)S(1)} %get-tuple-element.28), channel_id=1, source_target_pairs={{0,24},{8,0},{16,8},{24,16},{1,25},{9,1},{17,9},{25,17},{2,26},{10... | collective-permute-start | bytes 393224 | tf_op jit(solution)/shard_map/ppermute | solution.py:14
  23.2 1.7 %collective-permute-start.4 = (bf16[128,512]{1,0:T(8,128)(2,1)S(1)}, bf16[128,512]{1,0:T(8,128)(2,1)S(1)}, u32[]{:S(2)}, u32[]{:S(2)}) collective-permute-start(bf16[128,512]{1,0:T(8,128)(2,1)S(1)} %get-tuple-element.29), channel_id=1, source_target_pairs={{0,16},{8,24},{16,0},{24,8},{1,17},{9,25},{17,1},{25,9},{2,18},{10... | collective-permute-start | bytes 393224 | tf_op jit(solution)/shard_map/ppermute | solution.py:14
  24.9 1.1 collective-permute-start.3
  26.0 1.6 %collective-permute-done.5 = bf16[128,512]{1,0:T(8,128)(2,1)S(1)} collective-permute-done((bf16[128,512]{1,0:T(8,128)(2,1)S(1)}, bf16[128,512]{1,0:T(8,128)(2,1)S(1)}, u32[]{:S(2)}, u32[]{:S(2)}) %collective-permute-start.5) | collective-permute-done | bytes 131104 | tf_op jit(solution)/shard_map/ppermute | solution.py:14
  27.6 9.4 %collective-permute-done.4 = bf16[128,512]{1,0:T(8,128)(2,1)S(1)} collective-permute-done((bf16[128,512]{1,0:T(8,128)(2,1)S(1)}, bf16[128,512]{1,0:T(8,128)(2,1)S(1)}, u32[]{:S(2)}, u32[]{:S(2)}) %collective-permute-start.4) | collective-permute-done | bytes 131104 | tf_op jit(solution)/shard_map/ppermute | solution.py:14
  37.1 0.6 select_reduce_fusion.5
  38.0 9.5 %all_to_all.15 = bf16[8,32,512]{2,1,0:T(8,128)(2,1)S(1)} all-to-all(bf16[8,32,512]{2,1,0:T(8,128)(2,1)S(1)} %select_add_fusion.5), channel_id=1, replica_groups=mesh['group'=4,'member'=8] {'member'}, dimensions={0} | all-to-all | bytes 524288 | tf_op jit(solution)/shard_map/all_to_all | solution.py:92
  47.7 8.4 %all-gather.1 = bf16[256,512]{1,0:T(8,128)(2,1)S(1)} all-gather(bf16[32,512]{1,0:T(8,128)(2,1)S(1)} %get-tuple-element.115), channel_id=3, replica_groups=mesh['group'=4,'member'=8] {'member'}, dimensions={0}, use_global_device_ids=true | all-gather | bytes 294912 | tf_op jit(solution)/shard_map/all_gather | solution.py:98
  56.7 1.3 %collective-permute-start.7 = (bf16[128,512]{1,0:T(8,128)(2,1)S(1)}, bf16[128,512]{1,0:T(8,128)(2,1)S(1)}, u32[]{:S(2)}, u32[]{:S(2)}) collective-permute-start(bf16[128,512]{1,0:T(8,128)(2,1)S(1)} %get-tuple-element.25), channel_id=1, source_target_pairs={{0,16},{8,24},{16,0},{24,8},{1,17},{9,25},{17,1},{25,9},{2,18},{10... | collective-permute-start | bytes 393224 | tf_op jit(solution)/shard_map/ppermute | solution.py:14
  58.0 1.9 %collective-permute-start.6 = (bf16[128,512]{1,0:T(8,128)(2,1)S(1)}, bf16[128,512]{1,0:T(8,128)(2,1)S(1)}, u32[]{:S(2)}, u32[]{:S(2)}) collective-permute-start(bf16[128,512]{1,0:T(8,128)(2,1)S(1)} %get-tuple-element.26), channel_id=1, source_target_pairs={{0,8},{8,16},{16,24},{24,0},{1,9},{9,17},{17,25},{25,1},{2,10},{10... | collective-permute-start | bytes 393224 | tf_op jit(solution)/shard_map/ppermute | solution.py:14
  60.0 3.6 %collective-permute-done.8 = bf16[128,512]{1,0:T(8,128)(2,1)S(1)} collective-permute-done((bf16[128,512]{1,0:T(8,128)(2,1)S(1)}, bf16[128,512]{1,0:T(8,128)(2,1)S(1)}, u32[]{:S(2)}, u32[]{:S(2)}) %collective-permute-start.8) | collective-permute-done | bytes 131104 | tf_op jit(solution)/shard_map/ppermute | solution.py:14
  63.6 6.8 %collective-permute-done.7 = bf16[128,512]{1,0:T(8,128)(2,1)S(1)} collective-permute-done((bf16[128,512]{1,0:T(8,128)(2,1)S(1)}, bf16[128,512]{1,0:T(8,128)(2,1)S(1)}, u32[]{:S(2)}, u32[]{:S(2)}) %collective-permute-start.7) | collective-permute-done | bytes 131104 | tf_op jit(solution)/shard_map/ppermute | solution.py:14
  70.4 0.6 select_reduce_fusion.3
  71.3 9.5 %all_to_all.16 = bf16[8,32,512]{2,1,0:T(8,128)(2,1)S(1)} all-to-all(bf16[8,32,512]{2,1,0:T(8,128)(2,1)S(1)} %select_add_fusion.3), channel_id=1, replica_groups=mesh['group'=4,'member'=8] {'member'}, dimensions={0} | all-to-all | bytes 524288 | tf_op jit(solution)/shard_map/all_to_all | solution.py:92
  81.0 8.4 %all-gather.2 = bf16[256,512]{1,0:T(8,128)(2,1)S(1)} all-gather(bf16[32,512]{1,0:T(8,128)(2,1)S(1)} %get-tuple-element.117), channel_id=4, replica_groups=mesh['group'=4,'member'=8] {'member'}, dimensions={0}, use_global_device_ids=true | all-gather | bytes 294912 | tf_op jit(solution)/shard_map/all_gather | solution.py:98
  90.0 1.7 %collective-permute-start.10 = (bf16[128,512]{1,0:T(8,128)(2,1)S(1)}, bf16[128,512]{1,0:T(8,128)(2,1)S(1)}, u32[]{:S(2)}, u32[]{:S(2)}) collective-permute-start(bf16[128,512]{1,0:T(8,128)(2,1)S(1)} %get-tuple-element.21), channel_id=1, source_target_pairs={{0,16},{8,24},{16,0},{24,8},{1,17},{9,25},{17,1},{25,9},{2,18},{10... | collective-permute-start | bytes 393224 | tf_op jit(solution)/shard_map/ppermute | solution.py:14
  91.7 1.9 %collective-permute-start.9 = (bf16[128,512]{1,0:T(8,128)(2,1)S(1)}, bf16[128,512]{1,0:T(8,128)(2,1)S(1)}, u32[]{:S(2)}, u32[]{:S(2)}) collective-permute-start(bf16[128,512]{1,0:T(8,128)(2,1)S(1)} %get-tuple-element.22), channel_id=1, source_target_pairs={{0,8},{8,16},{16,24},{24,0},{1,9},{9,17},{17,25},{25,1},{2,10},{10... | collective-permute-start | bytes 393224 | tf_op jit(solution)/shard_map/ppermute | solution.py:14
  93.7 2.4 %collective-permute-done.11 = bf16[128,512]{1,0:T(8,128)(2,1)S(1)} collective-permute-done((bf16[128,512]{1,0:T(8,128)(2,1)S(1)}, bf16[128,512]{1,0:T(8,128)(2,1)S(1)}, u32[]{:S(2)}, u32[]{:S(2)}) %collective-permute-start.11) | collective-permute-done | bytes 131104 | tf_op jit(solution)/shard_map/ppermute | solution.py:14
  96.1 8.0 %collective-permute-done.10 = bf16[128,512]{1,0:T(8,128)(2,1)S(1)} collective-permute-done((bf16[128,512]{1,0:T(8,128)(2,1)S(1)}, bf16[128,512]{1,0:T(8,128)(2,1)S(1)}, u32[]{:S(2)}, u32[]{:S(2)}) %collective-permute-start.10) | collective-permute-done | bytes 131104 | tf_op jit(solution)/shard_map/ppermute | solution.py:14
  104.1 0.6 select_reduce_fusion.1
  105.0 9.5 %all_to_all.17 = bf16[8,32,512]{2,1,0:T(8,128)(2,1)S(1)} all-to-all(bf16[8,32,512]{2,1,0:T(8,128)(2,1)S(1)} %select_add_fusion.1), channel_id=1, replica_groups=mesh['group'=4,'member'=8] {'member'}, dimensions={0} | all-to-all | bytes 524288 | tf_op jit(solution)/shard_map/all_to_all | solution.py:92
  114.7 0.7 maximum_bitcast_fusion
  (62 shorter events, 3.8 us)
Async XLA Ops:
  0.0 37.1 %copy-start = (bf16[4,512,512]{2,1,0:T(8,128)(2,1)S(1)}, bf16[4,512,512]{2,1,0:T(8,128)(2,1)}, u32[]{:S(2)}) copy-start(bf16[4,512,512]{2,1,0:T(8,128)(2,1)} %param.6) | copy-start | bytes 6291460
  0.0 20.4 %copy-start.3 = (s32[4,3]{1,0:T(4,128)S(1)}, s32[4,3]{1,0:T(4,128)}, u32[]{:S(2)}) copy-start(s32[4,3]{1,0:T(4,128)} %param.7) | copy-start | bytes 148
  0.0 20.4 %collective-permute-start = (s32[4,3]{1,0:T(4,128)}, s32[4,3]{1,0:T(4,128)S(1)}, u32[]{:S(2)}, u32[]{:S(2)}) collective-permute-start(s32[4,3]{1,0:T(4,128)} %param.7), channel_id=1, source_target_pairs={{0,8},{8,16},{16,24},{24,0},{1,9},{9,17},{17,25},{25,1},{2,10},{10... | collective-permute-start | bytes 152 | tf_op jit(solution)/shard_map/ppermute | solution.py:14
  3.0 17.4 %collective-permute-start.2 = (s32[4,3]{1,0:T(4,128)}, s32[4,3]{1,0:T(4,128)S(1)}, u32[]{:S(2)}, u32[]{:S(2)}) collective-permute-start(s32[4,3]{1,0:T(4,128)} %param.7), channel_id=1, source_target_pairs={{0,24},{8,0},{16,8},{24,16},{1,25},{9,1},{17,9},{25,17},{2,26},{10... | collective-permute-start | bytes 152 | tf_op jit(solution)/shard_map/ppermute | solution.py:14
  5.1 15.3 %collective-permute-start.1 = (s32[4,3]{1,0:T(4,128)}, s32[4,3]{1,0:T(4,128)S(1)}, u32[]{:S(2)}, u32[]{:S(2)}) collective-permute-start(s32[4,3]{1,0:T(4,128)} %param.7), channel_id=1, source_target_pairs={{0,16},{8,24},{16,0},{24,8},{1,17},{9,25},{17,1},{25,9},{2,18},{10... | collective-permute-start | bytes 152 | tf_op jit(solution)/shard_map/ppermute | solution.py:14
  21.8 5.8 %collective-permute-start.5 = (bf16[128,512]{1,0:T(8,128)(2,1)S(1)}, bf16[128,512]{1,0:T(8,128)(2,1)S(1)}, u32[]{:S(2)}, u32[]{:S(2)}) collective-permute-start(bf16[128,512]{1,0:T(8,128)(2,1)S(1)} %get-tuple-element.28), channel_id=1, source_target_pairs={{0,24},{8,0},{16,8},{24,16},{1,25},{9,1},{17,9},{25,17},{2,26},{10... | collective-permute-start | bytes 393224 | tf_op jit(solution)/shard_map/ppermute | solution.py:14
  23.2 13.8 %collective-permute-start.4 = (bf16[128,512]{1,0:T(8,128)(2,1)S(1)}, bf16[128,512]{1,0:T(8,128)(2,1)S(1)}, u32[]{:S(2)}, u32[]{:S(2)}) collective-permute-start(bf16[128,512]{1,0:T(8,128)(2,1)S(1)} %get-tuple-element.29), channel_id=1, source_target_pairs={{0,16},{8,24},{16,0},{24,8},{1,17},{9,25},{17,1},{25,9},{2,18},{10... | collective-permute-start | bytes 393224 | tf_op jit(solution)/shard_map/ppermute | solution.py:14
  24.9 12.2 %collective-permute-start.3 = (bf16[128,512]{1,0:T(8,128)(2,1)S(1)}, bf16[128,512]{1,0:T(8,128)(2,1)S(1)}, u32[]{:S(2)}, u32[]{:S(2)}) collective-permute-start(bf16[128,512]{1,0:T(8,128)(2,1)S(1)} %get-tuple-element.30), channel_id=1, source_target_pairs={{0,8},{8,16},{16,24},{24,0},{1,9},{9,17},{17,25},{25,1},{2,10},{10... | collective-permute-start | bytes 393224 | tf_op jit(solution)/shard_map/ppermute | solution.py:14
  37.7 9.8 %copy-start.1 = (bf16[1,512,512]{2,1,0:T(8,128)(2,1)S(1)}, bf16[1,512,512]{2,1,0:T(8,128)(2,1)}, u32[]{:S(2)}) copy-start(bf16[1,512,512]{2,1,0:T(8,128)(2,1)} %param.9) | copy-start | bytes 1572868
  37.7 9.8 %copy-start.2 = (f32[3,1,32,512]{3,2,1,0:T(8,128)S(1)}, f32[3,1,32,512]{3,2,1,0:T(8,128)}, u32[]{:S(2)}) copy-start(f32[3,1,32,512]{3,2,1,0:T(8,128)} %param.10) | copy-start | bytes 589828
  56.7 6.9 %collective-permute-start.8 = (bf16[128,512]{1,0:T(8,128)(2,1)S(1)}, bf16[128,512]{1,0:T(8,128)(2,1)S(1)}, u32[]{:S(2)}, u32[]{:S(2)}) collective-permute-start(bf16[128,512]{1,0:T(8,128)(2,1)S(1)} %get-tuple-element.24), channel_id=1, source_target_pairs={{0,24},{8,0},{16,8},{24,16},{1,25},{9,1},{17,9},{25,17},{2,26},{10... | collective-permute-start | bytes 393224 | tf_op jit(solution)/shard_map/ppermute | solution.py:14
  56.7 13.7 %collective-permute-start.7 = (bf16[128,512]{1,0:T(8,128)(2,1)S(1)}, bf16[128,512]{1,0:T(8,128)(2,1)S(1)}, u32[]{:S(2)}, u32[]{:S(2)}) collective-permute-start(bf16[128,512]{1,0:T(8,128)(2,1)S(1)} %get-tuple-element.25), channel_id=1, source_target_pairs={{0,16},{8,24},{16,0},{24,8},{1,17},{9,25},{17,1},{25,9},{2,18},{10... | collective-permute-start | bytes 393224 | tf_op jit(solution)/shard_map/ppermute | solution.py:14
  58.0 12.4 %collective-permute-start.6 = (bf16[128,512]{1,0:T(8,128)(2,1)S(1)}, bf16[128,512]{1,0:T(8,128)(2,1)S(1)}, u32[]{:S(2)}, u32[]{:S(2)}) collective-permute-start(bf16[128,512]{1,0:T(8,128)(2,1)S(1)} %get-tuple-element.26), channel_id=1, source_target_pairs={{0,8},{8,16},{16,24},{24,0},{1,9},{9,17},{17,25},{25,1},{2,10},{10... | collective-permute-start | bytes 393224 | tf_op jit(solution)/shard_map/ppermute | solution.py:14
  89.9 6.2 %collective-permute-start.11 = (bf16[128,512]{1,0:T(8,128)(2,1)S(1)}, bf16[128,512]{1,0:T(8,128)(2,1)S(1)}, u32[]{:S(2)}, u32[]{:S(2)}) collective-permute-start(bf16[128,512]{1,0:T(8,128)(2,1)S(1)} %get-tuple-element.20), channel_id=1, source_target_pairs={{0,24},{8,0},{16,8},{24,16},{1,25},{9,1},{17,9},{25,17},{2,26},{10... | collective-permute-start | bytes 393224 | tf_op jit(solution)/shard_map/ppermute | solution.py:14
  90.0 14.1 %collective-permute-start.10 = (bf16[128,512]{1,0:T(8,128)(2,1)S(1)}, bf16[128,512]{1,0:T(8,128)(2,1)S(1)}, u32[]{:S(2)}, u32[]{:S(2)}) collective-permute-start(bf16[128,512]{1,0:T(8,128)(2,1)S(1)} %get-tuple-element.21), channel_id=1, source_target_pairs={{0,16},{8,24},{16,0},{24,8},{1,17},{9,25},{17,1},{25,9},{2,18},{10... | collective-permute-start | bytes 393224 | tf_op jit(solution)/shard_map/ppermute | solution.py:14
  91.7 12.4 %collective-permute-start.9 = (bf16[128,512]{1,0:T(8,128)(2,1)S(1)}, bf16[128,512]{1,0:T(8,128)(2,1)S(1)}, u32[]{:S(2)}, u32[]{:S(2)}) collective-permute-start(bf16[128,512]{1,0:T(8,128)(2,1)S(1)} %get-tuple-element.22), channel_id=1, source_target_pairs={{0,8},{8,16},{16,24},{24,0},{1,9},{9,17},{17,25},{25,1},{2,10},{10... | collective-permute-start | bytes 393224 | tf_op jit(solution)/shard_map/ppermute | solution.py:14

commit v10 on v9

--- a/solution.py
+++ b/solution.py
@@ -59,7 +59,8 @@
     delays_here = tile_lists[:, 2]
     source_shift = (group_here - source_group) % groups
 
-    hist_got = lax.all_gather(history[:, 0], "member", axis=0, tiled=False)
+    spread_hist = jnp.broadcast_to(history[:, 0][None], (members,) + history[:, 0].shape)
+    hist_got = lax.all_to_all(spread_hist, "member", 0, 0, tiled=True)
     hist_placed = pick([hist_got[m] for m in range(members)], owners)
     blocks = [
         hist_placed[:, t].reshape(group_blocks, EXCITE, BLOCK) for t in range(DELAYS)

time: 116 us -> 115 us (level)
  blocking collectives: 55.3 us -> 46.8 us
  starting transfers between devices: 17.3 us -> 21.1 us
  local copies, waits for them, and re-layouts: 1.2 us -> 2.87 us
  waiting for transfers between devices: 31.9 us -> 33.4 us
    all_gather x1 -> x0, blocking collectives: 10.2 us -> none  [body(): hist_got = lax.all_gather(history[:, 0], 'member', axis=0, tiled=False)]
    all_to_all x0 -> x1, waiting for transfers between devices: none -> 4.4 us  [body(): hist_got = lax.all_to_all(spread_hist, 'member', 0, 0, tiled=True)]
    all_to_all x0 -> x1, starting transfers between devices: none -> 3.72 us  [body(): hist_got = lax.all_to_all(spread_hist, 'member', 0, 0, tiled=True)]
    ppermute x12, waiting for transfers between devices: 31.9 us -> 29 us  [shifted(): return lax.ppermute(x, axis, [(i, (i + k) % n) for i in range(n)])]
    broadcast_in_dim x0 -> x1, local copies, waits for them, and re-layouts: none -> 1.68 us  [body(): jnp.broadcast_to(history[:, 0][None], (members,) + history[:, 0].shape)]
    all_to_all x3, blocking collectives: 28.4 us -> 30.1 us  [body(): got = lax.all_to_all(sent, 'member', 0, 0, tiled=True)]
  transfers between devices with their start and end apart: 12 -> 13, of which waited for: 6 -> 7; matrix products, arithmetic and copies ran while one was open for 4% -> 6% of each run, Pallas kernels for 0% -> 0%
where the time goes in v10:
time: 115 us; the launch traced here: 114 us
  blocking collectives  46.8 us (41%)
  waiting for transfers between devices  33.4 us (29%)
  starting transfers between devices  21.1 us (18%)
  other arithmetic  7.67 us (7%)
  local copies, waits for them, and re-layouts  2.87 us (2%)
  matrix products  2.3 us (2%)
    all_to_all x3, blocking collectives, body(): got = lax.all_to_all(sent, 'member', 0, 0, tiled=True)  30.1 us
    ppermute x12, waiting for transfers between devices, shifted(): return lax.ppermute(x, axis, [(i, (i + k) % n) for i in range(n)])  29 us
    ppermute x12, starting transfers between devices, shifted(): return lax.ppermute(x, axis, [(i, (i + k) % n) for i in range(n)])  17.3 us
    all_gather x2, blocking collectives, body(): lax.all_gather(current.astype(jnp.bfloat16), 'member', axis=0, tiled=False)  16.7 us
    all_to_all x1, waiting for transfers between devices, body(): hist_got = lax.all_to_all(spread_hist, 'member', 0, 0, tiled=True)  4.4 us
    all_to_all x1, starting transfers between devices, body(): hist_got = lax.all_to_all(spread_hist, 'member', 0, 0, tiled=True)  3.72 us
  transfers between devices with their start and end apart: 13, of which 7 were waited for; matrix products, arithmetic and copies ran while one was open for 6% of the time, Pallas kernels for 0%

profile of v10, /device:TPU:0, one launch (start us, length us, event | category | flops | bytes accessed | tf_op | source)
XLA Modules:
  0.0 114.5 jit_solution(7818081615894602312)
XLA Ops:
  0.0 3.0 %collective-permute-start = (s32[4,3]{1,0:T(4,128)}, s32[4,3]{1,0:T(4,128)S(1)}, u32[]{:S(2)}, u32[]{:S(2)}) collective-permute-start(s32[4,3]{1,0:T(4,128)} %param.7), channel_id=1, source_target_pairs={{0,8},{8,16},{16,24},{24,0},{1,9},{9,17},{17,25},{25,1},{2,10},{10... | collective-permute-start | bytes 152 | tf_op jit(solution)/shard_map/ppermute | solution.py:14
  3.0 2.1 %collective-permute-start.2 = (s32[4,3]{1,0:T(4,128)}, s32[4,3]{1,0:T(4,128)S(1)}, u32[]{:S(2)}, u32[]{:S(2)}) collective-permute-start(s32[4,3]{1,0:T(4,128)} %param.7), channel_id=1, source_target_pairs={{0,24},{8,0},{16,8},{24,16},{1,25},{9,1},{17,9},{25,17},{2,26},{10... | collective-permute-start | bytes 152 | tf_op jit(solution)/shard_map/ppermute | solution.py:14
  5.1 1.0 collective-permute-start.1
  6.1 1.7 %broadcast_in_dim.1149 = bf16[8,2,32,512]{3,2,1,0:T(8,128)(2,1)} broadcast(bf16[2,32,512]{2,1,0:T(8,128)(2,1)} %bitcast.254), dimensions={1,2,3} | broadcast | bytes 589824 | tf_op jit(solution)/shard_map/broadcast_in_dim | solution.py:62
  7.7 3.7 %all-to-all-start = ((bf16[8,2,32,512]{3,2,1,0:T(8,128)(2,1)}), bf16[8,2,32,512]{3,2,1,0:T(8,128)(2,1)S(1)}, u32[]{:S(2)}, u32[]{:S(2)}) async-start(bf16[8,2,32,512]{3,2,1,0:T(8,128)(2,1)} %broadcast_in_dim.1149), calls=%async_computation | async-start | bytes 1048576 | tf_op jit(solution)/shard_map/all_to_all | solution.py:63
  11.5 0.9 fusion.74
  12.5 0.8 select_reduce_fusion.6
  13.3 0.7 iota_compare_fusion.1
  13.9 1.0 slice_reduce_fusion.2
  15.0 0.7 pad_add_fusion
  16.8 4.4 %all-to-all-done = bf16[8,2,32,512]{3,2,1,0:T(8,128)(2,1)S(1)} async-done(((bf16[8,2,32,512]{3,2,1,0:T(8,128)(2,1)}), bf16[8,2,32,512]{3,2,1,0:T(8,128)(2,1)S(1)}, u32[]{:S(2)}, u32[]{:S(2)}) %all-to-all-start) | async-done | bytes 524320 | tf_op jit(solution)/shard_map/all_to_all | solution.py:63
  22.1 1.4 %collective-permute-start.5 = (bf16[128,512]{1,0:T(8,128)(2,1)S(1)}, bf16[128,512]{1,0:T(8,128)(2,1)S(1)}, u32[]{:S(2)}, u32[]{:S(2)}) collective-permute-start(bf16[128,512]{1,0:T(8,128)(2,1)S(1)} %get-tuple-element.28), channel_id=1, source_target_pairs={{0,24},{8,0},{16,8},{24,16},{1,25},{9,1},{17,9},{25,17},{2,26},{10... | collective-permute-start | bytes 393224 | tf_op jit(solution)/shard_map/ppermute | solution.py:14
  23.5 1.7 %collective-permute-start.4 = (bf16[128,512]{1,0:T(8,128)(2,1)S(1)}, bf16[128,512]{1,0:T(8,128)(2,1)S(1)}, u32[]{:S(2)}, u32[]{:S(2)}) collective-permute-start(bf16[128,512]{1,0:T(8,128)(2,1)S(1)} %get-tuple-element.29), channel_id=1, source_target_pairs={{0,16},{8,24},{16,0},{24,8},{1,17},{9,25},{17,1},{25,9},{2,18},{10... | collective-permute-start | bytes 393224 | tf_op jit(solution)/shard_map/ppermute | solution.py:14
  25.2 1.1 collective-permute-start.3
  26.3 2.7 %collective-permute-done.5 = bf16[128,512]{1,0:T(8,128)(2,1)S(1)} collective-permute-done((bf16[128,512]{1,0:T(8,128)(2,1)S(1)}, bf16[128,512]{1,0:T(8,128)(2,1)S(1)}, u32[]{:S(2)}, u32[]{:S(2)}) %collective-permute-start.5) | collective-permute-done | bytes 131104 | tf_op jit(solution)/shard_map/ppermute | solution.py:14
  29.0 5.5 %collective-permute-done.4 = bf16[128,512]{1,0:T(8,128)(2,1)S(1)} collective-permute-done((bf16[128,512]{1,0:T(8,128)(2,1)S(1)}, bf16[128,512]{1,0:T(8,128)(2,1)S(1)}, u32[]{:S(2)}, u32[]{:S(2)}) %collective-permute-start.4) | collective-permute-done | bytes 131104 | tf_op jit(solution)/shard_map/ppermute | solution.py:14
  34.5 0.6 select_reduce_fusion.5
  35.4 11.1 %all_to_all.20 = bf16[8,32,512]{2,1,0:T(8,128)(2,1)S(1)} all-to-all(bf16[8,32,512]{2,1,0:T(8,128)(2,1)S(1)} %select_add_fusion.5), channel_id=1, replica_groups=mesh['group'=4,'member'=8] {'member'}, dimensions={0} | all-to-all | bytes 524288 | tf_op jit(solution)/shard_map/all_to_all | solution.py:93
  46.8 8.4 %all-gather = bf16[256,512]{1,0:T(8,128)(2,1)S(1)} all-gather(bf16[32,512]{1,0:T(8,128)(2,1)S(1)} %get-tuple-element.115), channel_id=2, replica_groups=mesh['group'=4,'member'=8] {'member'}, dimensions={0}, use_global_device_ids=true | all-gather | bytes 294912 | tf_op jit(solution)/shard_map/all_gather | solution.py:99
  55.8 1.3 %collective-permute-start.7 = (bf16[128,512]{1,0:T(8,128)(2,1)S(1)}, bf16[128,512]{1,0:T(8,128)(2,1)S(1)}, u32[]{:S(2)}, u32[]{:S(2)}) collective-permute-start(bf16[128,512]{1,0:T(8,128)(2,1)S(1)} %get-tuple-element.25), channel_id=1, source_target_pairs={{0,16},{8,24},{16,0},{24,8},{1,17},{9,25},{17,1},{25,9},{2,18},{10... | collective-permute-start | bytes 393224 | tf_op jit(solution)/shard_map/ppermute | solution.py:14
  57.1 1.9 %collective-permute-start.6 = (bf16[128,512]{1,0:T(8,128)(2,1)S(1)}, bf16[128,512]{1,0:T(8,128)(2,1)S(1)}, u32[]{:S(2)}, u32[]{:S(2)}) collective-permute-start(bf16[128,512]{1,0:T(8,128)(2,1)S(1)} %get-tuple-element.26), channel_id=1, source_target_pairs={{0,8},{8,16},{16,24},{24,0},{1,9},{9,17},{17,25},{25,1},{2,10},{10... | collective-permute-start | bytes 393224 | tf_op jit(solution)/shard_map/ppermute | solution.py:14
  59.1 3.6 %collective-permute-done.8 = bf16[128,512]{1,0:T(8,128)(2,1)S(1)} collective-permute-done((bf16[128,512]{1,0:T(8,128)(2,1)S(1)}, bf16[128,512]{1,0:T(8,128)(2,1)S(1)}, u32[]{:S(2)}, u32[]{:S(2)}) %collective-permute-start.8) | collective-permute-done | bytes 131104 | tf_op jit(solution)/shard_map/ppermute | solution.py:14
  62.7 6.8 %collective-permute-done.7 = bf16[128,512]{1,0:T(8,128)(2,1)S(1)} collective-permute-done((bf16[128,512]{1,0:T(8,128)(2,1)S(1)}, bf16[128,512]{1,0:T(8,128)(2,1)S(1)}, u32[]{:S(2)}, u32[]{:S(2)}) %collective-permute-start.7) | collective-permute-done | bytes 131104 | tf_op jit(solution)/shard_map/ppermute | solution.py:14
  70.4 9.5 %all_to_all.21 = bf16[8,32,512]{2,1,0:T(8,128)(2,1)S(1)} all-to-all(bf16[8,32,512]{2,1,0:T(8,128)(2,1)S(1)} %select_add_fusion.3), channel_id=1, replica_groups=mesh['group'=4,'member'=8] {'member'}, dimensions={0} | all-to-all | bytes 524288 | tf_op jit(solution)/shard_map/all_to_all | solution.py:93
  80.1 8.4 %all-gather.1 = bf16[256,512]{1,0:T(8,128)(2,1)S(1)} all-gather(bf16[32,512]{1,0:T(8,128)(2,1)S(1)} %get-tuple-element.117), channel_id=3, replica_groups=mesh['group'=4,'member'=8] {'member'}, dimensions={0}, use_global_device_ids=true | all-gather | bytes 294912 | tf_op jit(solution)/shard_map/all_gather | solution.py:99
  89.1 1.8 %collective-permute-start.10 = (bf16[128,512]{1,0:T(8,128)(2,1)S(1)}, bf16[128,512]{1,0:T(8,128)(2,1)S(1)}, u32[]{:S(2)}, u32[]{:S(2)}) collective-permute-start(bf16[128,512]{1,0:T(8,128)(2,1)S(1)} %get-tuple-element.21), channel_id=1, source_target_pairs={{0,16},{8,24},{16,0},{24,8},{1,17},{9,25},{17,1},{25,9},{2,18},{10... | collective-permute-start | bytes 393224 | tf_op jit(solution)/shard_map/ppermute | solution.py:14
  90.8 1.9 %collective-permute-start.9 = (bf16[128,512]{1,0:T(8,128)(2,1)S(1)}, bf16[128,512]{1,0:T(8,128)(2,1)S(1)}, u32[]{:S(2)}, u32[]{:S(2)}) collective-permute-start(bf16[128,512]{1,0:T(8,128)(2,1)S(1)} %get-tuple-element.22), channel_id=1, source_target_pairs={{0,8},{8,16},{16,24},{24,0},{1,9},{9,17},{17,25},{25,1},{2,10},{10... | collective-permute-start | bytes 393224 | tf_op jit(solution)/shard_map/ppermute | solution.py:14
  92.8 2.4 %collective-permute-done.11 = bf16[128,512]{1,0:T(8,128)(2,1)S(1)} collective-permute-done((bf16[128,512]{1,0:T(8,128)(2,1)S(1)}, bf16[128,512]{1,0:T(8,128)(2,1)S(1)}, u32[]{:S(2)}, u32[]{:S(2)}) %collective-permute-start.11) | collective-permute-done | bytes 131104 | tf_op jit(solution)/shard_map/ppermute | solution.py:14
  95.2 8.0 %collective-permute-done.10 = bf16[128,512]{1,0:T(8,128)(2,1)S(1)} collective-permute-done((bf16[128,512]{1,0:T(8,128)(2,1)S(1)}, bf16[128,512]{1,0:T(8,128)(2,1)S(1)}, u32[]{:S(2)}, u32[]{:S(2)}) %collective-permute-start.10) | collective-permute-done | bytes 131104 | tf_op jit(solution)/shard_map/ppermute | solution.py:14
  103.2 0.6 select_reduce_fusion.1
  104.1 9.5 %all_to_all.22 = bf16[8,32,512]{2,1,0:T(8,128)(2,1)S(1)} all-to-all(bf16[8,32,512]{2,1,0:T(8,128)(2,1)S(1)} %select_add_fusion.1), channel_id=1, replica_groups=mesh['group'=4,'member'=8] {'member'}, dimensions={0} | all-to-all | bytes 524288 | tf_op jit(solution)/shard_map/all_to_all | solution.py:93
  113.8 0.7 maximum_bitcast_fusion
  (62 shorter events, 5.5 us)
Async XLA Ops:
  0.0 34.5 %copy-start = (bf16[4,512,512]{2,1,0:T(8,128)(2,1)S(1)}, bf16[4,512,512]{2,1,0:T(8,128)(2,1)}, u32[]{:S(2)}) copy-start(bf16[4,512,512]{2,1,0:T(8,128)(2,1)} %param.6) | copy-start | bytes 6291460
  0.0 15.0 %collective-permute-start = (s32[4,3]{1,0:T(4,128)}, s32[4,3]{1,0:T(4,128)S(1)}, u32[]{:S(2)}, u32[]{:S(2)}) collective-permute-start(s32[4,3]{1,0:T(4,128)} %param.7), channel_id=1, source_target_pairs={{0,8},{8,16},{16,24},{24,0},{1,9},{9,17},{17,25},{25,1},{2,10},{10... | collective-permute-start | bytes 152 | tf_op jit(solution)/shard_map/ppermute | solution.py:14
  3.0 12.0 %collective-permute-start.2 = (s32[4,3]{1,0:T(4,128)}, s32[4,3]{1,0:T(4,128)S(1)}, u32[]{:S(2)}, u32[]{:S(2)}) collective-permute-start(s32[4,3]{1,0:T(4,128)} %param.7), channel_id=1, source_target_pairs={{0,24},{8,0},{16,8},{24,16},{1,25},{9,1},{17,9},{25,17},{2,26},{10... | collective-permute-start | bytes 152 | tf_op jit(solution)/shard_map/ppermute | solution.py:14
  5.1 9.9 %collective-permute-start.1 = (s32[4,3]{1,0:T(4,128)}, s32[4,3]{1,0:T(4,128)S(1)}, u32[]{:S(2)}, u32[]{:S(2)}) collective-permute-start(s32[4,3]{1,0:T(4,128)} %param.7), channel_id=1, source_target_pairs={{0,16},{8,24},{16,0},{24,8},{1,17},{9,25},{17,1},{25,9},{2,18},{10... | collective-permute-start | bytes 152 | tf_op jit(solution)/shard_map/ppermute | solution.py:14
  7.7 13.5 %all-to-all-start = ((bf16[8,2,32,512]{3,2,1,0:T(8,128)(2,1)}), bf16[8,2,32,512]{3,2,1,0:T(8,128)(2,1)S(1)}, u32[]{:S(2)}, u32[]{:S(2)}) async-start(bf16[8,2,32,512]{3,2,1,0:T(8,128)(2,1)} %broadcast_in_dim.1149), calls=%async_computation | async-start | bytes 1048576 | tf_op jit(solution)/shard_map/all_to_all | solution.py:63
  22.1 6.9 %collective-permute-start.5 = (bf16[128,512]{1,0:T(8,128)(2,1)S(1)}, bf16[128,512]{1,0:T(8,128)(2,1)S(1)}, u32[]{:S(2)}, u32[]{:S(2)}) collective-permute-start(bf16[128,512]{1,0:T(8,128)(2,1)S(1)} %get-tuple-element.28), channel_id=1, source_target_pairs={{0,24},{8,0},{16,8},{24,16},{1,25},{9,1},{17,9},{25,17},{2,26},{10... | collective-permute-start | bytes 393224 | tf_op jit(solution)/shard_map/ppermute | solution.py:14
  23.5 11.0 %collective-permute-start.4 = (bf16[128,512]{1,0:T(8,128)(2,1)S(1)}, bf16[128,512]{1,0:T(8,128)(2,1)S(1)}, u32[]{:S(2)}, u32[]{:S(2)}) collective-permute-start(bf16[128,512]{1,0:T(8,128)(2,1)S(1)} %get-tuple-element.29), channel_id=1, source_target_pairs={{0,16},{8,24},{16,0},{24,8},{1,17},{9,25},{17,1},{25,9},{2,18},{10... | collective-permute-start | bytes 393224 | tf_op jit(solution)/shard_map/ppermute | solution.py:14
  25.2 9.3 %collective-permute-start.3 = (bf16[128,512]{1,0:T(8,128)(2,1)S(1)}, bf16[128,512]{1,0:T(8,128)(2,1)S(1)}, u32[]{:S(2)}, u32[]{:S(2)}) collective-permute-start(bf16[128,512]{1,0:T(8,128)(2,1)S(1)} %get-tuple-element.30), channel_id=1, source_target_pairs={{0,8},{8,16},{16,24},{24,0},{1,9},{9,17},{17,25},{25,1},{2,10},{10... | collective-permute-start | bytes 393224 | tf_op jit(solution)/shard_map/ppermute | solution.py:14
  35.1 11.5 %copy-start.1 = (bf16[1,512,512]{2,1,0:T(8,128)(2,1)S(1)}, bf16[1,512,512]{2,1,0:T(8,128)(2,1)}, u32[]{:S(2)}) copy-start(bf16[1,512,512]{2,1,0:T(8,128)(2,1)} %param.9) | copy-start | bytes 1572868
  35.1 11.5 %copy-start.2 = (f32[3,1,32,512]{3,2,1,0:T(8,128)S(1)}, f32[3,1,32,512]{3,2,1,0:T(8,128)}, u32[]{:S(2)}) copy-start(f32[3,1,32,512]{3,2,1,0:T(8,128)} %param.10) | copy-start | bytes 589828
  55.7 6.9 %collective-permute-start.8 = (bf16[128,512]{1,0:T(8,128)(2,1)S(1)}, bf16[128,512]{1,0:T(8,128)(2,1)S(1)}, u32[]{:S(2)}, u32[]{:S(2)}) collective-permute-start(bf16[128,512]{1,0:T(8,128)(2,1)S(1)} %get-tuple-element.24), channel_id=1, source_target_pairs={{0,24},{8,0},{16,8},{24,16},{1,25},{9,1},{17,9},{25,17},{2,26},{10... | collective-permute-start | bytes 393224 | tf_op jit(solution)/shard_map/ppermute | solution.py:14
  55.8 13.7 %collective-permute-start.7 = (bf16[128,512]{1,0:T(8,128)(2,1)S(1)}, bf16[128,512]{1,0:T(8,128)(2,1)S(1)}, u32[]{:S(2)}, u32[]{:S(2)}) collective-permute-start(bf16[128,512]{1,0:T(8,128)(2,1)S(1)} %get-tuple-element.25), channel_id=1, source_target_pairs={{0,16},{8,24},{16,0},{24,8},{1,17},{9,25},{17,1},{25,9},{2,18},{10... | collective-permute-start | bytes 393224 | tf_op jit(solution)/shard_map/ppermute | solution.py:14
  57.1 12.4 %collective-permute-start.6 = (bf16[128,512]{1,0:T(8,128)(2,1)S(1)}, bf16[128,512]{1,0:T(8,128)(2,1)S(1)}, u32[]{:S(2)}, u32[]{:S(2)}) collective-permute-start(bf16[128,512]{1,0:T(8,128)(2,1)S(1)} %get-tuple-element.26), channel_id=1, source_target_pairs={{0,8},{8,16},{16,24},{24,0},{1,9},{9,17},{17,25},{25,1},{2,10},{10... | collective-permute-start | bytes 393224 | tf_op jit(solution)/shard_map/ppermute | solution.py:14
  89.0 6.2 %collective-permute-start.11 = (bf16[128,512]{1,0:T(8,128)(2,1)S(1)}, bf16[128,512]{1,0:T(8,128)(2,1)S(1)}, u32[]{:S(2)}, u32[]{:S(2)}) collective-permute-start(bf16[128,512]{1,0:T(8,128)(2,1)S(1)} %get-tuple-element.20), channel_id=1, source_target_pairs={{0,24},{8,0},{16,8},{24,16},{1,25},{9,1},{17,9},{25,17},{2,26},{10... | collective-permute-start | bytes 393224 | tf_op jit(solution)/shard_map/ppermute | solution.py:14
  89.1 14.1 %collective-permute-start.10 = (bf16[128,512]{1,0:T(8,128)(2,1)S(1)}, bf16[128,512]{1,0:T(8,128)(2,1)S(1)}, u32[]{:S(2)}, u32[]{:S(2)}) collective-permute-start(bf16[128,512]{1,0:T(8,128)(2,1)S(1)} %get-tuple-element.21), channel_id=1, source_target_pairs={{0,16},{8,24},{16,0},{24,8},{1,17},{9,25},{17,1},{25,9},{2,18},{10... | collective-permute-start | bytes 393224 | tf_op jit(solution)/shard_map/ppermute | solution.py:14
  90.8 12.4 %collective-permute-start.9 = (bf16[128,512]{1,0:T(8,128)(2,1)S(1)}, bf16[128,512]{1,0:T(8,128)(2,1)S(1)}, u32[]{:S(2)}, u32[]{:S(2)}) collective-permute-start(bf16[128,512]{1,0:T(8,128)(2,1)S(1)} %get-tuple-element.22), channel_id=1, source_target_pairs={{0,8},{8,16},{16,24},{24,0},{1,9},{9,17},{17,25},{25,1},{2,10},{10... | collective-permute-start | bytes 393224 | tf_op jit(solution)/shard_map/ppermute | solution.py:14

commit v11 on v7

--- a/solution.py
+++ b/solution.py
@@ -69,15 +69,23 @@
     for step in range(STEPS):
         near = blocks[DELAYS + step - 1]
         far = blocks[DELAYS + step - 2]
-        outgoing = None
-        for block in range(group_blocks):
-            term = jnp.where(from_near[:, block, None, None], near[block][None], 0) + jnp.where(
-                from_far[:, block, None, None], far[block][None], 0
-            )
-            outgoing = term if outgoing is None else outgoing + term
-        received = [outgoing[0]] + [
-            shifted(outgoing[k], "group", groups, k) for k in range(1, groups)
-        ]
+        def piece_for(k, near, far):
+            total = None
+            for block in range(group_blocks):
+                term = jnp.where(from_near[k, block], near[block], 0) + jnp.where(
+                    from_far[k, block], far[block], 0
+                )
+                total = term if total is None else total + term
+            return total
+
+        middle = groups // 2
+        first = piece_for(middle, near, far)
+        arrived = {middle: shifted(first, "group", groups, middle)}
+        first, near, far = lax.optimization_barrier((first, near, far))
+        for k in range(1, groups):
+            if k != middle:
+                arrived[k] = shifted(piece_for(k, near, far), "group", groups, k)
+        received = [piece_for(0, near, far)] + [arrived[k] for k in range(1, groups)]
         blocks_in = pick(received, source_shift)
         terms = jnp.einsum(
             "kes,kso->keo", blocks_in, tile_values, preferred_element_type=jnp.float32

time: 114 us -> 157 us (1.38); the launches traced: 114 us -> 155 us
  other arithmetic: 7.67 us -> 36.7 us
  local copies, waits for them, and re-layouts: 2.94 us -> 31.1 us
  blocking collectives: 48.5 us -> 38.6 us
  waiting for transfers between devices: 31.2 us -> 22.2 us
  starting transfers between devices: 21 us -> 22.8 us
    broadcast_in_dim x12 -> x48, local copies, waits for them, and re-layouts: 0.28 us -> 26.4 us  [pick(): jnp.where(chosen[:, k][spread], piece[None], jnp.zeros_like(piece)[None])]
    broadcast_in_dim x0 -> x3, other arithmetic: none -> 15.2 us  [pick(): jnp.where(chosen[:, k][spread], piece[None], jnp.zeros_like(piece)[None])]
    all_to_all x2 -> x1, blocking collectives: 18.7 us -> 9.35 us  [body(): got = lax.all_to_all(spread, 'member', 0, 0, tiled=True)]
    add x3 -> x5, other arithmetic: 0.65 us -> 9.77 us  [piece_for(): total = term if total is None else total + term]
    ppermute x12, waiting for transfers between devices: 26.8 us -> 19.2 us  [shifted(): return lax.ppermute(x, axis, [(i, (i + k) % n) for i in range(n)])]
    select_n x0 -> x2, other arithmetic: none -> 3.73 us  [the longest x1 2.5 us: piece_for(): jnp.where(from_far[k, block], far[block], 0)]
    all_to_all x0 -> x1, starting transfers between devices: none -> 3.41 us  [body(): got = lax.all_to_all(spread, 'member', 0, 0, tiled=True)]
  transfers between devices with their start and end apart: 13 -> 14, of which waited for: 7 -> 7; matrix products, arithmetic and copies ran while one was open for 6% -> 37% of each run, Pallas kernels for 0% -> 0%
where the time goes in v11:
time: 157 us; the launch traced here: 155 us
  blocking collectives  38.6 us (25%)
  other arithmetic  36.7 us (23%)
  local copies, waits for them, and re-layouts  31.1 us (20%)
  starting transfers between devices  22.8 us (15%)
  waiting for transfers between devices  22.2 us (14%)
  matrix products  3.2 us (2%)
    all_to_all x3, blocking collectives, body(): got = lax.all_to_all(sent, 'member', 0, 0, tiled=True)  29.3 us
    broadcast_in_dim x48, local copies, waits for them, and re-layouts, pick(): jnp.where(chosen[:, k][spread], piece[None], jnp.zeros_like(piece)[None])  26.4 us
    ppermute x12, waiting for transfers between devices, shifted(): return lax.ppermute(x, axis, [(i, (i + k) % n) for i in range(n)])  19.2 us
    ppermute x12, starting transfers between devices, shifted(): return lax.ppermute(x, axis, [(i, (i + k) % n) for i in range(n)])  15.7 us
    broadcast_in_dim x3, other arithmetic, pick(): jnp.where(chosen[:, k][spread], piece[None], jnp.zeros_like(piece)[None])  15.2 us
    add x5, other arithmetic, piece_for(): total = term if total is None else total + term  9.77 us
    all_to_all x1, blocking collectives, body(): got = lax.all_to_all(spread, 'member', 0, 0, tiled=True)  9.35 us
    all_to_all x1, starting transfers between devices, body(): hist_got = lax.all_to_all(spread_hist, 'member', 0, 0, tiled=True)  3.72 us
  transfers between devices with their start and end apart: 14, of which 7 were waited for; matrix products, arithmetic and copies ran while one was open for 37% of the time, Pallas kernels for 0%

profile of v11, /device:TPU:0, one launch (start us, length us, event | category | flops | bytes accessed | tf_op | source)
XLA Modules:
  0.0 155.3 jit_solution(17189246643983220529)
XLA Ops:
  0.0 5.0 %collective-permute-start.2 = (s32[4,3]{1,0:T(4,128)}, s32[4,3]{1,0:T(4,128)S(1)}, u32[]{:S(2)}, u32[]{:S(2)}) collective-permute-start(s32[4,3]{1,0:T(4,128)} %param.7), channel_id=1, source_target_pairs={{0,24},{8,0},{16,8},{24,16},{1,25},{9,1},{17,9},{25,17},{2,26},{10... | collective-permute-start | bytes 152 | tf_op jit(solution)/shard_map/ppermute | solution.py:14
  6.1 1.7 %broadcast_in_dim.1176 = bf16[8,2,32,512]{3,2,1,0:T(8,128)(2,1)} broadcast(bf16[2,32,512]{2,1,0:T(8,128)(2,1)} %bitcast.412), dimensions={1,2,3} | broadcast | bytes 589824 | tf_op jit(solution)/shard_map/broadcast_in_dim | solution.py:62
  7.7 3.7 %all-to-all-start = ((bf16[8,2,32,512]{3,2,1,0:T(8,128)(2,1)}), bf16[8,2,32,512]{3,2,1,0:T(8,128)(2,1)S(1)}, u32[]{:S(2)}, u32[]{:S(2)}) async-start(bf16[8,2,32,512]{3,2,1,0:T(8,128)(2,1)} %broadcast_in_dim.1176), calls=%async_computation | async-start | bytes 1048576 | tf_op jit(solution)/shard_map/all_to_all | solution.py:63
  18.2 3.0 %all-to-all-done = bf16[8,2,32,512]{3,2,1,0:T(8,128)(2,1)S(1)} async-done(((bf16[8,2,32,512]{3,2,1,0:T(8,128)(2,1)}), bf16[8,2,32,512]{3,2,1,0:T(8,128)(2,1)S(1)}, u32[]{:S(2)}, u32[]{:S(2)}) %all-to-all-start) | async-done | bytes 524320 | tf_op jit(solution)/shard_map/all_to_all | solution.py:63
  21.8 2.5 %broadcast_select_fusion.3 = (bf16[4,1,32,512]{3,2,0,1:T(8,128)(2,1)S(1)}, bf16[4,1,32,512]{3,2,0,1:T(8,128)(2,1)S(1)}, bf16[4,1,32,512]{3,2,0,1:T(8,128)(2,1)S(1)}) fusion(pred[]{:T(512)} %bitcast.26, bf16[8,2,32,512]{3,2,0,1:T(8,128)(2,1)S(1)} %select_add_fusion, pred[]{:T(512)} %bitcast.28, pred[]{:T(512)} %bitcast.27, pred[]{:T(512)} %bitcast.8), kind=kLoop, calls=%fused_computation.138 | loop fusion | flops 589824 | bytes 917508 | tf_op jit(solution)/shard_map/jit(_where)/select_n | solution.py:75
  24.3 2.0 %collective-permute-start.4 = (bf16[128,512]{1,0:T(8,128)(2,1)S(1)}, bf16[128,512]{1,0:T(8,128)(2,1)S(1)}, u32[]{:S(2)}, u32[]{:S(2)}) collective-permute-start(bf16[128,512]{1,0:T(8,128)(2,1)S(1)} %bitcast.405), channel_id=1, source_target_pairs={{0,16},{8,24},{16,0},{24,8},{1,17},{9,25},{17,1},{25,9},{2,18},{10... | collective-permute-start | bytes 393224 | tf_op jit(solution)/shard_map/ppermute | solution.py:14
  26.3 5.1 %add_bitcast_fusion.8 = (bf16[128,512]{1,0:T(8,128)(2,1)S(1)}, bf16[128,512]{1,0:T(8,128)(2,1)S(1)}) fusion(pred[]{:T(512)} %bitcast.34, pred[]{:T(512)} %bitcast.33, pred[]{:T(512)} %bitcast.32, pred[]{:T(512)} %bitcast.7, bf16[2,128,512]{2,1,0:T(8,128)(2,1)S(1)} %bitcast.381, bf16[2,128,512]{2,1,0:T(8,128)(2,1)S(1)} %bitcast.377, pred[]{:T(512)} %bitcast.47, ...), kind=kLoop, calls=%fused_computation.134 | loop fusion | flops 917504 | bytes 786440 | tf_op jit(solution)/shard_map/jit(_where)/broadcast_in_dim | solution.py:28
  31.4 3.0 %collective-permute-start.5 = (bf16[128,512]{1,0:T(8,128)(2,1)S(1)}, bf16[128,512]{1,0:T(8,128)(2,1)S(1)}, u32[]{:S(2)}, u32[]{:S(2)}) collective-permute-start(bf16[128,512]{1,0:T(8,128)(2,1)S(1)} %get-tuple-element.47), channel_id=1, source_target_pairs={{0,24},{8,0},{16,8},{24,16},{1,25},{9,1},{17,9},{25,17},{2,26},{10... | collective-permute-start | bytes 393224 | tf_op jit(solution)/shard_map/ppermute | solution.py:14
  34.3 2.4 %add_bitcast_fusion.7 = bf16[128,512]{1,0:T(8,128)(2,1)S(1)} fusion(pred[]{:T(512)} %bitcast.40, pred[]{:T(512)} %bitcast.39, pred[]{:T(512)} %bitcast.38, pred[]{:T(512)} %bitcast.37, bf16[2,128,512]{2,1,0:T(8,128)(2,1)S(1)} %bitcast.382, bf16[2,128,512]{2,1,0:T(8,128)(2,1)S(1)} %bitcast.378), kind=kLoop, calls=%fused_computation.133 | loop fusion | flops 458752 | bytes 655364 | tf_op jit(solution)/shard_map/add | solution.py:78
  37.0 6.6 %collective-permute-done.3 = bf16[128,512]{1,0:T(8,128)(2,1)S(1)} collective-permute-done((bf16[128,512]{1,0:T(8,128)(2,1)S(1)}, bf16[128,512]{1,0:T(8,128)(2,1)S(1)}, u32[]{:S(2)}, u32[]{:S(2)}) %collective-permute-start.3) | collective-permute-done | bytes 131104 | tf_op jit(solution)/shard_map/ppermute | solution.py:14
  44.6 9.3 %all_to_all.30 = bf16[8,32,512]{2,1,0:T(8,128)(2,1)S(1)} all-to-all(bf16[8,32,512]{2,1,0:T(8,128)(2,1)S(1)} %select_add_fusion.5), channel_id=1, replica_groups=mesh['group'=4,'member'=8] {'member'}, dimensions={0} | all-to-all | bytes 524288 | tf_op jit(solution)/shard_map/all_to_all | solution.py:101
  55.8 3.4 %all-to-all-start.2 = ((bf16[8,32,512]{2,1,0:T(8,128)(2,1)}), bf16[8,32,512]{2,1,0:T(8,128)(2,1)S(1)}, u32[]{:S(2)}, u32[]{:S(2)}) async-start(bf16[8,32,512]{2,1,0:T(8,128)(2,1)} %broadcast_in_dim.1256), calls=%async_computation.2 | async-start | bytes 524288 | tf_op jit(solution)/shard_map/all_to_all | solution.py:108
  72.2 1.3 broadcast_in_dim.1299
  77.2 1.3 broadcast_in_dim.1287
  78.5 1.3 broadcast_in_dim.1288
  79.8 1.4 broadcast_in_dim.1289
  81.1 1.3 broadcast_in_dim.1281
  82.4 1.3 broadcast_in_dim.1282
  83.8 1.4 broadcast_in_dim.1283
  87.6 5.1 %add_bitcast_fusion.5 = (bf16[128,512]{1,0:T(8,128)(2,1)S(1)}, bf16[128,512]{1,0:T(8,128)(2,1)S(1)}) fusion(pred[]{:T(512)} %bitcast.34, pred[]{:T(512)} %bitcast.33, pred[]{:T(512)} %bitcast.32, pred[]{:T(512)} %bitcast.7, bf16[2,128,512]{2,1,0:T(8,128)(2,1)S(1)} %bitcast.379, bf16[2,128,512]{2,1,0:T(8,128)(2,1)S(1)} %fusion.48, pred[]{:T(512)} %bitcast.47, ...), kind=kLoop, calls=%fused_computation.129 | loop fusion | flops 917504 | bytes 786440 | tf_op jit(solution)/shard_map/jit(_where)/broadcast_in_dim | solution.py:28
  93.3 2.4 %add_bitcast_fusion.4 = bf16[128,512]{1,0:T(8,128)(2,1)S(1)} fusion(pred[]{:T(512)} %bitcast.40, pred[]{:T(512)} %bitcast.39, pred[]{:T(512)} %bitcast.38, pred[]{:T(512)} %bitcast.37, bf16[2,128,512]{2,1,0:T(8,128)(2,1)S(1)} %bitcast.380, bf16[2,128,512]{2,1,0:T(8,128)(2,1)S(1)} %fusion.48), kind=kLoop, calls=%fused_computation.128 | loop fusion | flops 458752 | bytes 655364 | tf_op jit(solution)/shard_map/add | solution.py:78
  95.7 1.5 collective-permute-start.6
  97.2 1.3 collective-permute-done.8
  98.6 4.9 %collective-permute-done.6 = bf16[128,512]{1,0:T(8,128)(2,1)S(1)} collective-permute-done((bf16[128,512]{1,0:T(8,128)(2,1)S(1)}, bf16[128,512]{1,0:T(8,128)(2,1)S(1)}, u32[]{:S(2)}, u32[]{:S(2)}) %collective-permute-start.6) | collective-permute-done | bytes 131104 | tf_op jit(solution)/shard_map/ppermute | solution.py:14
  104.4 10.6 %all_to_all.31 = bf16[8,32,512]{2,1,0:T(8,128)(2,1)S(1)} all-to-all(bf16[8,32,512]{2,1,0:T(8,128)(2,1)S(1)} %select_add_fusion.3), channel_id=1, replica_groups=mesh['group'=4,'member'=8] {'member'}, dimensions={0} | all-to-all | bytes 524288 | tf_op jit(solution)/shard_map/all_to_all | solution.py:101
  115.2 9.3 %all_to_all.32 = bf16[8,32,512]{2,1,0:T(8,128)(2,1)S(1)} all-to-all(bf16[8,32,512]{2,1,0:T(8,128)(2,1)S(1)} %broadcast_in_dim.1343), channel_id=1, replica_groups=mesh['group'=4,'member'=8] {'member'}, dimensions={0} | all-to-all | bytes 524288 | tf_op jit(solution)/shard_map/all_to_all | solution.py:108
  124.9 2.5 %fusion.71 = bf16[4,32,512]{2,1,0:T(8,128)(2,1)S(1)} fusion(bf16[8,32,512]{2,1,0:T(8,128)(2,1)S(1)} %select_add_fusion.2, pred[]{:T(512)} %bitcast.28, pred[]{:T(512)} %bitcast.26, pred[]{:T(512)} %bitcast.27, pred[]{:T(512)} %bitcast.8, bf16[8,32,512]{2,1,0:T(8,128)(2,1)S(1)} %select_add_fusion.4), kind=kLoop, calls=%fused_computation.109 | loop fusion | flops 458752 | bytes 655364 | tf_op jit(solution)/shard_map/add | solution.py:78
  128.4 5.1 %add_bitcast_fusion.2 = (bf16[128,512]{1,0:T(8,128)(2,1)S(1)}, bf16[128,512]{1,0:T(8,128)(2,1)S(1)}) fusion(pred[]{:T(512)} %bitcast.34, pred[]{:T(512)} %bitcast.33, pred[]{:T(512)} %bitcast.32, pred[]{:T(512)} %bitcast.7, bf16[2,128,512]{2,1,0:T(8,128)(2,1)S(1)} %fusion.48, bf16[2,128,512]{2,1,0:T(8,128)(2,1)S(1)} %fusion.41, pred[]{:T(512)} %bitcast.47, ...), kind=kLoop, calls=%fused_computation.124 | loop fusion | flops 917504 | bytes 786440 | tf_op jit(solution)/shard_map/jit(_where)/broadcast_in_dim | solution.py:28
  133.4 1.5 collective-permute-start.11
  134.9 2.4 %add_bitcast_fusion.1 = bf16[128,512]{1,0:T(8,128)(2,1)S(1)} fusion(pred[]{:T(512)} %bitcast.40, pred[]{:T(512)} %bitcast.39, pred[]{:T(512)} %bitcast.38, pred[]{:T(512)} %bitcast.37, bf16[2,128,512]{2,1,0:T(8,128)(2,1)S(1)} %fusion.48, bf16[2,128,512]{2,1,0:T(8,128)(2,1)S(1)} %fusion.41), kind=kLoop, calls=%fused_computation.123 | loop fusion | flops 458752 | bytes 655364 | tf_op jit(solution)/shard_map/add | solution.py:78
  138.4 5.7 %collective-permute-done.9 = bf16[128,512]{1,0:T(8,128)(2,1)S(1)} collective-permute-done((bf16[128,512]{1,0:T(8,128)(2,1)S(1)}, bf16[128,512]{1,0:T(8,128)(2,1)S(1)}, u32[]{:S(2)}, u32[]{:S(2)}) %collective-permute-start.9) | collective-permute-done | bytes 131104 | tf_op jit(solution)/shard_map/ppermute | solution.py:14
  145.1 9.3 %all_to_all.33 = bf16[8,32,512]{2,1,0:T(8,128)(2,1)S(1)} all-to-all(bf16[8,32,512]{2,1,0:T(8,128)(2,1)S(1)} %select_add_fusion.1), channel_id=1, replica_groups=mesh['group'=4,'member'=8] {'member'}, dimensions={0} | all-to-all | bytes 524288 | tf_op jit(solution)/shard_map/all_to_all | solution.py:101
  (141 shorter events, 36.0 us)
Async XLA Ops:
  0.0 43.6 %copy-start = (bf16[4,512,512]{2,1,0:T(8,128)(2,1)S(1)}, bf16[4,512,512]{2,1,0:T(8,128)(2,1)}, u32[]{:S(2)}) copy-start(bf16[4,512,512]{2,1,0:T(8,128)(2,1)} %param.6) | copy-start | bytes 6291460
  0.0 15.6 %collective-permute-start.2 = (s32[4,3]{1,0:T(4,128)}, s32[4,3]{1,0:T(4,128)S(1)}, u32[]{:S(2)}, u32[]{:S(2)}) collective-permute-start(s32[4,3]{1,0:T(4,128)} %param.7), channel_id=1, source_target_pairs={{0,24},{8,0},{16,8},{24,16},{1,25},{9,1},{17,9},{25,17},{2,26},{10... | collective-permute-start | bytes 152 | tf_op jit(solution)/shard_map/ppermute | solution.py:14
  5.1 10.6 %collective-permute-start.1 = (s32[4,3]{1,0:T(4,128)}, s32[4,3]{1,0:T(4,128)S(1)}, u32[]{:S(2)}, u32[]{:S(2)}) collective-permute-start(s32[4,3]{1,0:T(4,128)} %param.7), channel_id=1, source_target_pairs={{0,16},{8,24},{16,0},{24,8},{1,17},{9,25},{17,1},{25,9},{2,18},{10... | collective-permute-start | bytes 152 | tf_op jit(solution)/shard_map/ppermute | solution.py:14
  5.1 10.6 %collective-permute-start = (s32[4,3]{1,0:T(4,128)}, s32[4,3]{1,0:T(4,128)S(1)}, u32[]{:S(2)}, u32[]{:S(2)}) collective-permute-start(s32[4,3]{1,0:T(4,128)} %param.7), channel_id=1, source_target_pairs={{0,8},{8,16},{16,24},{24,0},{1,9},{9,17},{17,25},{25,1},{2,10},{10... | collective-permute-start | bytes 152 | tf_op jit(solution)/shard_map/ppermute | solution.py:14
  7.7 13.5 %all-to-all-start = ((bf16[8,2,32,512]{3,2,1,0:T(8,128)(2,1)}), bf16[8,2,32,512]{3,2,1,0:T(8,128)(2,1)S(1)}, u32[]{:S(2)}, u32[]{:S(2)}) async-start(bf16[8,2,32,512]{3,2,1,0:T(8,128)(2,1)} %broadcast_in_dim.1176), calls=%async_computation | async-start | bytes 1048576 | tf_op jit(solution)/shard_map/all_to_all | solution.py:63
  14.9 28.6 %copy-start.9 = (pred[4]{0:T(512)(128)(4,1)}, pred[4]{0:T(512)(128)(4,1)S(1)}, u32[]{:S(2)}) copy-start(pred[4]{0:T(512)(128)(4,1)S(1)} %get-tuple-element.136) | copy-start | bytes 16
  15.0 28.6 %copy-start.11 = (pred[4]{0:T(512)(128)(4,1)}, pred[4]{0:T(512)(128)(4,1)S(1)}, u32[]{:S(2)}) copy-start(pred[4]{0:T(512)(128)(4,1)S(1)} %get-tuple-element.137) | copy-start | bytes 16
  15.0 28.6 %copy-start.13 = (pred[4]{0:T(512)(128)(4,1)}, pred[4]{0:T(512)(128)(4,1)S(1)}, u32[]{:S(2)}) copy-start(pred[4]{0:T(512)(128)(4,1)S(1)} %get-tuple-element.138) | copy-start | bytes 16
  15.0 28.6 %copy-start.15 = (pred[4]{0:T(512)(128)(4,1)}, pred[4]{0:T(512)(128)(4,1)S(1)}, u32[]{:S(2)}) copy-start(pred[4]{0:T(512)(128)(4,1)S(1)} %get-tuple-element.139) | copy-start | bytes 16
  15.6 28.0 %copy-start.7 = (pred[4]{0:T(512)(128)(4,1)}, pred[4]{0:T(512)(128)(4,1)S(1)}, u32[]{:S(2)}) copy-start(pred[4]{0:T(512)(128)(4,1)S(1)} %get-tuple-element.37) | copy-start | bytes 16
  24.3 12.6 %collective-permute-start.4 = (bf16[128,512]{1,0:T(8,128)(2,1)S(1)}, bf16[128,512]{1,0:T(8,128)(2,1)S(1)}, u32[]{:S(2)}, u32[]{:S(2)}) collective-permute-start(bf16[128,512]{1,0:T(8,128)(2,1)S(1)} %bitcast.405), channel_id=1, source_target_pairs={{0,16},{8,24},{16,0},{24,8},{1,17},{9,25},{17,1},{25,9},{2,18},{10... | collective-permute-start | bytes 393224 | tf_op jit(solution)/shard_map/ppermute | solution.py:14
  31.4 5.6 %collective-permute-start.5 = (bf16[128,512]{1,0:T(8,128)(2,1)S(1)}, bf16[128,512]{1,0:T(8,128)(2,1)S(1)}, u32[]{:S(2)}, u32[]{:S(2)}) collective-permute-start(bf16[128,512]{1,0:T(8,128)(2,1)S(1)} %get-tuple-element.47), channel_id=1, source_target_pairs={{0,24},{8,0},{16,8},{24,16},{1,25},{9,1},{17,9},{25,17},{2,26},{10... | collective-permute-start | bytes 393224 | tf_op jit(solution)/shard_map/ppermute | solution.py:14
  36.8 6.8 %collective-permute-start.3 = (bf16[128,512]{1,0:T(8,128)(2,1)S(1)}, bf16[128,512]{1,0:T(8,128)(2,1)S(1)}, u32[]{:S(2)}, u32[]{:S(2)}) collective-permute-start(bf16[128,512]{1,0:T(8,128)(2,1)S(1)} %add_bitcast_fusion.7), channel_id=1, source_target_pairs={{0,8},{8,16},{16,24},{24,0},{1,9},{9,17},{17,25},{25,1},{2,10},{10... | collective-permute-start | bytes 393224 | tf_op jit(solution)/shard_map/ppermute | solution.py:14
  36.8 7.4 %copy-start.17 = (pred[4]{0:T(512)(128)(4,1)}, pred[4]{0:T(512)(128)(4,1)S(1)}, u32[]{:S(2)}) copy-start(pred[4]{0:T(512)(128)(4,1)S(1)} %compare_and_fusion.3) | copy-start | bytes 16
  44.3 9.7 %copy-start.1 = (bf16[1,512,512]{2,1,0:T(8,128)(2,1)S(1)}, bf16[1,512,512]{2,1,0:T(8,128)(2,1)}, u32[]{:S(2)}) copy-start(bf16[1,512,512]{2,1,0:T(8,128)(2,1)} %param.9) | copy-start | bytes 1572868
  55.8 29.3 %all-to-all-start.2 = ((bf16[8,32,512]{2,1,0:T(8,128)(2,1)}), bf16[8,32,512]{2,1,0:T(8,128)(2,1)S(1)}, u32[]{:S(2)}, u32[]{:S(2)}) async-start(bf16[8,32,512]{2,1,0:T(8,128)(2,1)} %broadcast_in_dim.1256), calls=%async_computation.2 | async-start | bytes 524288 | tf_op jit(solution)/shard_map/all_to_all | solution.py:108
  85.1 2.0 %copy-start.3 = (pred[2,128]{1,0:T(4,128)(4,1)S(1)}, pred[2,128]{1,0:T(4,128)(4,1)}, u32[]{:S(2)}) copy-start(pred[2,128]{1,0:T(4,128)(4,1)} %broadcast_in_dim.1299) | copy-start | bytes 772
  85.1 2.0 %copy-start.4 = (pred[2,128]{1,0:T(4,128)(4,1)S(1)}, pred[2,128]{1,0:T(4,128)(4,1)}, u32[]{:S(2)}) copy-start(pred[2,128]{1,0:T(4,128)(4,1)} %broadcast_in_dim.1294) | copy-start | bytes 772
  85.2 2.0 %copy-start.5 = (pred[2,128]{1,0:T(4,128)(4,1)S(1)}, pred[2,128]{1,0:T(4,128)(4,1)}, u32[]{:S(2)}) copy-start(pred[2,128]{1,0:T(4,128)(4,1)} %broadcast_in_dim.1289) | copy-start | bytes 772
  86.7 11.8 %collective-permute-start.7 = (bf16[128,512]{1,0:T(8,128)(2,1)S(1)}, bf16[128,512]{1,0:T(8,128)(2,1)S(1)}, u32[]{:S(2)}, u32[]{:S(2)}) collective-permute-start(bf16[128,512]{1,0:T(8,128)(2,1)S(1)} %fusion.76), channel_id=1, source_target_pairs={{0,16},{8,24},{16,0},{24,8},{1,17},{9,25},{17,1},{25,9},{2,18},{10... | collective-permute-start | bytes 393224 | tf_op jit(solution)/shard_map/ppermute | solution.py:14
  87.0 16.4 %copy-start.8 = (pred[4]{0:T(512)(128)(4,1)S(1)}, pred[4]{0:T(512)(128)(4,1)}, u32[]{:S(2)}) copy-start(pred[4]{0:T(512)(128)(4,1)} %copy-done.7) | copy-start | bytes 16
  87.0 16.4 %copy-start.10 = (pred[4]{0:T(512)(128)(4,1)S(1)}, pred[4]{0:T(512)(128)(4,1)}, u32[]{:S(2)}) copy-start(pred[4]{0:T(512)(128)(4,1)} %copy-done.9) | copy-start | bytes 16
  87.0 16.4 %copy-start.12 = (pred[4]{0:T(512)(128)(4,1)S(1)}, pred[4]{0:T(512)(128)(4,1)}, u32[]{:S(2)}) copy-start(pred[4]{0:T(512)(128)(4,1)} %copy-done.11) | copy-start | bytes 16
  87.0 16.4 %copy-start.14 = (pred[4]{0:T(512)(128)(4,1)S(1)}, pred[4]{0:T(512)(128)(4,1)}, u32[]{:S(2)}) copy-start(pred[4]{0:T(512)(128)(4,1)} %copy-done.13) | copy-start | bytes 16
  87.0 16.4 %copy-start.16 = (pred[4]{0:T(512)(128)(4,1)S(1)}, pred[4]{0:T(512)(128)(4,1)}, u32[]{:S(2)}) copy-start(pred[4]{0:T(512)(128)(4,1)} %copy-done.15) | copy-start | bytes 16
  87.0 16.4 %copy-start.18 = (pred[4]{0:T(512)(128)(4,1)S(1)}, pred[4]{0:T(512)(128)(4,1)}, u32[]{:S(2)}) copy-start(pred[4]{0:T(512)(128)(4,1)} %copy-done.17) | copy-start | bytes 16
  92.7 5.9 %collective-permute-start.8 = (bf16[128,512]{1,0:T(8,128)(2,1)S(1)}, bf16[128,512]{1,0:T(8,128)(2,1)S(1)}, u32[]{:S(2)}, u32[]{:S(2)}) collective-permute-start(bf16[128,512]{1,0:T(8,128)(2,1)S(1)} %get-tuple-element.42), channel_id=1, source_target_pairs={{0,24},{8,0},{16,8},{24,16},{1,25},{9,1},{17,9},{25,17},{2,26},{10... | collective-permute-start | bytes 393224 | tf_op jit(solution)/shard_map/ppermute | solution.py:14
  95.7 7.7 %collective-permute-start.6 = (bf16[128,512]{1,0:T(8,128)(2,1)S(1)}, bf16[128,512]{1,0:T(8,128)(2,1)S(1)}, u32[]{:S(2)}, u32[]{:S(2)}) collective-permute-start(bf16[128,512]{1,0:T(8,128)(2,1)S(1)} %add_bitcast_fusion.4), channel_id=1, source_target_pairs={{0,8},{8,16},{16,24},{24,0},{1,9},{9,17},{17,25},{25,1},{2,10},{10... | collective-permute-start | bytes 393224 | tf_op jit(solution)/shard_map/ppermute | solution.py:14
  104.1 11.0 %copy-start.2 = (f32[3,1,32,512]{3,2,1,0:T(8,128)S(1)}, f32[3,1,32,512]{3,2,1,0:T(8,128)}, u32[]{:S(2)}) copy-start(f32[3,1,32,512]{3,2,1,0:T(8,128)} %param.10) | copy-start | bytes 589828
  127.4 11.1 %collective-permute-start.10 = (bf16[128,512]{1,0:T(8,128)(2,1)S(1)}, bf16[128,512]{1,0:T(8,128)(2,1)S(1)}, u32[]{:S(2)}, u32[]{:S(2)}) collective-permute-start(bf16[128,512]{1,0:T(8,128)(2,1)S(1)} %bitcast.404), channel_id=1, source_target_pairs={{0,16},{8,24},{16,0},{24,8},{1,17},{9,25},{17,1},{25,9},{2,18},{10... | collective-permute-start | bytes 393224 | tf_op jit(solution)/shard_map/ppermute | solution.py:14
  133.4 5.0 %collective-permute-start.11 = (bf16[128,512]{1,0:T(8,128)(2,1)S(1)}, bf16[128,512]{1,0:T(8,128)(2,1)S(1)}, u32[]{:S(2)}, u32[]{:S(2)}) collective-permute-start(bf16[128,512]{1,0:T(8,128)(2,1)S(1)} %get-tuple-element.40), channel_id=1, source_target_pairs={{0,24},{8,0},{16,8},{24,16},{1,25},{9,1},{17,9},{25,17},{2,26},{10... | collective-permute-start | bytes 393224 | tf_op jit(solution)/shard_map/ppermute | solution.py:14
  137.3 6.8 %collective-permute-start.9 = (bf16[128,512]{1,0:T(8,128)(2,1)S(1)}, bf16[128,512]{1,0:T(8,128)(2,1)S(1)}, u32[]{:S(2)}, u32[]{:S(2)}) collective-permute-start(bf16[128,512]{1,0:T(8,128)(2,1)S(1)} %add_bitcast_fusion.1), channel_id=1, source_target_pairs={{0,8},{8,16},{16,24},{24,0},{1,9},{9,17},{17,25},{25,1},{2,10},{10... | collective-permute-start | bytes 393224 | tf_op jit(solution)/shard_map/ppermute | solution.py:14
  (1 other events, 2.0 us)

commit v12 on v11

--- a/solution.py
+++ b/solution.py
@@ -69,23 +69,24 @@
     for step in range(STEPS):
         near = blocks[DELAYS + step - 1]
         far = blocks[DELAYS + step - 2]
-        def piece_for(k, near, far):
+        def pieces_for(rows, take_near, take_far):
             total = None
             for block in range(group_blocks):
-                term = jnp.where(from_near[k, block], near[block], 0) + jnp.where(
-                    from_far[k, block], far[block], 0
+                term = jnp.where(take_near[rows, block, None, None], near[block][None], 0) + jnp.where(
+                    take_far[rows, block, None, None], far[block][None], 0
                 )
                 total = term if total is None else total + term
             return total
 
         middle = groups // 2
-        first = piece_for(middle, near, far)
+        first = pieces_for(slice(middle, middle + 1), from_near, from_far)[0]
         arrived = {middle: shifted(first, "group", groups, middle)}
-        first, near, far = lax.optimization_barrier((first, near, far))
+        first, take_near, take_far = lax.optimization_barrier((first, from_near, from_far))
+        outgoing = pieces_for(slice(None), take_near, take_far)
         for k in range(1, groups):
             if k != middle:
-                arrived[k] = shifted(piece_for(k, near, far), "group", groups, k)
-        received = [piece_for(0, near, far)] + [arrived[k] for k in range(1, groups)]
+                arrived[k] = shifted(outgoing[k], "group", groups, k)
+        received = [outgoing[0]] + [arrived[k] for k in range(1, groups)]
         blocks_in = pick(received, source_shift)
         terms = jnp.einsum(
             "kes,kso->keo", blocks_in, tile_values, preferred_element_type=jnp.float32

time: 157 us -> 122 us (0.78)
  local copies, waits for them, and re-layouts: 31.1 us -> 3.62 us
  other arithmetic: 36.7 us -> 15.5 us
  blocking collectives: 38.6 us -> 47.9 us
  waiting for transfers between devices: 22.2 us -> 28.4 us
    broadcast_in_dim x48 -> x12, local copies, waits for them, and re-layouts: 26.4 us -> 0.25 us  [pick(): jnp.where(chosen[:, k][spread], piece[None], jnp.zeros_like(piece)[None])]
    broadcast_in_dim x3 -> x0, other arithmetic: 15.2 us -> none  [pick(): jnp.where(chosen[:, k][spread], piece[None], jnp.zeros_like(piece)[None])]
    all_to_all x1 -> x2, blocking collectives: 9.35 us -> 18.7 us  [body(): got = lax.all_to_all(spread, 'member', 0, 0, tiled=True)]
    ppermute x12, waiting for transfers between devices: 19.2 us -> 24.6 us  [shifted(): return lax.ppermute(x, axis, [(i, (i + k) % n) for i in range(n)])]
    select_n x2 -> x0, other arithmetic: 3.73 us -> none  [the longest x1 2.5 us: piece_for(): jnp.where(from_far[k, block], far[block], 0)]
    ppermute x12, starting transfers between devices: 15.7 us -> 19.2 us  [shifted(): return lax.ppermute(x, axis, [(i, (i + k) % n) for i in range(n)])]
    all_to_all x1 -> x0, starting transfers between devices: 3.41 us -> none  [body(): got = lax.all_to_all(spread, 'member', 0, 0, tiled=True)]
    add x5 -> x6, other arithmetic: 9.77 us -> 8.46 us  [pieces_for(): total = term if total is None else total + term]
  transfers between devices with their start and end apart: 14 -> 13, of which waited for: 7 -> 9; matrix products, arithmetic and copies ran while one was open for 37% -> 7% of each run, Pallas kernels for 0% -> 0%
where the time goes in v12:
time: 122 us; the launch traced here: 121 us
  blocking collectives  47.9 us (39%)
  waiting for transfers between devices  28.4 us (23%)
  starting transfers between devices  22.9 us (19%)
  other arithmetic  15.5 us (13%)
  local copies, waits for them, and re-layouts  3.62 us (3%)
  matrix products  2.31 us (2%)
    all_to_all x3, blocking collectives, body(): got = lax.all_to_all(sent, 'member', 0, 0, tiled=True)  29.2 us
    ppermute x12, waiting for transfers between devices, shifted(): return lax.ppermute(x, axis, [(i, (i + k) % n) for i in range(n)])  24.6 us
    ppermute x12, starting transfers between devices, shifted(): return lax.ppermute(x, axis, [(i, (i + k) % n) for i in range(n)])  19.2 us
    all_to_all x2, blocking collectives, body(): got = lax.all_to_all(spread, 'member', 0, 0, tiled=True)  18.7 us
    add x6, other arithmetic, pieces_for(): total = term if total is None else total + term  8.46 us
    all_to_all x1, waiting for transfers between devices, body(): hist_got = lax.all_to_all(spread_hist, 'member', 0, 0, tiled=True)  3.74 us
    all_to_all x1, starting transfers between devices, body(): hist_got = lax.all_to_all(spread_hist, 'member', 0, 0, tiled=True)  3.72 us
  transfers between devices with their start and end apart: 13, of which 9 were waited for; matrix products, arithmetic and copies ran while one was open for 7% of the time, Pallas kernels for 0%

profile of v12, /device:TPU:0, one launch (start us, length us, event | category | flops | bytes accessed | tf_op | source)
XLA Modules:
  0.0 121.0 jit_solution(13335405242835256209)
XLA Ops:
  0.0 3.0 %collective-permute-start = (s32[4,3]{1,0:T(4,128)}, s32[4,3]{1,0:T(4,128)S(1)}, u32[]{:S(2)}, u32[]{:S(2)}) collective-permute-start(s32[4,3]{1,0:T(4,128)} %param.7), channel_id=1, source_target_pairs={{0,8},{8,16},{16,24},{24,0},{1,9},{9,17},{17,25},{25,1},{2,10},{10... | collective-permute-start | bytes 152 | tf_op jit(solution)/shard_map/ppermute | solution.py:14
  3.0 2.1 %collective-permute-start.2 = (s32[4,3]{1,0:T(4,128)}, s32[4,3]{1,0:T(4,128)S(1)}, u32[]{:S(2)}, u32[]{:S(2)}) collective-permute-start(s32[4,3]{1,0:T(4,128)} %param.7), channel_id=1, source_target_pairs={{0,24},{8,0},{16,8},{24,16},{1,25},{9,1},{17,9},{25,17},{2,26},{10... | collective-permute-start | bytes 152 | tf_op jit(solution)/shard_map/ppermute | solution.py:14
  5.1 1.0 collective-permute-start.1
  6.1 1.7 %broadcast_in_dim.1247 = bf16[8,2,32,512]{3,2,1,0:T(8,128)(2,1)} broadcast(bf16[2,32,512]{2,1,0:T(8,128)(2,1)} %bitcast.312), dimensions={1,2,3} | broadcast | bytes 589824 | tf_op jit(solution)/shard_map/broadcast_in_dim | solution.py:62
  7.7 3.7 %all-to-all-start = ((bf16[8,2,32,512]{3,2,1,0:T(8,128)(2,1)}), bf16[8,2,32,512]{3,2,1,0:T(8,128)(2,1)S(1)}, u32[]{:S(2)}, u32[]{:S(2)}) async-start(bf16[8,2,32,512]{3,2,1,0:T(8,128)(2,1)} %broadcast_in_dim.1247), calls=%async_computation | async-start | bytes 1048576 | tf_op jit(solution)/shard_map/all_to_all | solution.py:63
  11.5 0.9 fusion.74
  12.5 0.8 select_reduce_fusion.6
  13.9 1.0 slice_reduce_fusion.2
  15.0 0.7 pad_add_fusion
  17.5 3.7 %all-to-all-done = bf16[8,2,32,512]{3,2,1,0:T(8,128)(2,1)S(1)} async-done(((bf16[8,2,32,512]{3,2,1,0:T(8,128)(2,1)}), bf16[8,2,32,512]{3,2,1,0:T(8,128)(2,1)S(1)}, u32[]{:S(2)}, u32[]{:S(2)}) %all-to-all-start) | async-done | bytes 524320 | tf_op jit(solution)/shard_map/all_to_all | solution.py:63
  21.8 2.6 %add_add_fusion.5 = bf16[128,512]{1,0:T(8,128)(2,1)S(1)} fusion(pred[]{:T(512)} %bitcast.30, pred[]{:T(512)} %bitcast.28, pred[]{:T(512)} %bitcast.26, pred[]{:T(512)} %bitcast.7, bf16[4,1,32,512]{3,2,0,1:T(8,128)(2,1)S(1)} %get-tuple-element.41, bf16[4,1,32,512]{3,2,0,1:T(8,128)(2,1)S(1)} %get-tuple-element.42, ...), kind=kLoop, calls=%fused_computation.97 | loop fusion | flops 458752 | bytes 655364 | tf_op jit(solution)/shard_map/add | solution.py:78
  24.4 2.2 %collective-permute-start.4 = (bf16[128,512]{1,0:T(8,128)(2,1)S(1)}, bf16[128,512]{1,0:T(8,128)(2,1)S(1)}, u32[]{:S(2)}, u32[]{:S(2)}) collective-permute-start(bf16[128,512]{1,0:T(8,128)(2,1)S(1)} %add_add_fusion.5), channel_id=1, source_target_pairs={{0,16},{8,24},{16,0},{24,8},{1,17},{9,25},{17,1},{25,9},{2,18},{10... | collective-permute-start | bytes 393224 | tf_op jit(solution)/shard_map/ppermute | solution.py:14
  26.9 1.9 %collective-permute-start.5 = (bf16[128,512]{1,0:T(8,128)(2,1)S(1)}, bf16[128,512]{1,0:T(8,128)(2,1)S(1)}, u32[]{:S(2)}, u32[]{:S(2)}) collective-permute-start(bf16[128,512]{1,0:T(8,128)(2,1)S(1)} %get-tuple-element.38), channel_id=1, source_target_pairs={{0,24},{8,0},{16,8},{24,16},{1,25},{9,1},{17,9},{25,17},{2,26},{10... | collective-permute-start | bytes 393224 | tf_op jit(solution)/shard_map/ppermute | solution.py:14
  29.0 5.0 %collective-permute-done.4 = bf16[128,512]{1,0:T(8,128)(2,1)S(1)} collective-permute-done((bf16[128,512]{1,0:T(8,128)(2,1)S(1)}, bf16[128,512]{1,0:T(8,128)(2,1)S(1)}, u32[]{:S(2)}, u32[]{:S(2)}) %collective-permute-start.4) | collective-permute-done | bytes 131104 | tf_op jit(solution)/shard_map/ppermute | solution.py:14
  34.0 1.7 %collective-permute-done.3 = bf16[128,512]{1,0:T(8,128)(2,1)S(1)} collective-permute-done((bf16[128,512]{1,0:T(8,128)(2,1)S(1)}, bf16[128,512]{1,0:T(8,128)(2,1)S(1)}, u32[]{:S(2)}, u32[]{:S(2)}) %collective-permute-start.3) | collective-permute-done | bytes 131104 | tf_op jit(solution)/shard_map/ppermute | solution.py:14
  36.7 10.5 %all_to_all.30 = bf16[8,32,512]{2,1,0:T(8,128)(2,1)S(1)} all-to-all(bf16[8,32,512]{2,1,0:T(8,128)(2,1)S(1)} %select_add_fusion.5), channel_id=1, replica_groups=mesh['group'=4,'member'=8] {'member'}, dimensions={0} | all-to-all | bytes 524288 | tf_op jit(solution)/shard_map/all_to_all | solution.py:102
  47.5 9.3 %all_to_all.31 = bf16[8,32,512]{2,1,0:T(8,128)(2,1)S(1)} all-to-all(bf16[8,32,512]{2,1,0:T(8,128)(2,1)S(1)} %broadcast_in_dim.1344), channel_id=1, replica_groups=mesh['group'=4,'member'=8] {'member'}, dimensions={0} | all-to-all | bytes 524288 | tf_op jit(solution)/shard_map/all_to_all | solution.py:109
  57.1 2.6 %add_add_fusion.4 = bf16[128,512]{1,0:T(8,128)(2,1)S(1)} fusion(pred[]{:T(512)} %bitcast.30, pred[]{:T(512)} %bitcast.28, pred[]{:T(512)} %bitcast.26, pred[]{:T(512)} %bitcast.7, bf16[4,32,512]{2,1,0:T(8,128)(2,1)S(1)} %get-tuple-element.79, bf16[4,32,512]{2,1,0:T(8,128)(2,1)S(1)} %get-tuple-element.78, bf16[4,1,32,512]{3,2,0,1:T(8,128)(2,1)S(1)} %get-tuple-element.42, ...), kind=kLoop, calls=%fused_computation.94 | loop fusion | flops 458752 | bytes 655364 | tf_op jit(solution)/shard_map/add | solution.py:78
  59.7 2.2 %collective-permute-start.7 = (bf16[128,512]{1,0:T(8,128)(2,1)S(1)}, bf16[128,512]{1,0:T(8,128)(2,1)S(1)}, u32[]{:S(2)}, u32[]{:S(2)}) collective-permute-start(bf16[128,512]{1,0:T(8,128)(2,1)S(1)} %add_add_fusion.4), channel_id=1, source_target_pairs={{0,16},{8,24},{16,0},{24,8},{1,17},{9,25},{17,1},{25,9},{2,18},{10... | collective-permute-start | bytes 393224 | tf_op jit(solution)/shard_map/ppermute | solution.py:14
  62.2 2.5 %collective-permute-start.8 = (bf16[128,512]{1,0:T(8,128)(2,1)S(1)}, bf16[128,512]{1,0:T(8,128)(2,1)S(1)}, u32[]{:S(2)}, u32[]{:S(2)}) collective-permute-start(bf16[128,512]{1,0:T(8,128)(2,1)S(1)} %get-tuple-element.35), channel_id=1, source_target_pairs={{0,24},{8,0},{16,8},{24,16},{1,25},{9,1},{17,9},{25,17},{2,26},{10... | collective-permute-start | bytes 393224 | tf_op jit(solution)/shard_map/ppermute | solution.py:14
  64.7 6.2 %collective-permute-done.7 = bf16[128,512]{1,0:T(8,128)(2,1)S(1)} collective-permute-done((bf16[128,512]{1,0:T(8,128)(2,1)S(1)}, bf16[128,512]{1,0:T(8,128)(2,1)S(1)}, u32[]{:S(2)}, u32[]{:S(2)}) %collective-permute-start.7) | collective-permute-done | bytes 131104 | tf_op jit(solution)/shard_map/ppermute | solution.py:14
  70.9 1.7 %collective-permute-done.6 = bf16[128,512]{1,0:T(8,128)(2,1)S(1)} collective-permute-done((bf16[128,512]{1,0:T(8,128)(2,1)S(1)}, bf16[128,512]{1,0:T(8,128)(2,1)S(1)}, u32[]{:S(2)}, u32[]{:S(2)}) %collective-permute-start.6) | collective-permute-done | bytes 131104 | tf_op jit(solution)/shard_map/ppermute | solution.py:14
  73.5 9.4 %all_to_all.32 = bf16[8,32,512]{2,1,0:T(8,128)(2,1)S(1)} all-to-all(bf16[8,32,512]{2,1,0:T(8,128)(2,1)S(1)} %select_add_fusion.3), channel_id=1, replica_groups=mesh['group'=4,'member'=8] {'member'}, dimensions={0} | all-to-all | bytes 524288 | tf_op jit(solution)/shard_map/all_to_all | solution.py:102
  83.2 9.3 %all_to_all.33 = bf16[8,32,512]{2,1,0:T(8,128)(2,1)S(1)} all-to-all(bf16[8,32,512]{2,1,0:T(8,128)(2,1)S(1)} %broadcast_in_dim.1399), channel_id=1, replica_groups=mesh['group'=4,'member'=8] {'member'}, dimensions={0} | all-to-all | bytes 524288 | tf_op jit(solution)/shard_map/all_to_all | solution.py:109
  92.8 2.6 %add_add_fusion.3 = bf16[128,512]{1,0:T(8,128)(2,1)S(1)} fusion(pred[]{:T(512)} %bitcast.30, pred[]{:T(512)} %bitcast.28, pred[]{:T(512)} %bitcast.26, pred[]{:T(512)} %bitcast.7, bf16[4,32,512]{2,1,0:T(8,128)(2,1)S(1)} %get-tuple-element.61, bf16[4,32,512]{2,1,0:T(8,128)(2,1)S(1)} %get-tuple-element.60, bf16[4,32,512]{2,1,0:T(8,128)(2,1)S(1)} %get-tuple-element.79, ...), kind=kLoop, calls=%fused_computation.91 | loop fusion | flops 458752 | bytes 655364 | tf_op jit(solution)/shard_map/add | solution.py:78
  95.7 1.5 %collective-permute-start.11 = (bf16[128,512]{1,0:T(8,128)(2,1)S(1)}, bf16[128,512]{1,0:T(8,128)(2,1)S(1)}, u32[]{:S(2)}, u32[]{:S(2)}) collective-permute-start(bf16[128,512]{1,0:T(8,128)(2,1)S(1)} %get-tuple-element.32), channel_id=1, source_target_pairs={{0,24},{8,0},{16,8},{24,16},{1,25},{9,1},{17,9},{25,17},{2,26},{10... | collective-permute-start | bytes 393224 | tf_op jit(solution)/shard_map/ppermute | solution.py:14
  97.8 2.1 %collective-permute-start.10 = (bf16[128,512]{1,0:T(8,128)(2,1)S(1)}, bf16[128,512]{1,0:T(8,128)(2,1)S(1)}, u32[]{:S(2)}, u32[]{:S(2)}) collective-permute-start(bf16[128,512]{1,0:T(8,128)(2,1)S(1)} %add_add_fusion.3), channel_id=1, source_target_pairs={{0,16},{8,24},{16,0},{24,8},{1,17},{9,25},{17,1},{25,9},{2,18},{10... | collective-permute-start | bytes 393224 | tf_op jit(solution)/shard_map/ppermute | solution.py:14
  99.9 3.3 %collective-permute-done.11 = bf16[128,512]{1,0:T(8,128)(2,1)S(1)} collective-permute-done((bf16[128,512]{1,0:T(8,128)(2,1)S(1)}, bf16[128,512]{1,0:T(8,128)(2,1)S(1)}, u32[]{:S(2)}, u32[]{:S(2)}) %collective-permute-start.11) | collective-permute-done | bytes 131104 | tf_op jit(solution)/shard_map/ppermute | solution.py:14
  103.2 2.9 %collective-permute-done.9 = bf16[128,512]{1,0:T(8,128)(2,1)S(1)} collective-permute-done((bf16[128,512]{1,0:T(8,128)(2,1)S(1)}, bf16[128,512]{1,0:T(8,128)(2,1)S(1)}, u32[]{:S(2)}, u32[]{:S(2)}) %collective-permute-start.9) | collective-permute-done | bytes 131104 | tf_op jit(solution)/shard_map/ppermute | solution.py:14
  106.1 3.7 %collective-permute-done.10 = bf16[128,512]{1,0:T(8,128)(2,1)S(1)} collective-permute-done((bf16[128,512]{1,0:T(8,128)(2,1)S(1)}, bf16[128,512]{1,0:T(8,128)(2,1)S(1)}, u32[]{:S(2)}, u32[]{:S(2)}) %collective-permute-start.10) | collective-permute-done | bytes 131104 | tf_op jit(solution)/shard_map/ppermute | solution.py:14
  110.7 9.3 %all_to_all.34 = bf16[8,32,512]{2,1,0:T(8,128)(2,1)S(1)} all-to-all(bf16[8,32,512]{2,1,0:T(8,128)(2,1)S(1)} %select_add_fusion.1), channel_id=1, replica_groups=mesh['group'=4,'member'=8] {'member'}, dimensions={0} | all-to-all | bytes 524288 | tf_op jit(solution)/shard_map/all_to_all | solution.py:102
  120.3 0.7 maximum_bitcast_fusion
  (73 shorter events, 8.8 us)
Async XLA Ops:
  0.0 35.7 %copy-start = (bf16[4,512,512]{2,1,0:T(8,128)(2,1)S(1)}, bf16[4,512,512]{2,1,0:T(8,128)(2,1)}, u32[]{:S(2)}) copy-start(bf16[4,512,512]{2,1,0:T(8,128)(2,1)} %param.6) | copy-start | bytes 6291460
  0.0 15.0 %collective-permute-start = (s32[4,3]{1,0:T(4,128)}, s32[4,3]{1,0:T(4,128)S(1)}, u32[]{:S(2)}, u32[]{:S(2)}) collective-permute-start(s32[4,3]{1,0:T(4,128)} %param.7), channel_id=1, source_target_pairs={{0,8},{8,16},{16,24},{24,0},{1,9},{9,17},{17,25},{25,1},{2,10},{10... | collective-permute-start | bytes 152 | tf_op jit(solution)/shard_map/ppermute | solution.py:14
  3.0 12.0 %collective-permute-start.2 = (s32[4,3]{1,0:T(4,128)}, s32[4,3]{1,0:T(4,128)S(1)}, u32[]{:S(2)}, u32[]{:S(2)}) collective-permute-start(s32[4,3]{1,0:T(4,128)} %param.7), channel_id=1, source_target_pairs={{0,24},{8,0},{16,8},{24,16},{1,25},{9,1},{17,9},{25,17},{2,26},{10... | collective-permute-start | bytes 152 | tf_op jit(solution)/shard_map/ppermute | solution.py:14
  5.1 9.9 %collective-permute-start.1 = (s32[4,3]{1,0:T(4,128)}, s32[4,3]{1,0:T(4,128)S(1)}, u32[]{:S(2)}, u32[]{:S(2)}) collective-permute-start(s32[4,3]{1,0:T(4,128)} %param.7), channel_id=1, source_target_pairs={{0,16},{8,24},{16,0},{24,8},{1,17},{9,25},{17,1},{25,9},{2,18},{10... | collective-permute-start | bytes 152 | tf_op jit(solution)/shard_map/ppermute | solution.py:14
  7.7 13.5 %all-to-all-start = ((bf16[8,2,32,512]{3,2,1,0:T(8,128)(2,1)}), bf16[8,2,32,512]{3,2,1,0:T(8,128)(2,1)S(1)}, u32[]{:S(2)}, u32[]{:S(2)}) async-start(bf16[8,2,32,512]{3,2,1,0:T(8,128)(2,1)} %broadcast_in_dim.1247), calls=%async_computation | async-start | bytes 1048576 | tf_op jit(solution)/shard_map/all_to_all | solution.py:63
  24.4 9.5 %collective-permute-start.4 = (bf16[128,512]{1,0:T(8,128)(2,1)S(1)}, bf16[128,512]{1,0:T(8,128)(2,1)S(1)}, u32[]{:S(2)}, u32[]{:S(2)}) collective-permute-start(bf16[128,512]{1,0:T(8,128)(2,1)S(1)} %add_add_fusion.5), channel_id=1, source_target_pairs={{0,16},{8,24},{16,0},{24,8},{1,17},{9,25},{17,1},{25,9},{2,18},{10... | collective-permute-start | bytes 393224 | tf_op jit(solution)/shard_map/ppermute | solution.py:14
  26.9 7.1 %collective-permute-start.5 = (bf16[128,512]{1,0:T(8,128)(2,1)S(1)}, bf16[128,512]{1,0:T(8,128)(2,1)S(1)}, u32[]{:S(2)}, u32[]{:S(2)}) collective-permute-start(bf16[128,512]{1,0:T(8,128)(2,1)S(1)} %get-tuple-element.38), channel_id=1, source_target_pairs={{0,24},{8,0},{16,8},{24,16},{1,25},{9,1},{17,9},{25,17},{2,26},{10... | collective-permute-start | bytes 393224 | tf_op jit(solution)/shard_map/ppermute | solution.py:14
  28.8 7.0 %collective-permute-start.3 = (bf16[128,512]{1,0:T(8,128)(2,1)S(1)}, bf16[128,512]{1,0:T(8,128)(2,1)S(1)}, u32[]{:S(2)}, u32[]{:S(2)}) collective-permute-start(bf16[128,512]{1,0:T(8,128)(2,1)S(1)} %get-tuple-element.39), channel_id=1, source_target_pairs={{0,8},{8,16},{16,24},{24,0},{1,9},{9,17},{17,25},{25,1},{2,10},{10... | collective-permute-start | bytes 393224 | tf_op jit(solution)/shard_map/ppermute | solution.py:14
  36.4 10.9 %copy-start.1 = (bf16[1,512,512]{2,1,0:T(8,128)(2,1)S(1)}, bf16[1,512,512]{2,1,0:T(8,128)(2,1)}, u32[]{:S(2)}) copy-start(bf16[1,512,512]{2,1,0:T(8,128)(2,1)} %param.9) | copy-start | bytes 1572868
  36.4 10.9 %copy-start.2 = (f32[3,1,32,512]{3,2,1,0:T(8,128)S(1)}, f32[3,1,32,512]{3,2,1,0:T(8,128)}, u32[]{:S(2)}) copy-start(f32[3,1,32,512]{3,2,1,0:T(8,128)} %param.10) | copy-start | bytes 589828
  59.7 11.2 %collective-permute-start.7 = (bf16[128,512]{1,0:T(8,128)(2,1)S(1)}, bf16[128,512]{1,0:T(8,128)(2,1)S(1)}, u32[]{:S(2)}, u32[]{:S(2)}) collective-permute-start(bf16[128,512]{1,0:T(8,128)(2,1)S(1)} %add_add_fusion.4), channel_id=1, source_target_pairs={{0,16},{8,24},{16,0},{24,8},{1,17},{9,25},{17,1},{25,9},{2,18},{10... | collective-permute-start | bytes 393224 | tf_op jit(solution)/shard_map/ppermute | solution.py:14
  62.2 8.7 %collective-permute-start.8 = (bf16[128,512]{1,0:T(8,128)(2,1)S(1)}, bf16[128,512]{1,0:T(8,128)(2,1)S(1)}, u32[]{:S(2)}, u32[]{:S(2)}) collective-permute-start(bf16[128,512]{1,0:T(8,128)(2,1)S(1)} %get-tuple-element.35), channel_id=1, source_target_pairs={{0,24},{8,0},{16,8},{24,16},{1,25},{9,1},{17,9},{25,17},{2,26},{10... | collective-permute-start | bytes 393224 | tf_op jit(solution)/shard_map/ppermute | solution.py:14
  64.7 8.0 %collective-permute-start.6 = (bf16[128,512]{1,0:T(8,128)(2,1)S(1)}, bf16[128,512]{1,0:T(8,128)(2,1)S(1)}, u32[]{:S(2)}, u32[]{:S(2)}) collective-permute-start(bf16[128,512]{1,0:T(8,128)(2,1)S(1)} %get-tuple-element.36), channel_id=1, source_target_pairs={{0,8},{8,16},{16,24},{24,0},{1,9},{9,17},{17,25},{25,1},{2,10},{10... | collective-permute-start | bytes 393224 | tf_op jit(solution)/shard_map/ppermute | solution.py:14
  95.7 7.5 %collective-permute-start.11 = (bf16[128,512]{1,0:T(8,128)(2,1)S(1)}, bf16[128,512]{1,0:T(8,128)(2,1)S(1)}, u32[]{:S(2)}, u32[]{:S(2)}) collective-permute-start(bf16[128,512]{1,0:T(8,128)(2,1)S(1)} %get-tuple-element.32), channel_id=1, source_target_pairs={{0,24},{8,0},{16,8},{24,16},{1,25},{9,1},{17,9},{25,17},{2,26},{10... | collective-permute-start | bytes 393224 | tf_op jit(solution)/shard_map/ppermute | solution.py:14
  97.2 8.9 %collective-permute-start.9 = (bf16[128,512]{1,0:T(8,128)(2,1)S(1)}, bf16[128,512]{1,0:T(8,128)(2,1)S(1)}, u32[]{:S(2)}, u32[]{:S(2)}) collective-permute-start(bf16[128,512]{1,0:T(8,128)(2,1)S(1)} %get-tuple-element.33), channel_id=1, source_target_pairs={{0,8},{8,16},{16,24},{24,0},{1,9},{9,17},{17,25},{25,1},{2,10},{10... | collective-permute-start | bytes 393224 | tf_op jit(solution)/shard_map/ppermute | solution.py:14
  97.8 12.0 %collective-permute-start.10 = (bf16[128,512]{1,0:T(8,128)(2,1)S(1)}, bf16[128,512]{1,0:T(8,128)(2,1)S(1)}, u32[]{:S(2)}, u32[]{:S(2)}) collective-permute-start(bf16[128,512]{1,0:T(8,128)(2,1)S(1)} %add_add_fusion.3), channel_id=1, source_target_pairs={{0,16},{8,24},{16,0},{24,8},{1,17},{9,25},{17,1},{25,9},{2,18},{10... | collective-permute-start | bytes 393224 | tf_op jit(solution)/shard_map/ppermute | solution.py:14

commit v13 on v7

--- a/solution.py
+++ b/solution.py
@@ -43,7 +43,10 @@
     slot_of_member = jnp.sum(jnp.where(matches, member_ids[:, None], 0), axis=0)
     send_slot = jnp.take(slot_of_member, (member_here + member_ids) % members)
 
-    lists_by_shift = jnp.stack(shift_gather(tile_lists, "group", groups))
+    spread_hist = jnp.broadcast_to(history[:, 0][None], (members,) + history[:, 0].shape)
+    hist_got = lax.all_to_all(spread_hist, "member", 0, 0, tiled=True)
+    lists_later, _ = lax.optimization_barrier((tile_lists, spread_hist))
+    lists_by_shift = jnp.stack(shift_gather(lists_later, "group", groups))
     group_ids = jnp.arange(groups, dtype=jnp.int32)
     ahead = jnp.take(lists_by_shift, (groups - group_ids) % groups, axis=0)
     wanted = (ahead[:, :, 0] // group_blocks == group_here) & (ahead[:, :, 2] > 0)
@@ -59,8 +62,6 @@
     delays_here = tile_lists[:, 2]
     source_shift = (group_here - source_group) % groups
 
-    spread_hist = jnp.broadcast_to(history[:, 0][None], (members,) + history[:, 0].shape)
-    hist_got = lax.all_to_all(spread_hist, "member", 0, 0, tiled=True)
     hist_placed = pick([hist_got[m] for m in range(members)], owners)
     blocks = [
         hist_placed[:, t].reshape(group_blocks, EXCITE, BLOCK) for t in range(DELAYS)

time: 114 us -> 113 us (level)
    all_to_all x1, waiting for transfers between devices: 4.4 us -> 0.01 us  [body(): hist_got = lax.all_to_all(spread_hist, 'member', 0, 0, tiled=True)]
    ppermute x12, waiting for transfers between devices: 26.8 us -> 30.6 us  [shifted(): return lax.ppermute(x, axis, [(i, (i + k) % n) for i in range(n)])]
    ppermute x12, starting transfers between devices: 17.3 us -> 15.2 us  [shifted(): return lax.ppermute(x, axis, [(i, (i + k) % n) for i in range(n)])]
    all_to_all x1, starting transfers between devices: 3.72 us -> 5.17 us  [body(): hist_got = lax.all_to_all(spread_hist, 'member', 0, 0, tiled=True)]
  transfers between devices with their start and end apart: 13 -> 13, of which waited for: 7 -> 8; matrix products, arithmetic and copies ran while one was open for 6% -> 5% of each run, Pallas kernels for 0% -> 0%
where the time goes in v13:
time: 113 us; the launch traced here: 112 us
  blocking collectives  48 us (42%)
  waiting for transfers between devices  30.6 us (27%)
  starting transfers between devices  20.4 us (18%)
  other arithmetic  7.7 us (7%)
  local copies, waits for them, and re-layouts  3.09 us (3%)
  matrix products  2.3 us (2%)
    ppermute x12, waiting for transfers between devices, shifted(): return lax.ppermute(x, axis, [(i, (i + k) % n) for i in range(n)])  30.6 us
    all_to_all x3, blocking collectives, body(): got = lax.all_to_all(sent, 'member', 0, 0, tiled=True)  29.3 us
    all_to_all x2, blocking collectives, body(): got = lax.all_to_all(spread, 'member', 0, 0, tiled=True)  18.7 us
    ppermute x12, starting transfers between devices, shifted(): return lax.ppermute(x, axis, [(i, (i + k) % n) for i in range(n)])  15.2 us
    all_to_all x1, starting transfers between devices, body(): hist_got = lax.all_to_all(spread_hist, 'member', 0, 0, tiled=True)  5.17 us
  transfers between devices with their start and end apart: 13, of which 8 were waited for; matrix products, arithmetic and copies ran while one was open for 5% of the time, Pallas kernels for 0%

profile of v13, /device:TPU:0, one launch (start us, length us, event | category | flops | bytes accessed | tf_op | source)
XLA Modules:
  0.0 112.3 jit_solution(13233545866715993623)
XLA Ops:
  0.0 1.8 %broadcast_in_dim.1156 = bf16[8,2,32,512]{3,2,1,0:T(8,128)(2,1)} broadcast(bf16[2,32,512]{2,1,0:T(8,128)(2,1)} %bitcast.286), dimensions={1,2,3} | broadcast | bytes 589824 | tf_op jit(solution)/shard_map/broadcast_in_dim | solution.py:46
  1.8 5.2 %all-to-all-start = ((bf16[8,2,32,512]{3,2,1,0:T(8,128)(2,1)}), bf16[8,2,32,512]{3,2,1,0:T(8,128)(2,1)S(1)}, u32[]{:S(2)}, u32[]{:S(2)}) async-start(bf16[8,2,32,512]{3,2,1,0:T(8,128)(2,1)} %broadcast_in_dim.1156), calls=%async_computation | async-start | bytes 1048576 | tf_op jit(solution)/shard_map/all_to_all | solution.py:47
  7.0 3.6 %collective-permute-start.2 = (s32[4,3]{1,0:T(4,128)}, s32[4,3]{1,0:T(4,128)S(1)}, u32[]{:S(2)}, u32[]{:S(2)}) collective-permute-start(s32[4,3]{1,0:T(4,128)} %param.7), channel_id=1, source_target_pairs={{0,24},{8,0},{16,8},{24,16},{1,25},{9,1},{17,9},{25,17},{2,26},{10... | collective-permute-start | bytes 152 | tf_op jit(solution)/shard_map/ppermute | solution.py:14
  10.6 1.0 collective-permute-start
  11.6 0.9 fusion.74
  12.7 0.8 select_reduce_fusion.6
  13.4 0.7 iota_compare_fusion.1
  14.1 1.0 slice_reduce_fusion.2
  15.3 0.9 collective-permute-done
  16.2 0.7 pad_add_fusion
  16.9 0.6 gather_fusion
  18.9 2.4 %collective-permute-start.5 = (bf16[128,512]{1,0:T(8,128)(2,1)S(1)}, bf16[128,512]{1,0:T(8,128)(2,1)S(1)}, u32[]{:S(2)}, u32[]{:S(2)}) collective-permute-start(bf16[128,512]{1,0:T(8,128)(2,1)S(1)} %get-tuple-element.30), channel_id=1, source_target_pairs={{0,24},{8,0},{16,8},{24,16},{1,25},{9,1},{17,9},{25,17},{2,26},{10... | collective-permute-start | bytes 393224 | tf_op jit(solution)/shard_map/ppermute | solution.py:14
  21.3 0.6 collective-permute-start.4
  22.3 2.9 %collective-permute-done.5 = bf16[128,512]{1,0:T(8,128)(2,1)S(1)} collective-permute-done((bf16[128,512]{1,0:T(8,128)(2,1)S(1)}, bf16[128,512]{1,0:T(8,128)(2,1)S(1)}, u32[]{:S(2)}, u32[]{:S(2)}) %collective-permute-start.5) | collective-permute-done | bytes 131104 | tf_op jit(solution)/shard_map/ppermute | solution.py:14
  25.2 8.1 %collective-permute-done.4 = bf16[128,512]{1,0:T(8,128)(2,1)S(1)} collective-permute-done((bf16[128,512]{1,0:T(8,128)(2,1)S(1)}, bf16[128,512]{1,0:T(8,128)(2,1)S(1)}, u32[]{:S(2)}, u32[]{:S(2)}) %collective-permute-start.4) | collective-permute-done | bytes 131104 | tf_op jit(solution)/shard_map/ppermute | solution.py:14
  33.4 0.6 select_reduce_fusion.5
  34.3 10.6 %all_to_all.30 = bf16[8,32,512]{2,1,0:T(8,128)(2,1)S(1)} all-to-all(bf16[8,32,512]{2,1,0:T(8,128)(2,1)S(1)} %select_add_fusion.5), channel_id=1, replica_groups=mesh['group'=4,'member'=8] {'member'}, dimensions={0} | all-to-all | bytes 524288 | tf_op jit(solution)/shard_map/all_to_all | solution.py:94
  45.2 9.3 %all_to_all.31 = bf16[8,32,512]{2,1,0:T(8,128)(2,1)S(1)} all-to-all(bf16[8,32,512]{2,1,0:T(8,128)(2,1)S(1)} %broadcast_in_dim.1253), channel_id=1, replica_groups=mesh['group'=4,'member'=8] {'member'}, dimensions={0} | all-to-all | bytes 524288 | tf_op jit(solution)/shard_map/all_to_all | solution.py:101
  55.5 1.2 %collective-permute-start.7 = (bf16[128,512]{1,0:T(8,128)(2,1)S(1)}, bf16[128,512]{1,0:T(8,128)(2,1)S(1)}, u32[]{:S(2)}, u32[]{:S(2)}) collective-permute-start(bf16[128,512]{1,0:T(8,128)(2,1)S(1)} %get-tuple-element.27), channel_id=1, source_target_pairs={{0,16},{8,24},{16,0},{24,8},{1,17},{9,25},{17,1},{25,9},{2,18},{10... | collective-permute-start | bytes 393224 | tf_op jit(solution)/shard_map/ppermute | solution.py:14
  56.7 1.9 %collective-permute-start.6 = (bf16[128,512]{1,0:T(8,128)(2,1)S(1)}, bf16[128,512]{1,0:T(8,128)(2,1)S(1)}, u32[]{:S(2)}, u32[]{:S(2)}) collective-permute-start(bf16[128,512]{1,0:T(8,128)(2,1)S(1)} %get-tuple-element.28), channel_id=1, source_target_pairs={{0,8},{8,16},{16,24},{24,0},{1,9},{9,17},{17,25},{25,1},{2,10},{10... | collective-permute-start | bytes 393224 | tf_op jit(solution)/shard_map/ppermute | solution.py:14
  58.6 2.0 %collective-permute-done.8 = bf16[128,512]{1,0:T(8,128)(2,1)S(1)} collective-permute-done((bf16[128,512]{1,0:T(8,128)(2,1)S(1)}, bf16[128,512]{1,0:T(8,128)(2,1)S(1)}, u32[]{:S(2)}, u32[]{:S(2)}) %collective-permute-start.8) | collective-permute-done | bytes 131104 | tf_op jit(solution)/shard_map/ppermute | solution.py:14
  60.6 7.3 %collective-permute-done.7 = bf16[128,512]{1,0:T(8,128)(2,1)S(1)} collective-permute-done((bf16[128,512]{1,0:T(8,128)(2,1)S(1)}, bf16[128,512]{1,0:T(8,128)(2,1)S(1)}, u32[]{:S(2)}, u32[]{:S(2)}) %collective-permute-start.7) | collective-permute-done | bytes 131104 | tf_op jit(solution)/shard_map/ppermute | solution.py:14
  67.9 0.6 select_reduce_fusion.3
  68.8 9.3 %all_to_all.32 = bf16[8,32,512]{2,1,0:T(8,128)(2,1)S(1)} all-to-all(bf16[8,32,512]{2,1,0:T(8,128)(2,1)S(1)} %select_add_fusion.3), channel_id=1, replica_groups=mesh['group'=4,'member'=8] {'member'}, dimensions={0} | all-to-all | bytes 524288 | tf_op jit(solution)/shard_map/all_to_all | solution.py:94
  78.4 9.3 %all_to_all.33 = bf16[8,32,512]{2,1,0:T(8,128)(2,1)S(1)} all-to-all(bf16[8,32,512]{2,1,0:T(8,128)(2,1)S(1)} %broadcast_in_dim.1302), channel_id=1, replica_groups=mesh['group'=4,'member'=8] {'member'}, dimensions={0} | all-to-all | bytes 524288 | tf_op jit(solution)/shard_map/all_to_all | solution.py:101
  88.4 1.6 %collective-permute-start.10 = (bf16[128,512]{1,0:T(8,128)(2,1)S(1)}, bf16[128,512]{1,0:T(8,128)(2,1)S(1)}, u32[]{:S(2)}, u32[]{:S(2)}) collective-permute-start(bf16[128,512]{1,0:T(8,128)(2,1)S(1)} %get-tuple-element.23), channel_id=1, source_target_pairs={{0,16},{8,24},{16,0},{24,8},{1,17},{9,25},{17,1},{25,9},{2,18},{10... | collective-permute-start | bytes 393224 | tf_op jit(solution)/shard_map/ppermute | solution.py:14
  90.0 1.9 %collective-permute-start.9 = (bf16[128,512]{1,0:T(8,128)(2,1)S(1)}, bf16[128,512]{1,0:T(8,128)(2,1)S(1)}, u32[]{:S(2)}, u32[]{:S(2)}) collective-permute-start(bf16[128,512]{1,0:T(8,128)(2,1)S(1)} %get-tuple-element.24), channel_id=1, source_target_pairs={{0,8},{8,16},{16,24},{24,0},{1,9},{9,17},{17,25},{25,1},{2,10},{10... | collective-permute-start | bytes 393224 | tf_op jit(solution)/shard_map/ppermute | solution.py:14
  91.9 1.9 %collective-permute-done.11 = bf16[128,512]{1,0:T(8,128)(2,1)S(1)} collective-permute-done((bf16[128,512]{1,0:T(8,128)(2,1)S(1)}, bf16[128,512]{1,0:T(8,128)(2,1)S(1)}, u32[]{:S(2)}, u32[]{:S(2)}) %collective-permute-start.11) | collective-permute-done | bytes 131104 | tf_op jit(solution)/shard_map/ppermute | solution.py:14
  93.9 7.3 %collective-permute-done.10 = bf16[128,512]{1,0:T(8,128)(2,1)S(1)} collective-permute-done((bf16[128,512]{1,0:T(8,128)(2,1)S(1)}, bf16[128,512]{1,0:T(8,128)(2,1)S(1)}, u32[]{:S(2)}, u32[]{:S(2)}) %collective-permute-start.10) | collective-permute-done | bytes 131104 | tf_op jit(solution)/shard_map/ppermute | solution.py:14
  101.2 0.6 select_reduce_fusion.1
  102.1 9.3 %all_to_all.34 = bf16[8,32,512]{2,1,0:T(8,128)(2,1)S(1)} all-to-all(bf16[8,32,512]{2,1,0:T(8,128)(2,1)S(1)} %select_add_fusion.1), channel_id=1, replica_groups=mesh['group'=4,'member'=8] {'member'}, dimensions={0} | all-to-all | bytes 524288 | tf_op jit(solution)/shard_map/all_to_all | solution.py:94
  111.6 0.7 maximum_bitcast_fusion
  (64 shorter events, 5.2 us)
Async XLA Ops:
  0.0 33.4 %copy-start = (bf16[4,512,512]{2,1,0:T(8,128)(2,1)S(1)}, bf16[4,512,512]{2,1,0:T(8,128)(2,1)}, u32[]{:S(2)}) copy-start(bf16[4,512,512]{2,1,0:T(8,128)(2,1)} %param.6) | copy-start | bytes 6291460
  1.8 16.2 %all-to-all-start = ((bf16[8,2,32,512]{3,2,1,0:T(8,128)(2,1)}), bf16[8,2,32,512]{3,2,1,0:T(8,128)(2,1)S(1)}, u32[]{:S(2)}, u32[]{:S(2)}) async-start(bf16[8,2,32,512]{3,2,1,0:T(8,128)(2,1)} %broadcast_in_dim.1156), calls=%async_computation | async-start | bytes 1048576 | tf_op jit(solution)/shard_map/all_to_all | solution.py:47
  7.0 8.2 %collective-permute-start.2 = (s32[4,3]{1,0:T(4,128)}, s32[4,3]{1,0:T(4,128)S(1)}, u32[]{:S(2)}, u32[]{:S(2)}) collective-permute-start(s32[4,3]{1,0:T(4,128)} %param.7), channel_id=1, source_target_pairs={{0,24},{8,0},{16,8},{24,16},{1,25},{9,1},{17,9},{25,17},{2,26},{10... | collective-permute-start | bytes 152 | tf_op jit(solution)/shard_map/ppermute | solution.py:14
  10.6 4.7 %collective-permute-start.1 = (s32[4,3]{1,0:T(4,128)}, s32[4,3]{1,0:T(4,128)S(1)}, u32[]{:S(2)}, u32[]{:S(2)}) collective-permute-start(s32[4,3]{1,0:T(4,128)} %param.7), channel_id=1, source_target_pairs={{0,16},{8,24},{16,0},{24,8},{1,17},{9,25},{17,1},{25,9},{2,18},{10... | collective-permute-start | bytes 152 | tf_op jit(solution)/shard_map/ppermute | solution.py:14
  10.6 5.6 %collective-permute-start = (s32[4,3]{1,0:T(4,128)}, s32[4,3]{1,0:T(4,128)S(1)}, u32[]{:S(2)}, u32[]{:S(2)}) collective-permute-start(s32[4,3]{1,0:T(4,128)} %param.7), channel_id=1, source_target_pairs={{0,8},{8,16},{16,24},{24,0},{1,9},{9,17},{17,25},{25,1},{2,10},{10... | collective-permute-start | bytes 152 | tf_op jit(solution)/shard_map/ppermute | solution.py:14
  18.9 6.4 %collective-permute-start.5 = (bf16[128,512]{1,0:T(8,128)(2,1)S(1)}, bf16[128,512]{1,0:T(8,128)(2,1)S(1)}, u32[]{:S(2)}, u32[]{:S(2)}) collective-permute-start(bf16[128,512]{1,0:T(8,128)(2,1)S(1)} %get-tuple-element.30), channel_id=1, source_target_pairs={{0,24},{8,0},{16,8},{24,16},{1,25},{9,1},{17,9},{25,17},{2,26},{10... | collective-permute-start | bytes 393224 | tf_op jit(solution)/shard_map/ppermute | solution.py:14
  21.3 12.1 %collective-permute-start.4 = (bf16[128,512]{1,0:T(8,128)(2,1)S(1)}, bf16[128,512]{1,0:T(8,128)(2,1)S(1)}, u32[]{:S(2)}, u32[]{:S(2)}) collective-permute-start(bf16[128,512]{1,0:T(8,128)(2,1)S(1)} %get-tuple-element.31), channel_id=1, source_target_pairs={{0,16},{8,24},{16,0},{24,8},{1,17},{9,25},{17,1},{25,9},{2,18},{10... | collective-permute-start | bytes 393224 | tf_op jit(solution)/shard_map/ppermute | solution.py:14
  21.9 11.5 %collective-permute-start.3 = (bf16[128,512]{1,0:T(8,128)(2,1)S(1)}, bf16[128,512]{1,0:T(8,128)(2,1)S(1)}, u32[]{:S(2)}, u32[]{:S(2)}) collective-permute-start(bf16[128,512]{1,0:T(8,128)(2,1)S(1)} %get-tuple-element.32), channel_id=1, source_target_pairs={{0,8},{8,16},{16,24},{24,0},{1,9},{9,17},{17,25},{25,1},{2,10},{10... | collective-permute-start | bytes 393224 | tf_op jit(solution)/shard_map/ppermute | solution.py:14
  34.0 11.0 %copy-start.1 = (bf16[1,512,512]{2,1,0:T(8,128)(2,1)S(1)}, bf16[1,512,512]{2,1,0:T(8,128)(2,1)}, u32[]{:S(2)}) copy-start(bf16[1,512,512]{2,1,0:T(8,128)(2,1)} %param.9) | copy-start | bytes 1572868
  34.0 11.0 %copy-start.2 = (f32[3,1,32,512]{3,2,1,0:T(8,128)S(1)}, f32[3,1,32,512]{3,2,1,0:T(8,128)}, u32[]{:S(2)}) copy-start(f32[3,1,32,512]{3,2,1,0:T(8,128)} %param.10) | copy-start | bytes 589828
  55.1 5.5 %collective-permute-start.8 = (bf16[128,512]{1,0:T(8,128)(2,1)S(1)}, bf16[128,512]{1,0:T(8,128)(2,1)S(1)}, u32[]{:S(2)}, u32[]{:S(2)}) collective-permute-start(bf16[128,512]{1,0:T(8,128)(2,1)S(1)} %get-tuple-element.26), channel_id=1, source_target_pairs={{0,24},{8,0},{16,8},{24,16},{1,25},{9,1},{17,9},{25,17},{2,26},{10... | collective-permute-start | bytes 393224 | tf_op jit(solution)/shard_map/ppermute | solution.py:14
  55.5 12.4 %collective-permute-start.7 = (bf16[128,512]{1,0:T(8,128)(2,1)S(1)}, bf16[128,512]{1,0:T(8,128)(2,1)S(1)}, u32[]{:S(2)}, u32[]{:S(2)}) collective-permute-start(bf16[128,512]{1,0:T(8,128)(2,1)S(1)} %get-tuple-element.27), channel_id=1, source_target_pairs={{0,16},{8,24},{16,0},{24,8},{1,17},{9,25},{17,1},{25,9},{2,18},{10... | collective-permute-start | bytes 393224 | tf_op jit(solution)/shard_map/ppermute | solution.py:14
  56.7 11.2 %collective-permute-start.6 = (bf16[128,512]{1,0:T(8,128)(2,1)S(1)}, bf16[128,512]{1,0:T(8,128)(2,1)S(1)}, u32[]{:S(2)}, u32[]{:S(2)}) collective-permute-start(bf16[128,512]{1,0:T(8,128)(2,1)S(1)} %get-tuple-element.28), channel_id=1, source_target_pairs={{0,8},{8,16},{16,24},{24,0},{1,9},{9,17},{17,25},{25,1},{2,10},{10... | collective-permute-start | bytes 393224 | tf_op jit(solution)/shard_map/ppermute | solution.py:14
  88.3 5.5 %collective-permute-start.11 = (bf16[128,512]{1,0:T(8,128)(2,1)S(1)}, bf16[128,512]{1,0:T(8,128)(2,1)S(1)}, u32[]{:S(2)}, u32[]{:S(2)}) collective-permute-start(bf16[128,512]{1,0:T(8,128)(2,1)S(1)} %get-tuple-element.22), channel_id=1, source_target_pairs={{0,24},{8,0},{16,8},{24,16},{1,25},{9,1},{17,9},{25,17},{2,26},{10... | collective-permute-start | bytes 393224 | tf_op jit(solution)/shard_map/ppermute | solution.py:14
  88.4 12.8 %collective-permute-start.10 = (bf16[128,512]{1,0:T(8,128)(2,1)S(1)}, bf16[128,512]{1,0:T(8,128)(2,1)S(1)}, u32[]{:S(2)}, u32[]{:S(2)}) collective-permute-start(bf16[128,512]{1,0:T(8,128)(2,1)S(1)} %get-tuple-element.23), channel_id=1, source_target_pairs={{0,16},{8,24},{16,0},{24,8},{1,17},{9,25},{17,1},{25,9},{2,18},{10... | collective-permute-start | bytes 393224 | tf_op jit(solution)/shard_map/ppermute | solution.py:14
  90.0 11.2 %collective-permute-start.9 = (bf16[128,512]{1,0:T(8,128)(2,1)S(1)}, bf16[128,512]{1,0:T(8,128)(2,1)S(1)}, u32[]{:S(2)}, u32[]{:S(2)}) collective-permute-start(bf16[128,512]{1,0:T(8,128)(2,1)S(1)} %get-tuple-element.24), channel_id=1, source_target_pairs={{0,8},{8,16},{16,24},{24,0},{1,9},{9,17},{17,25},{25,1},{2,10},{10... | collective-permute-start | bytes 393224 | tf_op jit(solution)/shard_map/ppermute | solution.py:14

commit v14 on v13

--- a/solution.py
+++ b/solution.py
@@ -46,9 +46,8 @@
     spread_hist = jnp.broadcast_to(history[:, 0][None], (members,) + history[:, 0].shape)
     hist_got = lax.all_to_all(spread_hist, "member", 0, 0, tiled=True)
     lists_later, _ = lax.optimization_barrier((tile_lists, spread_hist))
-    lists_by_shift = jnp.stack(shift_gather(lists_later, "group", groups))
-    group_ids = jnp.arange(groups, dtype=jnp.int32)
-    ahead = jnp.take(lists_by_shift, (groups - group_ids) % groups, axis=0)
+    lists_by_shift = shift_gather(lists_later, "group", groups)
+    ahead = jnp.stack([lists_by_shift[(groups - k) % groups] for k in range(groups)])
     wanted = (ahead[:, :, 0] // group_blocks == group_here) & (ahead[:, :, 2] > 0)
     want_block = jnp.sum(jnp.where(wanted, ahead[:, :, 0] % group_blocks, 0), axis=1)
     want_delay = jnp.sum(jnp.where(wanted, ahead[:, :, 2], 0), axis=1)

time: 113 us -> 111 us (0.982)
  waiting for transfers between devices: 30.6 us -> 28.3 us
  starting transfers between devices: 20.4 us -> 22.2 us
    ppermute x12, waiting for transfers between devices: 30.6 us -> 28.3 us  [shifted(): return lax.ppermute(x, axis, [(i, (i + k) % n) for i in range(n)])]
    ppermute x12, starting transfers between devices: 15.2 us -> 17 us  [shifted(): return lax.ppermute(x, axis, [(i, (i + k) % n) for i in range(n)])]
  transfers between devices with their start and end apart: 13 -> 13, of which waited for: 8 -> 6; matrix products, arithmetic and copies ran while one was open for 5% -> 4% of each run, Pallas kernels for 0% -> 0%
where the time goes in v14:
time: 111 us
  blocking collectives  47.8 us (43%)
  waiting for transfers between devices  28.3 us (25%)
  starting transfers between devices  22.2 us (20%)
  other arithmetic  7.47 us (7%)
  local copies, waits for them, and re-layouts  2.52 us (2%)
  matrix products  2.29 us (2%)
    all_to_all x3, blocking collectives, body(): got = lax.all_to_all(sent, 'member', 0, 0, tiled=True)  29.1 us
    ppermute x12, waiting for transfers between devices, shifted(): return lax.ppermute(x, axis, [(i, (i + k) % n) for i in range(n)])  28.3 us
    all_to_all x2, blocking collectives, body(): got = lax.all_to_all(spread, 'member', 0, 0, tiled=True)  18.7 us
    ppermute x12, starting transfers between devices, shifted(): return lax.ppermute(x, axis, [(i, (i + k) % n) for i in range(n)])  17 us
    all_to_all x1, starting transfers between devices, body(): hist_got = lax.all_to_all(spread_hist, 'member', 0, 0, tiled=True)  5.17 us
  transfers between devices with their start and end apart: 13, of which 6 were waited for; matrix products, arithmetic and copies ran while one was open for 4% of the time, Pallas kernels for 0%

profile of v14, /device:TPU:0, one launch (start us, length us, event | category | flops | bytes accessed | tf_op | source)
XLA Modules:
  0.0 110.9 jit_solution(14729045641306109321)
XLA Ops:
  0.0 1.8 %broadcast_in_dim.1145 = bf16[8,2,32,512]{3,2,1,0:T(8,128)(2,1)} broadcast(bf16[2,32,512]{2,1,0:T(8,128)(2,1)} %bitcast.286), dimensions={1,2,3} | broadcast | bytes 589824 | tf_op jit(solution)/shard_map/broadcast_in_dim | solution.py:46
  1.8 5.2 %all-to-all-start = ((bf16[8,2,32,512]{3,2,1,0:T(8,128)(2,1)}), bf16[8,2,32,512]{3,2,1,0:T(8,128)(2,1)S(1)}, u32[]{:S(2)}, u32[]{:S(2)}) async-start(bf16[8,2,32,512]{3,2,1,0:T(8,128)(2,1)} %broadcast_in_dim.1145), calls=%async_computation | async-start | bytes 1048576 | tf_op jit(solution)/shard_map/all_to_all | solution.py:47
  7.0 1.6 %collective-permute-start.2 = (s32[4,3]{1,0:T(4,128)}, s32[4,3]{1,0:T(4,128)S(1)}, u32[]{:S(2)}, u32[]{:S(2)}) collective-permute-start(s32[4,3]{1,0:T(4,128)} %param.7), channel_id=1, source_target_pairs={{0,8},{8,16},{16,24},{24,0},{1,9},{9,17},{17,25},{25,1},{2,10},{10... | collective-permute-start | bytes 152 | tf_op jit(solution)/shard_map/ppermute | solution.py:14
  8.6 2.6 %collective-permute-start.1 = (s32[4,3]{1,0:T(4,128)}, s32[4,3]{1,0:T(4,128)S(1)}, u32[]{:S(2)}, u32[]{:S(2)}) collective-permute-start(s32[4,3]{1,0:T(4,128)} %param.7), channel_id=1, source_target_pairs={{0,16},{8,24},{16,0},{24,8},{1,17},{9,25},{17,1},{25,9},{2,18},{10... | collective-permute-start | bytes 152 | tf_op jit(solution)/shard_map/ppermute | solution.py:14
  11.2 1.3 %collective-permute-start = (s32[4,3]{1,0:T(4,128)}, s32[4,3]{1,0:T(4,128)S(1)}, u32[]{:S(2)}, u32[]{:S(2)}) collective-permute-start(s32[4,3]{1,0:T(4,128)} %param.7), channel_id=1, source_target_pairs={{0,24},{8,0},{16,8},{24,16},{1,25},{9,1},{17,9},{25,17},{2,26},{10... | collective-permute-start | bytes 152 | tf_op jit(solution)/shard_map/ppermute | solution.py:14
  12.5 0.9 fusion.72
  13.4 0.8 select_reduce_fusion.6
  14.2 0.7 iota_compare_fusion.1
  14.9 1.0 slice_reduce_fusion.2
  15.9 0.7 pad_add_fusion
  17.1 0.5 select_add_fusion
  18.0 3.3 %collective-permute-start.5 = (bf16[128,512]{1,0:T(8,128)(2,1)S(1)}, bf16[128,512]{1,0:T(8,128)(2,1)S(1)}, u32[]{:S(2)}, u32[]{:S(2)}) collective-permute-start(bf16[128,512]{1,0:T(8,128)(2,1)S(1)} %get-tuple-element.30), channel_id=1, source_target_pairs={{0,24},{8,0},{16,8},{24,16},{1,25},{9,1},{17,9},{25,17},{2,26},{10... | collective-permute-start | bytes 393224 | tf_op jit(solution)/shard_map/ppermute | solution.py:14
  21.3 1.0 collective-permute-start.3
  22.3 2.5 %collective-permute-done.5 = bf16[128,512]{1,0:T(8,128)(2,1)S(1)} collective-permute-done((bf16[128,512]{1,0:T(8,128)(2,1)S(1)}, bf16[128,512]{1,0:T(8,128)(2,1)S(1)}, u32[]{:S(2)}, u32[]{:S(2)}) %collective-permute-start.5) | collective-permute-done | bytes 131104 | tf_op jit(solution)/shard_map/ppermute | solution.py:14
  24.8 7.3 %collective-permute-done.4 = bf16[128,512]{1,0:T(8,128)(2,1)S(1)} collective-permute-done((bf16[128,512]{1,0:T(8,128)(2,1)S(1)}, bf16[128,512]{1,0:T(8,128)(2,1)S(1)}, u32[]{:S(2)}, u32[]{:S(2)}) %collective-permute-start.4) | collective-permute-done | bytes 131104 | tf_op jit(solution)/shard_map/ppermute | solution.py:14
  32.1 0.6 select_reduce_fusion.5
  33.0 10.4 %all_to_all.30 = bf16[8,32,512]{2,1,0:T(8,128)(2,1)S(1)} all-to-all(bf16[8,32,512]{2,1,0:T(8,128)(2,1)S(1)} %select_add_fusion.5), channel_id=1, replica_groups=mesh['group'=4,'member'=8] {'member'}, dimensions={0} | all-to-all | bytes 524288 | tf_op jit(solution)/shard_map/all_to_all | solution.py:93
  43.7 9.3 %all_to_all.31 = bf16[8,32,512]{2,1,0:T(8,128)(2,1)S(1)} all-to-all(bf16[8,32,512]{2,1,0:T(8,128)(2,1)S(1)} %broadcast_in_dim.1241), channel_id=1, replica_groups=mesh['group'=4,'member'=8] {'member'}, dimensions={0} | all-to-all | bytes 524288 | tf_op jit(solution)/shard_map/all_to_all | solution.py:100
  54.0 1.1 %collective-permute-start.7 = (bf16[128,512]{1,0:T(8,128)(2,1)S(1)}, bf16[128,512]{1,0:T(8,128)(2,1)S(1)}, u32[]{:S(2)}, u32[]{:S(2)}) collective-permute-start(bf16[128,512]{1,0:T(8,128)(2,1)S(1)} %get-tuple-element.27), channel_id=1, source_target_pairs={{0,16},{8,24},{16,0},{24,8},{1,17},{9,25},{17,1},{25,9},{2,18},{10... | collective-permute-start | bytes 393224 | tf_op jit(solution)/shard_map/ppermute | solution.py:14
  55.2 1.9 %collective-permute-start.6 = (bf16[128,512]{1,0:T(8,128)(2,1)S(1)}, bf16[128,512]{1,0:T(8,128)(2,1)S(1)}, u32[]{:S(2)}, u32[]{:S(2)}) collective-permute-start(bf16[128,512]{1,0:T(8,128)(2,1)S(1)} %get-tuple-element.28), channel_id=1, source_target_pairs={{0,8},{8,16},{16,24},{24,0},{1,9},{9,17},{17,25},{25,1},{2,10},{10... | collective-permute-start | bytes 393224 | tf_op jit(solution)/shard_map/ppermute | solution.py:14
  57.1 2.0 %collective-permute-done.8 = bf16[128,512]{1,0:T(8,128)(2,1)S(1)} collective-permute-done((bf16[128,512]{1,0:T(8,128)(2,1)S(1)}, bf16[128,512]{1,0:T(8,128)(2,1)S(1)}, u32[]{:S(2)}, u32[]{:S(2)}) %collective-permute-start.8) | collective-permute-done | bytes 131104 | tf_op jit(solution)/shard_map/ppermute | solution.py:14
  59.2 7.2 %collective-permute-done.7 = bf16[128,512]{1,0:T(8,128)(2,1)S(1)} collective-permute-done((bf16[128,512]{1,0:T(8,128)(2,1)S(1)}, bf16[128,512]{1,0:T(8,128)(2,1)S(1)}, u32[]{:S(2)}, u32[]{:S(2)}) %collective-permute-start.7) | collective-permute-done | bytes 131104 | tf_op jit(solution)/shard_map/ppermute | solution.py:14
  66.4 0.6 select_reduce_fusion.3
  67.3 9.3 %all_to_all.32 = bf16[8,32,512]{2,1,0:T(8,128)(2,1)S(1)} all-to-all(bf16[8,32,512]{2,1,0:T(8,128)(2,1)S(1)} %select_add_fusion.3), channel_id=1, replica_groups=mesh['group'=4,'member'=8] {'member'}, dimensions={0} | all-to-all | bytes 524288 | tf_op jit(solution)/shard_map/all_to_all | solution.py:93
  76.9 9.3 %all_to_all.33 = bf16[8,32,512]{2,1,0:T(8,128)(2,1)S(1)} all-to-all(bf16[8,32,512]{2,1,0:T(8,128)(2,1)S(1)} %broadcast_in_dim.1290), channel_id=1, replica_groups=mesh['group'=4,'member'=8] {'member'}, dimensions={0} | all-to-all | bytes 524288 | tf_op jit(solution)/shard_map/all_to_all | solution.py:100
  86.9 1.7 %collective-permute-start.10 = (bf16[128,512]{1,0:T(8,128)(2,1)S(1)}, bf16[128,512]{1,0:T(8,128)(2,1)S(1)}, u32[]{:S(2)}, u32[]{:S(2)}) collective-permute-start(bf16[128,512]{1,0:T(8,128)(2,1)S(1)} %get-tuple-element.23), channel_id=1, source_target_pairs={{0,16},{8,24},{16,0},{24,8},{1,17},{9,25},{17,1},{25,9},{2,18},{10... | collective-permute-start | bytes 393224 | tf_op jit(solution)/shard_map/ppermute | solution.py:14
  88.6 1.9 %collective-permute-start.9 = (bf16[128,512]{1,0:T(8,128)(2,1)S(1)}, bf16[128,512]{1,0:T(8,128)(2,1)S(1)}, u32[]{:S(2)}, u32[]{:S(2)}) collective-permute-start(bf16[128,512]{1,0:T(8,128)(2,1)S(1)} %get-tuple-element.24), channel_id=1, source_target_pairs={{0,8},{8,16},{16,24},{24,0},{1,9},{9,17},{17,25},{25,1},{2,10},{10... | collective-permute-start | bytes 393224 | tf_op jit(solution)/shard_map/ppermute | solution.py:14
  90.5 1.9 %collective-permute-done.11 = bf16[128,512]{1,0:T(8,128)(2,1)S(1)} collective-permute-done((bf16[128,512]{1,0:T(8,128)(2,1)S(1)}, bf16[128,512]{1,0:T(8,128)(2,1)S(1)}, u32[]{:S(2)}, u32[]{:S(2)}) %collective-permute-start.11) | collective-permute-done | bytes 131104 | tf_op jit(solution)/shard_map/ppermute | solution.py:14
  92.4 7.4 %collective-permute-done.10 = bf16[128,512]{1,0:T(8,128)(2,1)S(1)} collective-permute-done((bf16[128,512]{1,0:T(8,128)(2,1)S(1)}, bf16[128,512]{1,0:T(8,128)(2,1)S(1)}, u32[]{:S(2)}, u32[]{:S(2)}) %collective-permute-start.10) | collective-permute-done | bytes 131104 | tf_op jit(solution)/shard_map/ppermute | solution.py:14
  99.8 0.6 select_reduce_fusion.1
  100.6 9.3 %all_to_all.34 = bf16[8,32,512]{2,1,0:T(8,128)(2,1)S(1)} all-to-all(bf16[8,32,512]{2,1,0:T(8,128)(2,1)S(1)} %select_add_fusion.1), channel_id=1, replica_groups=mesh['group'=4,'member'=8] {'member'}, dimensions={0} | all-to-all | bytes 524288 | tf_op jit(solution)/shard_map/all_to_all | solution.py:93
  110.2 0.7 maximum_bitcast_fusion
  (59 shorter events, 4.0 us)
Async XLA Ops:
  0.0 32.1 %copy-start = (bf16[4,512,512]{2,1,0:T(8,128)(2,1)S(1)}, bf16[4,512,512]{2,1,0:T(8,128)(2,1)}, u32[]{:S(2)}) copy-start(bf16[4,512,512]{2,1,0:T(8,128)(2,1)} %param.6) | copy-start | bytes 6291460
  1.8 15.3 %all-to-all-start = ((bf16[8,2,32,512]{3,2,1,0:T(8,128)(2,1)}), bf16[8,2,32,512]{3,2,1,0:T(8,128)(2,1)S(1)}, u32[]{:S(2)}, u32[]{:S(2)}) async-start(bf16[8,2,32,512]{3,2,1,0:T(8,128)(2,1)} %broadcast_in_dim.1145), calls=%async_computation | async-start | bytes 1048576 | tf_op jit(solution)/shard_map/all_to_all | solution.py:47
  7.0 8.9 %collective-permute-start.2 = (s32[4,3]{1,0:T(4,128)}, s32[4,3]{1,0:T(4,128)S(1)}, u32[]{:S(2)}, u32[]{:S(2)}) collective-permute-start(s32[4,3]{1,0:T(4,128)} %param.7), channel_id=1, source_target_pairs={{0,8},{8,16},{16,24},{24,0},{1,9},{9,17},{17,25},{25,1},{2,10},{10... | collective-permute-start | bytes 152 | tf_op jit(solution)/shard_map/ppermute | solution.py:14
  8.6 7.3 %collective-permute-start.1 = (s32[4,3]{1,0:T(4,128)}, s32[4,3]{1,0:T(4,128)S(1)}, u32[]{:S(2)}, u32[]{:S(2)}) collective-permute-start(s32[4,3]{1,0:T(4,128)} %param.7), channel_id=1, source_target_pairs={{0,16},{8,24},{16,0},{24,8},{1,17},{9,25},{17,1},{25,9},{2,18},{10... | collective-permute-start | bytes 152 | tf_op jit(solution)/shard_map/ppermute | solution.py:14
  11.2 4.8 %collective-permute-start = (s32[4,3]{1,0:T(4,128)}, s32[4,3]{1,0:T(4,128)S(1)}, u32[]{:S(2)}, u32[]{:S(2)}) collective-permute-start(s32[4,3]{1,0:T(4,128)} %param.7), channel_id=1, source_target_pairs={{0,24},{8,0},{16,8},{24,16},{1,25},{9,1},{17,9},{25,17},{2,26},{10... | collective-permute-start | bytes 152 | tf_op jit(solution)/shard_map/ppermute | solution.py:14
  18.0 6.9 %collective-permute-start.5 = (bf16[128,512]{1,0:T(8,128)(2,1)S(1)}, bf16[128,512]{1,0:T(8,128)(2,1)S(1)}, u32[]{:S(2)}, u32[]{:S(2)}) collective-permute-start(bf16[128,512]{1,0:T(8,128)(2,1)S(1)} %get-tuple-element.30), channel_id=1, source_target_pairs={{0,24},{8,0},{16,8},{24,16},{1,25},{9,1},{17,9},{25,17},{2,26},{10... | collective-permute-start | bytes 393224 | tf_op jit(solution)/shard_map/ppermute | solution.py:14
  21.3 10.8 %collective-permute-start.4 = (bf16[128,512]{1,0:T(8,128)(2,1)S(1)}, bf16[128,512]{1,0:T(8,128)(2,1)S(1)}, u32[]{:S(2)}, u32[]{:S(2)}) collective-permute-start(bf16[128,512]{1,0:T(8,128)(2,1)S(1)} %get-tuple-element.31), channel_id=1, source_target_pairs={{0,16},{8,24},{16,0},{24,8},{1,17},{9,25},{17,1},{25,9},{2,18},{10... | collective-permute-start | bytes 393224 | tf_op jit(solution)/shard_map/ppermute | solution.py:14
  21.3 10.8 %collective-permute-start.3 = (bf16[128,512]{1,0:T(8,128)(2,1)S(1)}, bf16[128,512]{1,0:T(8,128)(2,1)S(1)}, u32[]{:S(2)}, u32[]{:S(2)}) collective-permute-start(bf16[128,512]{1,0:T(8,128)(2,1)S(1)} %get-tuple-element.32), channel_id=1, source_target_pairs={{0,8},{8,16},{16,24},{24,0},{1,9},{9,17},{17,25},{25,1},{2,10},{10... | collective-permute-start | bytes 393224 | tf_op jit(solution)/shard_map/ppermute | solution.py:14
  32.7 10.8 %copy-start.1 = (bf16[1,512,512]{2,1,0:T(8,128)(2,1)S(1)}, bf16[1,512,512]{2,1,0:T(8,128)(2,1)}, u32[]{:S(2)}) copy-start(bf16[1,512,512]{2,1,0:T(8,128)(2,1)} %param.9) | copy-start | bytes 1572868
  32.7 10.8 %copy-start.2 = (f32[3,1,32,512]{3,2,1,0:T(8,128)S(1)}, f32[3,1,32,512]{3,2,1,0:T(8,128)}, u32[]{:S(2)}) copy-start(f32[3,1,32,512]{3,2,1,0:T(8,128)} %param.10) | copy-start | bytes 589828
  53.6 5.6 %collective-permute-start.8 = (bf16[128,512]{1,0:T(8,128)(2,1)S(1)}, bf16[128,512]{1,0:T(8,128)(2,1)S(1)}, u32[]{:S(2)}, u32[]{:S(2)}) collective-permute-start(bf16[128,512]{1,0:T(8,128)(2,1)S(1)} %get-tuple-element.26), channel_id=1, source_target_pairs={{0,24},{8,0},{16,8},{24,16},{1,25},{9,1},{17,9},{25,17},{2,26},{10... | collective-permute-start | bytes 393224 | tf_op jit(solution)/shard_map/ppermute | solution.py:14
  54.0 12.3 %collective-permute-start.7 = (bf16[128,512]{1,0:T(8,128)(2,1)S(1)}, bf16[128,512]{1,0:T(8,128)(2,1)S(1)}, u32[]{:S(2)}, u32[]{:S(2)}) collective-permute-start(bf16[128,512]{1,0:T(8,128)(2,1)S(1)} %get-tuple-element.27), channel_id=1, source_target_pairs={{0,16},{8,24},{16,0},{24,8},{1,17},{9,25},{17,1},{25,9},{2,18},{10... | collective-permute-start | bytes 393224 | tf_op jit(solution)/shard_map/ppermute | solution.py:14
  55.2 11.2 %collective-permute-start.6 = (bf16[128,512]{1,0:T(8,128)(2,1)S(1)}, bf16[128,512]{1,0:T(8,128)(2,1)S(1)}, u32[]{:S(2)}, u32[]{:S(2)}) collective-permute-start(bf16[128,512]{1,0:T(8,128)(2,1)S(1)} %get-tuple-element.28), channel_id=1, source_target_pairs={{0,8},{8,16},{16,24},{24,0},{1,9},{9,17},{17,25},{25,1},{2,10},{10... | collective-permute-start | bytes 393224 | tf_op jit(solution)/shard_map/ppermute | solution.py:14
  86.8 5.6 %collective-permute-start.11 = (bf16[128,512]{1,0:T(8,128)(2,1)S(1)}, bf16[128,512]{1,0:T(8,128)(2,1)S(1)}, u32[]{:S(2)}, u32[]{:S(2)}) collective-permute-start(bf16[128,512]{1,0:T(8,128)(2,1)S(1)} %get-tuple-element.22), channel_id=1, source_target_pairs={{0,24},{8,0},{16,8},{24,16},{1,25},{9,1},{17,9},{25,17},{2,26},{10... | collective-permute-start | bytes 393224 | tf_op jit(solution)/shard_map/ppermute | solution.py:14
  86.9 12.9 %collective-permute-start.10 = (bf16[128,512]{1,0:T(8,128)(2,1)S(1)}, bf16[128,512]{1,0:T(8,128)(2,1)S(1)}, u32[]{:S(2)}, u32[]{:S(2)}) collective-permute-start(bf16[128,512]{1,0:T(8,128)(2,1)S(1)} %get-tuple-element.23), channel_id=1, source_target_pairs={{0,16},{8,24},{16,0},{24,8},{1,17},{9,25},{17,1},{25,9},{2,18},{10... | collective-permute-start | bytes 393224 | tf_op jit(solution)/shard_map/ppermute | solution.py:14
  88.6 11.2 %collective-permute-start.9 = (bf16[128,512]{1,0:T(8,128)(2,1)S(1)}, bf16[128,512]{1,0:T(8,128)(2,1)S(1)}, u32[]{:S(2)}, u32[]{:S(2)}) collective-permute-start(bf16[128,512]{1,0:T(8,128)(2,1)S(1)} %get-tuple-element.24), channel_id=1, source_target_pairs={{0,8},{8,16},{16,24},{24,0},{1,9},{9,17},{17,25},{25,1},{2,10},{10... | collective-permute-start | bytes 393224 | tf_op jit(solution)/shard_map/ppermute | solution.py:14

commit v15 on v14

--- a/solution.py
+++ b/solution.py
@@ -39,9 +39,6 @@
     member_here = lax.axis_index("member")
     owners = owner_map[0]
     member_ids = jnp.arange(members, dtype=jnp.int32)
-    matches = owners[:, None] == member_ids[None, :]
-    slot_of_member = jnp.sum(jnp.where(matches, member_ids[:, None], 0), axis=0)
-    send_slot = jnp.take(slot_of_member, (member_here + member_ids) % members)
 
     spread_hist = jnp.broadcast_to(history[:, 0][None], (members,) + history[:, 0].shape)
     hist_got = lax.all_to_all(spread_hist, "member", 0, 0, tiled=True)
@@ -55,11 +52,6 @@
     which_block = want_block[:, None] == block_ids[None, :]
     from_near = which_block & (want_delay[:, None] == 1)
     from_far = which_block & (want_delay[:, None] == 2)
-
-    source_group = tile_lists[:, 0] // group_blocks
-    observer_local = tile_lists[:, 1] % group_blocks
-    delays_here = tile_lists[:, 2]
-    source_shift = (group_here - source_group) % groups
 
     hist_placed = pick([hist_got[m] for m in range(members)], owners)
     blocks = [
@@ -78,6 +70,15 @@
         received = [outgoing[0]] + [
             shifted(outgoing[k], "group", groups, k) for k in range(1, groups)
         ]
+        if step == 0:
+            late_lists, late_owners, _ = lax.optimization_barrier(
+                (tile_lists, owners, received[groups - 1])
+            )
+            matches = late_owners[:, None] == member_ids[None, :]
+            slot_of_member = jnp.sum(jnp.where(matches, member_ids[:, None], 0), axis=0)
+            observer_local = late_lists[:, 1] % group_blocks
+            delays_here = late_lists[:, 2]
+            source_shift = (group_here - late_lists[:, 0] // group_blocks) % groups
         blocks_in = pick(received, source_shift)
         terms = jnp.einsum(
             "kes,kso->keo", blocks_in, tile_values, preferred_element_type=jnp.float32

time: 111 us -> 112 us (level)
  other arithmetic: 7.47 us -> 5.28 us
  starting transfers between devices: 22.2 us -> 23.6 us
    ppermute x12, starting transfers between devices: 17 us -> 18.4 us  [shifted(): return lax.ppermute(x, axis, [(i, (i + k) % n) for i in range(n)])]
  transfers between devices with their start and end apart: 13 -> 13, of which waited for: 6 -> 9; matrix products, arithmetic and copies ran while one was open for 4% -> 2% of each run, Pallas kernels for 0% -> 0%
where the time goes in v15:
time: 112 us; the launch traced here: 111 us
  blocking collectives  47.7 us (43%)
  waiting for transfers between devices  29.2 us (26%)
  starting transfers between devices  23.6 us (21%)
  other arithmetic  5.28 us (5%)
  local copies, waits for them, and re-layouts  2.53 us (2%)
  matrix products  2.46 us (2%)
    all_to_all x3, blocking collectives, body(): got = lax.all_to_all(sent, 'member', 0, 0, tiled=True)  29 us
    ppermute x12, waiting for transfers between devices, shifted(): return lax.ppermute(x, axis, [(i, (i + k) % n) for i in range(n)])  28.6 us
    all_to_all x2, blocking collectives, body(): got = lax.all_to_all(spread, 'member', 0, 0, tiled=True)  18.7 us
    ppermute x12, starting transfers between devices, shifted(): return lax.ppermute(x, axis, [(i, (i + k) % n) for i in range(n)])  18.4 us
    all_to_all x1, starting transfers between devices, body(): hist_got = lax.all_to_all(spread_hist, 'member', 0, 0, tiled=True)  5.17 us
  transfers between devices with their start and end apart: 13, of which 9 were waited for; matrix products, arithmetic and copies ran while one was open for 2% of the time, Pallas kernels for 0%

profile of v15, /device:TPU:0, one launch (start us, length us, event | category | flops | bytes accessed | tf_op | source)
XLA Modules:
  0.0 111.1 jit_solution(10334133469038463910)
XLA Ops:
  0.0 1.8 %broadcast_in_dim.1139 = bf16[8,2,32,512]{3,2,1,0:T(8,128)(2,1)} broadcast(bf16[2,32,512]{2,1,0:T(8,128)(2,1)} %bitcast.286), dimensions={1,2,3} | broadcast | bytes 589824 | tf_op jit(solution)/shard_map/broadcast_in_dim | solution.py:43
  1.8 5.2 %all-to-all-start = ((bf16[8,2,32,512]{3,2,1,0:T(8,128)(2,1)}), bf16[8,2,32,512]{3,2,1,0:T(8,128)(2,1)S(1)}, u32[]{:S(2)}, u32[]{:S(2)}) async-start(bf16[8,2,32,512]{3,2,1,0:T(8,128)(2,1)} %broadcast_in_dim.1139), calls=%async_computation | async-start | bytes 1048576 | tf_op jit(solution)/shard_map/all_to_all | solution.py:44
  7.0 1.6 %collective-permute-start.2 = (s32[4,3]{1,0:T(4,128)}, s32[4,3]{1,0:T(4,128)S(1)}, u32[]{:S(2)}, u32[]{:S(2)}) collective-permute-start(s32[4,3]{1,0:T(4,128)} %param.7), channel_id=1, source_target_pairs={{0,8},{8,16},{16,24},{24,0},{1,9},{9,17},{17,25},{25,1},{2,10},{10... | collective-permute-start | bytes 152 | tf_op jit(solution)/shard_map/ppermute | solution.py:14
  8.6 2.6 %collective-permute-start.1 = (s32[4,3]{1,0:T(4,128)}, s32[4,3]{1,0:T(4,128)S(1)}, u32[]{:S(2)}, u32[]{:S(2)}) collective-permute-start(s32[4,3]{1,0:T(4,128)} %param.7), channel_id=1, source_target_pairs={{0,16},{8,24},{16,0},{24,8},{1,17},{9,25},{17,1},{25,9},{2,18},{10... | collective-permute-start | bytes 152 | tf_op jit(solution)/shard_map/ppermute | solution.py:14
  11.2 1.3 %collective-permute-start = (s32[4,3]{1,0:T(4,128)}, s32[4,3]{1,0:T(4,128)S(1)}, u32[]{:S(2)}, u32[]{:S(2)}) collective-permute-start(s32[4,3]{1,0:T(4,128)} %param.7), channel_id=1, source_target_pairs={{0,24},{8,0},{16,8},{24,16},{1,25},{9,1},{17,9},{25,17},{2,26},{10... | collective-permute-start | bytes 152 | tf_op jit(solution)/shard_map/ppermute | solution.py:14
  12.5 0.7 iota_compare_fusion.2
  13.3 1.7 %collective-permute-done = s32[4,3]{1,0:T(4,128)S(1)} collective-permute-done((s32[4,3]{1,0:T(4,128)}, s32[4,3]{1,0:T(4,128)S(1)}, u32[]{:S(2)}, u32[]{:S(2)}) %collective-permute-start) | collective-permute-done | bytes 80 | tf_op jit(solution)/shard_map/ppermute | solution.py:14
  15.0 0.7 pad_add_fusion
  16.1 0.6 all-to-all-done
  16.8 0.5 select_add_fusion
  17.7 3.7 %collective-permute-start.3 = (bf16[128,512]{1,0:T(8,128)(2,1)S(1)}, bf16[128,512]{1,0:T(8,128)(2,1)S(1)}, u32[]{:S(2)}, u32[]{:S(2)}) collective-permute-start(bf16[128,512]{1,0:T(8,128)(2,1)S(1)} %get-tuple-element.36), channel_id=1, source_target_pairs={{0,24},{8,0},{16,8},{24,16},{1,25},{9,1},{17,9},{25,17},{2,26},{10... | collective-permute-start | bytes 393224 | tf_op jit(solution)/shard_map/ppermute | solution.py:14
  21.3 1.0 collective-permute-start.4
  22.3 2.5 %collective-permute-done.3 = bf16[128,512]{1,0:T(8,128)(2,1)S(1)} collective-permute-done((bf16[128,512]{1,0:T(8,128)(2,1)S(1)}, bf16[128,512]{1,0:T(8,128)(2,1)S(1)}, u32[]{:S(2)}, u32[]{:S(2)}) %collective-permute-start.3) | collective-permute-done | bytes 131104 | tf_op jit(solution)/shard_map/ppermute | solution.py:14
  25.4 5.8 %collective-permute-done.5 = bf16[128,512]{1,0:T(8,128)(2,1)S(1)} collective-permute-done((bf16[128,512]{1,0:T(8,128)(2,1)S(1)}, bf16[128,512]{1,0:T(8,128)(2,1)S(1)}, u32[]{:S(2)}, u32[]{:S(2)}) %collective-permute-start.5) | collective-permute-done | bytes 131104 | tf_op jit(solution)/shard_map/ppermute | solution.py:14
  31.2 0.6 select_reduce_fusion.5
  32.2 10.3 %all_to_all.30 = bf16[8,32,512]{2,1,0:T(8,128)(2,1)S(1)} all-to-all(bf16[8,32,512]{2,1,0:T(8,128)(2,1)S(1)} %select_add_fusion.5), channel_id=1, replica_groups=mesh['group'=4,'member'=8] {'member'}, dimensions={0} | all-to-all | bytes 524288 | tf_op jit(solution)/shard_map/all_to_all | solution.py:94
  42.8 9.3 %all_to_all.31 = bf16[8,32,512]{2,1,0:T(8,128)(2,1)S(1)} all-to-all(bf16[8,32,512]{2,1,0:T(8,128)(2,1)S(1)} %broadcast_in_dim.1242), channel_id=1, replica_groups=mesh['group'=4,'member'=8] {'member'}, dimensions={0} | all-to-all | bytes 524288 | tf_op jit(solution)/shard_map/all_to_all | solution.py:101
  52.7 1.5 %collective-permute-start.8 = (bf16[128,512]{1,0:T(8,128)(2,1)S(1)}, bf16[128,512]{1,0:T(8,128)(2,1)S(1)}, u32[]{:S(2)}, u32[]{:S(2)}) collective-permute-start(bf16[128,512]{1,0:T(8,128)(2,1)S(1)} %get-tuple-element.30), channel_id=1, source_target_pairs={{0,24},{8,0},{16,8},{24,16},{1,25},{9,1},{17,9},{25,17},{2,26},{10... | collective-permute-start | bytes 393224 | tf_op jit(solution)/shard_map/ppermute | solution.py:14
  54.2 1.1 %collective-permute-start.7 = (bf16[128,512]{1,0:T(8,128)(2,1)S(1)}, bf16[128,512]{1,0:T(8,128)(2,1)S(1)}, u32[]{:S(2)}, u32[]{:S(2)}) collective-permute-start(bf16[128,512]{1,0:T(8,128)(2,1)S(1)} %get-tuple-element.31), channel_id=1, source_target_pairs={{0,16},{8,24},{16,0},{24,8},{1,17},{9,25},{17,1},{25,9},{2,18},{10... | collective-permute-start | bytes 393224 | tf_op jit(solution)/shard_map/ppermute | solution.py:14
  55.3 1.9 %collective-permute-start.6 = (bf16[128,512]{1,0:T(8,128)(2,1)S(1)}, bf16[128,512]{1,0:T(8,128)(2,1)S(1)}, u32[]{:S(2)}, u32[]{:S(2)}) collective-permute-start(bf16[128,512]{1,0:T(8,128)(2,1)S(1)} %get-tuple-element.32), channel_id=1, source_target_pairs={{0,8},{8,16},{16,24},{24,0},{1,9},{9,17},{17,25},{25,1},{2,10},{10... | collective-permute-start | bytes 393224 | tf_op jit(solution)/shard_map/ppermute | solution.py:14
  57.2 1.2 %collective-permute-done.8 = bf16[128,512]{1,0:T(8,128)(2,1)S(1)} collective-permute-done((bf16[128,512]{1,0:T(8,128)(2,1)S(1)}, bf16[128,512]{1,0:T(8,128)(2,1)S(1)}, u32[]{:S(2)}, u32[]{:S(2)}) %collective-permute-start.8) | collective-permute-done | bytes 131104 | tf_op jit(solution)/shard_map/ppermute | solution.py:14
  58.4 8.1 %collective-permute-done.7 = bf16[128,512]{1,0:T(8,128)(2,1)S(1)} collective-permute-done((bf16[128,512]{1,0:T(8,128)(2,1)S(1)}, bf16[128,512]{1,0:T(8,128)(2,1)S(1)}, u32[]{:S(2)}, u32[]{:S(2)}) %collective-permute-start.7) | collective-permute-done | bytes 131104 | tf_op jit(solution)/shard_map/ppermute | solution.py:14
  66.5 0.6 select_reduce_fusion.3
  67.5 9.3 %all_to_all.32 = bf16[8,32,512]{2,1,0:T(8,128)(2,1)S(1)} all-to-all(bf16[8,32,512]{2,1,0:T(8,128)(2,1)S(1)} %select_add_fusion.3), channel_id=1, replica_groups=mesh['group'=4,'member'=8] {'member'}, dimensions={0} | all-to-all | bytes 524288 | tf_op jit(solution)/shard_map/all_to_all | solution.py:94
  77.1 9.3 %all_to_all.33 = bf16[8,32,512]{2,1,0:T(8,128)(2,1)S(1)} all-to-all(bf16[8,32,512]{2,1,0:T(8,128)(2,1)S(1)} %broadcast_in_dim.1291), channel_id=1, replica_groups=mesh['group'=4,'member'=8] {'member'}, dimensions={0} | all-to-all | bytes 524288 | tf_op jit(solution)/shard_map/all_to_all | solution.py:101
  87.1 1.7 %collective-permute-start.10 = (bf16[128,512]{1,0:T(8,128)(2,1)S(1)}, bf16[128,512]{1,0:T(8,128)(2,1)S(1)}, u32[]{:S(2)}, u32[]{:S(2)}) collective-permute-start(bf16[128,512]{1,0:T(8,128)(2,1)S(1)} %get-tuple-element.27), channel_id=1, source_target_pairs={{0,16},{8,24},{16,0},{24,8},{1,17},{9,25},{17,1},{25,9},{2,18},{10... | collective-permute-start | bytes 393224 | tf_op jit(solution)/shard_map/ppermute | solution.py:14
  88.7 1.9 %collective-permute-start.9 = (bf16[128,512]{1,0:T(8,128)(2,1)S(1)}, bf16[128,512]{1,0:T(8,128)(2,1)S(1)}, u32[]{:S(2)}, u32[]{:S(2)}) collective-permute-start(bf16[128,512]{1,0:T(8,128)(2,1)S(1)} %get-tuple-element.28), channel_id=1, source_target_pairs={{0,8},{8,16},{16,24},{24,0},{1,9},{9,17},{17,25},{25,1},{2,10},{10... | collective-permute-start | bytes 393224 | tf_op jit(solution)/shard_map/ppermute | solution.py:14
  90.7 1.9 %collective-permute-done.11 = bf16[128,512]{1,0:T(8,128)(2,1)S(1)} collective-permute-done((bf16[128,512]{1,0:T(8,128)(2,1)S(1)}, bf16[128,512]{1,0:T(8,128)(2,1)S(1)}, u32[]{:S(2)}, u32[]{:S(2)}) %collective-permute-start.11) | collective-permute-done | bytes 131104 | tf_op jit(solution)/shard_map/ppermute | solution.py:14
  92.5 7.4 %collective-permute-done.10 = bf16[128,512]{1,0:T(8,128)(2,1)S(1)} collective-permute-done((bf16[128,512]{1,0:T(8,128)(2,1)S(1)}, bf16[128,512]{1,0:T(8,128)(2,1)S(1)}, u32[]{:S(2)}, u32[]{:S(2)}) %collective-permute-start.10) | collective-permute-done | bytes 131104 | tf_op jit(solution)/shard_map/ppermute | solution.py:14
  99.9 0.6 select_reduce_fusion.1
  100.8 9.3 %all_to_all.34 = bf16[8,32,512]{2,1,0:T(8,128)(2,1)S(1)} all-to-all(bf16[8,32,512]{2,1,0:T(8,128)(2,1)S(1)} %select_add_fusion.1), channel_id=1, replica_groups=mesh['group'=4,'member'=8] {'member'}, dimensions={0} | all-to-all | bytes 524288 | tf_op jit(solution)/shard_map/all_to_all | solution.py:94
  110.4 0.7 maximum_bitcast_fusion
  (63 shorter events, 4.1 us)
Async XLA Ops:
  0.0 31.2 %copy-start = (bf16[4,512,512]{2,1,0:T(8,128)(2,1)S(1)}, bf16[4,512,512]{2,1,0:T(8,128)(2,1)}, u32[]{:S(2)}) copy-start(bf16[4,512,512]{2,1,0:T(8,128)(2,1)} %param.6) | copy-start | bytes 6291460
  1.8 14.9 %all-to-all-start = ((bf16[8,2,32,512]{3,2,1,0:T(8,128)(2,1)}), bf16[8,2,32,512]{3,2,1,0:T(8,128)(2,1)S(1)}, u32[]{:S(2)}, u32[]{:S(2)}) async-start(bf16[8,2,32,512]{3,2,1,0:T(8,128)(2,1)} %broadcast_in_dim.1139), calls=%async_computation | async-start | bytes 1048576 | tf_op jit(solution)/shard_map/all_to_all | solution.py:44
  7.0 6.2 %collective-permute-start.2 = (s32[4,3]{1,0:T(4,128)}, s32[4,3]{1,0:T(4,128)S(1)}, u32[]{:S(2)}, u32[]{:S(2)}) collective-permute-start(s32[4,3]{1,0:T(4,128)} %param.7), channel_id=1, source_target_pairs={{0,8},{8,16},{16,24},{24,0},{1,9},{9,17},{17,25},{25,1},{2,10},{10... | collective-permute-start | bytes 152 | tf_op jit(solution)/shard_map/ppermute | solution.py:14
  8.6 4.7 %collective-permute-start.1 = (s32[4,3]{1,0:T(4,128)}, s32[4,3]{1,0:T(4,128)S(1)}, u32[]{:S(2)}, u32[]{:S(2)}) collective-permute-start(s32[4,3]{1,0:T(4,128)} %param.7), channel_id=1, source_target_pairs={{0,16},{8,24},{16,0},{24,8},{1,17},{9,25},{17,1},{25,9},{2,18},{10... | collective-permute-start | bytes 152 | tf_op jit(solution)/shard_map/ppermute | solution.py:14
  11.2 3.8 %collective-permute-start = (s32[4,3]{1,0:T(4,128)}, s32[4,3]{1,0:T(4,128)S(1)}, u32[]{:S(2)}, u32[]{:S(2)}) collective-permute-start(s32[4,3]{1,0:T(4,128)} %param.7), channel_id=1, source_target_pairs={{0,24},{8,0},{16,8},{24,16},{1,25},{9,1},{17,9},{25,17},{2,26},{10... | collective-permute-start | bytes 152 | tf_op jit(solution)/shard_map/ppermute | solution.py:14
  16.8 8.1 %copy-start.3 = (s32[4,3]{1,0:T(4,128)S(1)}, s32[4,3]{1,0:T(4,128)}, u32[]{:S(2)}) copy-start(s32[4,3]{1,0:T(4,128)} %param.7) | copy-start | bytes 148
  16.8 8.4 %copy-start.4 = (s32[1,8]{1,0:T(1,128)S(1)}, s32[1,8]{1,0:T(1,128)}, u32[]{:S(2)}) copy-start(s32[1,8]{1,0:T(1,128)} %param.8) | copy-start | bytes 100
  17.7 7.2 %collective-permute-start.3 = (bf16[128,512]{1,0:T(8,128)(2,1)S(1)}, bf16[128,512]{1,0:T(8,128)(2,1)S(1)}, u32[]{:S(2)}, u32[]{:S(2)}) collective-permute-start(bf16[128,512]{1,0:T(8,128)(2,1)S(1)} %get-tuple-element.36), channel_id=1, source_target_pairs={{0,24},{8,0},{16,8},{24,16},{1,25},{9,1},{17,9},{25,17},{2,26},{10... | collective-permute-start | bytes 393224 | tf_op jit(solution)/shard_map/ppermute | solution.py:14
  21.3 9.9 %collective-permute-start.5 = (bf16[128,512]{1,0:T(8,128)(2,1)S(1)}, bf16[128,512]{1,0:T(8,128)(2,1)S(1)}, u32[]{:S(2)}, u32[]{:S(2)}) collective-permute-start(bf16[128,512]{1,0:T(8,128)(2,1)S(1)} %get-tuple-element.34), channel_id=1, source_target_pairs={{0,16},{8,24},{16,0},{24,8},{1,17},{9,25},{17,1},{25,9},{2,18},{10... | collective-permute-start | bytes 393224 | tf_op jit(solution)/shard_map/ppermute | solution.py:14
  21.3 9.9 %collective-permute-start.4 = (bf16[128,512]{1,0:T(8,128)(2,1)S(1)}, bf16[128,512]{1,0:T(8,128)(2,1)S(1)}, u32[]{:S(2)}, u32[]{:S(2)}) collective-permute-start(bf16[128,512]{1,0:T(8,128)(2,1)S(1)} %get-tuple-element.35), channel_id=1, source_target_pairs={{0,8},{8,16},{16,24},{24,0},{1,9},{9,17},{17,25},{25,1},{2,10},{10... | collective-permute-start | bytes 393224 | tf_op jit(solution)/shard_map/ppermute | solution.py:14
  31.8 10.7 %copy-start.1 = (bf16[1,512,512]{2,1,0:T(8,128)(2,1)S(1)}, bf16[1,512,512]{2,1,0:T(8,128)(2,1)}, u32[]{:S(2)}) copy-start(bf16[1,512,512]{2,1,0:T(8,128)(2,1)} %param.9) | copy-start | bytes 1572868
  31.8 10.7 %copy-start.2 = (f32[3,1,32,512]{3,2,1,0:T(8,128)S(1)}, f32[3,1,32,512]{3,2,1,0:T(8,128)}, u32[]{:S(2)}) copy-start(f32[3,1,32,512]{3,2,1,0:T(8,128)} %param.10) | copy-start | bytes 589828
  52.7 5.7 %collective-permute-start.8 = (bf16[128,512]{1,0:T(8,128)(2,1)S(1)}, bf16[128,512]{1,0:T(8,128)(2,1)S(1)}, u32[]{:S(2)}, u32[]{:S(2)}) collective-permute-start(bf16[128,512]{1,0:T(8,128)(2,1)S(1)} %get-tuple-element.30), channel_id=1, source_target_pairs={{0,24},{8,0},{16,8},{24,16},{1,25},{9,1},{17,9},{25,17},{2,26},{10... | collective-permute-start | bytes 393224 | tf_op jit(solution)/shard_map/ppermute | solution.py:14
  54.2 12.3 %collective-permute-start.7 = (bf16[128,512]{1,0:T(8,128)(2,1)S(1)}, bf16[128,512]{1,0:T(8,128)(2,1)S(1)}, u32[]{:S(2)}, u32[]{:S(2)}) collective-permute-start(bf16[128,512]{1,0:T(8,128)(2,1)S(1)} %get-tuple-element.31), channel_id=1, source_target_pairs={{0,16},{8,24},{16,0},{24,8},{1,17},{9,25},{17,1},{25,9},{2,18},{10... | collective-permute-start | bytes 393224 | tf_op jit(solution)/shard_map/ppermute | solution.py:14
  55.3 11.2 %collective-permute-start.6 = (bf16[128,512]{1,0:T(8,128)(2,1)S(1)}, bf16[128,512]{1,0:T(8,128)(2,1)S(1)}, u32[]{:S(2)}, u32[]{:S(2)}) collective-permute-start(bf16[128,512]{1,0:T(8,128)(2,1)S(1)} %get-tuple-element.32), channel_id=1, source_target_pairs={{0,8},{8,16},{16,24},{24,0},{1,9},{9,17},{17,25},{25,1},{2,10},{10... | collective-permute-start | bytes 393224 | tf_op jit(solution)/shard_map/ppermute | solution.py:14
  87.0 5.6 %collective-permute-start.11 = (bf16[128,512]{1,0:T(8,128)(2,1)S(1)}, bf16[128,512]{1,0:T(8,128)(2,1)S(1)}, u32[]{:S(2)}, u32[]{:S(2)}) collective-permute-start(bf16[128,512]{1,0:T(8,128)(2,1)S(1)} %get-tuple-element.26), channel_id=1, source_target_pairs={{0,24},{8,0},{16,8},{24,16},{1,25},{9,1},{17,9},{25,17},{2,26},{10... | collective-permute-start | bytes 393224 | tf_op jit(solution)/shard_map/ppermute | solution.py:14
  87.1 12.8 %collective-permute-start.10 = (bf16[128,512]{1,0:T(8,128)(2,1)S(1)}, bf16[128,512]{1,0:T(8,128)(2,1)S(1)}, u32[]{:S(2)}, u32[]{:S(2)}) collective-permute-start(bf16[128,512]{1,0:T(8,128)(2,1)S(1)} %get-tuple-element.27), channel_id=1, source_target_pairs={{0,16},{8,24},{16,0},{24,8},{1,17},{9,25},{17,1},{25,9},{2,18},{10... | collective-permute-start | bytes 393224 | tf_op jit(solution)/shard_map/ppermute | solution.py:14
  88.7 11.2 %collective-permute-start.9 = (bf16[128,512]{1,0:T(8,128)(2,1)S(1)}, bf16[128,512]{1,0:T(8,128)(2,1)S(1)}, u32[]{:S(2)}, u32[]{:S(2)}) collective-permute-start(bf16[128,512]{1,0:T(8,128)(2,1)S(1)} %get-tuple-element.28), channel_id=1, source_target_pairs={{0,8},{8,16},{16,24},{24,0},{1,9},{9,17},{17,25},{25,1},{2,10},{10... | collective-permute-start | bytes 393224 | tf_op jit(solution)/shard_map/ppermute | solution.py:14

commit v16 on v15

--- a/solution.py
+++ b/solution.py
@@ -43,8 +43,8 @@
     spread_hist = jnp.broadcast_to(history[:, 0][None], (members,) + history[:, 0].shape)
     hist_got = lax.all_to_all(spread_hist, "member", 0, 0, tiled=True)
     lists_later, _ = lax.optimization_barrier((tile_lists, spread_hist))
-    lists_by_shift = shift_gather(lists_later, "group", groups)
-    ahead = jnp.stack([lists_by_shift[(groups - k) % groups] for k in range(groups)])
+    lists_by_group = lax.all_gather(lists_later, "group", axis=0, tiled=False)
+    ahead = jnp.take(lists_by_group, (group_here + jnp.arange(groups)) % groups, axis=0)
     wanted = (ahead[:, :, 0] // group_blocks == group_here) & (ahead[:, :, 2] > 0)
     want_block = jnp.sum(jnp.where(wanted, ahead[:, :, 0] % group_blocks, 0), axis=1)
     want_delay = jnp.sum(jnp.where(wanted, ahead[:, :, 2], 0), axis=1)

time: 112 us -> 115 us (1.027)
  blocking collectives: 47.7 us -> 60.5 us
  starting transfers between devices: 23.6 us -> 15.5 us
  waiting for transfers between devices: 29.2 us -> 27.7 us
    all_gather x0 -> x1, blocking collectives: none -> 12.2 us  [body(): lists_by_group = lax.all_gather(lists_later, 'group', axis=0, tiled=False)]
    ppermute x12 -> x9, starting transfers between devices: 18.4 us -> 10.4 us  [shifted(): return lax.ppermute(x, axis, [(i, (i + k) % n) for i in range(n)])]
    ppermute x12 -> x9, waiting for transfers between devices: 28.6 us -> 27.7 us  [shifted(): return lax.ppermute(x, axis, [(i, (i + k) % n) for i in range(n)])]
  transfers between devices with their start and end apart: 13 -> 10, of which waited for: 9 -> 6; matrix products, arithmetic and copies ran while one was open for 2% -> 2% of each run, Pallas kernels for 0% -> 0%
where the time goes in v16:
time: 115 us
  blocking collectives  60.5 us (53%)
  waiting for transfers between devices  27.7 us (24%)
  starting transfers between devices  15.5 us (13%)
  other arithmetic  4.82 us (4%)
  local copies, waits for them, and re-layouts  3.11 us (3%)
  matrix products  2.47 us (2%)
    all_to_all x3, blocking collectives, body(): got = lax.all_to_all(sent, 'member', 0, 0, tiled=True)  29.6 us
    ppermute x9, waiting for transfers between devices, shifted(): return lax.ppermute(x, axis, [(i, (i + k) % n) for i in range(n)])  27.7 us
    all_to_all x2, blocking collectives, body(): got = lax.all_to_all(spread, 'member', 0, 0, tiled=True)  18.7 us
    all_gather x1, blocking collectives, body(): lists_by_group = lax.all_gather(lists_later, 'group', axis=0, tiled=False)  12.2 us
    ppermute x9, starting transfers between devices, shifted(): return lax.ppermute(x, axis, [(i, (i + k) % n) for i in range(n)])  10.4 us
    all_to_all x1, starting transfers between devices, body(): hist_got = lax.all_to_all(spread_hist, 'member', 0, 0, tiled=True)  5.17 us
  transfers between devices with their start and end apart: 10, of which 6 were waited for; matrix products, arithmetic and copies ran while one was open for 2% of the time, Pallas kernels for 0%

profile of v16, /device:TPU:0, one launch (start us, length us, event | category | flops | bytes accessed | tf_op | source)
XLA Modules:
  0.0 114.5 jit_solution(12462486157337075906)
XLA Ops:
  0.0 1.8 %broadcast_in_dim.1150 = bf16[8,2,32,512]{3,2,1,0:T(8,128)(2,1)} broadcast(bf16[2,32,512]{2,1,0:T(8,128)(2,1)} %bitcast.283), dimensions={1,2,3} | broadcast | bytes 589824 | tf_op jit(solution)/shard_map/broadcast_in_dim | solution.py:43
  1.8 5.2 %all-to-all-start = ((bf16[8,2,32,512]{3,2,1,0:T(8,128)(2,1)}), bf16[8,2,32,512]{3,2,1,0:T(8,128)(2,1)S(1)}, u32[]{:S(2)}, u32[]{:S(2)}) async-start(bf16[8,2,32,512]{3,2,1,0:T(8,128)(2,1)} %broadcast_in_dim.1150), calls=%async_computation | async-start | bytes 1048576 | tf_op jit(solution)/shard_map/all_to_all | solution.py:44
  7.2 12.2 %all-gather.1 = s32[4,4,3]{2,1,0:T(4,128)S(1)} all-gather(s32[1,4,3]{2,1,0:T(4,128)} %bitcast.284), channel_id=2, replica_groups=mesh['group'=4,'member'=8] {'group'}, dimensions={0}, use_global_device_ids=true | all-gather | bytes 240 | tf_op jit(solution)/shard_map/all_gather | solution.py:46
  19.4 0.6 gather_fusion
  20.0 0.2 slice_reduce_fusion.1
  20.5 0.7 iota_compare_fusion.2
  21.2 0.5 select_add_fusion
  22.1 2.2 %collective-permute-start = (bf16[128,512]{1,0:T(8,128)(2,1)S(1)}, bf16[128,512]{1,0:T(8,128)(2,1)S(1)}, u32[]{:S(2)}, u32[]{:S(2)}) collective-permute-start(bf16[128,512]{1,0:T(8,128)(2,1)S(1)} %get-tuple-element.36), channel_id=1, source_target_pairs={{0,24},{8,0},{16,8},{24,16},{1,25},{9,1},{17,9},{25,17},{2,26},{10... | collective-permute-start | bytes 393224 | tf_op jit(solution)/shard_map/ppermute | solution.py:14
  24.3 0.9 collective-permute-start.2
  25.2 3.8 %collective-permute-done = bf16[128,512]{1,0:T(8,128)(2,1)S(1)} collective-permute-done((bf16[128,512]{1,0:T(8,128)(2,1)S(1)}, bf16[128,512]{1,0:T(8,128)(2,1)S(1)}, u32[]{:S(2)}, u32[]{:S(2)}) %collective-permute-start) | collective-permute-done | bytes 131104 | tf_op jit(solution)/shard_map/ppermute | solution.py:14
  29.5 5.4 %collective-permute-done.2 = bf16[128,512]{1,0:T(8,128)(2,1)S(1)} collective-permute-done((bf16[128,512]{1,0:T(8,128)(2,1)S(1)}, bf16[128,512]{1,0:T(8,128)(2,1)S(1)}, u32[]{:S(2)}, u32[]{:S(2)}) %collective-permute-start.2) | collective-permute-done | bytes 131104 | tf_op jit(solution)/shard_map/ppermute | solution.py:14
  34.9 0.6 select_reduce_fusion.5
  35.9 10.9 %all_to_all.30 = bf16[8,32,512]{2,1,0:T(8,128)(2,1)S(1)} all-to-all(bf16[8,32,512]{2,1,0:T(8,128)(2,1)S(1)} %select_add_fusion.5), channel_id=1, replica_groups=mesh['group'=4,'member'=8] {'member'}, dimensions={0} | all-to-all | bytes 524288 | tf_op jit(solution)/shard_map/all_to_all | solution.py:94
  47.1 9.3 %all_to_all.31 = bf16[8,32,512]{2,1,0:T(8,128)(2,1)S(1)} all-to-all(bf16[8,32,512]{2,1,0:T(8,128)(2,1)S(1)} %broadcast_in_dim.1254), channel_id=1, replica_groups=mesh['group'=4,'member'=8] {'member'}, dimensions={0} | all-to-all | bytes 524288 | tf_op jit(solution)/shard_map/all_to_all | solution.py:101
  56.4 0.2 select_add_fusion.4
  57.0 0.6 collective-permute-start.5
  57.6 1.0 collective-permute-start.4
  58.6 1.9 %collective-permute-start.3 = (bf16[128,512]{1,0:T(8,128)(2,1)S(1)}, bf16[128,512]{1,0:T(8,128)(2,1)S(1)}, u32[]{:S(2)}, u32[]{:S(2)}) collective-permute-start(bf16[128,512]{1,0:T(8,128)(2,1)S(1)} %get-tuple-element.32), channel_id=1, source_target_pairs={{0,8},{8,16},{16,24},{24,0},{1,9},{9,17},{17,25},{25,1},{2,10},{10... | collective-permute-start | bytes 393224 | tf_op jit(solution)/shard_map/ppermute | solution.py:14
  60.5 2.0 %collective-permute-done.5 = bf16[128,512]{1,0:T(8,128)(2,1)S(1)} collective-permute-done((bf16[128,512]{1,0:T(8,128)(2,1)S(1)}, bf16[128,512]{1,0:T(8,128)(2,1)S(1)}, u32[]{:S(2)}, u32[]{:S(2)}) %collective-permute-start.5) | collective-permute-done | bytes 131104 | tf_op jit(solution)/shard_map/ppermute | solution.py:14
  62.5 7.3 %collective-permute-done.4 = bf16[128,512]{1,0:T(8,128)(2,1)S(1)} collective-permute-done((bf16[128,512]{1,0:T(8,128)(2,1)S(1)}, bf16[128,512]{1,0:T(8,128)(2,1)S(1)}, u32[]{:S(2)}, u32[]{:S(2)}) %collective-permute-start.4) | collective-permute-done | bytes 131104 | tf_op jit(solution)/shard_map/ppermute | solution.py:14
  69.8 0.7 select_reduce_fusion.3
  70.8 9.3 %all_to_all.32 = bf16[8,32,512]{2,1,0:T(8,128)(2,1)S(1)} all-to-all(bf16[8,32,512]{2,1,0:T(8,128)(2,1)S(1)} %select_add_fusion.3), channel_id=1, replica_groups=mesh['group'=4,'member'=8] {'member'}, dimensions={0} | all-to-all | bytes 524288 | tf_op jit(solution)/shard_map/all_to_all | solution.py:94
  80.4 9.3 %all_to_all.33 = bf16[8,32,512]{2,1,0:T(8,128)(2,1)S(1)} all-to-all(bf16[8,32,512]{2,1,0:T(8,128)(2,1)S(1)} %broadcast_in_dim.1303), channel_id=1, replica_groups=mesh['group'=4,'member'=8] {'member'}, dimensions={0} | all-to-all | bytes 524288 | tf_op jit(solution)/shard_map/all_to_all | solution.py:101
  89.8 0.2 select_add_fusion.2
  90.4 1.7 %collective-permute-start.7 = (bf16[128,512]{1,0:T(8,128)(2,1)S(1)}, bf16[128,512]{1,0:T(8,128)(2,1)S(1)}, u32[]{:S(2)}, u32[]{:S(2)}) collective-permute-start(bf16[128,512]{1,0:T(8,128)(2,1)S(1)} %get-tuple-element.27), channel_id=1, source_target_pairs={{0,16},{8,24},{16,0},{24,8},{1,17},{9,25},{17,1},{25,9},{2,18},{10... | collective-permute-start | bytes 393224 | tf_op jit(solution)/shard_map/ppermute | solution.py:14
  92.1 1.9 %collective-permute-start.6 = (bf16[128,512]{1,0:T(8,128)(2,1)S(1)}, bf16[128,512]{1,0:T(8,128)(2,1)S(1)}, u32[]{:S(2)}, u32[]{:S(2)}) collective-permute-start(bf16[128,512]{1,0:T(8,128)(2,1)S(1)} %get-tuple-element.28), channel_id=1, source_target_pairs={{0,8},{8,16},{16,24},{24,0},{1,9},{9,17},{17,25},{25,1},{2,10},{10... | collective-permute-start | bytes 393224 | tf_op jit(solution)/shard_map/ppermute | solution.py:14
  94.1 1.8 %collective-permute-done.8 = bf16[128,512]{1,0:T(8,128)(2,1)S(1)} collective-permute-done((bf16[128,512]{1,0:T(8,128)(2,1)S(1)}, bf16[128,512]{1,0:T(8,128)(2,1)S(1)}, u32[]{:S(2)}, u32[]{:S(2)}) %collective-permute-start.8) | collective-permute-done | bytes 131104 | tf_op jit(solution)/shard_map/ppermute | solution.py:14
  95.9 7.4 %collective-permute-done.7 = bf16[128,512]{1,0:T(8,128)(2,1)S(1)} collective-permute-done((bf16[128,512]{1,0:T(8,128)(2,1)S(1)}, bf16[128,512]{1,0:T(8,128)(2,1)S(1)}, u32[]{:S(2)}, u32[]{:S(2)}) %collective-permute-start.7) | collective-permute-done | bytes 131104 | tf_op jit(solution)/shard_map/ppermute | solution.py:14
  103.3 0.6 select_reduce_fusion.1
  104.0 0.2 select_add_fusion.1
  104.3 9.3 %all_to_all.34 = bf16[8,32,512]{2,1,0:T(8,128)(2,1)S(1)} all-to-all(bf16[8,32,512]{2,1,0:T(8,128)(2,1)S(1)} %select_add_fusion.1), channel_id=1, replica_groups=mesh['group'=4,'member'=8] {'member'}, dimensions={0} | all-to-all | bytes 524288 | tf_op jit(solution)/shard_map/all_to_all | solution.py:94
  113.8 0.7 maximum_bitcast_fusion
  (62 shorter events, 3.3 us)
Async XLA Ops:
  0.0 34.9 %copy-start = (bf16[4,512,512]{2,1,0:T(8,128)(2,1)S(1)}, bf16[4,512,512]{2,1,0:T(8,128)(2,1)}, u32[]{:S(2)}) copy-start(bf16[4,512,512]{2,1,0:T(8,128)(2,1)} %param.6) | copy-start | bytes 6291460
  1.8 19.3 %all-to-all-start = ((bf16[8,2,32,512]{3,2,1,0:T(8,128)(2,1)}), bf16[8,2,32,512]{3,2,1,0:T(8,128)(2,1)S(1)}, u32[]{:S(2)}, u32[]{:S(2)}) async-start(bf16[8,2,32,512]{3,2,1,0:T(8,128)(2,1)} %broadcast_in_dim.1150), calls=%async_computation | async-start | bytes 1048576 | tf_op jit(solution)/shard_map/all_to_all | solution.py:44
  21.2 7.7 %copy-start.3 = (s32[4,3]{1,0:T(4,128)S(1)}, s32[4,3]{1,0:T(4,128)}, u32[]{:S(2)}) copy-start(s32[4,3]{1,0:T(4,128)} %param.7) | copy-start | bytes 148
  21.2 8.1 %copy-start.4 = (s32[1,8]{1,0:T(1,128)S(1)}, s32[1,8]{1,0:T(1,128)}, u32[]{:S(2)}) copy-start(s32[1,8]{1,0:T(1,128)} %param.8) | copy-start | bytes 100
  22.1 6.9 %collective-permute-start = (bf16[128,512]{1,0:T(8,128)(2,1)S(1)}, bf16[128,512]{1,0:T(8,128)(2,1)S(1)}, u32[]{:S(2)}, u32[]{:S(2)}) collective-permute-start(bf16[128,512]{1,0:T(8,128)(2,1)S(1)} %get-tuple-element.36), channel_id=1, source_target_pairs={{0,24},{8,0},{16,8},{24,16},{1,25},{9,1},{17,9},{25,17},{2,26},{10... | collective-permute-start | bytes 393224 | tf_op jit(solution)/shard_map/ppermute | solution.py:14
  24.3 10.6 %collective-permute-start.2 = (bf16[128,512]{1,0:T(8,128)(2,1)S(1)}, bf16[128,512]{1,0:T(8,128)(2,1)S(1)}, u32[]{:S(2)}, u32[]{:S(2)}) collective-permute-start(bf16[128,512]{1,0:T(8,128)(2,1)S(1)} %get-tuple-element.34), channel_id=1, source_target_pairs={{0,16},{8,24},{16,0},{24,8},{1,17},{9,25},{17,1},{25,9},{2,18},{10... | collective-permute-start | bytes 393224 | tf_op jit(solution)/shard_map/ppermute | solution.py:14
  25.2 9.7 %collective-permute-start.1 = (bf16[128,512]{1,0:T(8,128)(2,1)S(1)}, bf16[128,512]{1,0:T(8,128)(2,1)S(1)}, u32[]{:S(2)}, u32[]{:S(2)}) collective-permute-start(bf16[128,512]{1,0:T(8,128)(2,1)S(1)} %get-tuple-element.35), channel_id=1, source_target_pairs={{0,8},{8,16},{16,24},{24,0},{1,9},{9,17},{17,25},{25,1},{2,10},{10... | collective-permute-start | bytes 393224 | tf_op jit(solution)/shard_map/ppermute | solution.py:14
  35.5 11.3 %copy-start.1 = (bf16[1,512,512]{2,1,0:T(8,128)(2,1)S(1)}, bf16[1,512,512]{2,1,0:T(8,128)(2,1)}, u32[]{:S(2)}) copy-start(bf16[1,512,512]{2,1,0:T(8,128)(2,1)} %param.9) | copy-start | bytes 1572868
  35.6 11.3 %copy-start.2 = (f32[3,1,32,512]{3,2,1,0:T(8,128)S(1)}, f32[3,1,32,512]{3,2,1,0:T(8,128)}, u32[]{:S(2)}) copy-start(f32[3,1,32,512]{3,2,1,0:T(8,128)} %param.10) | copy-start | bytes 589828
  57.0 5.5 %collective-permute-start.5 = (bf16[128,512]{1,0:T(8,128)(2,1)S(1)}, bf16[128,512]{1,0:T(8,128)(2,1)S(1)}, u32[]{:S(2)}, u32[]{:S(2)}) collective-permute-start(bf16[128,512]{1,0:T(8,128)(2,1)S(1)} %get-tuple-element.30), channel_id=1, source_target_pairs={{0,24},{8,0},{16,8},{24,16},{1,25},{9,1},{17,9},{25,17},{2,26},{10... | collective-permute-start | bytes 393224 | tf_op jit(solution)/shard_map/ppermute | solution.py:14
  57.6 12.2 %collective-permute-start.4 = (bf16[128,512]{1,0:T(8,128)(2,1)S(1)}, bf16[128,512]{1,0:T(8,128)(2,1)S(1)}, u32[]{:S(2)}, u32[]{:S(2)}) collective-permute-start(bf16[128,512]{1,0:T(8,128)(2,1)S(1)} %get-tuple-element.31), channel_id=1, source_target_pairs={{0,16},{8,24},{16,0},{24,8},{1,17},{9,25},{17,1},{25,9},{2,18},{10... | collective-permute-start | bytes 393224 | tf_op jit(solution)/shard_map/ppermute | solution.py:14
  58.6 11.2 %collective-permute-start.3 = (bf16[128,512]{1,0:T(8,128)(2,1)S(1)}, bf16[128,512]{1,0:T(8,128)(2,1)S(1)}, u32[]{:S(2)}, u32[]{:S(2)}) collective-permute-start(bf16[128,512]{1,0:T(8,128)(2,1)S(1)} %get-tuple-element.32), channel_id=1, source_target_pairs={{0,8},{8,16},{16,24},{24,0},{1,9},{9,17},{17,25},{25,1},{2,10},{10... | collective-permute-start | bytes 393224 | tf_op jit(solution)/shard_map/ppermute | solution.py:14
  90.3 5.6 %collective-permute-start.8 = (bf16[128,512]{1,0:T(8,128)(2,1)S(1)}, bf16[128,512]{1,0:T(8,128)(2,1)S(1)}, u32[]{:S(2)}, u32[]{:S(2)}) collective-permute-start(bf16[128,512]{1,0:T(8,128)(2,1)S(1)} %get-tuple-element.26), channel_id=1, source_target_pairs={{0,24},{8,0},{16,8},{24,16},{1,25},{9,1},{17,9},{25,17},{2,26},{10... | collective-permute-start | bytes 393224 | tf_op jit(solution)/shard_map/ppermute | solution.py:14
  90.4 12.9 %collective-permute-start.7 = (bf16[128,512]{1,0:T(8,128)(2,1)S(1)}, bf16[128,512]{1,0:T(8,128)(2,1)S(1)}, u32[]{:S(2)}, u32[]{:S(2)}) collective-permute-start(bf16[128,512]{1,0:T(8,128)(2,1)S(1)} %get-tuple-element.27), channel_id=1, source_target_pairs={{0,16},{8,24},{16,0},{24,8},{1,17},{9,25},{17,1},{25,9},{2,18},{10... | collective-permute-start | bytes 393224 | tf_op jit(solution)/shard_map/ppermute | solution.py:14
  92.1 11.2 %collective-permute-start.6 = (bf16[128,512]{1,0:T(8,128)(2,1)S(1)}, bf16[128,512]{1,0:T(8,128)(2,1)S(1)}, u32[]{:S(2)}, u32[]{:S(2)}) collective-permute-start(bf16[128,512]{1,0:T(8,128)(2,1)S(1)} %get-tuple-element.28), channel_id=1, source_target_pairs={{0,8},{8,16},{16,24},{24,0},{1,9},{9,17},{17,25},{25,1},{2,10},{10... | collective-permute-start | bytes 393224 | tf_op jit(solution)/shard_map/ppermute | solution.py:14

commit v17 on v15

--- a/solution.py
+++ b/solution.py
@@ -97,8 +97,7 @@
         current = jnp.dot(residual, inverses[0], preferred_element_type=jnp.float32)
         results.append(current)
         if step + 1 < STEPS:
-            spread = jnp.broadcast_to(current.astype(jnp.bfloat16)[None], (members, share, BLOCK))
-            got = lax.all_to_all(spread, "member", 0, 0, tiled=True)
+            got = lax.all_gather(current.astype(jnp.bfloat16), "member", axis=0, tiled=False)
             placed = pick([got[m] for m in range(members)], owners)
             blocks.append(placed.reshape(group_blocks, EXCITE, BLOCK))
     return jnp.stack(results)[:, None]

time: 112 us -> 112 us (level)
  waiting for transfers between devices: 29.2 us -> 31.6 us
  blocking collectives: 47.7 us -> 46 us
    all_to_all x2 -> x0, blocking collectives: 18.7 us -> none  [body(): got = lax.all_to_all(spread, 'member', 0, 0, tiled=True)]
    all_gather x0 -> x2, blocking collectives: none -> 16.7 us  [body(): lax.all_gather(current.astype(jnp.bfloat16), 'member', axis=0, tiled=False)]
    ppermute x12, waiting for transfers between devices: 28.6 us -> 30.9 us  [shifted(): return lax.ppermute(x, axis, [(i, (i + k) % n) for i in range(n)])]
where the time goes in v17:
time: 112 us
  blocking collectives  46 us (41%)
  waiting for transfers between devices  31.6 us (28%)
  starting transfers between devices  23.6 us (21%)
  other arithmetic  5.28 us (5%)
  local copies, waits for them, and re-layouts  2.47 us (2%)
  matrix products  2.46 us (2%)
    ppermute x12, waiting for transfers between devices, shifted(): return lax.ppermute(x, axis, [(i, (i + k) % n) for i in range(n)])  30.9 us
    all_to_all x3, blocking collectives, body(): got = lax.all_to_all(sent, 'member', 0, 0, tiled=True)  29.2 us
    ppermute x12, starting transfers between devices, shifted(): return lax.ppermute(x, axis, [(i, (i + k) % n) for i in range(n)])  18.4 us
    all_gather x2, blocking collectives, body(): lax.all_gather(current.astype(jnp.bfloat16), 'member', axis=0, tiled=False)  16.7 us
    all_to_all x1, starting transfers between devices, body(): hist_got = lax.all_to_all(spread_hist, 'member', 0, 0, tiled=True)  5.17 us
  transfers between devices with their start and end apart: 13, of which 9 were waited for; matrix products, arithmetic and copies ran while one was open for 2% of the time, Pallas kernels for 0%

profile of v17, /device:TPU:0, one launch (start us, length us, event | category | flops | bytes accessed | tf_op | source)
XLA Modules:
  0.0 111.7 jit_solution(2650968530621800858)
XLA Ops:
  0.0 1.8 %broadcast_in_dim.1127 = bf16[8,2,32,512]{3,2,1,0:T(8,128)(2,1)} broadcast(bf16[2,32,512]{2,1,0:T(8,128)(2,1)} %bitcast.254), dimensions={1,2,3} | broadcast | bytes 589824 | tf_op jit(solution)/shard_map/broadcast_in_dim | solution.py:43
  1.8 5.2 %all-to-all-start = ((bf16[8,2,32,512]{3,2,1,0:T(8,128)(2,1)}), bf16[8,2,32,512]{3,2,1,0:T(8,128)(2,1)S(1)}, u32[]{:S(2)}, u32[]{:S(2)}) async-start(bf16[8,2,32,512]{3,2,1,0:T(8,128)(2,1)} %broadcast_in_dim.1127), calls=%async_computation | async-start | bytes 1048576 | tf_op jit(solution)/shard_map/all_to_all | solution.py:44
  7.0 1.6 %collective-permute-start.2 = (s32[4,3]{1,0:T(4,128)}, s32[4,3]{1,0:T(4,128)S(1)}, u32[]{:S(2)}, u32[]{:S(2)}) collective-permute-start(s32[4,3]{1,0:T(4,128)} %param.7), channel_id=1, source_target_pairs={{0,8},{8,16},{16,24},{24,0},{1,9},{9,17},{17,25},{25,1},{2,10},{10... | collective-permute-start | bytes 152 | tf_op jit(solution)/shard_map/ppermute | solution.py:14
  8.6 2.6 %collective-permute-start.1 = (s32[4,3]{1,0:T(4,128)}, s32[4,3]{1,0:T(4,128)S(1)}, u32[]{:S(2)}, u32[]{:S(2)}) collective-permute-start(s32[4,3]{1,0:T(4,128)} %param.7), channel_id=1, source_target_pairs={{0,16},{8,24},{16,0},{24,8},{1,17},{9,25},{17,1},{25,9},{2,18},{10... | collective-permute-start | bytes 152 | tf_op jit(solution)/shard_map/ppermute | solution.py:14
  11.2 1.3 %collective-permute-start = (s32[4,3]{1,0:T(4,128)}, s32[4,3]{1,0:T(4,128)S(1)}, u32[]{:S(2)}, u32[]{:S(2)}) collective-permute-start(s32[4,3]{1,0:T(4,128)} %param.7), channel_id=1, source_target_pairs={{0,24},{8,0},{16,8},{24,16},{1,25},{9,1},{17,9},{25,17},{2,26},{10... | collective-permute-start | bytes 152 | tf_op jit(solution)/shard_map/ppermute | solution.py:14
  12.5 0.7 iota_compare_fusion.2
  13.3 1.7 %collective-permute-done = s32[4,3]{1,0:T(4,128)S(1)} collective-permute-done((s32[4,3]{1,0:T(4,128)}, s32[4,3]{1,0:T(4,128)S(1)}, u32[]{:S(2)}, u32[]{:S(2)}) %collective-permute-start) | collective-permute-done | bytes 80 | tf_op jit(solution)/shard_map/ppermute | solution.py:14
  15.0 0.7 pad_add_fusion
  16.1 0.6 all-to-all-done
  16.8 0.5 select_add_fusion
  17.7 3.7 %collective-permute-start.3 = (bf16[128,512]{1,0:T(8,128)(2,1)S(1)}, bf16[128,512]{1,0:T(8,128)(2,1)S(1)}, u32[]{:S(2)}, u32[]{:S(2)}) collective-permute-start(bf16[128,512]{1,0:T(8,128)(2,1)S(1)} %get-tuple-element.36), channel_id=1, source_target_pairs={{0,24},{8,0},{16,8},{24,16},{1,25},{9,1},{17,9},{25,17},{2,26},{10... | collective-permute-start | bytes 393224 | tf_op jit(solution)/shard_map/ppermute | solution.py:14
  21.3 1.0 collective-permute-start.4
  22.3 2.5 %collective-permute-done.3 = bf16[128,512]{1,0:T(8,128)(2,1)S(1)} collective-permute-done((bf16[128,512]{1,0:T(8,128)(2,1)S(1)}, bf16[128,512]{1,0:T(8,128)(2,1)S(1)}, u32[]{:S(2)}, u32[]{:S(2)}) %collective-permute-start.3) | collective-permute-done | bytes 131104 | tf_op jit(solution)/shard_map/ppermute | solution.py:14
  25.4 5.8 %collective-permute-done.5 = bf16[128,512]{1,0:T(8,128)(2,1)S(1)} collective-permute-done((bf16[128,512]{1,0:T(8,128)(2,1)S(1)}, bf16[128,512]{1,0:T(8,128)(2,1)S(1)}, u32[]{:S(2)}, u32[]{:S(2)}) %collective-permute-start.5) | collective-permute-done | bytes 131104 | tf_op jit(solution)/shard_map/ppermute | solution.py:14
  31.2 0.6 select_reduce_fusion.5
  32.2 10.3 %all_to_all.20 = bf16[8,32,512]{2,1,0:T(8,128)(2,1)S(1)} all-to-all(bf16[8,32,512]{2,1,0:T(8,128)(2,1)S(1)} %select_add_fusion.5), channel_id=1, replica_groups=mesh['group'=4,'member'=8] {'member'}, dimensions={0} | all-to-all | bytes 524288 | tf_op jit(solution)/shard_map/all_to_all | solution.py:94
  42.7 8.4 %all-gather = bf16[256,512]{1,0:T(8,128)(2,1)S(1)} all-gather(bf16[32,512]{1,0:T(8,128)(2,1)S(1)} %get-tuple-element.121), channel_id=2, replica_groups=mesh['group'=4,'member'=8] {'member'}, dimensions={0}, use_global_device_ids=true | all-gather | bytes 294912 | tf_op jit(solution)/shard_map/all_gather | solution.py:100
  51.6 1.5 %collective-permute-start.8 = (bf16[128,512]{1,0:T(8,128)(2,1)S(1)}, bf16[128,512]{1,0:T(8,128)(2,1)S(1)}, u32[]{:S(2)}, u32[]{:S(2)}) collective-permute-start(bf16[128,512]{1,0:T(8,128)(2,1)S(1)} %get-tuple-element.30), channel_id=1, source_target_pairs={{0,24},{8,0},{16,8},{24,16},{1,25},{9,1},{17,9},{25,17},{2,26},{10... | collective-permute-start | bytes 393224 | tf_op jit(solution)/shard_map/ppermute | solution.py:14
  53.1 1.1 %collective-permute-start.7 = (bf16[128,512]{1,0:T(8,128)(2,1)S(1)}, bf16[128,512]{1,0:T(8,128)(2,1)S(1)}, u32[]{:S(2)}, u32[]{:S(2)}) collective-permute-start(bf16[128,512]{1,0:T(8,128)(2,1)S(1)} %get-tuple-element.31), channel_id=1, source_target_pairs={{0,16},{8,24},{16,0},{24,8},{1,17},{9,25},{17,1},{25,9},{2,18},{10... | collective-permute-start | bytes 393224 | tf_op jit(solution)/shard_map/ppermute | solution.py:14
  54.3 1.9 %collective-permute-start.6 = (bf16[128,512]{1,0:T(8,128)(2,1)S(1)}, bf16[128,512]{1,0:T(8,128)(2,1)S(1)}, u32[]{:S(2)}, u32[]{:S(2)}) collective-permute-start(bf16[128,512]{1,0:T(8,128)(2,1)S(1)} %get-tuple-element.32), channel_id=1, source_target_pairs={{0,8},{8,16},{16,24},{24,0},{1,9},{9,17},{17,25},{25,1},{2,10},{10... | collective-permute-start | bytes 393224 | tf_op jit(solution)/shard_map/ppermute | solution.py:14
  56.2 1.2 %collective-permute-done.8 = bf16[128,512]{1,0:T(8,128)(2,1)S(1)} collective-permute-done((bf16[128,512]{1,0:T(8,128)(2,1)S(1)}, bf16[128,512]{1,0:T(8,128)(2,1)S(1)}, u32[]{:S(2)}, u32[]{:S(2)}) %collective-permute-start.8) | collective-permute-done | bytes 131104 | tf_op jit(solution)/shard_map/ppermute | solution.py:14
  57.5 9.2 %collective-permute-done.7 = bf16[128,512]{1,0:T(8,128)(2,1)S(1)} collective-permute-done((bf16[128,512]{1,0:T(8,128)(2,1)S(1)}, bf16[128,512]{1,0:T(8,128)(2,1)S(1)}, u32[]{:S(2)}, u32[]{:S(2)}) %collective-permute-start.7) | collective-permute-done | bytes 131104 | tf_op jit(solution)/shard_map/ppermute | solution.py:14
  66.6 0.6 select_reduce_fusion.3
  67.6 9.5 %all_to_all.21 = bf16[8,32,512]{2,1,0:T(8,128)(2,1)S(1)} all-to-all(bf16[8,32,512]{2,1,0:T(8,128)(2,1)S(1)} %select_add_fusion.3), channel_id=1, replica_groups=mesh['group'=4,'member'=8] {'member'}, dimensions={0} | all-to-all | bytes 524288 | tf_op jit(solution)/shard_map/all_to_all | solution.py:94
  77.3 8.4 %all-gather.1 = bf16[256,512]{1,0:T(8,128)(2,1)S(1)} all-gather(bf16[32,512]{1,0:T(8,128)(2,1)S(1)} %get-tuple-element.123), channel_id=3, replica_groups=mesh['group'=4,'member'=8] {'member'}, dimensions={0}, use_global_device_ids=true | all-gather | bytes 294912 | tf_op jit(solution)/shard_map/all_gather | solution.py:100
  86.3 1.7 %collective-permute-start.10 = (bf16[128,512]{1,0:T(8,128)(2,1)S(1)}, bf16[128,512]{1,0:T(8,128)(2,1)S(1)}, u32[]{:S(2)}, u32[]{:S(2)}) collective-permute-start(bf16[128,512]{1,0:T(8,128)(2,1)S(1)} %get-tuple-element.27), channel_id=1, source_target_pairs={{0,16},{8,24},{16,0},{24,8},{1,17},{9,25},{17,1},{25,9},{2,18},{10... | collective-permute-start | bytes 393224 | tf_op jit(solution)/shard_map/ppermute | solution.py:14
  88.0 1.9 %collective-permute-start.9 = (bf16[128,512]{1,0:T(8,128)(2,1)S(1)}, bf16[128,512]{1,0:T(8,128)(2,1)S(1)}, u32[]{:S(2)}, u32[]{:S(2)}) collective-permute-start(bf16[128,512]{1,0:T(8,128)(2,1)S(1)} %get-tuple-element.28), channel_id=1, source_target_pairs={{0,8},{8,16},{16,24},{24,0},{1,9},{9,17},{17,25},{25,1},{2,10},{10... | collective-permute-start | bytes 393224 | tf_op jit(solution)/shard_map/ppermute | solution.py:14
  89.9 2.8 %collective-permute-done.11 = bf16[128,512]{1,0:T(8,128)(2,1)S(1)} collective-permute-done((bf16[128,512]{1,0:T(8,128)(2,1)S(1)}, bf16[128,512]{1,0:T(8,128)(2,1)S(1)}, u32[]{:S(2)}, u32[]{:S(2)}) %collective-permute-start.11) | collective-permute-done | bytes 131104 | tf_op jit(solution)/shard_map/ppermute | solution.py:14
  92.8 7.6 %collective-permute-done.10 = bf16[128,512]{1,0:T(8,128)(2,1)S(1)} collective-permute-done((bf16[128,512]{1,0:T(8,128)(2,1)S(1)}, bf16[128,512]{1,0:T(8,128)(2,1)S(1)}, u32[]{:S(2)}, u32[]{:S(2)}) %collective-permute-start.10) | collective-permute-done | bytes 131104 | tf_op jit(solution)/shard_map/ppermute | solution.py:14
  100.3 0.6 select_reduce_fusion.1
  101.3 9.5 %all_to_all.22 = bf16[8,32,512]{2,1,0:T(8,128)(2,1)S(1)} all-to-all(bf16[8,32,512]{2,1,0:T(8,128)(2,1)S(1)} %select_add_fusion.1), channel_id=1, replica_groups=mesh['group'=4,'member'=8] {'member'}, dimensions={0} | all-to-all | bytes 524288 | tf_op jit(solution)/shard_map/all_to_all | solution.py:94
  111.0 0.7 maximum_bitcast_fusion
  (61 shorter events, 4.1 us)
Async XLA Ops:
  0.0 31.2 %copy-start = (bf16[4,512,512]{2,1,0:T(8,128)(2,1)S(1)}, bf16[4,512,512]{2,1,0:T(8,128)(2,1)}, u32[]{:S(2)}) copy-start(bf16[4,512,512]{2,1,0:T(8,128)(2,1)} %param.6) | copy-start | bytes 6291460
  1.8 14.9 %all-to-all-start = ((bf16[8,2,32,512]{3,2,1,0:T(8,128)(2,1)}), bf16[8,2,32,512]{3,2,1,0:T(8,128)(2,1)S(1)}, u32[]{:S(2)}, u32[]{:S(2)}) async-start(bf16[8,2,32,512]{3,2,1,0:T(8,128)(2,1)} %broadcast_in_dim.1127), calls=%async_computation | async-start | bytes 1048576 | tf_op jit(solution)/shard_map/all_to_all | solution.py:44
  7.0 6.2 %collective-permute-start.2 = (s32[4,3]{1,0:T(4,128)}, s32[4,3]{1,0:T(4,128)S(1)}, u32[]{:S(2)}, u32[]{:S(2)}) collective-permute-start(s32[4,3]{1,0:T(4,128)} %param.7), channel_id=1, source_target_pairs={{0,8},{8,16},{16,24},{24,0},{1,9},{9,17},{17,25},{25,1},{2,10},{10... | collective-permute-start | bytes 152 | tf_op jit(solution)/shard_map/ppermute | solution.py:14
  8.6 4.7 %collective-permute-start.1 = (s32[4,3]{1,0:T(4,128)}, s32[4,3]{1,0:T(4,128)S(1)}, u32[]{:S(2)}, u32[]{:S(2)}) collective-permute-start(s32[4,3]{1,0:T(4,128)} %param.7), channel_id=1, source_target_pairs={{0,16},{8,24},{16,0},{24,8},{1,17},{9,25},{17,1},{25,9},{2,18},{10... | collective-permute-start | bytes 152 | tf_op jit(solution)/shard_map/ppermute | solution.py:14
  11.2 3.8 %collective-permute-start = (s32[4,3]{1,0:T(4,128)}, s32[4,3]{1,0:T(4,128)S(1)}, u32[]{:S(2)}, u32[]{:S(2)}) collective-permute-start(s32[4,3]{1,0:T(4,128)} %param.7), channel_id=1, source_target_pairs={{0,24},{8,0},{16,8},{24,16},{1,25},{9,1},{17,9},{25,17},{2,26},{10... | collective-permute-start | bytes 152 | tf_op jit(solution)/shard_map/ppermute | solution.py:14
  16.8 8.1 %copy-start.3 = (s32[4,3]{1,0:T(4,128)S(1)}, s32[4,3]{1,0:T(4,128)}, u32[]{:S(2)}) copy-start(s32[4,3]{1,0:T(4,128)} %param.7) | copy-start | bytes 148
  16.8 8.4 %copy-start.4 = (s32[1,8]{1,0:T(1,128)S(1)}, s32[1,8]{1,0:T(1,128)}, u32[]{:S(2)}) copy-start(s32[1,8]{1,0:T(1,128)} %param.8) | copy-start | bytes 100
  17.7 7.2 %collective-permute-start.3 = (bf16[128,512]{1,0:T(8,128)(2,1)S(1)}, bf16[128,512]{1,0:T(8,128)(2,1)S(1)}, u32[]{:S(2)}, u32[]{:S(2)}) collective-permute-start(bf16[128,512]{1,0:T(8,128)(2,1)S(1)} %get-tuple-element.36), channel_id=1, source_target_pairs={{0,24},{8,0},{16,8},{24,16},{1,25},{9,1},{17,9},{25,17},{2,26},{10... | collective-permute-start | bytes 393224 | tf_op jit(solution)/shard_map/ppermute | solution.py:14
  21.3 9.9 %collective-permute-start.5 = (bf16[128,512]{1,0:T(8,128)(2,1)S(1)}, bf16[128,512]{1,0:T(8,128)(2,1)S(1)}, u32[]{:S(2)}, u32[]{:S(2)}) collective-permute-start(bf16[128,512]{1,0:T(8,128)(2,1)S(1)} %get-tuple-element.34), channel_id=1, source_target_pairs={{0,16},{8,24},{16,0},{24,8},{1,17},{9,25},{17,1},{25,9},{2,18},{10... | collective-permute-start | bytes 393224 | tf_op jit(solution)/shard_map/ppermute | solution.py:14
  21.3 9.9 %collective-permute-start.4 = (bf16[128,512]{1,0:T(8,128)(2,1)S(1)}, bf16[128,512]{1,0:T(8,128)(2,1)S(1)}, u32[]{:S(2)}, u32[]{:S(2)}) collective-permute-start(bf16[128,512]{1,0:T(8,128)(2,1)S(1)} %get-tuple-element.35), channel_id=1, source_target_pairs={{0,8},{8,16},{16,24},{24,0},{1,9},{9,17},{17,25},{25,1},{2,10},{10... | collective-permute-start | bytes 393224 | tf_op jit(solution)/shard_map/ppermute | solution.py:14
  31.8 10.7 %copy-start.1 = (bf16[1,512,512]{2,1,0:T(8,128)(2,1)S(1)}, bf16[1,512,512]{2,1,0:T(8,128)(2,1)}, u32[]{:S(2)}) copy-start(bf16[1,512,512]{2,1,0:T(8,128)(2,1)} %param.9) | copy-start | bytes 1572868
  31.8 10.7 %copy-start.2 = (f32[3,1,32,512]{3,2,1,0:T(8,128)S(1)}, f32[3,1,32,512]{3,2,1,0:T(8,128)}, u32[]{:S(2)}) copy-start(f32[3,1,32,512]{3,2,1,0:T(8,128)} %param.10) | copy-start | bytes 589828
  51.6 5.8 %collective-permute-start.8 = (bf16[128,512]{1,0:T(8,128)(2,1)S(1)}, bf16[128,512]{1,0:T(8,128)(2,1)S(1)}, u32[]{:S(2)}, u32[]{:S(2)}) collective-permute-start(bf16[128,512]{1,0:T(8,128)(2,1)S(1)} %get-tuple-element.30), channel_id=1, source_target_pairs={{0,24},{8,0},{16,8},{24,16},{1,25},{9,1},{17,9},{25,17},{2,26},{10... | collective-permute-start | bytes 393224 | tf_op jit(solution)/shard_map/ppermute | solution.py:14
  53.1 13.5 %collective-permute-start.7 = (bf16[128,512]{1,0:T(8,128)(2,1)S(1)}, bf16[128,512]{1,0:T(8,128)(2,1)S(1)}, u32[]{:S(2)}, u32[]{:S(2)}) collective-permute-start(bf16[128,512]{1,0:T(8,128)(2,1)S(1)} %get-tuple-element.31), channel_id=1, source_target_pairs={{0,16},{8,24},{16,0},{24,8},{1,17},{9,25},{17,1},{25,9},{2,18},{10... | collective-permute-start | bytes 393224 | tf_op jit(solution)/shard_map/ppermute | solution.py:14
  54.3 12.4 %collective-permute-start.6 = (bf16[128,512]{1,0:T(8,128)(2,1)S(1)}, bf16[128,512]{1,0:T(8,128)(2,1)S(1)}, u32[]{:S(2)}, u32[]{:S(2)}) collective-permute-start(bf16[128,512]{1,0:T(8,128)(2,1)S(1)} %get-tuple-element.32), channel_id=1, source_target_pairs={{0,8},{8,16},{16,24},{24,0},{1,9},{9,17},{17,25},{25,1},{2,10},{10... | collective-permute-start | bytes 393224 | tf_op jit(solution)/shard_map/ppermute | solution.py:14
  86.2 6.5 %collective-permute-start.11 = (bf16[128,512]{1,0:T(8,128)(2,1)S(1)}, bf16[128,512]{1,0:T(8,128)(2,1)S(1)}, u32[]{:S(2)}, u32[]{:S(2)}) collective-permute-start(bf16[128,512]{1,0:T(8,128)(2,1)S(1)} %get-tuple-element.26), channel_id=1, source_target_pairs={{0,24},{8,0},{16,8},{24,16},{1,25},{9,1},{17,9},{25,17},{2,26},{10... | collective-permute-start | bytes 393224 | tf_op jit(solution)/shard_map/ppermute | solution.py:14
  86.3 14.0 %collective-permute-start.10 = (bf16[128,512]{1,0:T(8,128)(2,1)S(1)}, bf16[128,512]{1,0:T(8,128)(2,1)S(1)}, u32[]{:S(2)}, u32[]{:S(2)}) collective-permute-start(bf16[128,512]{1,0:T(8,128)(2,1)S(1)} %get-tuple-element.27), channel_id=1, source_target_pairs={{0,16},{8,24},{16,0},{24,8},{1,17},{9,25},{17,1},{25,9},{2,18},{10... | collective-permute-start | bytes 393224 | tf_op jit(solution)/shard_map/ppermute | solution.py:14
  88.0 12.4 %collective-permute-start.9 = (bf16[128,512]{1,0:T(8,128)(2,1)S(1)}, bf16[128,512]{1,0:T(8,128)(2,1)S(1)}, u32[]{:S(2)}, u32[]{:S(2)}) collective-permute-start(bf16[128,512]{1,0:T(8,128)(2,1)S(1)} %get-tuple-element.28), channel_id=1, source_target_pairs={{0,8},{8,16},{16,24},{24,0},{1,9},{9,17},{17,25},{25,1},{2,10},{10... | collective-permute-start | bytes 393224 | tf_op jit(solution)/shard_map/ppermute | solution.py:14

commit v18 on v15

--- a/solution.py
+++ b/solution.py
@@ -48,25 +48,23 @@
     wanted = (ahead[:, :, 0] // group_blocks == group_here) & (ahead[:, :, 2] > 0)
     want_block = jnp.sum(jnp.where(wanted, ahead[:, :, 0] % group_blocks, 0), axis=1)
     want_delay = jnp.sum(jnp.where(wanted, ahead[:, :, 2], 0), axis=1)
-    block_ids = jnp.arange(group_blocks, dtype=jnp.int32)
-    which_block = want_block[:, None] == block_ids[None, :]
-    from_near = which_block & (want_delay[:, None] == 1)
-    from_far = which_block & (want_delay[:, None] == 2)
+    owner_of_row = owners[OWNERS * want_block[:, None] + jnp.arange(OWNERS, dtype=jnp.int32)[None, :]]
+    row_from = owner_of_row[:, :, None] == member_ids[None, None, :]
+    from_near = row_from & (want_delay[:, None, None] == 1)
+    from_far = row_from & (want_delay[:, None, None] == 2)
 
-    hist_placed = pick([hist_got[m] for m in range(members)], owners)
-    blocks = [
-        hist_placed[:, t].reshape(group_blocks, EXCITE, BLOCK) for t in range(DELAYS)
-    ]
+    times = [hist_got[:, t] for t in range(DELAYS)]
     results = []
     for step in range(STEPS):
-        near = blocks[DELAYS + step - 1]
-        far = blocks[DELAYS + step - 2]
+        near = times[DELAYS + step - 1]
+        far = times[DELAYS + step - 2]
         outgoing = None
-        for block in range(group_blocks):
-            term = jnp.where(from_near[:, block, None, None], near[block][None], 0) + jnp.where(
-                from_far[:, block, None, None], far[block][None], 0
+        for m in range(members):
+            term = jnp.where(from_near[:, :, m, None, None], near[m][None, None], 0) + jnp.where(
+                from_far[:, :, m, None, None], far[m][None, None], 0
             )
             outgoing = term if outgoing is None else outgoing + term
+        outgoing = outgoing.reshape(groups, EXCITE, BLOCK)
         received = [outgoing[0]] + [
             shifted(outgoing[k], "group", groups, k) for k in range(1, groups)
         ]
@@ -98,9 +96,7 @@
         results.append(current)
         if step + 1 < STEPS:
             spread = jnp.broadcast_to(current.astype(jnp.bfloat16)[None], (members, share, BLOCK))
-            got = lax.all_to_all(spread, "member", 0, 0, tiled=True)
-            placed = pick([got[m] for m in range(members)], owners)
-            blocks.append(placed.reshape(group_blocks, EXCITE, BLOCK))
+            times.append(lax.all_to_all(spread, "member", 0, 0, tiled=True))
     return jnp.stack(results)[:, None]
 
 

time: 112 us -> 113 us (level)
    add x3, other arithmetic: 0.65 us -> 2.33 us  [body(): outgoing = term if outgoing is None else outgoing + term]
    ppermute x12, waiting for transfers between devices: 28.6 us -> 30.2 us  [shifted(): return lax.ppermute(x, axis, [(i, (i + k) % n) for i in range(n)])]
where the time goes in v18:
time: 113 us; the launch traced here: 112 us
  blocking collectives  47.3 us (42%)
  waiting for transfers between devices  30.2 us (27%)
  starting transfers between devices  23.3 us (21%)
  other arithmetic  5.46 us (5%)
  local copies, waits for them, and re-layouts  3.28 us (3%)
  matrix products  2.47 us (2%)
    ppermute x12, waiting for transfers between devices, shifted(): return lax.ppermute(x, axis, [(i, (i + k) % n) for i in range(n)])  30.2 us
    all_to_all x3, blocking collectives, body(): got = lax.all_to_all(sent, 'member', 0, 0, tiled=True)  28.6 us
    all_to_all x2, blocking collectives, body(): times.append(lax.all_to_all(spread, 'member', 0, 0, tiled=True))  18.7 us
    ppermute x12, starting transfers between devices, shifted(): return lax.ppermute(x, axis, [(i, (i + k) % n) for i in range(n)])  18.1 us
    all_to_all x1, starting transfers between devices, body(): hist_got = lax.all_to_all(spread_hist, 'member', 0, 0, tiled=True)  5.17 us
    add x3, other arithmetic, body(): outgoing = term if outgoing is None else outgoing + term  2.33 us
  transfers between devices with their start and end apart: 13, of which 9 were waited for; matrix products, arithmetic and copies ran while one was open for 2% of the time, Pallas kernels for 0%

profile of v18, /device:TPU:0, one launch (start us, length us, event | category | flops | bytes accessed | tf_op | source)
XLA Modules:
  0.0 112.4 jit_solution(12580954036692240290)
XLA Ops:
  0.0 1.8 %broadcast_in_dim.1166 = bf16[8,2,32,512]{3,2,1,0:T(8,128)(2,1)} broadcast(bf16[2,32,512]{2,1,0:T(8,128)(2,1)} %bitcast.294), dimensions={1,2,3} | broadcast | bytes 589824 | tf_op jit(solution)/shard_map/broadcast_in_dim | solution.py:43
  1.8 5.2 %all-to-all-start = ((bf16[8,2,32,512]{3,2,1,0:T(8,128)(2,1)}), bf16[8,2,32,512]{3,2,1,0:T(8,128)(2,1)S(1)}, u32[]{:S(2)}, u32[]{:S(2)}) async-start(bf16[8,2,32,512]{3,2,1,0:T(8,128)(2,1)} %broadcast_in_dim.1166), calls=%async_computation | async-start | bytes 1048576 | tf_op jit(solution)/shard_map/all_to_all | solution.py:44
  7.0 1.6 %collective-permute-start.2 = (s32[4,3]{1,0:T(4,128)}, s32[4,3]{1,0:T(4,128)S(1)}, u32[]{:S(2)}, u32[]{:S(2)}) collective-permute-start(s32[4,3]{1,0:T(4,128)} %param.7), channel_id=1, source_target_pairs={{0,8},{8,16},{16,24},{24,0},{1,9},{9,17},{17,25},{25,1},{2,10},{10... | collective-permute-start | bytes 152 | tf_op jit(solution)/shard_map/ppermute | solution.py:14
  8.6 2.6 %collective-permute-start.1 = (s32[4,3]{1,0:T(4,128)}, s32[4,3]{1,0:T(4,128)S(1)}, u32[]{:S(2)}, u32[]{:S(2)}) collective-permute-start(s32[4,3]{1,0:T(4,128)} %param.7), channel_id=1, source_target_pairs={{0,16},{8,24},{16,0},{24,8},{1,17},{9,25},{17,1},{25,9},{2,18},{10... | collective-permute-start | bytes 152 | tf_op jit(solution)/shard_map/ppermute | solution.py:14
  11.2 1.3 %collective-permute-start = (s32[4,3]{1,0:T(4,128)}, s32[4,3]{1,0:T(4,128)S(1)}, u32[]{:S(2)}, u32[]{:S(2)}) collective-permute-start(s32[4,3]{1,0:T(4,128)} %param.7), channel_id=1, source_target_pairs={{0,24},{8,0},{16,8},{24,16},{1,25},{9,1},{17,9},{25,17},{2,26},{10... | collective-permute-start | bytes 152 | tf_op jit(solution)/shard_map/ppermute | solution.py:14
  12.6 0.7 collective-permute-done.1
  13.3 1.7 %collective-permute-done = s32[4,3]{1,0:T(4,128)S(1)} collective-permute-done((s32[4,3]{1,0:T(4,128)}, s32[4,3]{1,0:T(4,128)S(1)}, u32[]{:S(2)}, u32[]{:S(2)}) %collective-permute-start) | collective-permute-done | bytes 80 | tf_op jit(solution)/shard_map/ppermute | solution.py:14
  15.0 0.7 pad_add_fusion
  16.3 0.7 gather_fusion
  17.2 0.8 add_add_fusion.2
  18.0 3.3 %collective-permute-start.3 = (bf16[128,512]{1,0:T(8,128)(2,1)S(1)}, bf16[128,512]{1,0:T(8,128)(2,1)S(1)}, u32[]{:S(2)}, u32[]{:S(2)}) collective-permute-start(bf16[128,512]{1,0:T(8,128)(2,1)S(1)} %bitcast.291), channel_id=1, source_target_pairs={{0,24},{8,0},{16,8},{24,16},{1,25},{9,1},{17,9},{25,17},{2,26},{10... | collective-permute-start | bytes 393224 | tf_op jit(solution)/shard_map/ppermute | solution.py:14
  21.3 1.0 collective-permute-start.4
  22.3 2.9 %collective-permute-done.3 = bf16[128,512]{1,0:T(8,128)(2,1)S(1)} collective-permute-done((bf16[128,512]{1,0:T(8,128)(2,1)S(1)}, bf16[128,512]{1,0:T(8,128)(2,1)S(1)}, u32[]{:S(2)}, u32[]{:S(2)}) %collective-permute-start.3) | collective-permute-done | bytes 131104 | tf_op jit(solution)/shard_map/ppermute | solution.py:14
  25.8 6.3 %collective-permute-done.5 = bf16[128,512]{1,0:T(8,128)(2,1)S(1)} collective-permute-done((bf16[128,512]{1,0:T(8,128)(2,1)S(1)}, bf16[128,512]{1,0:T(8,128)(2,1)S(1)}, u32[]{:S(2)}, u32[]{:S(2)}) %collective-permute-start.5) | collective-permute-done | bytes 131104 | tf_op jit(solution)/shard_map/ppermute | solution.py:14
  33.1 10.0 %all_to_all.30 = bf16[8,32,512]{2,1,0:T(8,128)(2,1)S(1)} all-to-all(bf16[8,32,512]{2,1,0:T(8,128)(2,1)S(1)} %select_add_fusion.2), channel_id=1, replica_groups=mesh['group'=4,'member'=8] {'member'}, dimensions={0} | all-to-all | bytes 524288 | tf_op jit(solution)/shard_map/all_to_all | solution.py:92
  43.4 9.3 %all_to_all.31 = bf16[8,32,512]{2,1,0:T(8,128)(2,1)S(1)} all-to-all(bf16[8,32,512]{2,1,0:T(8,128)(2,1)S(1)} %broadcast_in_dim.1284), channel_id=1, replica_groups=mesh['group'=4,'member'=8] {'member'}, dimensions={0} | all-to-all | bytes 524288 | tf_op jit(solution)/shard_map/all_to_all | solution.py:99
  52.7 0.8 add_add_fusion.1
  53.5 1.6 %collective-permute-start.8 = (bf16[128,512]{1,0:T(8,128)(2,1)S(1)}, bf16[128,512]{1,0:T(8,128)(2,1)S(1)}, u32[]{:S(2)}, u32[]{:S(2)}) collective-permute-start(bf16[128,512]{1,0:T(8,128)(2,1)S(1)} %bitcast.292), channel_id=1, source_target_pairs={{0,24},{8,0},{16,8},{24,16},{1,25},{9,1},{17,9},{25,17},{2,26},{10... | collective-permute-start | bytes 393224 | tf_op jit(solution)/shard_map/ppermute | solution.py:14
  55.2 1.0 collective-permute-start.7
  56.2 1.9 %collective-permute-start.6 = (bf16[128,512]{1,0:T(8,128)(2,1)S(1)}, bf16[128,512]{1,0:T(8,128)(2,1)S(1)}, u32[]{:S(2)}, u32[]{:S(2)}) collective-permute-start(bf16[128,512]{1,0:T(8,128)(2,1)S(1)} %bitcast.287), channel_id=1, source_target_pairs={{0,8},{8,16},{16,24},{24,0},{1,9},{9,17},{17,25},{25,1},{2,10},{10... | collective-permute-start | bytes 393224 | tf_op jit(solution)/shard_map/ppermute | solution.py:14
  58.1 1.1 collective-permute-done.8
  59.2 8.2 %collective-permute-done.7 = bf16[128,512]{1,0:T(8,128)(2,1)S(1)} collective-permute-done((bf16[128,512]{1,0:T(8,128)(2,1)S(1)}, bf16[128,512]{1,0:T(8,128)(2,1)S(1)}, u32[]{:S(2)}, u32[]{:S(2)}) %collective-permute-start.7) | collective-permute-done | bytes 131104 | tf_op jit(solution)/shard_map/ppermute | solution.py:14
  67.4 0.7 select_reduce_fusion.3
  68.4 9.3 %all_to_all.32 = bf16[8,32,512]{2,1,0:T(8,128)(2,1)S(1)} all-to-all(bf16[8,32,512]{2,1,0:T(8,128)(2,1)S(1)} %select_add_fusion.1), channel_id=1, replica_groups=mesh['group'=4,'member'=8] {'member'}, dimensions={0} | all-to-all | bytes 524288 | tf_op jit(solution)/shard_map/all_to_all | solution.py:92
  78.0 9.3 %all_to_all.33 = bf16[8,32,512]{2,1,0:T(8,128)(2,1)S(1)} all-to-all(bf16[8,32,512]{2,1,0:T(8,128)(2,1)S(1)} %broadcast_in_dim.1322), channel_id=1, replica_groups=mesh['group'=4,'member'=8] {'member'}, dimensions={0} | all-to-all | bytes 524288 | tf_op jit(solution)/shard_map/all_to_all | solution.py:99
  87.4 0.8 add_add_fusion
  88.2 1.7 %collective-permute-start.10 = (bf16[128,512]{1,0:T(8,128)(2,1)S(1)}, bf16[128,512]{1,0:T(8,128)(2,1)S(1)}, u32[]{:S(2)}, u32[]{:S(2)}) collective-permute-start(bf16[128,512]{1,0:T(8,128)(2,1)S(1)} %bitcast.290), channel_id=1, source_target_pairs={{0,16},{8,24},{16,0},{24,8},{1,17},{9,25},{17,1},{25,9},{2,18},{10... | collective-permute-start | bytes 393224 | tf_op jit(solution)/shard_map/ppermute | solution.py:14
  90.0 1.9 %collective-permute-start.9 = (bf16[128,512]{1,0:T(8,128)(2,1)S(1)}, bf16[128,512]{1,0:T(8,128)(2,1)S(1)}, u32[]{:S(2)}, u32[]{:S(2)}) collective-permute-start(bf16[128,512]{1,0:T(8,128)(2,1)S(1)} %bitcast.288), channel_id=1, source_target_pairs={{0,8},{8,16},{16,24},{24,0},{1,9},{9,17},{17,25},{25,1},{2,10},{10... | collective-permute-start | bytes 393224 | tf_op jit(solution)/shard_map/ppermute | solution.py:14
  91.9 1.8 %collective-permute-done.11 = bf16[128,512]{1,0:T(8,128)(2,1)S(1)} collective-permute-done((bf16[128,512]{1,0:T(8,128)(2,1)S(1)}, bf16[128,512]{1,0:T(8,128)(2,1)S(1)}, u32[]{:S(2)}, u32[]{:S(2)}) %collective-permute-start.11) | collective-permute-done | bytes 131104 | tf_op jit(solution)/shard_map/ppermute | solution.py:14
  93.8 7.4 %collective-permute-done.10 = bf16[128,512]{1,0:T(8,128)(2,1)S(1)} collective-permute-done((bf16[128,512]{1,0:T(8,128)(2,1)S(1)}, bf16[128,512]{1,0:T(8,128)(2,1)S(1)}, u32[]{:S(2)}, u32[]{:S(2)}) %collective-permute-start.10) | collective-permute-done | bytes 131104 | tf_op jit(solution)/shard_map/ppermute | solution.py:14
  102.1 9.3 %all_to_all.34 = bf16[8,32,512]{2,1,0:T(8,128)(2,1)S(1)} all-to-all(bf16[8,32,512]{2,1,0:T(8,128)(2,1)S(1)} %select_add_fusion), channel_id=1, replica_groups=mesh['group'=4,'member'=8] {'member'}, dimensions={0} | all-to-all | bytes 524288 | tf_op jit(solution)/shard_map/all_to_all | solution.py:92
  111.7 0.7 maximum_bitcast_fusion
  (61 shorter events, 4.5 us)
Async XLA Ops:
  0.0 32.1 %copy-start = (bf16[4,512,512]{2,1,0:T(8,128)(2,1)S(1)}, bf16[4,512,512]{2,1,0:T(8,128)(2,1)}, u32[]{:S(2)}) copy-start(bf16[4,512,512]{2,1,0:T(8,128)(2,1)} %param.6) | copy-start | bytes 6291460
  0.0 16.3 %copy-start.1 = (s32[1,8]{1,0:T(1,128)S(1)}, s32[1,8]{1,0:T(1,128)}, u32[]{:S(2)}) copy-start(s32[1,8]{1,0:T(1,128)} %param.8) | copy-start | bytes 100
  1.8 15.3 %all-to-all-start = ((bf16[8,2,32,512]{3,2,1,0:T(8,128)(2,1)}), bf16[8,2,32,512]{3,2,1,0:T(8,128)(2,1)S(1)}, u32[]{:S(2)}, u32[]{:S(2)}) async-start(bf16[8,2,32,512]{3,2,1,0:T(8,128)(2,1)} %broadcast_in_dim.1166), calls=%async_computation | async-start | bytes 1048576 | tf_op jit(solution)/shard_map/all_to_all | solution.py:44
  7.0 5.6 %collective-permute-start.2 = (s32[4,3]{1,0:T(4,128)}, s32[4,3]{1,0:T(4,128)S(1)}, u32[]{:S(2)}, u32[]{:S(2)}) collective-permute-start(s32[4,3]{1,0:T(4,128)} %param.7), channel_id=1, source_target_pairs={{0,8},{8,16},{16,24},{24,0},{1,9},{9,17},{17,25},{25,1},{2,10},{10... | collective-permute-start | bytes 152 | tf_op jit(solution)/shard_map/ppermute | solution.py:14
  8.6 4.7 %collective-permute-start.1 = (s32[4,3]{1,0:T(4,128)}, s32[4,3]{1,0:T(4,128)S(1)}, u32[]{:S(2)}, u32[]{:S(2)}) collective-permute-start(s32[4,3]{1,0:T(4,128)} %param.7), channel_id=1, source_target_pairs={{0,16},{8,24},{16,0},{24,8},{1,17},{9,25},{17,1},{25,9},{2,18},{10... | collective-permute-start | bytes 152 | tf_op jit(solution)/shard_map/ppermute | solution.py:14
  11.2 3.8 %collective-permute-start = (s32[4,3]{1,0:T(4,128)}, s32[4,3]{1,0:T(4,128)S(1)}, u32[]{:S(2)}, u32[]{:S(2)}) collective-permute-start(s32[4,3]{1,0:T(4,128)} %param.7), channel_id=1, source_target_pairs={{0,24},{8,0},{16,8},{24,16},{1,25},{9,1},{17,9},{25,17},{2,26},{10... | collective-permute-start | bytes 152 | tf_op jit(solution)/shard_map/ppermute | solution.py:14
  16.9 8.3 %copy-start.4 = (s32[4,3]{1,0:T(4,128)S(1)}, s32[4,3]{1,0:T(4,128)}, u32[]{:S(2)}) copy-start(s32[4,3]{1,0:T(4,128)} %param.7) | copy-start | bytes 148
  18.0 7.2 %collective-permute-start.3 = (bf16[128,512]{1,0:T(8,128)(2,1)S(1)}, bf16[128,512]{1,0:T(8,128)(2,1)S(1)}, u32[]{:S(2)}, u32[]{:S(2)}) collective-permute-start(bf16[128,512]{1,0:T(8,128)(2,1)S(1)} %bitcast.291), channel_id=1, source_target_pairs={{0,24},{8,0},{16,8},{24,16},{1,25},{9,1},{17,9},{25,17},{2,26},{10... | collective-permute-start | bytes 393224 | tf_op jit(solution)/shard_map/ppermute | solution.py:14
  21.3 10.8 %collective-permute-start.5 = (bf16[128,512]{1,0:T(8,128)(2,1)S(1)}, bf16[128,512]{1,0:T(8,128)(2,1)S(1)}, u32[]{:S(2)}, u32[]{:S(2)}) collective-permute-start(bf16[128,512]{1,0:T(8,128)(2,1)S(1)} %bitcast.284), channel_id=1, source_target_pairs={{0,16},{8,24},{16,0},{24,8},{1,17},{9,25},{17,1},{25,9},{2,18},{10... | collective-permute-start | bytes 393224 | tf_op jit(solution)/shard_map/ppermute | solution.py:14
  21.3 10.8 %collective-permute-start.4 = (bf16[128,512]{1,0:T(8,128)(2,1)S(1)}, bf16[128,512]{1,0:T(8,128)(2,1)S(1)}, u32[]{:S(2)}, u32[]{:S(2)}) collective-permute-start(bf16[128,512]{1,0:T(8,128)(2,1)S(1)} %bitcast.283), channel_id=1, source_target_pairs={{0,8},{8,16},{16,24},{24,0},{1,9},{9,17},{17,25},{25,1},{2,10},{10... | collective-permute-start | bytes 393224 | tf_op jit(solution)/shard_map/ppermute | solution.py:14
  32.8 10.3 %copy-start.2 = (bf16[1,512,512]{2,1,0:T(8,128)(2,1)S(1)}, bf16[1,512,512]{2,1,0:T(8,128)(2,1)}, u32[]{:S(2)}) copy-start(bf16[1,512,512]{2,1,0:T(8,128)(2,1)} %param.9) | copy-start | bytes 1572868
  32.8 10.3 %copy-start.3 = (f32[3,1,32,512]{3,2,1,0:T(8,128)S(1)}, f32[3,1,32,512]{3,2,1,0:T(8,128)}, u32[]{:S(2)}) copy-start(f32[3,1,32,512]{3,2,1,0:T(8,128)} %param.10) | copy-start | bytes 589828
  53.5 5.7 %collective-permute-start.8 = (bf16[128,512]{1,0:T(8,128)(2,1)S(1)}, bf16[128,512]{1,0:T(8,128)(2,1)S(1)}, u32[]{:S(2)}, u32[]{:S(2)}) collective-permute-start(bf16[128,512]{1,0:T(8,128)(2,1)S(1)} %bitcast.292), channel_id=1, source_target_pairs={{0,24},{8,0},{16,8},{24,16},{1,25},{9,1},{17,9},{25,17},{2,26},{10... | collective-permute-start | bytes 393224 | tf_op jit(solution)/shard_map/ppermute | solution.py:14
  55.2 12.2 %collective-permute-start.7 = (bf16[128,512]{1,0:T(8,128)(2,1)S(1)}, bf16[128,512]{1,0:T(8,128)(2,1)S(1)}, u32[]{:S(2)}, u32[]{:S(2)}) collective-permute-start(bf16[128,512]{1,0:T(8,128)(2,1)S(1)} %bitcast.289), channel_id=1, source_target_pairs={{0,16},{8,24},{16,0},{24,8},{1,17},{9,25},{17,1},{25,9},{2,18},{10... | collective-permute-start | bytes 393224 | tf_op jit(solution)/shard_map/ppermute | solution.py:14
  56.2 11.2 %collective-permute-start.6 = (bf16[128,512]{1,0:T(8,128)(2,1)S(1)}, bf16[128,512]{1,0:T(8,128)(2,1)S(1)}, u32[]{:S(2)}, u32[]{:S(2)}) collective-permute-start(bf16[128,512]{1,0:T(8,128)(2,1)S(1)} %bitcast.287), channel_id=1, source_target_pairs={{0,8},{8,16},{16,24},{24,0},{1,9},{9,17},{17,25},{25,1},{2,10},{10... | collective-permute-start | bytes 393224 | tf_op jit(solution)/shard_map/ppermute | solution.py:14
  88.2 5.6 %collective-permute-start.11 = (bf16[128,512]{1,0:T(8,128)(2,1)S(1)}, bf16[128,512]{1,0:T(8,128)(2,1)S(1)}, u32[]{:S(2)}, u32[]{:S(2)}) collective-permute-start(bf16[128,512]{1,0:T(8,128)(2,1)S(1)} %bitcast.293), channel_id=1, source_target_pairs={{0,24},{8,0},{16,8},{24,16},{1,25},{9,1},{17,9},{25,17},{2,26},{10... | collective-permute-start | bytes 393224 | tf_op jit(solution)/shard_map/ppermute | solution.py:14
  88.2 12.9 %collective-permute-start.10 = (bf16[128,512]{1,0:T(8,128)(2,1)S(1)}, bf16[128,512]{1,0:T(8,128)(2,1)S(1)}, u32[]{:S(2)}, u32[]{:S(2)}) collective-permute-start(bf16[128,512]{1,0:T(8,128)(2,1)S(1)} %bitcast.290), channel_id=1, source_target_pairs={{0,16},{8,24},{16,0},{24,8},{1,17},{9,25},{17,1},{25,9},{2,18},{10... | collective-permute-start | bytes 393224 | tf_op jit(solution)/shard_map/ppermute | solution.py:14
  90.0 11.2 %collective-permute-start.9 = (bf16[128,512]{1,0:T(8,128)(2,1)S(1)}, bf16[128,512]{1,0:T(8,128)(2,1)S(1)}, u32[]{:S(2)}, u32[]{:S(2)}) collective-permute-start(bf16[128,512]{1,0:T(8,128)(2,1)S(1)} %bitcast.288), channel_id=1, source_target_pairs={{0,8},{8,16},{16,24},{24,0},{1,9},{9,17},{17,25},{25,1},{2,10},{10... | collective-permute-start | bytes 393224 | tf_op jit(solution)/shard_map/ppermute | solution.py:14

commit v19 on v15

--- a/solution.py
+++ b/solution.py
@@ -57,7 +57,7 @@
     blocks = [
         hist_placed[:, t].reshape(group_blocks, EXCITE, BLOCK) for t in range(DELAYS)
     ]
-    results = []
+    results = jnp.zeros((STEPS, 1, share, BLOCK), jnp.float32)
     for step in range(STEPS):
         near = blocks[DELAYS + step - 1]
         far = blocks[DELAYS + step - 2]
@@ -95,13 +95,13 @@
         field = jnp.sum(got.astype(jnp.float32), axis=0)
         residual = (excitations[step, 0] - field).astype(jnp.bfloat16)
         current = jnp.dot(residual, inverses[0], preferred_element_type=jnp.float32)
-        results.append(current)
+        results = lax.dynamic_update_slice(results, current[None, None], (step, 0, 0, 0))
         if step + 1 < STEPS:
             spread = jnp.broadcast_to(current.astype(jnp.bfloat16)[None], (members, share, BLOCK))
             got = lax.all_to_all(spread, "member", 0, 0, tiled=True)
             placed = pick([got[m] for m in range(members)], owners)
             blocks.append(placed.reshape(group_blocks, EXCITE, BLOCK))
-    return jnp.stack(results)[:, None]
+    return results
 
 
 def solution(mesh):

time: 112 us -> 117 us (1.045)
  waiting for transfers between devices: 29.2 us -> 40.3 us
  blocking collectives: 47.7 us -> 39.1 us
  starting transfers between devices: 23.6 us -> 26.1 us
    all_to_all x3 -> x2, blocking collectives: 29 us -> 20.4 us  [body(): got = lax.all_to_all(sent, 'member', 0, 0, tiled=True)]
    all_to_all x1, waiting for transfers between devices: 0.65 us -> 7.75 us  [body(): hist_got = lax.all_to_all(spread_hist, 'member', 0, 0, tiled=True)]
    all_to_all x0 -> x1, waiting for transfers between devices: none -> 6.82 us  [body(): got = lax.all_to_all(sent, 'member', 0, 0, tiled=True)]
    all_to_all x0 -> x1, starting transfers between devices: none -> 3.41 us  [body(): got = lax.all_to_all(sent, 'member', 0, 0, tiled=True)]
    ppermute x12, waiting for transfers between devices: 28.6 us -> 25.8 us  [shifted(): return lax.ppermute(x, axis, [(i, (i + k) % n) for i in range(n)])]
    all_to_all x1, starting transfers between devices: 5.17 us -> 3.72 us  [body(): hist_got = lax.all_to_all(spread_hist, 'member', 0, 0, tiled=True)]
  transfers between devices with their start and end apart: 13 -> 14, of which waited for: 9 -> 10; matrix products, arithmetic and copies ran while one was open for 2% -> 2% of each run, Pallas kernels for 0% -> 0%
where the time goes in v19:
time: 117 us
  waiting for transfers between devices  40.3 us (34%)
  blocking collectives  39.1 us (33%)
  starting transfers between devices  26.1 us (22%)
  other arithmetic  5.24 us (4%)
  matrix products  2.98 us (3%)
  local copies, waits for them, and re-layouts  2.56 us (2%)
    ppermute x12, waiting for transfers between devices, shifted(): return lax.ppermute(x, axis, [(i, (i + k) % n) for i in range(n)])  25.8 us
    all_to_all x2, blocking collectives, body(): got = lax.all_to_all(sent, 'member', 0, 0, tiled=True)  20.4 us
    ppermute x12, starting transfers between devices, shifted(): return lax.ppermute(x, axis, [(i, (i + k) % n) for i in range(n)])  18.9 us
    all_to_all x2, blocking collectives, body(): got = lax.all_to_all(spread, 'member', 0, 0, tiled=True)  18.7 us
    all_to_all x1, waiting for transfers between devices, body(): hist_got = lax.all_to_all(spread_hist, 'member', 0, 0, tiled=True)  7.75 us
    all_to_all x1, waiting for transfers between devices, body(): got = lax.all_to_all(sent, 'member', 0, 0, tiled=True)  6.82 us
    all_to_all x1, starting transfers between devices, body(): hist_got = lax.all_to_all(spread_hist, 'member', 0, 0, tiled=True)  3.72 us
    all_to_all x1, starting transfers between devices, body(): got = lax.all_to_all(sent, 'member', 0, 0, tiled=True)  3.41 us
  transfers between devices with their start and end apart: 14, of which 10 were waited for; matrix products, arithmetic and copies ran while one was open for 2% of the time, Pallas kernels for 0%

profile of v19, /device:TPU:0, one launch (start us, length us, event | category | flops | bytes accessed | tf_op | source)
XLA Modules:
  0.0 116.6 jit_solution(4378424223546316689)
XLA Ops:
  0.0 1.8 %broadcast_in_dim.1146 = bf16[8,2,32,512]{3,2,1,0:T(8,128)(2,1)} broadcast(bf16[2,32,512]{2,1,0:T(8,128)(2,1)} %bitcast.284), dimensions={1,2,3} | broadcast | bytes 589824 | tf_op jit(solution)/shard_map/broadcast_in_dim | solution.py:43
  1.8 5.0 %collective-permute-start = (s32[4,3]{1,0:T(4,128)}, s32[4,3]{1,0:T(4,128)S(1)}, u32[]{:S(2)}, u32[]{:S(2)}) collective-permute-start(s32[4,3]{1,0:T(4,128)} %param.7), channel_id=1, source_target_pairs={{0,24},{8,0},{16,8},{24,16},{1,25},{9,1},{17,9},{25,17},{2,26},{10... | collective-permute-start | bytes 152 | tf_op jit(solution)/shard_map/ppermute | solution.py:14
  6.9 1.0 collective-permute-start.2
  7.9 3.7 %all-to-all-start = ((bf16[8,2,32,512]{3,2,1,0:T(8,128)(2,1)}), bf16[8,2,32,512]{3,2,1,0:T(8,128)(2,1)S(1)}, u32[]{:S(2)}, u32[]{:S(2)}) async-start(bf16[8,2,32,512]{3,2,1,0:T(8,128)(2,1)} %broadcast_in_dim.1146), calls=%async_computation | async-start | bytes 1048576 | tf_op jit(solution)/shard_map/all_to_all | solution.py:44
  11.6 0.7 iota_compare_fusion.2
  12.5 0.7 pad_add_fusion
  13.6 7.7 %all-to-all-done = bf16[8,2,32,512]{3,2,1,0:T(8,128)(2,1)S(1)} async-done(((bf16[8,2,32,512]{3,2,1,0:T(8,128)(2,1)}), bf16[8,2,32,512]{3,2,1,0:T(8,128)(2,1)S(1)}, u32[]{:S(2)}, u32[]{:S(2)}) %all-to-all-start) | async-done | bytes 524320 | tf_op jit(solution)/shard_map/all_to_all | solution.py:44
  21.4 0.5 select_add_fusion
  22.3 2.9 %collective-permute-start.3 = (bf16[128,512]{1,0:T(8,128)(2,1)S(1)}, bf16[128,512]{1,0:T(8,128)(2,1)S(1)}, u32[]{:S(2)}, u32[]{:S(2)}) collective-permute-start(bf16[128,512]{1,0:T(8,128)(2,1)S(1)} %get-tuple-element.36), channel_id=1, source_target_pairs={{0,24},{8,0},{16,8},{24,16},{1,25},{9,1},{17,9},{25,17},{2,26},{10... | collective-permute-start | bytes 393224 | tf_op jit(solution)/shard_map/ppermute | solution.py:14
  25.1 1.1 collective-permute-start.5
  26.3 3.8 %collective-permute-done.3 = bf16[128,512]{1,0:T(8,128)(2,1)S(1)} collective-permute-done((bf16[128,512]{1,0:T(8,128)(2,1)S(1)}, bf16[128,512]{1,0:T(8,128)(2,1)S(1)}, u32[]{:S(2)}, u32[]{:S(2)}) %collective-permute-start.3) | collective-permute-done | bytes 131104 | tf_op jit(solution)/shard_map/ppermute | solution.py:14
  30.5 1.9 %collective-permute-done.4 = bf16[128,512]{1,0:T(8,128)(2,1)S(1)} collective-permute-done((bf16[128,512]{1,0:T(8,128)(2,1)S(1)}, bf16[128,512]{1,0:T(8,128)(2,1)S(1)}, u32[]{:S(2)}, u32[]{:S(2)}) %collective-permute-start.4) | collective-permute-done | bytes 131104 | tf_op jit(solution)/shard_map/ppermute | solution.py:14
  32.4 3.3 %collective-permute-done.5 = bf16[128,512]{1,0:T(8,128)(2,1)S(1)} collective-permute-done((bf16[128,512]{1,0:T(8,128)(2,1)S(1)}, bf16[128,512]{1,0:T(8,128)(2,1)S(1)}, u32[]{:S(2)}, u32[]{:S(2)}) %collective-permute-start.5) | collective-permute-done | bytes 131104 | tf_op jit(solution)/shard_map/ppermute | solution.py:14
  35.7 0.6 select_reduce_fusion.5
  36.7 11.0 %all_to_all.30 = bf16[8,32,512]{2,1,0:T(8,128)(2,1)S(1)} all-to-all(bf16[8,32,512]{2,1,0:T(8,128)(2,1)S(1)} %select_add_fusion.5), channel_id=1, replica_groups=mesh['group'=4,'member'=8] {'member'}, dimensions={0} | all-to-all | bytes 524288 | tf_op jit(solution)/shard_map/all_to_all | solution.py:94
  48.0 9.3 %all_to_all.31 = bf16[8,32,512]{2,1,0:T(8,128)(2,1)S(1)} all-to-all(bf16[8,32,512]{2,1,0:T(8,128)(2,1)S(1)} %broadcast_in_dim.1250), channel_id=1, replica_groups=mesh['group'=4,'member'=8] {'member'}, dimensions={0} | all-to-all | bytes 524288 | tf_op jit(solution)/shard_map/all_to_all | solution.py:101
  58.0 3.2 %collective-permute-start.7 = (bf16[128,512]{1,0:T(8,128)(2,1)S(1)}, bf16[128,512]{1,0:T(8,128)(2,1)S(1)}, u32[]{:S(2)}, u32[]{:S(2)}) collective-permute-start(bf16[128,512]{1,0:T(8,128)(2,1)S(1)} %get-tuple-element.31), channel_id=1, source_target_pairs={{0,16},{8,24},{16,0},{24,8},{1,17},{9,25},{17,1},{25,9},{2,18},{10... | collective-permute-start | bytes 393224 | tf_op jit(solution)/shard_map/ppermute | solution.py:14
  61.2 0.6 collective-permute-start.8
  61.8 4.5 %collective-permute-done.6 = bf16[128,512]{1,0:T(8,128)(2,1)S(1)} collective-permute-done((bf16[128,512]{1,0:T(8,128)(2,1)S(1)}, bf16[128,512]{1,0:T(8,128)(2,1)S(1)}, u32[]{:S(2)}, u32[]{:S(2)}) %collective-permute-start.6) | collective-permute-done | bytes 131104 | tf_op jit(solution)/shard_map/ppermute | solution.py:14
  66.3 3.9 %collective-permute-done.7 = bf16[128,512]{1,0:T(8,128)(2,1)S(1)} collective-permute-done((bf16[128,512]{1,0:T(8,128)(2,1)S(1)}, bf16[128,512]{1,0:T(8,128)(2,1)S(1)}, u32[]{:S(2)}, u32[]{:S(2)}) %collective-permute-start.7) | collective-permute-done | bytes 131104 | tf_op jit(solution)/shard_map/ppermute | solution.py:14
  70.1 0.6 select_reduce_fusion.3
  71.0 9.3 %all_to_all.32 = bf16[8,32,512]{2,1,0:T(8,128)(2,1)S(1)} all-to-all(bf16[8,32,512]{2,1,0:T(8,128)(2,1)S(1)} %select_add_fusion.3), channel_id=1, replica_groups=mesh['group'=4,'member'=8] {'member'}, dimensions={0} | all-to-all | bytes 524288 | tf_op jit(solution)/shard_map/all_to_all | solution.py:94
  80.7 9.3 %all_to_all.33 = bf16[8,32,512]{2,1,0:T(8,128)(2,1)S(1)} all-to-all(bf16[8,32,512]{2,1,0:T(8,128)(2,1)S(1)} %broadcast_in_dim.1300), channel_id=1, replica_groups=mesh['group'=4,'member'=8] {'member'}, dimensions={0} | all-to-all | bytes 524288 | tf_op jit(solution)/shard_map/all_to_all | solution.py:101
  90.6 1.6 %collective-permute-start.10 = (bf16[128,512]{1,0:T(8,128)(2,1)S(1)}, bf16[128,512]{1,0:T(8,128)(2,1)S(1)}, u32[]{:S(2)}, u32[]{:S(2)}) collective-permute-start(bf16[128,512]{1,0:T(8,128)(2,1)S(1)} %get-tuple-element.27), channel_id=1, source_target_pairs={{0,16},{8,24},{16,0},{24,8},{1,17},{9,25},{17,1},{25,9},{2,18},{10... | collective-permute-start | bytes 393224 | tf_op jit(solution)/shard_map/ppermute | solution.py:14
  92.2 3.4 %collective-permute-start.11 = (bf16[128,512]{1,0:T(8,128)(2,1)S(1)}, bf16[128,512]{1,0:T(8,128)(2,1)S(1)}, u32[]{:S(2)}, u32[]{:S(2)}) collective-permute-start(bf16[128,512]{1,0:T(8,128)(2,1)S(1)} %get-tuple-element.26), channel_id=1, source_target_pairs={{0,24},{8,0},{16,8},{24,16},{1,25},{9,1},{17,9},{25,17},{2,26},{10... | collective-permute-start | bytes 393224 | tf_op jit(solution)/shard_map/ppermute | solution.py:14
  95.6 5.9 %collective-permute-done.10 = bf16[128,512]{1,0:T(8,128)(2,1)S(1)} collective-permute-done((bf16[128,512]{1,0:T(8,128)(2,1)S(1)}, bf16[128,512]{1,0:T(8,128)(2,1)S(1)}, u32[]{:S(2)}, u32[]{:S(2)}) %collective-permute-start.10) | collective-permute-done | bytes 131104 | tf_op jit(solution)/shard_map/ppermute | solution.py:14
  101.5 2.4 %collective-permute-done.9 = bf16[128,512]{1,0:T(8,128)(2,1)S(1)} collective-permute-done((bf16[128,512]{1,0:T(8,128)(2,1)S(1)}, bf16[128,512]{1,0:T(8,128)(2,1)S(1)}, u32[]{:S(2)}, u32[]{:S(2)}) %collective-permute-start.9) | collective-permute-done | bytes 131104 | tf_op jit(solution)/shard_map/ppermute | solution.py:14
  103.9 0.6 select_reduce_fusion.1
  104.5 0.9 select_add_fusion.1
  105.5 3.4 %all-to-all-start.5 = ((bf16[8,32,512]{2,1,0:T(8,128)(2,1)}), bf16[8,32,512]{2,1,0:T(8,128)(2,1)S(1)}, u32[]{:S(2)}, u32[]{:S(2)}) async-start(bf16[8,32,512]{2,1,0:T(8,128)(2,1)} %select_add_fusion.1), calls=%async_computation.5 | async-start | bytes 524288 | tf_op jit(solution)/shard_map/all_to_all | solution.py:94
  108.9 6.8 %all-to-all-done.5 = bf16[8,32,512]{2,1,0:T(8,128)(2,1)S(1)} async-done(((bf16[8,32,512]{2,1,0:T(8,128)(2,1)}), bf16[8,32,512]{2,1,0:T(8,128)(2,1)S(1)}, u32[]{:S(2)}, u32[]{:S(2)}) %all-to-all-start.5) | async-done | bytes 262176 | tf_op jit(solution)/shard_map/all_to_all | solution.py:94
  115.8 0.8 fusion
  (67 shorter events, 3.8 us)
Async XLA Ops:
  0.0 35.7 %copy-start = (bf16[4,512,512]{2,1,0:T(8,128)(2,1)S(1)}, bf16[4,512,512]{2,1,0:T(8,128)(2,1)}, u32[]{:S(2)}) copy-start(bf16[4,512,512]{2,1,0:T(8,128)(2,1)} %param.6) | copy-start | bytes 6291460
  1.8 10.5 %collective-permute-start = (s32[4,3]{1,0:T(4,128)}, s32[4,3]{1,0:T(4,128)S(1)}, u32[]{:S(2)}, u32[]{:S(2)}) collective-permute-start(s32[4,3]{1,0:T(4,128)} %param.7), channel_id=1, source_target_pairs={{0,24},{8,0},{16,8},{24,16},{1,25},{9,1},{17,9},{25,17},{2,26},{10... | collective-permute-start | bytes 152 | tf_op jit(solution)/shard_map/ppermute | solution.py:14
  6.9 5.4 %collective-permute-start.1 = (s32[4,3]{1,0:T(4,128)}, s32[4,3]{1,0:T(4,128)S(1)}, u32[]{:S(2)}, u32[]{:S(2)}) collective-permute-start(s32[4,3]{1,0:T(4,128)} %param.7), channel_id=1, source_target_pairs={{0,16},{8,24},{16,0},{24,8},{1,17},{9,25},{17,1},{25,9},{2,18},{10... | collective-permute-start | bytes 152 | tf_op jit(solution)/shard_map/ppermute | solution.py:14
  6.9 5.6 %collective-permute-start.2 = (s32[4,3]{1,0:T(4,128)}, s32[4,3]{1,0:T(4,128)S(1)}, u32[]{:S(2)}, u32[]{:S(2)}) collective-permute-start(s32[4,3]{1,0:T(4,128)} %param.7), channel_id=1, source_target_pairs={{0,8},{8,16},{16,24},{24,0},{1,9},{9,17},{17,25},{25,1},{2,10},{10... | collective-permute-start | bytes 152 | tf_op jit(solution)/shard_map/ppermute | solution.py:14
  7.9 13.5 %all-to-all-start = ((bf16[8,2,32,512]{3,2,1,0:T(8,128)(2,1)}), bf16[8,2,32,512]{3,2,1,0:T(8,128)(2,1)S(1)}, u32[]{:S(2)}, u32[]{:S(2)}) async-start(bf16[8,2,32,512]{3,2,1,0:T(8,128)(2,1)} %broadcast_in_dim.1146), calls=%async_computation | async-start | bytes 1048576 | tf_op jit(solution)/shard_map/all_to_all | solution.py:44
  21.4 8.6 %copy-start.4 = (s32[4,3]{1,0:T(4,128)S(1)}, s32[4,3]{1,0:T(4,128)}, u32[]{:S(2)}) copy-start(s32[4,3]{1,0:T(4,128)} %param.7) | copy-start | bytes 148
  22.3 7.8 %collective-permute-start.3 = (bf16[128,512]{1,0:T(8,128)(2,1)S(1)}, bf16[128,512]{1,0:T(8,128)(2,1)S(1)}, u32[]{:S(2)}, u32[]{:S(2)}) collective-permute-start(bf16[128,512]{1,0:T(8,128)(2,1)S(1)} %get-tuple-element.36), channel_id=1, source_target_pairs={{0,24},{8,0},{16,8},{24,16},{1,25},{9,1},{17,9},{25,17},{2,26},{10... | collective-permute-start | bytes 393224 | tf_op jit(solution)/shard_map/ppermute | solution.py:14
  25.1 7.3 %collective-permute-start.4 = (bf16[128,512]{1,0:T(8,128)(2,1)S(1)}, bf16[128,512]{1,0:T(8,128)(2,1)S(1)}, u32[]{:S(2)}, u32[]{:S(2)}) collective-permute-start(bf16[128,512]{1,0:T(8,128)(2,1)S(1)} %get-tuple-element.35), channel_id=1, source_target_pairs={{0,8},{8,16},{16,24},{24,0},{1,9},{9,17},{17,25},{25,1},{2,10},{10... | collective-permute-start | bytes 393224 | tf_op jit(solution)/shard_map/ppermute | solution.py:14
  25.1 10.5 %collective-permute-start.5 = (bf16[128,512]{1,0:T(8,128)(2,1)S(1)}, bf16[128,512]{1,0:T(8,128)(2,1)S(1)}, u32[]{:S(2)}, u32[]{:S(2)}) collective-permute-start(bf16[128,512]{1,0:T(8,128)(2,1)S(1)} %get-tuple-element.34), channel_id=1, source_target_pairs={{0,16},{8,24},{16,0},{24,8},{1,17},{9,25},{17,1},{25,9},{2,18},{10... | collective-permute-start | bytes 393224 | tf_op jit(solution)/shard_map/ppermute | solution.py:14
  35.7 0.7 copy-start.5
  36.3 11.5 %copy-start.1 = (bf16[1,512,512]{2,1,0:T(8,128)(2,1)S(1)}, bf16[1,512,512]{2,1,0:T(8,128)(2,1)}, u32[]{:S(2)}) copy-start(bf16[1,512,512]{2,1,0:T(8,128)(2,1)} %param.9) | copy-start | bytes 1572868
  36.3 11.5 %copy-start.3 = (f32[3,1,32,512]{3,2,1,0:T(8,128)S(1)}, f32[3,1,32,512]{3,2,1,0:T(8,128)}, u32[]{:S(2)}) copy-start(f32[3,1,32,512]{3,2,1,0:T(8,128)} %param.10) | copy-start | bytes 589828
  57.9 8.3 %collective-permute-start.6 = (bf16[128,512]{1,0:T(8,128)(2,1)S(1)}, bf16[128,512]{1,0:T(8,128)(2,1)S(1)}, u32[]{:S(2)}, u32[]{:S(2)}) collective-permute-start(bf16[128,512]{1,0:T(8,128)(2,1)S(1)} %get-tuple-element.32), channel_id=1, source_target_pairs={{0,8},{8,16},{16,24},{24,0},{1,9},{9,17},{17,25},{25,1},{2,10},{10... | collective-permute-start | bytes 393224 | tf_op jit(solution)/shard_map/ppermute | solution.py:14
  58.0 12.1 %collective-permute-start.7 = (bf16[128,512]{1,0:T(8,128)(2,1)S(1)}, bf16[128,512]{1,0:T(8,128)(2,1)S(1)}, u32[]{:S(2)}, u32[]{:S(2)}) collective-permute-start(bf16[128,512]{1,0:T(8,128)(2,1)S(1)} %get-tuple-element.31), channel_id=1, source_target_pairs={{0,16},{8,24},{16,0},{24,8},{1,17},{9,25},{17,1},{25,9},{2,18},{10... | collective-permute-start | bytes 393224 | tf_op jit(solution)/shard_map/ppermute | solution.py:14
  61.2 9.0 %collective-permute-start.8 = (bf16[128,512]{1,0:T(8,128)(2,1)S(1)}, bf16[128,512]{1,0:T(8,128)(2,1)S(1)}, u32[]{:S(2)}, u32[]{:S(2)}) collective-permute-start(bf16[128,512]{1,0:T(8,128)(2,1)S(1)} %get-tuple-element.30), channel_id=1, source_target_pairs={{0,24},{8,0},{16,8},{24,16},{1,25},{9,1},{17,9},{25,17},{2,26},{10... | collective-permute-start | bytes 393224 | tf_op jit(solution)/shard_map/ppermute | solution.py:14
  90.6 10.9 %collective-permute-start.10 = (bf16[128,512]{1,0:T(8,128)(2,1)S(1)}, bf16[128,512]{1,0:T(8,128)(2,1)S(1)}, u32[]{:S(2)}, u32[]{:S(2)}) collective-permute-start(bf16[128,512]{1,0:T(8,128)(2,1)S(1)} %get-tuple-element.27), channel_id=1, source_target_pairs={{0,16},{8,24},{16,0},{24,8},{1,17},{9,25},{17,1},{25,9},{2,18},{10... | collective-permute-start | bytes 393224 | tf_op jit(solution)/shard_map/ppermute | solution.py:14
  92.2 9.3 %collective-permute-start.11 = (bf16[128,512]{1,0:T(8,128)(2,1)S(1)}, bf16[128,512]{1,0:T(8,128)(2,1)S(1)}, u32[]{:S(2)}, u32[]{:S(2)}) collective-permute-start(bf16[128,512]{1,0:T(8,128)(2,1)S(1)} %get-tuple-element.26), channel_id=1, source_target_pairs={{0,24},{8,0},{16,8},{24,16},{1,25},{9,1},{17,9},{25,17},{2,26},{10... | collective-permute-start | bytes 393224 | tf_op jit(solution)/shard_map/ppermute | solution.py:14
  95.6 8.3 %collective-permute-start.9 = (bf16[128,512]{1,0:T(8,128)(2,1)S(1)}, bf16[128,512]{1,0:T(8,128)(2,1)S(1)}, u32[]{:S(2)}, u32[]{:S(2)}) collective-permute-start(bf16[128,512]{1,0:T(8,128)(2,1)S(1)} %get-tuple-element.28), channel_id=1, source_target_pairs={{0,8},{8,16},{16,24},{24,0},{1,9},{9,17},{17,25},{25,1},{2,10},{10... | collective-permute-start | bytes 393224 | tf_op jit(solution)/shard_map/ppermute | solution.py:14
  105.5 10.3 %all-to-all-start.5 = ((bf16[8,32,512]{2,1,0:T(8,128)(2,1)}), bf16[8,32,512]{2,1,0:T(8,128)(2,1)S(1)}, u32[]{:S(2)}, u32[]{:S(2)}) async-start(bf16[8,32,512]{2,1,0:T(8,128)(2,1)} %select_add_fusion.1), calls=%async_computation.5 | async-start | bytes 524288 | tf_op jit(solution)/shard_map/all_to_all | solution.py:94
  108.9 6.9 %copy-start.2 = (f32[3,1,32,512]{3,2,1,0:T(8,128)}, f32[3,1,32,512]{3,2,1,0:T(8,128)S(1)}, u32[]{:S(2)}) copy-start(f32[3,1,32,512]{3,2,1,0:T(8,128)S(1)} %bitcast_dynamic-update-slice_fusion) | copy-start | bytes 589828

commit v20 on v15

--- a/solution.py
+++ b/solution.py
@@ -79,18 +79,22 @@
             observer_local = late_lists[:, 1] % group_blocks
             delays_here = late_lists[:, 2]
             source_shift = (group_here - late_lists[:, 0] // group_blocks) % groups
+            live_here = (delays_here > 0)[None, :, None]
+            same_block = observer_local[None, :, None] == (slot_of_member // OWNERS)[:, None, None]
+            same_share = jnp.arange(OWNERS)[None, None, :] == (slot_of_member % OWNERS)[:, None, None]
+            to_member = live_here & same_block & same_share
         blocks_in = pick(received, source_shift)
         terms = jnp.einsum(
             "kes,kso->keo", blocks_in, tile_values, preferred_element_type=jnp.float32
         )
-        partial_sums = []
-        for block in range(group_blocks):
-            chosen = (observer_local == block) & (delays_here > 0)
-            partial_sums.append(
-                jnp.sum(jnp.where(chosen[:, None, None], terms, 0.0), axis=0)
-            )
-        slots = jnp.stack(partial_sums).astype(jnp.bfloat16).reshape(members, share, BLOCK)
-        sent = pick([slots[s] for s in range(members)], slot_of_member)
+        by_share = terms.reshape(terms.shape[0], OWNERS, share, BLOCK)
+        sent = None
+        for i in range(terms.shape[0]):
+            for q in range(OWNERS):
+                chosen = to_member[:, i, q, None, None]
+                term = jnp.where(chosen, by_share[i, q][None], 0.0)
+                sent = term if sent is None else sent + term
+        sent = sent.astype(jnp.bfloat16)
         got = lax.all_to_all(sent, "member", 0, 0, tiled=True)
         field = jnp.sum(got.astype(jnp.float32), axis=0)
         residual = (excitations[step, 0] - field).astype(jnp.bfloat16)

time: 112 us -> 113 us (level)
  other arithmetic: 5.28 us -> 6.56 us
    convert_element_type x0 -> x3, other arithmetic: none -> 2 us  [body(): sent = sent.astype(jnp.bfloat16)]
where the time goes in v20:
time: 113 us; the launch traced here: 112 us
  blocking collectives  47.7 us (42%)
  waiting for transfers between devices  29.1 us (26%)
  starting transfers between devices  23.6 us (21%)
  other arithmetic  6.56 us (6%)
  local copies, waits for them, and re-layouts  2.75 us (2%)
  matrix products  2.21 us (2%)
    all_to_all x3, blocking collectives, body(): got = lax.all_to_all(sent, 'member', 0, 0, tiled=True)  29 us
    ppermute x12, waiting for transfers between devices, shifted(): return lax.ppermute(x, axis, [(i, (i + k) % n) for i in range(n)])  28.5 us
    all_to_all x2, blocking collectives, body(): got = lax.all_to_all(spread, 'member', 0, 0, tiled=True)  18.7 us
    ppermute x12, starting transfers between devices, shifted(): return lax.ppermute(x, axis, [(i, (i + k) % n) for i in range(n)])  18.4 us
    all_to_all x1, starting transfers between devices, body(): hist_got = lax.all_to_all(spread_hist, 'member', 0, 0, tiled=True)  5.17 us
  transfers between devices with their start and end apart: 13, of which 9 were waited for; matrix products, arithmetic and copies ran while one was open for 2% of the time, Pallas kernels for 0%

profile of v20, /device:TPU:0, one launch (start us, length us, event | category | flops | bytes accessed | tf_op | source)
XLA Modules:
  0.0 112.2 jit_solution(13812916976933542184)
XLA Ops:
  0.0 1.8 %broadcast_in_dim.1355 = bf16[8,2,32,512]{3,2,1,0:T(8,128)(2,1)} broadcast(bf16[2,32,512]{2,1,0:T(8,128)(2,1)} %bitcast.326), dimensions={1,2,3} | broadcast | bytes 589824 | tf_op jit(solution)/shard_map/broadcast_in_dim | solution.py:43
  1.8 5.2 %all-to-all-start = ((bf16[8,2,32,512]{3,2,1,0:T(8,128)(2,1)}), bf16[8,2,32,512]{3,2,1,0:T(8,128)(2,1)S(1)}, u32[]{:S(2)}, u32[]{:S(2)}) async-start(bf16[8,2,32,512]{3,2,1,0:T(8,128)(2,1)} %broadcast_in_dim.1355), calls=%async_computation | async-start | bytes 1048576 | tf_op jit(solution)/shard_map/all_to_all | solution.py:44
  7.0 1.6 %collective-permute-start.2 = (s32[4,3]{1,0:T(4,128)}, s32[4,3]{1,0:T(4,128)S(1)}, u32[]{:S(2)}, u32[]{:S(2)}) collective-permute-start(s32[4,3]{1,0:T(4,128)} %param.7), channel_id=1, source_target_pairs={{0,8},{8,16},{16,24},{24,0},{1,9},{9,17},{17,25},{25,1},{2,10},{10... | collective-permute-start | bytes 152 | tf_op jit(solution)/shard_map/ppermute | solution.py:14
  8.6 2.6 %collective-permute-start.1 = (s32[4,3]{1,0:T(4,128)}, s32[4,3]{1,0:T(4,128)S(1)}, u32[]{:S(2)}, u32[]{:S(2)}) collective-permute-start(s32[4,3]{1,0:T(4,128)} %param.7), channel_id=1, source_target_pairs={{0,16},{8,24},{16,0},{24,8},{1,17},{9,25},{17,1},{25,9},{2,18},{10... | collective-permute-start | bytes 152 | tf_op jit(solution)/shard_map/ppermute | solution.py:14
  11.2 1.3 %collective-permute-start = (s32[4,3]{1,0:T(4,128)}, s32[4,3]{1,0:T(4,128)S(1)}, u32[]{:S(2)}, u32[]{:S(2)}) collective-permute-start(s32[4,3]{1,0:T(4,128)} %param.7), channel_id=1, source_target_pairs={{0,24},{8,0},{16,8},{24,16},{1,25},{9,1},{17,9},{25,17},{2,26},{10... | collective-permute-start | bytes 152 | tf_op jit(solution)/shard_map/ppermute | solution.py:14
  12.5 0.7 iota_compare_fusion.1
  13.3 1.7 %collective-permute-done = s32[4,3]{1,0:T(4,128)S(1)} collective-permute-done((s32[4,3]{1,0:T(4,128)}, s32[4,3]{1,0:T(4,128)S(1)}, u32[]{:S(2)}, u32[]{:S(2)}) %collective-permute-start) | collective-permute-done | bytes 80 | tf_op jit(solution)/shard_map/ppermute | solution.py:14
  15.0 0.7 pad_add_fusion
  16.1 0.6 all-to-all-done
  17.7 3.7 %collective-permute-start.3 = (bf16[128,512]{1,0:T(8,128)(2,1)S(1)}, bf16[128,512]{1,0:T(8,128)(2,1)S(1)}, u32[]{:S(2)}, u32[]{:S(2)}) collective-permute-start(bf16[128,512]{1,0:T(8,128)(2,1)S(1)} %get-tuple-element.76), channel_id=1, source_target_pairs={{0,24},{8,0},{16,8},{24,16},{1,25},{9,1},{17,9},{25,17},{2,26},{10... | collective-permute-start | bytes 393224 | tf_op jit(solution)/shard_map/ppermute | solution.py:14
  21.3 1.0 collective-permute-start.4
  22.3 2.5 %collective-permute-done.3 = bf16[128,512]{1,0:T(8,128)(2,1)S(1)} collective-permute-done((bf16[128,512]{1,0:T(8,128)(2,1)S(1)}, bf16[128,512]{1,0:T(8,128)(2,1)S(1)}, u32[]{:S(2)}, u32[]{:S(2)}) %collective-permute-start.3) | collective-permute-done | bytes 131104 | tf_op jit(solution)/shard_map/ppermute | solution.py:14
  25.5 5.7 %collective-permute-done.5 = bf16[128,512]{1,0:T(8,128)(2,1)S(1)} collective-permute-done((bf16[128,512]{1,0:T(8,128)(2,1)S(1)}, bf16[128,512]{1,0:T(8,128)(2,1)S(1)}, u32[]{:S(2)}, u32[]{:S(2)}) %collective-permute-start.5) | collective-permute-done | bytes 131104 | tf_op jit(solution)/shard_map/ppermute | solution.py:14
  31.9 0.7 add_convert_fusion.2
  32.5 10.3 %all_to_all.30 = bf16[8,32,512]{2,1,0:T(8,128)(2,1)S(1)} all-to-all(bf16[8,32,512]{2,1,0:T(8,128)(2,1)S(1)} %add_convert_fusion.2), channel_id=1, replica_groups=mesh['group'=4,'member'=8] {'member'}, dimensions={0} | all-to-all | bytes 524288 | tf_op jit(solution)/shard_map/all_to_all | solution.py:98
  43.1 9.3 %all_to_all.31 = bf16[8,32,512]{2,1,0:T(8,128)(2,1)S(1)} all-to-all(bf16[8,32,512]{2,1,0:T(8,128)(2,1)S(1)} %broadcast_in_dim.1487), channel_id=1, replica_groups=mesh['group'=4,'member'=8] {'member'}, dimensions={0} | all-to-all | bytes 524288 | tf_op jit(solution)/shard_map/all_to_all | solution.py:105
  53.0 1.5 %collective-permute-start.8 = (bf16[128,512]{1,0:T(8,128)(2,1)S(1)}, bf16[128,512]{1,0:T(8,128)(2,1)S(1)}, u32[]{:S(2)}, u32[]{:S(2)}) collective-permute-start(bf16[128,512]{1,0:T(8,128)(2,1)S(1)} %get-tuple-element.70), channel_id=1, source_target_pairs={{0,24},{8,0},{16,8},{24,16},{1,25},{9,1},{17,9},{25,17},{2,26},{10... | collective-permute-start | bytes 393224 | tf_op jit(solution)/shard_map/ppermute | solution.py:14
  54.5 1.1 %collective-permute-start.7 = (bf16[128,512]{1,0:T(8,128)(2,1)S(1)}, bf16[128,512]{1,0:T(8,128)(2,1)S(1)}, u32[]{:S(2)}, u32[]{:S(2)}) collective-permute-start(bf16[128,512]{1,0:T(8,128)(2,1)S(1)} %get-tuple-element.71), channel_id=1, source_target_pairs={{0,16},{8,24},{16,0},{24,8},{1,17},{9,25},{17,1},{25,9},{2,18},{10... | collective-permute-start | bytes 393224 | tf_op jit(solution)/shard_map/ppermute | solution.py:14
  55.6 1.9 %collective-permute-start.6 = (bf16[128,512]{1,0:T(8,128)(2,1)S(1)}, bf16[128,512]{1,0:T(8,128)(2,1)S(1)}, u32[]{:S(2)}, u32[]{:S(2)}) collective-permute-start(bf16[128,512]{1,0:T(8,128)(2,1)S(1)} %get-tuple-element.72), channel_id=1, source_target_pairs={{0,8},{8,16},{16,24},{24,0},{1,9},{9,17},{17,25},{25,1},{2,10},{10... | collective-permute-start | bytes 393224 | tf_op jit(solution)/shard_map/ppermute | solution.py:14
  57.6 1.2 %collective-permute-done.8 = bf16[128,512]{1,0:T(8,128)(2,1)S(1)} collective-permute-done((bf16[128,512]{1,0:T(8,128)(2,1)S(1)}, bf16[128,512]{1,0:T(8,128)(2,1)S(1)}, u32[]{:S(2)}, u32[]{:S(2)}) %collective-permute-start.8) | collective-permute-done | bytes 131104 | tf_op jit(solution)/shard_map/ppermute | solution.py:14
  58.8 8.1 %collective-permute-done.7 = bf16[128,512]{1,0:T(8,128)(2,1)S(1)} collective-permute-done((bf16[128,512]{1,0:T(8,128)(2,1)S(1)}, bf16[128,512]{1,0:T(8,128)(2,1)S(1)}, u32[]{:S(2)}, u32[]{:S(2)}) %collective-permute-start.7) | collective-permute-done | bytes 131104 | tf_op jit(solution)/shard_map/ppermute | solution.py:14
  67.5 0.7 add_convert_fusion.1
  68.1 9.3 %all_to_all.32 = bf16[8,32,512]{2,1,0:T(8,128)(2,1)S(1)} all-to-all(bf16[8,32,512]{2,1,0:T(8,128)(2,1)S(1)} %add_convert_fusion.1), channel_id=1, replica_groups=mesh['group'=4,'member'=8] {'member'}, dimensions={0} | all-to-all | bytes 524288 | tf_op jit(solution)/shard_map/all_to_all | solution.py:98
  77.8 9.3 %all_to_all.33 = bf16[8,32,512]{2,1,0:T(8,128)(2,1)S(1)} all-to-all(bf16[8,32,512]{2,1,0:T(8,128)(2,1)S(1)} %broadcast_in_dim.1553), channel_id=1, replica_groups=mesh['group'=4,'member'=8] {'member'}, dimensions={0} | all-to-all | bytes 524288 | tf_op jit(solution)/shard_map/all_to_all | solution.py:105
  87.7 1.6 %collective-permute-start.10 = (bf16[128,512]{1,0:T(8,128)(2,1)S(1)}, bf16[128,512]{1,0:T(8,128)(2,1)S(1)}, u32[]{:S(2)}, u32[]{:S(2)}) collective-permute-start(bf16[128,512]{1,0:T(8,128)(2,1)S(1)} %get-tuple-element.67), channel_id=1, source_target_pairs={{0,16},{8,24},{16,0},{24,8},{1,17},{9,25},{17,1},{25,9},{2,18},{10... | collective-permute-start | bytes 393224 | tf_op jit(solution)/shard_map/ppermute | solution.py:14
  89.4 1.9 %collective-permute-start.9 = (bf16[128,512]{1,0:T(8,128)(2,1)S(1)}, bf16[128,512]{1,0:T(8,128)(2,1)S(1)}, u32[]{:S(2)}, u32[]{:S(2)}) collective-permute-start(bf16[128,512]{1,0:T(8,128)(2,1)S(1)} %get-tuple-element.68), channel_id=1, source_target_pairs={{0,8},{8,16},{16,24},{24,0},{1,9},{9,17},{17,25},{25,1},{2,10},{10... | collective-permute-start | bytes 393224 | tf_op jit(solution)/shard_map/ppermute | solution.py:14
  91.3 1.9 %collective-permute-done.11 = bf16[128,512]{1,0:T(8,128)(2,1)S(1)} collective-permute-done((bf16[128,512]{1,0:T(8,128)(2,1)S(1)}, bf16[128,512]{1,0:T(8,128)(2,1)S(1)}, u32[]{:S(2)}, u32[]{:S(2)}) %collective-permute-start.11) | collective-permute-done | bytes 131104 | tf_op jit(solution)/shard_map/ppermute | solution.py:14
  93.2 7.4 %collective-permute-done.10 = bf16[128,512]{1,0:T(8,128)(2,1)S(1)} collective-permute-done((bf16[128,512]{1,0:T(8,128)(2,1)S(1)}, bf16[128,512]{1,0:T(8,128)(2,1)S(1)}, u32[]{:S(2)}, u32[]{:S(2)}) %collective-permute-start.10) | collective-permute-done | bytes 131104 | tf_op jit(solution)/shard_map/ppermute | solution.py:14
  100.6 0.6 fusion.5
  101.3 0.7 add_convert_fusion
  101.9 9.3 %all_to_all.34 = bf16[8,32,512]{2,1,0:T(8,128)(2,1)S(1)} all-to-all(bf16[8,32,512]{2,1,0:T(8,128)(2,1)S(1)} %add_convert_fusion), channel_id=1, replica_groups=mesh['group'=4,'member'=8] {'member'}, dimensions={0} | all-to-all | bytes 524288 | tf_op jit(solution)/shard_map/all_to_all | solution.py:98
  111.5 0.7 maximum_bitcast_fusion
  (62 shorter events, 5.2 us)
Async XLA Ops:
  0.0 31.2 %copy-start = (bf16[4,512,512]{2,1,0:T(8,128)(2,1)S(1)}, bf16[4,512,512]{2,1,0:T(8,128)(2,1)}, u32[]{:S(2)}) copy-start(bf16[4,512,512]{2,1,0:T(8,128)(2,1)} %param.6) | copy-start | bytes 6291460
  1.8 14.9 %all-to-all-start = ((bf16[8,2,32,512]{3,2,1,0:T(8,128)(2,1)}), bf16[8,2,32,512]{3,2,1,0:T(8,128)(2,1)S(1)}, u32[]{:S(2)}, u32[]{:S(2)}) async-start(bf16[8,2,32,512]{3,2,1,0:T(8,128)(2,1)} %broadcast_in_dim.1355), calls=%async_computation | async-start | bytes 1048576 | tf_op jit(solution)/shard_map/all_to_all | solution.py:44
  7.0 6.2 %collective-permute-start.2 = (s32[4,3]{1,0:T(4,128)}, s32[4,3]{1,0:T(4,128)S(1)}, u32[]{:S(2)}, u32[]{:S(2)}) collective-permute-start(s32[4,3]{1,0:T(4,128)} %param.7), channel_id=1, source_target_pairs={{0,8},{8,16},{16,24},{24,0},{1,9},{9,17},{17,25},{25,1},{2,10},{10... | collective-permute-start | bytes 152 | tf_op jit(solution)/shard_map/ppermute | solution.py:14
  8.6 4.7 %collective-permute-start.1 = (s32[4,3]{1,0:T(4,128)}, s32[4,3]{1,0:T(4,128)S(1)}, u32[]{:S(2)}, u32[]{:S(2)}) collective-permute-start(s32[4,3]{1,0:T(4,128)} %param.7), channel_id=1, source_target_pairs={{0,16},{8,24},{16,0},{24,8},{1,17},{9,25},{17,1},{25,9},{2,18},{10... | collective-permute-start | bytes 152 | tf_op jit(solution)/shard_map/ppermute | solution.py:14
  11.2 3.8 %collective-permute-start = (s32[4,3]{1,0:T(4,128)}, s32[4,3]{1,0:T(4,128)S(1)}, u32[]{:S(2)}, u32[]{:S(2)}) collective-permute-start(s32[4,3]{1,0:T(4,128)} %param.7), channel_id=1, source_target_pairs={{0,24},{8,0},{16,8},{24,16},{1,25},{9,1},{17,9},{25,17},{2,26},{10... | collective-permute-start | bytes 152 | tf_op jit(solution)/shard_map/ppermute | solution.py:14
  16.8 8.1 %copy-start.3 = (s32[4,3]{1,0:T(4,128)S(1)}, s32[4,3]{1,0:T(4,128)}, u32[]{:S(2)}) copy-start(s32[4,3]{1,0:T(4,128)} %param.7) | copy-start | bytes 148
  16.8 8.4 %copy-start.4 = (s32[1,8]{1,0:T(1,128)S(1)}, s32[1,8]{1,0:T(1,128)}, u32[]{:S(2)}) copy-start(s32[1,8]{1,0:T(1,128)} %param.8) | copy-start | bytes 100
  17.7 7.2 %collective-permute-start.3 = (bf16[128,512]{1,0:T(8,128)(2,1)S(1)}, bf16[128,512]{1,0:T(8,128)(2,1)S(1)}, u32[]{:S(2)}, u32[]{:S(2)}) collective-permute-start(bf16[128,512]{1,0:T(8,128)(2,1)S(1)} %get-tuple-element.76), channel_id=1, source_target_pairs={{0,24},{8,0},{16,8},{24,16},{1,25},{9,1},{17,9},{25,17},{2,26},{10... | collective-permute-start | bytes 393224 | tf_op jit(solution)/shard_map/ppermute | solution.py:14
  21.3 9.9 %collective-permute-start.5 = (bf16[128,512]{1,0:T(8,128)(2,1)S(1)}, bf16[128,512]{1,0:T(8,128)(2,1)S(1)}, u32[]{:S(2)}, u32[]{:S(2)}) collective-permute-start(bf16[128,512]{1,0:T(8,128)(2,1)S(1)} %get-tuple-element.74), channel_id=1, source_target_pairs={{0,16},{8,24},{16,0},{24,8},{1,17},{9,25},{17,1},{25,9},{2,18},{10... | collective-permute-start | bytes 393224 | tf_op jit(solution)/shard_map/ppermute | solution.py:14
  21.3 9.9 %collective-permute-start.4 = (bf16[128,512]{1,0:T(8,128)(2,1)S(1)}, bf16[128,512]{1,0:T(8,128)(2,1)S(1)}, u32[]{:S(2)}, u32[]{:S(2)}) collective-permute-start(bf16[128,512]{1,0:T(8,128)(2,1)S(1)} %get-tuple-element.75), channel_id=1, source_target_pairs={{0,8},{8,16},{16,24},{24,0},{1,9},{9,17},{17,25},{25,1},{2,10},{10... | collective-permute-start | bytes 393224 | tf_op jit(solution)/shard_map/ppermute | solution.py:14
  31.7 11.1 %copy-start.1 = (bf16[1,512,512]{2,1,0:T(8,128)(2,1)S(1)}, bf16[1,512,512]{2,1,0:T(8,128)(2,1)}, u32[]{:S(2)}) copy-start(bf16[1,512,512]{2,1,0:T(8,128)(2,1)} %param.9) | copy-start | bytes 1572868
  31.8 11.1 %copy-start.2 = (f32[3,1,32,512]{3,2,1,0:T(8,128)S(1)}, f32[3,1,32,512]{3,2,1,0:T(8,128)}, u32[]{:S(2)}) copy-start(f32[3,1,32,512]{3,2,1,0:T(8,128)} %param.10) | copy-start | bytes 589828
  53.0 5.7 %collective-permute-start.8 = (bf16[128,512]{1,0:T(8,128)(2,1)S(1)}, bf16[128,512]{1,0:T(8,128)(2,1)S(1)}, u32[]{:S(2)}, u32[]{:S(2)}) collective-permute-start(bf16[128,512]{1,0:T(8,128)(2,1)S(1)} %get-tuple-element.70), channel_id=1, source_target_pairs={{0,24},{8,0},{16,8},{24,16},{1,25},{9,1},{17,9},{25,17},{2,26},{10... | collective-permute-start | bytes 393224 | tf_op jit(solution)/shard_map/ppermute | solution.py:14
  54.5 12.3 %collective-permute-start.7 = (bf16[128,512]{1,0:T(8,128)(2,1)S(1)}, bf16[128,512]{1,0:T(8,128)(2,1)S(1)}, u32[]{:S(2)}, u32[]{:S(2)}) collective-permute-start(bf16[128,512]{1,0:T(8,128)(2,1)S(1)} %get-tuple-element.71), channel_id=1, source_target_pairs={{0,16},{8,24},{16,0},{24,8},{1,17},{9,25},{17,1},{25,9},{2,18},{10... | collective-permute-start | bytes 393224 | tf_op jit(solution)/shard_map/ppermute | solution.py:14
  55.6 11.2 %collective-permute-start.6 = (bf16[128,512]{1,0:T(8,128)(2,1)S(1)}, bf16[128,512]{1,0:T(8,128)(2,1)S(1)}, u32[]{:S(2)}, u32[]{:S(2)}) collective-permute-start(bf16[128,512]{1,0:T(8,128)(2,1)S(1)} %get-tuple-element.72), channel_id=1, source_target_pairs={{0,8},{8,16},{16,24},{24,0},{1,9},{9,17},{17,25},{25,1},{2,10},{10... | collective-permute-start | bytes 393224 | tf_op jit(solution)/shard_map/ppermute | solution.py:14
  87.7 5.5 %collective-permute-start.11 = (bf16[128,512]{1,0:T(8,128)(2,1)S(1)}, bf16[128,512]{1,0:T(8,128)(2,1)S(1)}, u32[]{:S(2)}, u32[]{:S(2)}) collective-permute-start(bf16[128,512]{1,0:T(8,128)(2,1)S(1)} %get-tuple-element.66), channel_id=1, source_target_pairs={{0,24},{8,0},{16,8},{24,16},{1,25},{9,1},{17,9},{25,17},{2,26},{10... | collective-permute-start | bytes 393224 | tf_op jit(solution)/shard_map/ppermute | solution.py:14
  87.7 12.8 %collective-permute-start.10 = (bf16[128,512]{1,0:T(8,128)(2,1)S(1)}, bf16[128,512]{1,0:T(8,128)(2,1)S(1)}, u32[]{:S(2)}, u32[]{:S(2)}) collective-permute-start(bf16[128,512]{1,0:T(8,128)(2,1)S(1)} %get-tuple-element.67), channel_id=1, source_target_pairs={{0,16},{8,24},{16,0},{24,8},{1,17},{9,25},{17,1},{25,9},{2,18},{10... | collective-permute-start | bytes 393224 | tf_op jit(solution)/shard_map/ppermute | solution.py:14
  89.4 11.2 %collective-permute-start.9 = (bf16[128,512]{1,0:T(8,128)(2,1)S(1)}, bf16[128,512]{1,0:T(8,128)(2,1)S(1)}, u32[]{:S(2)}, u32[]{:S(2)}) collective-permute-start(bf16[128,512]{1,0:T(8,128)(2,1)S(1)} %get-tuple-element.68), channel_id=1, source_target_pairs={{0,8},{8,16},{16,24},{24,0},{1,9},{9,17},{17,25},{25,1},{2,10},{10... | collective-permute-start | bytes 393224 | tf_op jit(solution)/shard_map/ppermute | solution.py:14
